TPU v7x, 32 devices: a whole 2x2x4 slice. The times are simulated.
32 devices in a mesh: groups: 2 (over y), seq: 4 (over z), head: 4 (over x, core).
Axes of the slice: x: 2, y: 2, z: 4, core: 2. Of those that a mesh axis runs over, the one named last changes fastest.
Arguments:
- frames: bfloat16 [16384, 1024], P(('groups', 'seq')), parts along dimension 0, may hold values from -14 to 14
- latents: bfloat16 [1024, 1024], replicated, may hold values from -12 to 12
- lengths: int32 [2], P('groups'), parts along dimension 0, may hold values from 4096 to 8192
- w_query: bfloat16 [1024, 1024], P(None, 'head'), may hold values from -0.1875 to 0.1875
- w_key: bfloat16 [1024, 1024], P(None, 'head'), may hold values from -0.1875 to 0.1875
- w_value: bfloat16 [1024, 1024], P(None, 'head'), may hold values from -0.1875 to 0.1875
- w_out: bfloat16 [1024, 1024], P('head'), may hold values from -0.1875 to 0.1875
- w_latent_query: bfloat16 [1024, 1024], P(None, 'head'), may hold values from -0.1875 to 0.1875
- w_latent_out: bfloat16 [1024, 1024], P('head'), may hold values from -0.1875 to 0.1875
Outputs:
- frames_out: bfloat16 [16384, 1024], P(('groups', 'seq'), 'head'), parts along dimension 0
- latents_out: bfloat16 [2048, 1024], P(('groups', 'seq'), 'head'), parts along dimension 0
There are 2 independent parts, one for each index of `groups`. A program takes and returns all parts, laid end to end along the dimension named above; an argument that names none is the same for every part. Nothing has to cross between parts.
All inputs are finite; a program needn't handle non-finite values.
Results may differ from a plain program's by a relative error of at most 0.04.
Values may be sent and summed in bfloat16 or wider, within the bound.
No kernel may reach another device: no remote copies, remote signals or barrier semaphores. Data moves between devices by JAX's collectives and lax.ppermute only.
A program may use at most 128 MiB of HBM per device.

v0:
```python
import jax
import jax.numpy as jnp
from jax import lax
from jax.sharding import PartitionSpec as P

HD = 64
HALF = 256


def extended(block, sides, width):
    for axis, dim in sides:
        count = lax.axis_size(axis)
        forward = [(i, i + 1) for i in range(count - 1)]
        backward = [(target, source) for source, target in forward]
        low = lax.ppermute(
            lax.slice_in_dim(block, block.shape[dim] - width, None, axis=dim), axis, forward
        )
        high = lax.ppermute(lax.slice_in_dim(block, 0, width, axis=dim), axis, backward)
        block = jnp.concatenate([low, block, high], axis=dim)
    return block


def combined_all(value, axis, combine):
    everything = jax.tree.map(
        lambda part, kind: lax.all_gather(part.astype(kind), axis),
        value,
        (jnp.bfloat16, jnp.bfloat16, jnp.bfloat16),
    )

    def take(k):
        return jax.tree.map(lambda part, own: part[k].astype(own.dtype), everything, value)

    return lax.fori_loop(
        1, lax.axis_size(axis), lambda k, so_far: combine(so_far, take(k)), take(0)
    )


def project(source, weight):
    return jnp.dot(source, weight, preferred_element_type=jnp.float32).astype(jnp.bfloat16)


def combine(earlier, latter):
    peak_first, total_first, accum_first = earlier
    peak_second, total_second, accum_second = latter
    joint = jnp.maximum(peak_first, peak_second)
    factor_first = jnp.exp(peak_first - joint)
    factor_second = jnp.exp(peak_second - joint)
    summed_total = total_first * factor_first + total_second * factor_second
    summed_accum = accum_first * jnp.repeat(factor_first, HD, axis=1) + accum_second * jnp.repeat(
        factor_second, HD, axis=1
    )
    return (joint, summed_total, summed_accum)


def per_device(
    frames, latents, lengths, w_query, w_key, w_value, w_out, w_latent_query, w_latent_out
):
    frame_count = frames.shape[0]
    head_width = w_query.shape[1]
    heads_here = head_width // HD
    seq_devices = lax.axis_size("seq")
    seq_place = lax.axis_index("seq")
    first_frame = seq_place * frame_count
    length = lengths[0]
    query = project(frames, w_query)
    keyed = project(frames, w_key)
    valued = project(frames, w_value)
    stacked = jnp.concatenate([keyed, valued], axis=1)
    padded = extended(stacked, (("seq", 0),), HALF)
    keys_wide = padded[:, :head_width]
    values_wide = padded[:, head_width:]
    score_scale = HD ** (-0.5)
    block_size = min(512, frame_count)
    block_count = frame_count // block_size
    span = block_size + 2 * HALF
    offsets = jnp.arange(span)[None, :] - jnp.arange(block_size)[:, None]
    in_window = (offsets >= 0) & (offsets <= 2 * HALF)

    def window_block(block_index):
        row_first = block_index * block_size
        query_block = lax.dynamic_slice_in_dim(query, row_first, block_size, 0).reshape(
            block_size, heads_here, HD
        )
        key_block = lax.dynamic_slice_in_dim(keys_wide, row_first, span, 0).reshape(
            span, heads_here, HD
        )
        value_block = lax.dynamic_slice_in_dim(values_wide, row_first, span, 0).reshape(
            span, heads_here, HD
        )
        scores = (
            jnp.einsum("qhd,khd->hqk", query_block, key_block, preferred_element_type=jnp.float32)
            * score_scale
        )
        key_pos = first_frame + row_first - HALF + jnp.arange(span)
        key_valid = (key_pos >= 0) & (key_pos < length)
        allowed = in_window & key_valid[None, :]
        masked = jnp.where(allowed[None], scores, -1e30)
        row_peak = jnp.max(masked, axis=2, keepdims=True)
        weights = jnp.where(allowed[None], jnp.exp(masked - row_peak), 0.0)
        denom = jnp.sum(weights, axis=2)
        blended = jnp.einsum(
            "hqk,khd->qhd",
            weights.astype(jnp.bfloat16),
            value_block,
            preferred_element_type=jnp.float32,
        )
        query_pos = first_frame + row_first + jnp.arange(block_size)
        query_valid = query_pos < length
        divisor = jnp.where(query_valid[None, :], denom, 1.0)
        normed = blended / divisor.T[:, :, None]
        return (
            jnp.where(query_valid[:, None, None], normed, 0.0)
            .astype(jnp.bfloat16)
            .reshape(block_size, head_width)
        )

    attended = lax.map(window_block, jnp.arange(block_count)).reshape(frame_count, head_width)
    frame_terms = jnp.dot(attended, w_out, preferred_element_type=jnp.float32)
    frames_out = lax.psum_scatter(
        frame_terms.astype(jnp.bfloat16), "head", scatter_dimension=1, tiled=True
    )
    latent_count = latents.shape[0]
    latent_query = project(latents, w_latent_query).reshape(latent_count, heads_here, HD)
    latent_scores = (
        jnp.einsum(
            "lhd,thd->hlt",
            latent_query,
            keyed.reshape(frame_count, heads_here, HD),
            preferred_element_type=jnp.float32,
        )
        * score_scale
    )
    frame_valid = first_frame + jnp.arange(frame_count) < length
    masked_latent = jnp.where(frame_valid[None, None, :], latent_scores, -1e30)
    local_peak = jnp.max(masked_latent, axis=2)
    latent_weights = jnp.where(
        frame_valid[None, None, :], jnp.exp(masked_latent - local_peak[:, :, None]), 0.0
    )
    local_total = jnp.sum(latent_weights, axis=2)
    local_accum = jnp.einsum(
        "hlt,thd->lhd",
        latent_weights.astype(jnp.bfloat16),
        valued.reshape(frame_count, heads_here, HD),
        preferred_element_type=jnp.float32,
    ).reshape(latent_count, head_width)
    peaks = local_peak.T
    totals = local_total.T
    rows_here = latent_count // seq_devices
    merged_peak, merged_total, merged_accum = combined_all(
        (peaks, totals, local_accum), "seq", combine
    )
    own_total = lax.dynamic_slice_in_dim(merged_total, seq_place * rows_here, rows_here, 0)
    own_accum = lax.dynamic_slice_in_dim(merged_accum, seq_place * rows_here, rows_here, 0)
    summary = (own_accum / jnp.repeat(own_total, HD, axis=1)).astype(jnp.bfloat16)
    latent_terms = jnp.dot(summary, w_latent_out, preferred_element_type=jnp.float32)
    latents_out = lax.psum_scatter(
        latent_terms.astype(jnp.bfloat16), "head", scatter_dimension=1, tiled=True
    )
    return (frames_out, latents_out)


def solution(mesh):
    return jax.shard_map(
        per_device,
        mesh=mesh,
        in_specs=(
            P(("groups", "seq"), None),
            P(),
            P("groups"),
            P(None, "head"),
            P(None, "head"),
            P(None, "head"),
            P("head", None),
            P(None, "head"),
            P("head", None),
        ),
        out_specs=(P(("groups", "seq"), "head"), P(("groups", "seq"), "head")),
        check_vma=False,
    )
```

profile of v0, /device:TPU:0, one launch (start us, length us, event | category | flops | bytes accessed | tf_op | source)
XLA Modules:
  0.0 229.5 jit_solution(4307274114849628718)
XLA Ops:
  7.2 3.7 %convolution_convert_fusion.3 = bf16[2048,256]{0,1:T(8,128)(2,1)S(1)} fusion(bf16[2048,1024]{1,0:T(8,128)(2,1)} %param.13, bf16[1024,256]{1,0:T(8,128)(2,1)} %param.17), kind=kOutput, calls=%fused_computation.53 | convolution fusion | flops 1074266112 | bytes 5767168 | tf_op jit(solution)/shard_map/dot_general | solution.py:39
  11.1 1.3 convolution_convert_fusion.2
  14.2 4.9 %collective-permute-start = (bf16[256,512]{0,1:T(8,128)(2,1)}, bf16[256,512]{0,1:T(8,128)(2,1)S(1)}, u32[]{:S(2)}, u32[]{:S(2)}) collective-permute-start(bf16[256,512]{0,1:T(8,128)(2,1)} %get-tuple-element.384), channel_id=1, source_target_pairs={{0,4},{4,8},{8,12},{1,5},{5,9},{9,13},{2,6},{6,10},{10,14},{3,7},{... | collective-permute-start | bytes 786440 | tf_op jit(solution)/shard_map/ppermute | solution.py:15
  19.1 1.3 collective-permute-start.1
  21.1 1.8 convolution_convert_fusion.5
  22.9 13.3 %fusion.35 = (f32[4,1024]{1,0:T(4,128)S(1)}, f32[4,1024,2048]{2,1,0:T(8,128)}) fusion(pred[2048]{0:T(1024)(128)(4,1)S(1)} %add_compare_fusion.1, bf16[1024,4,64]{0,2,1:T(8,128)(2,1)S(1)} %bitcast.115, bf16[2048,4,64]{0,2,1:T(8,128)(2,1)S(1)} %bitcast.111), kind=kOutput, calls=%fused_computation.44 | convolution fusion | flops 1098903552 | bytes 35145728 | tf_op jit(solution)/shard_map/lhd,thd->hlt/dot_general | solution.py:125
  36.2 14.1 %fusion.41 = bf16[4,64,1024]{2,1,0:T(8,128)(2,1)S(1)} fusion(bf16[2048,4,64]{0,2,1:T(8,128)(2,1)S(1)} %bitcast.114, f32[4,1024,2048]{2,1,0:T(8,128)} %get-tuple-element.387, f32[4,1024]{1,0:T(4,128)S(1)} %get-tuple-element.386, pred[2048]{0:T(1024)(128)(4,1)S(1)} %add_compare_fusion.1), kind=kOutput, calls=%fused_computation.54 | convolution fusion | flops 1115947008 | bytes 35145728 | tf_op jit(solution)/shard_map/hlt,thd->lhd/dot_general | solution.py:140
  51.4 15.6 %fusion.37 = bf16[4,1024]{1,0:T(4,128)(2,1)S(1)} fusion(f32[4,1024,2048]{2,1,0:T(8,128)} %get-tuple-element.387, f32[4,1024]{1,0:T(4,128)S(1)} %get-tuple-element.386, pred[2048]{0:T(1024)(128)(4,1)S(1)} %add_compare_fusion.1), kind=kLoop, calls=%fused_computation.46 | loop fusion | flops 41938944 | bytes 33581056 | tf_op jit(solution)/shard_map/reduce_sum | solution.py:139
  67.1 15.2 %all-gather.1 = bf16[4096,4]{0,1:T(4,128)(2,1)S(1)} all-gather(bf16[1024,4]{0,1:T(4,128)(2,1)S(1)} %bitcast.119), channel_id=3, replica_groups=mesh['groups'=2,'seq'=4,'head'=4] {'seq'}, dimensions={0}, use_global_device_ids=true | all-gather | bytes 40960 | tf_op jit(solution)/shard_map/all_gather | solution.py:25
  82.3 2.3 convolution_convert_fusion.1
  84.6 13.3 %all-gather = bf16[4096,4]{0,1:T(4,128)(2,1)S(1)} all-gather(bf16[1024,4]{0,1:T(4,128)(2,1)S(1)} %convert_bitcast_fusion.1), channel_id=2, replica_groups=mesh['groups'=2,'seq'=4,'head'=4] {'seq'}, dimensions={0}, use_global_device_ids=true | all-gather | bytes 40960 | tf_op jit(solution)/shard_map/all_gather | solution.py:25
  97.9 2.8 %pad_maximum_fusion = bf16[2560,512]{0,1:T(8,128)(2,1)S(1)} fusion(bf16[256,512]{0,1:T(8,128)(2,1)} %collective-permute-done.1, bf16[2048,256]{0,1:T(8,128)(2,1)S(1)} %copy-done.3, bf16[2048,256]{0,1:T(8,128)(2,1)S(1)} %convolution_convert_fusion.3, bf16[256,512]{0,1:T(8,128)(2,1)S(1)} %collective-permute-done), kind=kLoop, calls=%fused_computation.50 | loop fusion | flops 10485760 | bytes 5242880 | tf_op jit(solution)/shard_map/concatenate | solution.py:19
  100.8 1.3 fusion.51
  102.0 1.1 fusion.44
  103.5 5.6 %while.32 = (s32[]{:T(128)}, f32[1024,4]{0,1:T(4,128)S(1)}, f32[1024,4]{0,1:T(4,128)S(1)}, f32[1024,256]{0,1:T(8,128)S(1)}, bf16[4,1024,4]{1,2,0:T(4,128)(2,1)S(...) while((s32[]{:T(128)}, f32[1024,4]{0,1:T(4,128)S(1)}, ...), condition=%wide.region_8.9_spmd, body=%wide.region_7.8_spmd.sunk | while | flops 1081349 | bytes 4866191 | solution.py:33
  103.5 1.1 constant_dynamic-slice_fusion.8
  109.1 2.2 convolution_convert_fusion.4
  111.4 60.7 %while.33 = (s32[]{:T(128)}, bf16[4,512,256]{2,1,0:T(8,128)(2,1)}, s32[4]{0:T(128)S(1)}, s32[]{:T(128)}, s32[]{:T(128)}, /*index=5*/bf16[2560,256]{0,1:T(8,128)(...) while((s32[]{:T(128)}, bf16[4,512,256]{2,1,0:T(8,128)(2,1)}, ...), condition=%wide.region_3.4_spmd.clone, body=%wide.region_0.3_spmd.clone.sunk | while | flops 552476672 | bytes 15240980 | solution.py:117
  115.3 1.2 constant_dynamic-slice_fusion.9
  116.5 5.6 %fusion.91 = (f32[4,512]{1,0:T(4,128)S(1)}, bf16[4,512,1024]{2,1,0:T(8,128)(2,1)}) fusion(pred[512,1024]{1,0:T(8,128)(4,1)S(1)} %fusion.90, bf16[512,4,64]{0,2,1:T(8,128)(2,1)S(1)} %bitcast.112, bf16[1024,4,64]{0,2,1:T(8,128)(2,1)S(1)} %bitcast.110), kind=kOutput, calls=%fused_computation.72.clone.1 | convolution fusion | flops 281019392 | bytes 5513216 | tf_op jit(solution)/shard_map/while/body/eval_jaxpr/sub | solution.py:99
  122.1 3.6 %fusion.92 = bf16[512,4,64]{0,2,1:T(8,128)(2,1)S(1)} fusion(bf16[1024,4,64]{0,2,1:T(8,128)(2,1)S(1)} %bitcast.109, bf16[4,512,1024]{2,1,0:T(8,128)(2,1)} %get-tuple-element.496, f32[512,4]{0,1:T(4,128)S(1)} %select_bitcast_fusion.2, pred[512]{0:T(512)(128)(4,1)S(1)} %add_compare_fusion.3), kind=kOutput, calls=%fused_computation.28.clone.1 | convolution fusion | flops 268828672 | bytes 4989440 | tf_op jit(solution)/shard_map/while/body/eval_jaxpr/hqk,khd->qhd/dot_general | solution.py:101
  130.5 1.2 constant_dynamic-slice_fusion.9
  131.7 5.6 %fusion.91 = (f32[4,512]{1,0:T(4,128)S(1)}, bf16[4,512,1024]{2,1,0:T(8,128)(2,1)}) fusion(pred[512,1024]{1,0:T(8,128)(4,1)S(1)} %fusion.90, bf16[512,4,64]{0,2,1:T(8,128)(2,1)S(1)} %bitcast.112, bf16[1024,4,64]{0,2,1:T(8,128)(2,1)S(1)} %bitcast.110), kind=kOutput, calls=%fused_computation.72.clone.1 | convolution fusion | flops 281019392 | bytes 5513216 | tf_op jit(solution)/shard_map/while/body/eval_jaxpr/sub | solution.py:99
  137.3 3.6 %fusion.92 = bf16[512,4,64]{0,2,1:T(8,128)(2,1)S(1)} fusion(bf16[1024,4,64]{0,2,1:T(8,128)(2,1)S(1)} %bitcast.109, bf16[4,512,1024]{2,1,0:T(8,128)(2,1)} %get-tuple-element.496, f32[512,4]{0,1:T(4,128)S(1)} %select_bitcast_fusion.2, pred[512]{0:T(512)(128)(4,1)S(1)} %add_compare_fusion.3), kind=kOutput, calls=%fused_computation.28.clone.1 | convolution fusion | flops 268828672 | bytes 4989440 | tf_op jit(solution)/shard_map/while/body/eval_jaxpr/hqk,khd->qhd/dot_general | solution.py:101
  145.7 1.2 constant_dynamic-slice_fusion.9
  146.9 5.6 %fusion.91 = (f32[4,512]{1,0:T(4,128)S(1)}, bf16[4,512,1024]{2,1,0:T(8,128)(2,1)}) fusion(pred[512,1024]{1,0:T(8,128)(4,1)S(1)} %fusion.90, bf16[512,4,64]{0,2,1:T(8,128)(2,1)S(1)} %bitcast.112, bf16[1024,4,64]{0,2,1:T(8,128)(2,1)S(1)} %bitcast.110), kind=kOutput, calls=%fused_computation.72.clone.1 | convolution fusion | flops 281019392 | bytes 5513216 | tf_op jit(solution)/shard_map/while/body/eval_jaxpr/sub | solution.py:99
  152.5 3.6 %fusion.92 = bf16[512,4,64]{0,2,1:T(8,128)(2,1)S(1)} fusion(bf16[1024,4,64]{0,2,1:T(8,128)(2,1)S(1)} %bitcast.109, bf16[4,512,1024]{2,1,0:T(8,128)(2,1)} %get-tuple-element.496, f32[512,4]{0,1:T(4,128)S(1)} %select_bitcast_fusion.2, pred[512]{0:T(512)(128)(4,1)S(1)} %add_compare_fusion.3), kind=kOutput, calls=%fused_computation.28.clone.1 | convolution fusion | flops 268828672 | bytes 4989440 | tf_op jit(solution)/shard_map/while/body/eval_jaxpr/hqk,khd->qhd/dot_general | solution.py:101
  160.9 1.2 constant_dynamic-slice_fusion.9
  162.0 5.6 %fusion.91 = (f32[4,512]{1,0:T(4,128)S(1)}, bf16[4,512,1024]{2,1,0:T(8,128)(2,1)}) fusion(pred[512,1024]{1,0:T(8,128)(4,1)S(1)} %fusion.90, bf16[512,4,64]{0,2,1:T(8,128)(2,1)S(1)} %bitcast.112, bf16[1024,4,64]{0,2,1:T(8,128)(2,1)S(1)} %bitcast.110), kind=kOutput, calls=%fused_computation.72.clone.1 | convolution fusion | flops 281019392 | bytes 5513216 | tf_op jit(solution)/shard_map/while/body/eval_jaxpr/sub | solution.py:99
  167.7 3.6 %fusion.92 = bf16[512,4,64]{0,2,1:T(8,128)(2,1)S(1)} fusion(bf16[1024,4,64]{0,2,1:T(8,128)(2,1)S(1)} %bitcast.109, bf16[4,512,1024]{2,1,0:T(8,128)(2,1)} %get-tuple-element.496, f32[512,4]{0,1:T(4,128)S(1)} %select_bitcast_fusion.2, pred[512]{0:T(512)(128)(4,1)S(1)} %add_compare_fusion.3), kind=kOutput, calls=%fused_computation.28.clone.1 | convolution fusion | flops 268828672 | bytes 4989440 | tf_op jit(solution)/shard_map/while/body/eval_jaxpr/hqk,khd->qhd/dot_general | solution.py:101
  172.1 4.7 %convolution_convert_fusion = bf16[2048,1024]{1,0:T(8,128)(2,1)} fusion(bf16[2048,256]{1,0:T(8,128)(2,1)} %bitcast.7, bf16[256,1024]{1,0:T(8,128)(2,1)} %param.19), kind=kOutput, calls=%fused_computation.49 | convolution fusion | flops 1075838976 | bytes 5767168 | tf_op jit(solution)/shard_map/dot_general | solution.py:118
  176.9 46.1 %reduce-scatter.3.cloned.1.call-done = bf16[2048,256]{1,0:T(8,128)(2,1)} async-done(((bf16[2048,1024]{1,0:T(8,128)(2,1)}), bf16[2048,256]{1,0:T(8,128)(2,1)}) %reduce-scatter.3.cloned.1.call-update) | async-done | bytes 1048592 | tf_op jit(solution)/shard_map/reduce_scatter | solution.py:119
  (84 shorter events, 24.4 us)
Async XLA Ops:
  7.2 13.9 %copy-start = (bf16[1024,1024]{1,0:T(8,128)(2,1)S(1)}, bf16[1024,1024]{1,0:T(8,128)(2,1)}, u32[]{:S(2)}) copy-start(bf16[1024,1024]{1,0:T(8,128)(2,1)} %param.14) | copy-start | bytes 6291460
  7.2 94.8 %all-gather.4.cloned.1.call-start = ((), (), s32[]{:S(2)}) async-start(), calls=%async_computation.3 | async-start | bytes 2621440 | tf_op jit(solution)/shard_map/all_gather | solution.py:25
  7.2 3.8 %copy-start.4 = (bf16[2048,1024]{1,0:T(8,128)(2,1)S(1)}, bf16[2048,1024]{1,0:T(8,128)(2,1)}, u32[]{:S(2)}) copy-start(bf16[2048,1024]{1,0:T(8,128)(2,1)} %param.13) | copy-start | bytes 12582916
  7.2 3.9 %copy-start.6 = (bf16[1024,256]{1,0:T(8,128)(2,1)S(1)}, bf16[1024,256]{1,0:T(8,128)(2,1)}, u32[]{:S(2)}) copy-start(bf16[1024,256]{1,0:T(8,128)(2,1)} %param.18) | copy-start | bytes 1572868
  12.4 1.0 copy-start.2
  14.2 83.7 %collective-permute-start = (bf16[256,512]{0,1:T(8,128)(2,1)}, bf16[256,512]{0,1:T(8,128)(2,1)S(1)}, u32[]{:S(2)}, u32[]{:S(2)}) collective-permute-start(bf16[256,512]{0,1:T(8,128)(2,1)} %get-tuple-element.384), channel_id=1, source_target_pairs={{0,4},{4,8},{8,12},{1,5},{5,9},{9,13},{2,6},{6,10},{10,14},{3,7},{... | collective-permute-start | bytes 786440 | tf_op jit(solution)/shard_map/ppermute | solution.py:15
  19.1 78.8 %collective-permute-start.1 = (bf16[256,512]{0,1:T(8,128)(2,1)}, bf16[256,512]{0,1:T(8,128)(2,1)}, u32[]{:S(2)}, u32[]{:S(2)}) collective-permute-start(bf16[256,512]{0,1:T(8,128)(2,1)} %get-tuple-element.385), channel_id=1, source_target_pairs={{4,0},{8,4},{12,8},{5,1},{9,5},{13,9},{6,2},{10,6},{14,10},{7,3},{... | collective-permute-start | bytes 786440 | tf_op jit(solution)/shard_map/ppermute | solution.py:18
  22.9 13.3 %copy-start.3 = (bf16[2048,256]{0,1:T(8,128)(2,1)S(1)}, bf16[2048,256]{0,1:T(8,128)(2,1)}, u32[]{:S(2)}) copy-start(bf16[2048,256]{0,1:T(8,128)(2,1)} %copy-done.2) | copy-start | bytes 3145732
  51.4 30.9 %copy-start.7 = (bf16[1024,256]{1,0:T(8,128)(2,1)S(1)}, bf16[1024,256]{1,0:T(8,128)(2,1)}, u32[]{:S(2)}) copy-start(bf16[1024,256]{1,0:T(8,128)(2,1)} %param.16) | copy-start | bytes 1572868
  51.4 125.5 %reduce-scatter.5.cloned.1.call-start = ((), (), s32[]{:S(2)}) async-start(), calls=%async_computation.4 | async-start | bytes 655360 | tf_op jit(solution)/shard_map/reduce_scatter | solution.py:156
  51.4 30.9 %copy-start.5 = (bf16[2048,1024]{1,0:T(8,128)(2,1)S(1)}, bf16[2048,1024]{1,0:T(8,128)(2,1)}, u32[]{:S(2)}) copy-start(bf16[2048,1024]{1,0:T(8,128)(2,1)} %param.13) | copy-start | bytes 12582916
  111.3 111.6 %reduce-scatter.3.cloned.1.call-start = ((), (), s32[]{:S(2)}) async-start(), calls=%async_computation.2 | async-start | bytes 5242880 | tf_op jit(solution)/shard_map/reduce_scatter | solution.py:119
  172.1 50.8 %copy-start.1 = (bf16[1024,1024]{1,0:T(8,128)(2,1)S(1)}, bf16[1024,1024]{1,0:T(8,128)(2,1)}, u32[]{:S(2)}) copy-start(bf16[1024,1024]{1,0:T(8,128)(2,1)} %param.14) | copy-start | bytes 6291460
Sparse Core Ops, SparseCore 0:
  51.5 49.9 all-gather.3
  111.5 23.0 reduce-scatter.4
  177.0 45.9 reduce-scatter.2
where the time goes:
time: 231 us; the launch traced here: 229 us
  matrix products  80.2 us (35%)
  waiting for transfers between devices  46.2 us (20%)
  blocking collectives  28.5 us (12%)
  other arithmetic  28.1 us (12%)
  local copies, waits for them, and re-layouts  22.7 us (10%)
  between operations  14.6 us (6%)
  starting transfers between devices  6.34 us (3%)
  loops' own time  2.87 us (1%)
    reduce_scatter x1, waiting for transfers between devices, per_device(): lax.psum_scatter(frame_terms.astype(jnp.bfloat16), 'head', scatter_dimens...  46.1 us
    all_gather x2, blocking collectives, combined_all(): lax.all_gather(part.astype(kind), axis)  28.5 us
    sub x4, matrix products, window_block(): weights = jnp.where(allowed[None], jnp.exp(masked - row_peak), 0.0)  22.5 us
    reduce_sum x1, other arithmetic, per_device(): local_total = jnp.sum(latent_weights, axis=2)  15.6 us
    dot_general x4, matrix products, window_block(): jnp.einsum('hqk,khd->qhd', weights.astype(jnp.bfloat16), value_block, pre...  14.3 us
    dot_general x1, matrix products, per_device(): jnp.einsum('hlt,thd->lhd', latent_weights.astype(jnp.bfloat16), valued.re...  14.1 us
    dot_general x1, matrix products, per_device(): jnp.einsum('lhd,thd->hlt', latent_query, keyed.reshape(frame_count, heads...  13.3 us
    dot_general x4, matrix products, project(): jnp.dot(source, weight, preferred_element_type=jnp.float32)  9.11 us
  transfers between devices with their start and end apart: 5, of which 1 were waited for; matrix products, arithmetic and copies ran while one was open for 50% of the time, Pallas kernels for 0%

commit v1 on v0

v1 whole, which is shorter than its diff:
```python
import functools

import jax
import jax.numpy as jnp
from jax import lax
from jax.experimental import pallas as pl
from jax.experimental.pallas import tpu as pltpu
from jax.sharding import PartitionSpec as P

HD = 64
HALF = 256
NEG = -1e30


def extended(block, sides, width):
    for axis, dim in sides:
        count = lax.axis_size(axis)
        forward = [(i, i + 1) for i in range(count - 1)]
        backward = [(target, source) for source, target in forward]
        low = lax.ppermute(
            lax.slice_in_dim(block, block.shape[dim] - width, None, axis=dim), axis, forward
        )
        high = lax.ppermute(lax.slice_in_dim(block, 0, width, axis=dim), axis, backward)
        block = jnp.concatenate([low, block, high], axis=dim)
    return block


def combined_all(value, axis, combine):
    everything = jax.tree.map(
        lambda part, kind: lax.all_gather(part.astype(kind), axis),
        value,
        (jnp.bfloat16, jnp.bfloat16, jnp.bfloat16),
    )

    def take(k):
        return jax.tree.map(lambda part, own: part[k].astype(own.dtype), everything, value)

    return lax.fori_loop(
        1, lax.axis_size(axis), lambda k, so_far: combine(so_far, take(k)), take(0)
    )


def project(source, weight):
    return jnp.dot(source, weight, preferred_element_type=jnp.float32).astype(jnp.bfloat16)


def combine(earlier, latter):
    peak_first, total_first, accum_first = earlier
    peak_second, total_second, accum_second = latter
    joint = jnp.maximum(peak_first, peak_second)
    factor_first = jnp.exp(peak_first - joint)
    factor_second = jnp.exp(peak_second - joint)
    summed_total = total_first * factor_first + total_second * factor_second
    summed_accum = accum_first * jnp.repeat(factor_first, HD, axis=1) + accum_second * jnp.repeat(
        factor_second, HD, axis=1
    )
    return (joint, summed_total, summed_accum)


def window_kernel(scal_ref, q_ref, k_ref, v_ref, w_ref, o_ref, att_ref, *, heads, scale):
    tq = q_ref.shape[0]
    span = tq + 2 * HALF
    start = pl.multiple_of(pl.program_id(0) * tq, tq)
    first = scal_ref[0]
    length = scal_ref[1]
    row = lax.broadcasted_iota(jnp.int32, (tq, span), 0)
    col = lax.broadcasted_iota(jnp.int32, (tq, span), 1)
    offset = col - row
    key_pos = first + start - HALF + col
    allowed = (offset >= 0) & (offset <= 2 * HALF) & (key_pos >= 0) & (key_pos < length)
    query_pos = first + start + lax.broadcasted_iota(jnp.int32, (tq, 1), 0)
    query_valid = query_pos < length
    for h in range(heads):
        cols = slice(h * HD, (h + 1) * HD)
        q = q_ref[:, cols]
        k = k_ref[pl.ds(start, span), cols]
        v = v_ref[pl.ds(start, span), cols]
        s = lax.dot_general(
            q, k, (((1,), (1,)), ((), ())), preferred_element_type=jnp.float32
        ) * scale
        masked = jnp.where(allowed, s, NEG)
        peak = jnp.max(masked, axis=1, keepdims=True)
        weights = jnp.where(allowed, jnp.exp(masked - peak), 0.0)
        denom = jnp.sum(weights, axis=1, keepdims=True)
        blended = jnp.dot(weights.astype(jnp.bfloat16), v, preferred_element_type=jnp.float32)
        divisor = jnp.where(query_valid, denom, 1.0)
        att_ref[:, cols] = jnp.where(query_valid, blended / divisor, 0.0).astype(jnp.bfloat16)
    o_ref[...] = jnp.dot(
        att_ref[...], w_ref[...], preferred_element_type=jnp.float32
    ).astype(jnp.bfloat16)


def window_attention(query, keys_wide, values_wide, w_out, first_frame, length):
    frame_count, width = query.shape
    out_width = w_out.shape[1]
    tq = min(256, frame_count)
    scal = jnp.stack([first_frame, length]).astype(jnp.int32)
    kernel = functools.partial(window_kernel, heads=width // HD, scale=HD ** (-0.5))
    return pl.pallas_call(
        kernel,
        out_shape=jax.ShapeDtypeStruct((frame_count, out_width), jnp.bfloat16),
        grid_spec=pltpu.PrefetchScalarGridSpec(
            num_scalar_prefetch=1,
            grid=(frame_count // tq,),
            in_specs=[
                pl.BlockSpec((tq, width), lambda i, s: (i, 0)),
                pl.BlockSpec(keys_wide.shape, lambda i, s: (0, 0)),
                pl.BlockSpec(values_wide.shape, lambda i, s: (0, 0)),
                pl.BlockSpec(w_out.shape, lambda i, s: (0, 0)),
            ],
            out_specs=pl.BlockSpec((tq, out_width), lambda i, s: (i, 0)),
            scratch_shapes=[pltpu.VMEM((tq, width), jnp.bfloat16)],
        ),
    )(scal, query, keys_wide, values_wide, w_out)


def latent_kernel(scal_ref, q_ref, k_ref, v_ref, acc_ref, stat_ref, *, heads, scale):
    tl = q_ref.shape[0]
    frame_count = k_ref.shape[0]
    valid = lax.broadcasted_iota(jnp.int32, (tl, frame_count), 1) < scal_ref[0]
    stat_ref[...] = jnp.zeros_like(stat_ref)
    for h in range(heads):
        cols = slice(h * HD, (h + 1) * HD)
        s = lax.dot_general(
            q_ref[:, cols], k_ref[:, cols], (((1,), (1,)), ((), ())),
            preferred_element_type=jnp.float32,
        ) * scale
        masked = jnp.where(valid, s, NEG)
        peak = jnp.max(masked, axis=1, keepdims=True)
        weights = jnp.where(valid, jnp.exp(masked - peak), 0.0)
        total = jnp.sum(weights, axis=1, keepdims=True)
        acc_ref[:, cols] = jnp.dot(
            weights.astype(jnp.bfloat16), v_ref[:, cols], preferred_element_type=jnp.float32
        )
        stat_ref[:, h : h + 1] = peak
        stat_ref[:, heads + h : heads + h + 1] = total


def latent_attention(latent_query, keyed, valued, valid_count):
    latent_count, width = latent_query.shape
    heads = width // HD
    tl = min(256, latent_count)
    scal = jnp.reshape(valid_count, (1,)).astype(jnp.int32)
    kernel = functools.partial(latent_kernel, heads=heads, scale=HD ** (-0.5))
    acc, stat = pl.pallas_call(
        kernel,
        out_shape=(
            jax.ShapeDtypeStruct((latent_count, width), jnp.float32),
            jax.ShapeDtypeStruct((latent_count, 128), jnp.float32),
        ),
        grid_spec=pltpu.PrefetchScalarGridSpec(
            num_scalar_prefetch=1,
            grid=(latent_count // tl,),
            in_specs=[
                pl.BlockSpec((tl, width), lambda i, s: (i, 0)),
                pl.BlockSpec(keyed.shape, lambda i, s: (0, 0)),
                pl.BlockSpec(valued.shape, lambda i, s: (0, 0)),
            ],
            out_specs=[
                pl.BlockSpec((tl, width), lambda i, s: (i, 0)),
                pl.BlockSpec((tl, 128), lambda i, s: (i, 0)),
            ],
        ),
    )(scal, latent_query, keyed, valued)
    return stat[:, :heads], stat[:, heads : 2 * heads], acc


def per_device(
    frames, latents, lengths, w_query, w_key, w_value, w_out, w_latent_query, w_latent_out
):
    frame_count = frames.shape[0]
    head_width = w_query.shape[1]
    seq_devices = lax.axis_size("seq")
    seq_place = lax.axis_index("seq")
    first_frame = seq_place * frame_count
    length = lengths[0]
    query = project(frames, w_query)
    keyed = project(frames, w_key)
    valued = project(frames, w_value)
    stacked = jnp.concatenate([keyed, valued], axis=1)
    padded = extended(stacked, (("seq", 0),), HALF)
    keys_wide = padded[:, :head_width]
    values_wide = padded[:, head_width:]
    frame_terms = window_attention(query, keys_wide, values_wide, w_out, first_frame, length)
    frames_out = lax.psum_scatter(frame_terms, "head", scatter_dimension=1, tiled=True)
    latent_count = latents.shape[0]
    latent_query = project(latents, w_latent_query)
    valid_count = jnp.clip(length - first_frame, 0, frame_count)
    peaks, totals, local_accum = latent_attention(latent_query, keyed, valued, valid_count)
    rows_here = latent_count // seq_devices
    merged_peak, merged_total, merged_accum = combined_all(
        (peaks, totals, local_accum), "seq", combine
    )
    own_total = lax.dynamic_slice_in_dim(merged_total, seq_place * rows_here, rows_here, 0)
    own_accum = lax.dynamic_slice_in_dim(merged_accum, seq_place * rows_here, rows_here, 0)
    summary = (own_accum / jnp.repeat(own_total, HD, axis=1)).astype(jnp.bfloat16)
    latent_terms = jnp.dot(summary, w_latent_out, preferred_element_type=jnp.float32)
    latents_out = lax.psum_scatter(
        latent_terms.astype(jnp.bfloat16), "head", scatter_dimension=1, tiled=True
    )
    return (frames_out, latents_out)


def solution(mesh):
    return jax.shard_map(
        per_device,
        mesh=mesh,
        in_specs=(
            P(("groups", "seq"), None),
            P(),
            P("groups"),
            P(None, "head"),
            P(None, "head"),
            P(None, "head"),
            P("head", None),
            P(None, "head"),
            P("head", None),
        ),
        out_specs=(P(("groups", "seq"), "head"), P(("groups", "seq"), "head")),
        check_vma=False,
    )
```

time: 231 us -> 224 us (0.970)
  matrix products: 80.2 us -> 15.1 us
  blocking collectives: 28.5 us -> 73.4 us
  Pallas kernels: 0 us -> 39.3 us
  local copies, waits for them, and re-layouts: 22.7 us -> 10.2 us
  other arithmetic: 28.1 us -> 18.7 us
  loops' own time: 2.87 us -> 0.03 us
    dot_general x7 -> x0, matrix products: 46.5 us -> none  [the longest x4 14.3 us: window_block(): jnp.einsum('hqk,khd->qhd', weights.astype(jnp.bfloat16), value_block, pre...]
    all_gather x2, blocking collectives: 28.5 us -> 73.4 us  [combined_all(): lax.all_gather(part.astype(kind), axis)]
    pallas_call x0 -> x2, Pallas kernels: none -> 39.3 us  [the longest x1 21.4 us: window_attention(): pl.pallas_call(kernel, out_shape=jax.ShapeDtypeStruct((frame_count, out_w...]
    sub x4 -> x0, matrix products: 22.5 us -> none  [window_block(): weights = jnp.where(allowed[None], jnp.exp(masked - row_peak), 0.0)]
    reduce_sum x1 -> x0, other arithmetic: 15.6 us -> none  [per_device(): local_total = jnp.sum(latent_weights, axis=2)]
    dynamic_slice x16 -> x0, local copies, waits for them, and re-layouts: 11.6 us -> none  [the longest x4 4.65 us: window_block(): lax.dynamic_slice_in_dim(keys_wide, row_first, span, 0)]
    add x3, other arithmetic: 1.53 us -> 7.22 us  [combine(): accum_first * jnp.repeat(factor_first, HD, axis=1)]
    while x1 -> x5, local copies, waits for them, and re-layouts: 0.33 us -> 4.53 us  [combined_all(): lax.fori_loop(1, lax.axis_size(axis), lambda k, so_far: combine(so_far, t...]
  transfers between devices with their start and end apart: 5 -> 5, of which waited for: 1 -> 1; matrix products, arithmetic and copies ran while one was open for 50% -> 15% of each run, Pallas kernels for 0% -> 10%
where the time goes in v1:
time: 224 us
  blocking collectives  73.4 us (33%)
  waiting for transfers between devices  45 us (20%)
  Pallas kernels  39.3 us (18%)
  other arithmetic  18.7 us (8%)
  matrix products  15.1 us (7%)
  between operations  14.7 us (7%)
  local copies, waits for them, and re-layouts  10.2 us (5%)
  starting transfers between devices  7.23 us (3%)
    all_gather x2, blocking collectives, combined_all(): lax.all_gather(part.astype(kind), axis)  73.4 us
    reduce_scatter x1, waiting for transfers between devices, per_device(): lax.psum_scatter(frame_terms, 'head', scatter_dimension=1, tiled=True)  44.9 us
    pallas_call x1, Pallas kernels, window_attention(): pl.pallas_call(kernel, out_shape=jax.ShapeDtypeStruct((frame_count, out_w...  21.4 us
    pallas_call x1, Pallas kernels, latent_attention(): pl.pallas_call(kernel, out_shape=(jax.ShapeDtypeStruct((latent_count, wid...  17.9 us
    dot_general x4, matrix products, project(): jnp.dot(source, weight, preferred_element_type=jnp.float32)  13 us
    add x3, other arithmetic, combine(): accum_first * jnp.repeat(factor_first, HD, axis=1)  7.22 us
    ppermute x1, starting transfers between devices, extended(): lax.ppermute(lax.slice_in_dim(block, block.shape[dim] - width, None, axis...  5.64 us
    while x5, local copies, waits for them, and re-layouts, combined_all(): lax.fori_loop(1, lax.axis_size(axis), lambda k, so_far: combine(so_far, t...  4.53 us
  transfers between devices with their start and end apart: 5, of which 1 were waited for; matrix products, arithmetic and copies ran while one was open for 15% of the time, Pallas kernels for 10%

profile of v1, /device:TPU:0, one launch (start us, length us, event | category | flops | bytes accessed | tf_op | source)
XLA Modules:
  0.0 223.7 jit_solution(1545180402792737413)
XLA Ops:
  8.0 4.7 %convolution_convert_fusion.1.k_ref = bf16[2048,256]{1,0:T(8,128)(2,1)} fusion(bf16[2048,1024]{1,0:T(8,128)(2,1)} %param.11, bf16[1024,256]{1,0:T(8,128)(2,1)} %param.15), kind=kOutput, calls=%fused_computation.12 | convolution fusion | flops 1074266112 | bytes 5767168 | tf_op jit(solution)/shard_map/dot_general | solution.py:44
  12.8 2.2 %convolution_convert_fusion.v_ref = bf16[2048,256]{1,0:T(8,128)(2,1)} fusion(bf16[2048,1024]{1,0:T(8,128)(2,1)S(1)} %copy-done.3, bf16[1024,256]{1,0:T(8,128)(2,1)S(1)} %copy-done.4), kind=kOutput, calls=%fused_computation.11 | convolution fusion | flops 1074266112 | bytes 5767168 | tf_op jit(solution)/shard_map/dot_general | solution.py:44
  15.0 1.5 convolution_convert_fusion.4.q_ref
  16.5 17.9 %shard_map.105 = (f32[1024,256]{1,0:T(8,128)}, f32[1024,128]{1,0:T(8,128)}) custom-call(s32[1]{0:T(128)} %bitcast.8.scal_ref, bf16[1024,256]{1,0:T(8,128)(2,1)} %convolution_convert_fusion.4.q_ref, bf16[2048,256]{1,0:T(8,128)(2,1)} %convolution_convert_fusion.1.k_ref, bf16[2048,256]{1,0:T(8,128)(2,1)} %convolution_convert_fusion.v_ref), custom_call_target="tpu_custom_call" | custom-call | tf_op jit(solution)/shard_map/pallas_call | solution.py:145
  34.5 2.1 convert_element_type.88
  36.6 1.8 pad_maximum_fusion.2
  38.5 5.6 %collective-permute-start = (bf16[256,512]{1,0:T(8,128)(2,1)}, bf16[256,512]{1,0:T(8,128)(2,1)}, u32[]{:S(2)}, u32[]{:S(2)}) collective-permute-start(bf16[256,512]{1,0:T(8,128)(2,1)} %get-tuple-element.219), channel_id=1, source_target_pairs={{0,4},{4,8},{8,12},{1,5},{5,9},{9,13},{2,6},{6,10},{10,14},{3,7},{... | collective-permute-start | bytes 786440 | tf_op jit(solution)/shard_map/ppermute | solution.py:20
  44.1 1.3 collective-permute-start.1
  45.4 1.1 convert.10
  46.6 51.8 %all-gather.1 = bf16[4096,4]{1,0:T(8,128)(2,1)S(1)} all-gather(bf16[1024,4]{1,0:T(8,128)(2,1)S(1)} %get-tuple-element.221), channel_id=3, replica_groups=mesh['groups'=2,'seq'=4,'head'=4] {'seq'}, dimensions={0}, use_global_device_ids=true | all-gather | bytes 40960 | tf_op jit(solution)/shard_map/all_gather | solution.py:30
  98.8 0.8 slice_convert_fusion.1
  99.7 1.2 copy.23
  100.9 21.6 %all-gather = bf16[4096,4]{1,0:T(8,128)(2,1)S(1)} all-gather(bf16[1024,4]{1,0:T(8,128)(2,1)S(1)} %get-tuple-element.222), channel_id=2, replica_groups=mesh['groups'=2,'seq'=4,'head'=4] {'seq'}, dimensions={0}, use_global_device_ids=true | all-gather | bytes 40960 | tf_op jit(solution)/shard_map/all_gather | solution.py:30
  122.9 0.8 slice_convert_fusion.2
  123.7 1.2 copy.22
  125.0 0.6 pad_add_fusion.scal_ref
  125.6 4.5 %convolution_convert_fusion.2.q_ref = bf16[2048,256]{1,0:T(8,128)(2,1)} fusion(bf16[2048,1024]{1,0:T(8,128)(2,1)} %param.11, bf16[1024,256]{1,0:T(8,128)(2,1)} %param.14), kind=kOutput, calls=%fused_computation.13 | convolution fusion | flops 1074266112 | bytes 5767168 | tf_op jit(solution)/shard_map/dot_general | solution.py:44
  130.1 1.1 slice_convert_fusion
  131.2 1.3 copy.24
  132.5 11.2 %while.19 = (s32[]{:T(128)}, f32[1024,4]{0,1:T(4,128)S(1)}, f32[1024,4]{0,1:T(4,128)S(1)}, f32[1024,256]{0,1:T(8,128)}, bf16[4,1024,4]{1,2,0:T(4,128)(2,1)S(1)},...) while((s32[]{:T(128)}, f32[1024,4]{0,1:T(4,128)S(1)}, ...), condition=%wide.region_2.3_spmd, body=%wide.region_1.2_spmd.sunk | while | flops 1081349 | bytes 4866191 | solution.py:38
  132.6 1.1 constant_dynamic-slice_fusion.3
  133.9 2.4 %fusion.20 = f32[1024,256]{0,1:T(8,128)} fusion(f32[1024,256]{0,1:T(8,128)} %get-tuple-element.287, bf16[1,1024,256]{1,2,0:T(8,128)(2,1)S(1)} %copy.32, f32[1024,4]{0,1:T(4,128)S(1)} %get-tuple-element.272, f32[1024,4]{0,1:T(4,128)S(1)} %get-tuple-element.273), kind=kLoop, calls=%fused_computation.1.clone.1 | loop fusion | flops 1048576 | bytes 2654208 | tf_op jit(solution)/shard_map/while/body/eval_jaxpr/add | solution.py:54
  136.3 1.1 constant_dynamic-slice_fusion.3
  137.6 2.4 %fusion.20 = f32[1024,256]{0,1:T(8,128)} fusion(f32[1024,256]{0,1:T(8,128)} %get-tuple-element.287, bf16[1,1024,256]{1,2,0:T(8,128)(2,1)S(1)} %copy.32, f32[1024,4]{0,1:T(4,128)S(1)} %get-tuple-element.272, f32[1024,4]{0,1:T(4,128)S(1)} %get-tuple-element.273), kind=kLoop, calls=%fused_computation.1.clone.1 | loop fusion | flops 1048576 | bytes 2654208 | tf_op jit(solution)/shard_map/while/body/eval_jaxpr/add | solution.py:54
  140.1 1.1 constant_dynamic-slice_fusion.3
  141.4 2.4 %fusion.20 = f32[1024,256]{0,1:T(8,128)} fusion(f32[1024,256]{0,1:T(8,128)} %get-tuple-element.287, bf16[1,1024,256]{1,2,0:T(8,128)(2,1)S(1)} %copy.32, f32[1024,4]{0,1:T(4,128)S(1)} %get-tuple-element.272, f32[1024,4]{0,1:T(4,128)S(1)} %get-tuple-element.273), kind=kLoop, calls=%fused_computation.1.clone.1 | loop fusion | flops 1048576 | bytes 2654208 | tf_op jit(solution)/shard_map/while/body/eval_jaxpr/add | solution.py:54
  143.8 1.1 fusion.3
  144.8 2.2 convolution_convert_fusion.3
  147.3 1.9 pad_maximum_fusion
  149.1 1.7 fusion.5
  150.8 21.4 %shard_map.104 = bf16[2048,1024]{1,0:T(8,128)(2,1)} custom-call(s32[2]{0:T(128)} %pad_add_fusion.scal_ref, bf16[2048,256]{1,0:T(8,128)(2,1)} %convolution_convert_fusion.2.q_ref, bf16[2560,256]{1,0:T(8,128)(2,1)} %get-tuple-element.218.k_ref, bf16[2560,256]{1,0:T(8,128)(2,1)} %get-tuple-element.217.v_ref, bf16[256,1024]{1,0:T(8,128)(2,1)} %w_ref.1), custom_call_target="tpu_custom_call" | custom-call | tf_op jit(solution)/shard_map/pallas_call | solution.py:99
  172.2 44.9 %reduce-scatter.3.cloned.1.call-done = bf16[2048,256]{1,0:T(8,128)(2,1)} async-done(((bf16[2048,1024]{1,0:T(8,128)(2,1)}), bf16[2048,256]{1,0:T(8,128)(2,1)}) %reduce-scatter.3.cloned.1.call-update) | async-done | bytes 1048592 | tf_op jit(solution)/shard_map/reduce_scatter | solution.py:185
  (32 shorter events, 2.0 us)
Async XLA Ops:
  7.2 7.9 %copy-start = (bf16[1024,1024]{1,0:T(8,128)(2,1)S(1)}, bf16[1024,1024]{1,0:T(8,128)(2,1)}, u32[]{:S(2)}) copy-start(bf16[1024,1024]{1,0:T(8,128)(2,1)} %param.12) | copy-start | bytes 6291460
  7.2 122.9 %all-gather.5.cloned.1.call-start = ((), (), s32[]{:S(2)}) async-start(), calls=%async_computation.4 | async-start | bytes 2621440 | tf_op jit(solution)/shard_map/all_gather | solution.py:30
  8.0 4.7 %copy-start.3 = (bf16[2048,1024]{1,0:T(8,128)(2,1)S(1)}, bf16[2048,1024]{1,0:T(8,128)(2,1)}, u32[]{:S(2)}) copy-start(bf16[2048,1024]{1,0:T(8,128)(2,1)} %param.11) | copy-start | bytes 12582916
  8.0 4.7 %copy-start.4 = (bf16[1024,256]{1,0:T(8,128)(2,1)S(1)}, bf16[1024,256]{1,0:T(8,128)(2,1)}, u32[]{:S(2)}) copy-start(bf16[1024,256]{1,0:T(8,128)(2,1)} %param.16) | copy-start | bytes 1572868
  12.8 2.3 %copy-start.5 = (bf16[1024,256]{1,0:T(8,128)(2,1)S(1)}, bf16[1024,256]{1,0:T(8,128)(2,1)}, u32[]{:S(2)}) copy-start(bf16[1024,256]{1,0:T(8,128)(2,1)} %param.18) | copy-start | bytes 1572868
  16.5 20.1 %copy-start.1 = (bf16[2048,256]{1,0:T(8,128)(2,1)S(1)}, bf16[2048,256]{1,0:T(8,128)(2,1)}, u32[]{:S(2)}) copy-start(bf16[2048,256]{1,0:T(8,128)(2,1)} %convolution_convert_fusion.1.k_ref) | copy-start | bytes 3145732
  36.6 135.7 %reduce-scatter.5.cloned.1.call-start = ((), (), s32[]{:S(2)}) async-start(), calls=%async_computation.3 | async-start | bytes 655360 | tf_op jit(solution)/shard_map/reduce_scatter | solution.py:198
  38.5 108.8 %collective-permute-start = (bf16[256,512]{1,0:T(8,128)(2,1)}, bf16[256,512]{1,0:T(8,128)(2,1)}, u32[]{:S(2)}, u32[]{:S(2)}) collective-permute-start(bf16[256,512]{1,0:T(8,128)(2,1)} %get-tuple-element.219), channel_id=1, source_target_pairs={{0,4},{4,8},{8,12},{1,5},{5,9},{9,13},{2,6},{6,10},{10,14},{3,7},{... | collective-permute-start | bytes 786440 | tf_op jit(solution)/shard_map/ppermute | solution.py:20
  44.1 103.2 %collective-permute-start.1 = (bf16[256,512]{1,0:T(8,128)(2,1)}, bf16[256,512]{1,0:T(8,128)(2,1)}, u32[]{:S(2)}, u32[]{:S(2)}) collective-permute-start(bf16[256,512]{1,0:T(8,128)(2,1)} %get-tuple-element.220), channel_id=1, source_target_pairs={{4,0},{8,4},{12,8},{5,1},{9,5},{13,9},{6,2},{10,6},{14,10},{7,3},{... | collective-permute-start | bytes 786440 | tf_op jit(solution)/shard_map/ppermute | solution.py:23
  143.8 3.5 %copy-start.2 = (bf16[2048,256]{1,0:T(8,128)(2,1)S(1)}, bf16[2048,256]{1,0:T(8,128)(2,1)}, u32[]{:S(2)}) copy-start(bf16[2048,256]{1,0:T(8,128)(2,1)} %convolution_convert_fusion.1.k_ref) | copy-start | bytes 3145732
  147.0 70.1 %reduce-scatter.3.cloned.1.call-start = ((), (), s32[]{:S(2)}) async-start(), calls=%async_computation.2 | async-start | bytes 5242880 | tf_op jit(solution)/shard_map/reduce_scatter | solution.py:185
Sparse Core Ops, SparseCore 0:
  36.7 73.5 all-gather.4
  147.1 21.9 reduce-scatter.4
  172.4 44.6 reduce-scatter.2

commit v2 on v1

--- a/solution.py
+++ b/solution.py
@@ -25,42 +25,14 @@
     return block
 
 
-def combined_all(value, axis, combine):
-    everything = jax.tree.map(
-        lambda part, kind: lax.all_gather(part.astype(kind), axis),
-        value,
-        (jnp.bfloat16, jnp.bfloat16, jnp.bfloat16),
-    )
-
-    def take(k):
-        return jax.tree.map(lambda part, own: part[k].astype(own.dtype), everything, value)
-
-    return lax.fori_loop(
-        1, lax.axis_size(axis), lambda k, so_far: combine(so_far, take(k)), take(0)
-    )
-
-
 def project(source, weight):
     return jnp.dot(source, weight, preferred_element_type=jnp.float32).astype(jnp.bfloat16)
-
-
-def combine(earlier, latter):
-    peak_first, total_first, accum_first = earlier
-    peak_second, total_second, accum_second = latter
-    joint = jnp.maximum(peak_first, peak_second)
-    factor_first = jnp.exp(peak_first - joint)
-    factor_second = jnp.exp(peak_second - joint)
-    summed_total = total_first * factor_first + total_second * factor_second
-    summed_accum = accum_first * jnp.repeat(factor_first, HD, axis=1) + accum_second * jnp.repeat(
-        factor_second, HD, axis=1
-    )
-    return (joint, summed_total, summed_accum)
 
 
 def window_kernel(scal_ref, q_ref, k_ref, v_ref, w_ref, o_ref, att_ref, *, heads, scale):
     tq = q_ref.shape[0]
     span = tq + 2 * HALF
-    start = pl.multiple_of(pl.program_id(0) * tq, tq)
+    start = pl.multiple_of(scal_ref[2] + pl.program_id(0) * tq, tq)
     first = scal_ref[0]
     length = scal_ref[1]
     row = lax.broadcasted_iota(jnp.int32, (tq, span), 0)
@@ -90,20 +62,21 @@
     ).astype(jnp.bfloat16)
 
 
-def window_attention(query, keys_wide, values_wide, w_out, first_frame, length):
-    frame_count, width = query.shape
+def window_attention(query, keys_wide, values_wide, w_out, first_frame, length, row_base, rows):
+    width = query.shape[1]
     out_width = w_out.shape[1]
-    tq = min(256, frame_count)
-    scal = jnp.stack([first_frame, length]).astype(jnp.int32)
+    tq = min(256, rows)
+    block_base = row_base // tq
+    scal = jnp.array([0, 0, row_base], jnp.int32).at[0].set(first_frame).at[1].set(length)
     kernel = functools.partial(window_kernel, heads=width // HD, scale=HD ** (-0.5))
     return pl.pallas_call(
         kernel,
-        out_shape=jax.ShapeDtypeStruct((frame_count, out_width), jnp.bfloat16),
+        out_shape=jax.ShapeDtypeStruct((rows, out_width), jnp.bfloat16),
         grid_spec=pltpu.PrefetchScalarGridSpec(
             num_scalar_prefetch=1,
-            grid=(frame_count // tq,),
+            grid=(rows // tq,),
             in_specs=[
-                pl.BlockSpec((tq, width), lambda i, s: (i, 0)),
+                pl.BlockSpec((tq, width), lambda i, s: (i + block_base, 0)),
                 pl.BlockSpec(keys_wide.shape, lambda i, s: (0, 0)),
                 pl.BlockSpec(values_wide.shape, lambda i, s: (0, 0)),
                 pl.BlockSpec(w_out.shape, lambda i, s: (0, 0)),
@@ -165,11 +138,39 @@
     return stat[:, :heads], stat[:, heads : 2 * heads], acc
 
 
+def shifted_blocks(payload, axis, rows):
+    count = lax.axis_size(axis)
+    place = lax.axis_index(axis)
+    own = lax.dynamic_slice_in_dim(payload, place * rows, rows, 0)
+    parts = [own]
+    for shift in range(1, count):
+        target = (place + shift) % count
+        block = lax.dynamic_slice_in_dim(payload, target * rows, rows, 0)
+        pairs = [(i, (i + shift) % count) for i in range(count)]
+        parts.append(lax.ppermute(block, axis, pairs))
+    return jnp.stack(parts)
+
+
+def column_sum(partial, axis):
+    count = lax.axis_size(axis)
+    place = lax.axis_index(axis)
+    width = partial.shape[1] // count
+    own = lax.dynamic_slice_in_dim(partial, place * width, width, 1)
+    total = own.astype(jnp.float32)
+    for shift in range(1, count):
+        target = (place + shift) % count
+        block = lax.dynamic_slice_in_dim(partial, target * width, width, 1)
+        pairs = [(i, (i + shift) % count) for i in range(count)]
+        total = total + lax.ppermute(block, axis, pairs).astype(jnp.float32)
+    return total.astype(jnp.bfloat16)
+
+
 def per_device(
     frames, latents, lengths, w_query, w_key, w_value, w_out, w_latent_query, w_latent_out
 ):
     frame_count = frames.shape[0]
     head_width = w_query.shape[1]
+    heads_here = head_width // HD
     seq_devices = lax.axis_size("seq")
     seq_place = lax.axis_index("seq")
     first_frame = seq_place * frame_count
@@ -181,23 +182,34 @@
     padded = extended(stacked, (("seq", 0),), HALF)
     keys_wide = padded[:, :head_width]
     values_wide = padded[:, head_width:]
-    frame_terms = window_attention(query, keys_wide, values_wide, w_out, first_frame, length)
-    frames_out = lax.psum_scatter(frame_terms, "head", scatter_dimension=1, tiled=True)
+    chunks = 2 if frame_count % 512 == 0 else 1
+    chunk_rows = frame_count // chunks
+    frame_parts = []
+    for c in range(chunks):
+        terms = window_attention(
+            query, keys_wide, values_wide, w_out, first_frame, length, c * chunk_rows, chunk_rows
+        )
+        if c == 0:
+            terms, keyed, valued = lax.optimization_barrier((terms, keyed, valued))
+        frame_parts.append(lax.psum_scatter(terms, "head", scatter_dimension=1, tiled=True))
+    frames_out = jnp.concatenate(frame_parts, axis=0)
     latent_count = latents.shape[0]
     latent_query = project(latents, w_latent_query)
     valid_count = jnp.clip(length - first_frame, 0, frame_count)
     peaks, totals, local_accum = latent_attention(latent_query, keyed, valued, valid_count)
     rows_here = latent_count // seq_devices
-    merged_peak, merged_total, merged_accum = combined_all(
-        (peaks, totals, local_accum), "seq", combine
-    )
-    own_total = lax.dynamic_slice_in_dim(merged_total, seq_place * rows_here, rows_here, 0)
-    own_accum = lax.dynamic_slice_in_dim(merged_accum, seq_place * rows_here, rows_here, 0)
+    payload = jnp.concatenate([local_accum, peaks, totals], axis=1)
+    parts = shifted_blocks(payload, "seq", rows_here)
+    part_accum = parts[:, :, :head_width]
+    part_peak = parts[:, :, head_width : head_width + heads_here]
+    part_total = parts[:, :, head_width + heads_here :]
+    joint = jnp.max(part_peak, axis=0)
+    factor = jnp.exp(part_peak - joint[None])
+    own_total = jnp.sum(part_total * factor, axis=0)
+    own_accum = jnp.sum(part_accum * jnp.repeat(factor, HD, axis=2), axis=0)
     summary = (own_accum / jnp.repeat(own_total, HD, axis=1)).astype(jnp.bfloat16)
     latent_terms = jnp.dot(summary, w_latent_out, preferred_element_type=jnp.float32)
-    latents_out = lax.psum_scatter(
-        latent_terms.astype(jnp.bfloat16), "head", scatter_dimension=1, tiled=True
-    )
+    latents_out = column_sum(latent_terms.astype(jnp.bfloat16), "head")
     return (frames_out, latents_out)
 
 

time: 224 us -> 143 us (0.64)
  blocking collectives: 73.4 us -> 0 us
  other arithmetic: 18.7 us -> 10.8 us
  starting transfers between devices: 7.23 us -> 14.9 us
  waiting for transfers between devices: 45 us -> 38.7 us
  matrix products: 15.1 us -> 11.4 us
  Pallas kernels: 39.3 us -> 42.7 us
    all_gather x2 -> x0, blocking collectives: 73.4 us -> none  [combined_all(): lax.all_gather(part.astype(kind), axis)]
    reduce_scatter x2, waiting for transfers between devices: 44.9 us -> 0.01 us  [per_device(): lax.psum_scatter(terms, 'head', scatter_dimension=1, tiled=True)]
    ppermute x0 -> x6, waiting for transfers between devices: none -> 38.6 us  [the longest x3 31.7 us: shifted_blocks(): parts.append(lax.ppermute(block, axis, pairs))]
    add x6 -> x0, other arithmetic: 7.32 us -> none  [the longest x3 7.22 us: combine(): accum_first * jnp.repeat(factor_first, HD, axis=1)]
    ppermute x0 -> x6, starting transfers between devices: none -> 7.08 us  [the longest x3 5.48 us: shifted_blocks(): parts.append(lax.ppermute(block, axis, pairs))]
    convert_element_type x5 -> x1, other arithmetic: 5.94 us -> 0.72 us  [column_sum(): return total.astype(jnp.bfloat16)]
    while x5 -> x0, local copies, waits for them, and re-layouts: 4.53 us -> none  [combined_all(): lax.fori_loop(1, lax.axis_size(axis), lambda k, so_far: combine(so_far, t...]
    dynamic_slice x7 -> x1, local copies, waits for them, and re-layouts: 3.86 us -> 0.06 us  [column_sum(): block = lax.dynamic_slice_in_dim(partial, target * width, width, 1)]
  transfers between devices with their start and end apart: 5 -> 10, of which waited for: 1 -> 5; matrix products, arithmetic and copies ran while one was open for 15% -> 11% of each run, Pallas kernels for 10% -> 21%
where the time goes in v2:
time: 143 us
  Pallas kernels  42.7 us (30%)
  waiting for transfers between devices  38.7 us (27%)
  between operations  15 us (10%)
  starting transfers between devices  14.9 us (10%)
  matrix products  11.4 us (8%)
  other arithmetic  10.8 us (8%)
  local copies, waits for them, and re-layouts  9.37 us (7%)
    ppermute x3, waiting for transfers between devices, shifted_blocks(): parts.append(lax.ppermute(block, axis, pairs))  31.7 us
    pallas_call x2, Pallas kernels, window_attention(): pl.pallas_call(kernel, out_shape=jax.ShapeDtypeStruct((rows, out_width),...  24.9 us
    pallas_call x1, Pallas kernels, latent_attention(): pl.pallas_call(kernel, out_shape=(jax.ShapeDtypeStruct((latent_count, wid...  17.9 us
    dot_general x4, matrix products, project(): jnp.dot(source, weight, preferred_element_type=jnp.float32)  11.1 us
    ppermute x3, waiting for transfers between devices, column_sum(): total = total + lax.ppermute(block, axis, pairs).astype(jnp.float32)  6.91 us
    ppermute x1, starting transfers between devices, extended(): lax.ppermute(lax.slice_in_dim(block, block.shape[dim] - width, None, axis...  6.27 us
    ppermute x3, starting transfers between devices, shifted_blocks(): parts.append(lax.ppermute(block, axis, pairs))  5.48 us
    unnamed x27, local copies, waits for them, and re-layouts  3.82 us
  transfers between devices with their start and end apart: 10, of which 5 were waited for; matrix products, arithmetic and copies ran while one was open for 11% of the time, Pallas kernels for 21%

profile of v2, /device:TPU:0, one launch (start us, length us, event | category | flops | bytes accessed | tf_op | source)
XLA Modules:
  0.0 142.8 jit_solution(9404560827275262659)
XLA Ops:
  7.2 3.7 %convolution_convert_fusion.v_ref = bf16[2048,256]{1,0:T(8,128)(2,1)S(1)} fusion(bf16[2048,1024]{1,0:T(8,128)(2,1)} %param.19, bf16[1024,256]{1,0:T(8,128)(2,1)} %param.24), kind=kOutput, calls=%fused_computation.5 | convolution fusion | flops 1074266112 | bytes 5767168 | tf_op jit(solution)/shard_map/dot_general | solution.py:29
  11.1 1.3 convolution_convert_fusion.1.k_ref
  12.4 1.0 copy-done.3
  13.4 0.8 pad_maximum_fusion.4
  14.2 1.3 collective-permute-start.1
  15.5 6.3 %collective-permute-start = (bf16[256,512]{1,0:T(8,128)(2,1)}, bf16[256,512]{1,0:T(8,128)(2,1)}, u32[]{:S(2)}, u32[]{:S(2)}) collective-permute-start(bf16[256,512]{1,0:T(8,128)(2,1)} %get-tuple-element.64), channel_id=1, source_target_pairs={{0,4},{4,8},{8,12},{1,5},{5,9},{9,13},{2,6},{6,10},{10,14},{3,7},{... | collective-permute-start | bytes 786440 | tf_op jit(solution)/shard_map/ppermute | solution.py:20
  22.5 4.6 %convolution_convert_fusion.2.q_ref = bf16[2048,256]{1,0:T(8,128)(2,1)} fusion(bf16[2048,1024]{1,0:T(8,128)(2,1)} %param.19, bf16[1024,256]{1,0:T(8,128)(2,1)} %param.22), kind=kOutput, calls=%fused_computation.7 | convolution fusion | flops 1074266112 | bytes 5767168 | tf_op jit(solution)/shard_map/dot_general | solution.py:29
  27.1 1.8 %pad_maximum_fusion = bf16[2560,512]{1,0:T(8,128)(2,1)S(1)} fusion(bf16[256,512]{1,0:T(8,128)(2,1)S(1)} %collective-permute-done.1, bf16[2048,256]{1,0:T(8,128)(2,1)S(1)} %convolution_convert_fusion.v_ref, bf16[2048,256]{1,0:T(8,128)(2,1)S(1)} %copy-done.4, bf16[256,512]{1,0:T(8,128)(2,1)} %collective-permute-done), kind=kLoop, calls=%fused_computation.4 | loop fusion | flops 10485760 | bytes 5242880 | tf_op jit(solution)/shard_map/concatenate | solution.py:24
  28.9 1.7 %fusion.7 = (bf16[2560,256]{1,0:T(8,128)(2,1)}, bf16[2560,256]{1,0:T(8,128)(2,1)}) fusion(bf16[2560,512]{1,0:T(8,128)(2,1)S(1)} %pad_maximum_fusion), kind=kLoop, calls=%fused_computation.37 | loop fusion | bytes 5242880 | tf_op jit(solution)/shard_map/slice | solution.py:184
  30.6 12.4 %shard_map.123 = bf16[1024,1024]{1,0:T(8,128)(2,1)} custom-call(s32[3]{0:T(128)} %copy-done.7, bf16[2048,256]{1,0:T(8,128)(2,1)} %convolution_convert_fusion.2.q_ref, bf16[2560,256]{1,0:T(8,128)(2,1)} %get-tuple-element.63.k_ref, bf16[2560,256]{1,0:T(8,128)(2,1)} %get-tuple-element.62.v_ref, bf16[256,1024]{1,0:T(8,128)(2,1)} %w_ref.3), custom_call_target="tpu_custom_call" | custom-call | tf_op jit(solution)/shard_map/pallas_call | solution.py:72
  43.3 0.6 copy-done.8
  43.9 12.4 %shard_map.122 = bf16[1024,1024]{1,0:T(8,128)(2,1)} custom-call(s32[3]{0:T(128)} %copy-done.8, bf16[2048,256]{1,0:T(8,128)(2,1)} %convolution_convert_fusion.2.q_ref, bf16[2560,256]{1,0:T(8,128)(2,1)} %get-tuple-element.63.k_ref, bf16[2560,256]{1,0:T(8,128)(2,1)} %get-tuple-element.62.v_ref, bf16[256,1024]{1,0:T(8,128)(2,1)} %w_ref.3), custom_call_target="tpu_custom_call" | custom-call | tf_op jit(solution)/shard_map/pallas_call | solution.py:72
  56.4 1.0 copy-done.11
  57.4 1.5 %convolution_convert_fusion.4.q_ref = bf16[1024,256]{1,0:T(8,128)(2,1)} fusion(bf16[1024,1024]{1,0:T(8,128)(2,1)S(1)} %copy-done, bf16[1024,256]{1,0:T(8,128)(2,1)S(1)} %copy-done.11), kind=kOutput, calls=%fused_computation.14 | convolution fusion | flops 537133056 | bytes 3145728 | tf_op jit(solution)/shard_map/dot_general | solution.py:29
  58.9 17.9 %shard_map.124 = (f32[1024,256]{1,0:T(8,128)}, f32[1024,128]{1,0:T(8,128)}) custom-call(s32[1]{0:T(128)} %bitcast.2.scal_ref, bf16[1024,256]{1,0:T(8,128)(2,1)} %convolution_convert_fusion.4.q_ref, bf16[2048,256]{1,0:T(8,128)(2,1)} %copy-done.3, bf16[2048,256]{1,0:T(8,128)(2,1)} %copy-done.2), custom_call_target="tpu_custom_call" | custom-call | tf_op jit(solution)/shard_map/pallas_call | solution.py:118
  76.7 2.4 %fusion.4 = (f32[1,256,264]{2,1,0:T(8,128)S(1)}, f32[256,264]{1,0:T(8,128)}, f32[256,264]{1,0:T(8,128)}, f32[256,264]{1,0:T(8,128)}) fusion(s32[]{:T(128)S(6)} %select_n.51, f32[1024,256]{1,0:T(8,128)} %get-tuple-element.58, f32[1024,8]{1,0:T(8,128)} %bitcast.23, s32[]{:T(128)S(6)} %select_n.53, s32[]{:T(128)S(6)} %select_n.55, s32[]{:T(128)S(6)} %select_n.57), kind=kLoop, calls=%fused_computation.24 | loop fusion | flops 270336 | bytes 2162704 | tf_op jit(solution)/shard_map/stack | solution.py:151
  79.1 4.5 %collective-permute-start.4 = (f32[256,264]{1,0:T(8,128)}, f32[256,264]{1,0:T(8,128)S(1)}, u32[]{:S(2)}, u32[]{:S(2)}) collective-permute-start(f32[256,264]{1,0:T(8,128)} %get-tuple-element.69), channel_id=1, source_target_pairs={{0,12},{4,0},{8,4},{12,8},{1,13},{5,1},{9,5},{13,9},{2,14},{6,2},{... | collective-permute-start | bytes 811016 | tf_op jit(solution)/shard_map/ppermute | solution.py:150
  83.6 1.0 collective-permute-start.2
  84.6 8.9 %collective-permute-done.4 = f32[256,264]{1,0:T(8,128)S(1)} collective-permute-done((f32[256,264]{1,0:T(8,128)}, f32[256,264]{1,0:T(8,128)S(1)}, u32[]{:S(2)}, u32[]{:S(2)}) %collective-permute-start.4) | collective-permute-done | bytes 270368 | tf_op jit(solution)/shard_map/ppermute | solution.py:150
  93.5 22.8 %collective-permute-done.3 = f32[256,264]{1,0:T(8,128)S(1)} collective-permute-done((f32[256,264]{1,0:T(8,128)}, f32[256,264]{1,0:T(8,128)S(1)}, u32[]{:S(2)}, u32[]{:S(2)}) %collective-permute-start.3) | collective-permute-done | bytes 270368 | tf_op jit(solution)/shard_map/ppermute | solution.py:150
  116.3 1.1 pad_maximum_fusion.1
  117.5 1.1 copy-done.1
  119.0 1.1 broadcast_in_dim.7
  120.1 1.6 %copy.22 = f32[4,256,256]{2,1,0:T(8,128)S(1)} copy(f32[4,256,256]{1,2,0:T(8,128)} %bitcast.21) | data formatting | bytes 2097152 | tf_op jit(solution)/shard_map/reshape | solution.py:209
  121.8 0.8 copy.24
  122.6 1.5 %fusion = f32[256,256]{1,0:T(8,128)S(1)} fusion(f32[4,256,256]{2,1,0:T(8,128)S(1)} %copy.22, f32[4,256,264]{2,1,0:T(8,128)} %copy-done.1), kind=kLoop, calls=%fused_computation.16 | loop fusion | flops 458752 | bytes 2359296 | tf_op jit(solution)/shard_map/reduce_sum | solution.py:209
  124.1 0.3 convolution_convert_fusion.3
  124.5 1.4 collective-permute-start.6
  126.1 1.5 %collective-permute-done.7 = bf16[256,256]{1,0:T(8,128)(2,1)S(1)} collective-permute-done((bf16[256,256]{1,0:T(8,128)(2,1)S(1)}, bf16[256,256]{1,0:T(8,128)(2,1)S(1)}, u32[]{:S(2)}, u32[]{:S(2)}) %collective-permute-start.7) | collective-permute-done | bytes 131104 | tf_op jit(solution)/shard_map/ppermute | solution.py:164
  127.6 5.2 %collective-permute-done.6 = bf16[256,256]{1,0:T(8,128)(2,1)S(1)} collective-permute-done((bf16[256,256]{1,0:T(8,128)(2,1)S(1)}, bf16[256,256]{1,0:T(8,128)(2,1)S(1)}, u32[]{:S(2)}, u32[]{:S(2)}) %collective-permute-start.6) | collective-permute-done | bytes 131104 | tf_op jit(solution)/shard_map/ppermute | solution.py:164
  133.0 0.7 add_convert_fusion
  133.7 2.2 %pad_maximum_fusion.2 = bf16[2048,256]{1,0:T(8,128)(2,1)} fusion(bf16[1024,256]{1,0:T(8,128)(2,1)} %reduce-scatter.5.cloned.1.call-done, bf16[1024,256]{1,0:T(8,128)(2,1)} %reduce-scatter.3.cloned.1.call-done), kind=kLoop, calls=%fused_computation.17 | loop fusion | flops 2097152 | bytes 2097152 | tf_op jit(solution)/shard_map/concatenate | solution.py:195
  (46 shorter events, 1.6 us)
Async XLA Ops:
  7.2 49.2 %copy-start = (bf16[1024,1024]{1,0:T(8,128)(2,1)S(1)}, bf16[1024,1024]{1,0:T(8,128)(2,1)}, u32[]{:S(2)}) copy-start(bf16[1024,1024]{1,0:T(8,128)(2,1)} %param.20) | copy-start | bytes 6291460
  7.2 126.5 %reduce-scatter.5.cloned.1.call-start = ((), (), s32[]{:S(2)}) async-start(), calls=%async_computation.3 | async-start | bytes 2621440 | tf_op jit(solution)/shard_map/reduce_scatter | solution.py:194
  7.2 3.7 %copy-start.9 = (bf16[2048,1024]{1,0:T(8,128)(2,1)S(1)}, bf16[2048,1024]{1,0:T(8,128)(2,1)}, u32[]{:S(2)}) copy-start(bf16[2048,1024]{1,0:T(8,128)(2,1)} %param.19) | copy-start | bytes 12582916
  7.2 3.9 %copy-start.10 = (bf16[1024,256]{1,0:T(8,128)(2,1)S(1)}, bf16[1024,256]{1,0:T(8,128)(2,1)}, u32[]{:S(2)}) copy-start(bf16[1024,256]{1,0:T(8,128)(2,1)} %param.23) | copy-start | bytes 1572868
  11.1 16.0 %copy-start.2 = (bf16[2048,256]{1,0:T(8,128)(2,1)}, bf16[2048,256]{1,0:T(8,128)(2,1)S(1)}, u32[]{:S(2)}) copy-start(bf16[2048,256]{1,0:T(8,128)(2,1)S(1)} %convolution_convert_fusion.v_ref) | copy-start | bytes 3145732
  12.4 1.0 copy-start.3
  13.4 8.4 %copy-start.12 = (s32[3]{0:T(128)S(1)}, s32[3]{0:T(128)}, u32[]{:S(2)}) copy-start(s32[3]{0:T(128)} %constant.139.clone) | copy-start | bytes 40
  14.2 12.9 %collective-permute-start.1 = (bf16[256,512]{1,0:T(8,128)(2,1)}, bf16[256,512]{1,0:T(8,128)(2,1)S(1)}, u32[]{:S(2)}, u32[]{:S(2)}) collective-permute-start(bf16[256,512]{1,0:T(8,128)(2,1)} %get-tuple-element.65), channel_id=1, source_target_pairs={{4,0},{8,4},{12,8},{5,1},{9,5},{13,9},{6,2},{10,6},{14,10},{7,3},{... | collective-permute-start | bytes 786440 | tf_op jit(solution)/shard_map/ppermute | solution.py:23
  15.5 11.6 %collective-permute-start = (bf16[256,512]{1,0:T(8,128)(2,1)}, bf16[256,512]{1,0:T(8,128)(2,1)}, u32[]{:S(2)}, u32[]{:S(2)}) collective-permute-start(bf16[256,512]{1,0:T(8,128)(2,1)} %get-tuple-element.64), channel_id=1, source_target_pairs={{0,4},{4,8},{8,12},{1,5},{5,9},{9,13},{2,6},{6,10},{10,14},{3,7},{... | collective-permute-start | bytes 786440 | tf_op jit(solution)/shard_map/ppermute | solution.py:20
  22.5 4.6 %copy-start.7 = (s32[3]{0:T(128)}, s32[3]{0:T(128)S(1)}, u32[]{:S(2)}) copy-start(s32[3]{0:T(128)S(1)} %constant_dynamic-update-slice_fusion.1.scal_ref) | copy-start | bytes 40
  22.5 4.7 %copy-start.4 = (bf16[2048,256]{1,0:T(8,128)(2,1)S(1)}, bf16[2048,256]{1,0:T(8,128)(2,1)}, u32[]{:S(2)}) copy-start(bf16[2048,256]{1,0:T(8,128)(2,1)} %copy-done.3) | copy-start | bytes 3145732
  43.1 90.7 %reduce-scatter.3.cloned.1.call-start = ((), (), s32[]{:S(2)}) async-start(), calls=%async_computation.2 | async-start | bytes 2621440 | tf_op jit(solution)/shard_map/reduce_scatter | solution.py:194
  43.3 0.6 copy-start.8
  56.3 1.0 copy-start.11
  79.1 14.4 %collective-permute-start.4 = (f32[256,264]{1,0:T(8,128)}, f32[256,264]{1,0:T(8,128)S(1)}, u32[]{:S(2)}, u32[]{:S(2)}) collective-permute-start(f32[256,264]{1,0:T(8,128)} %get-tuple-element.69), channel_id=1, source_target_pairs={{0,12},{4,0},{8,4},{12,8},{1,13},{5,1},{9,5},{13,9},{2,14},{6,2},{... | collective-permute-start | bytes 811016 | tf_op jit(solution)/shard_map/ppermute | solution.py:150
  83.6 32.7 %collective-permute-start.3 = (f32[256,264]{1,0:T(8,128)}, f32[256,264]{1,0:T(8,128)S(1)}, u32[]{:S(2)}, u32[]{:S(2)}) collective-permute-start(f32[256,264]{1,0:T(8,128)} %get-tuple-element.68), channel_id=1, source_target_pairs={{0,8},{4,12},{8,0},{12,4},{1,9},{5,13},{9,1},{13,5},{2,10},{6,14},... | collective-permute-start | bytes 811016 | tf_op jit(solution)/shard_map/ppermute | solution.py:150
  83.6 32.7 %collective-permute-start.2 = (f32[256,264]{1,0:T(8,128)}, f32[256,264]{1,0:T(8,128)}, u32[]{:S(2)}, u32[]{:S(2)}) collective-permute-start(f32[256,264]{1,0:T(8,128)} %get-tuple-element.67), channel_id=1, source_target_pairs={{0,4},{4,8},{8,12},{12,0},{1,5},{5,9},{9,13},{13,1},{2,6},{6,10},{... | collective-permute-start | bytes 811016 | tf_op jit(solution)/shard_map/ppermute | solution.py:150
  117.4 1.2 copy-start.1
  122.6 1.5 %copy-start.5 = (f32[256,256]{1,0:T(8,128)S(1)}, f32[256,256]{1,0:T(8,128)}, u32[]{:S(2)}) copy-start(f32[256,256]{1,0:T(8,128)} %copy.24) | copy-start | bytes 786436
  122.6 1.5 %copy-start.6 = (bf16[256,1024]{1,0:T(8,128)(2,1)S(1)}, bf16[256,1024]{1,0:T(8,128)(2,1)}, u32[]{:S(2)}) copy-start(bf16[256,1024]{1,0:T(8,128)(2,1)} %param.27) | copy-start | bytes 1572868
  124.5 3.1 %collective-permute-start.7 = (bf16[256,256]{1,0:T(8,128)(2,1)S(1)}, bf16[256,256]{1,0:T(8,128)(2,1)S(1)}, u32[]{:S(2)}, u32[]{:S(2)}) collective-permute-start(bf16[256,256]{1,0:T(8,128)(2,1)S(1)} %get-tuple-element.71), channel_id=1, source_target_pairs={{0,3},{1,0},{2,1},{3,2},{4,7},{5,4},{6,5},{7,6},{8,11},{9,8},{10,9... | collective-permute-start | bytes 393224 | tf_op jit(solution)/shard_map/ppermute | solution.py:164
  124.5 8.2 %collective-permute-start.6 = (bf16[256,256]{1,0:T(8,128)(2,1)S(1)}, bf16[256,256]{1,0:T(8,128)(2,1)S(1)}, u32[]{:S(2)}, u32[]{:S(2)}) collective-permute-start(bf16[256,256]{1,0:T(8,128)(2,1)S(1)} %get-tuple-element.72), channel_id=1, source_target_pairs={{0,2},{1,3},{2,0},{3,1},{4,6},{5,7},{6,4},{7,5},{8,10},{9,11},{10,... | collective-permute-start | bytes 393224 | tf_op jit(solution)/shard_map/ppermute | solution.py:164
  125.9 7.1 %collective-permute-start.5 = (bf16[256,256]{1,0:T(8,128)(2,1)S(1)}, bf16[256,256]{1,0:T(8,128)(2,1)S(1)}, u32[]{:S(2)}, u32[]{:S(2)}) collective-permute-start(bf16[256,256]{1,0:T(8,128)(2,1)S(1)} %get-tuple-element.70), channel_id=1, source_target_pairs={{0,1},{1,2},{2,3},{3,0},{4,5},{5,6},{6,7},{7,4},{8,9},{9,10},{10,1... | collective-permute-start | bytes 393224 | tf_op jit(solution)/shard_map/ppermute | solution.py:164
Sparse Core Ops, SparseCore 0:
  43.2 33.5 reduce-scatter.4
  79.4 31.4 reduce-scatter.2

commit v3 on v2

--- a/solution.py
+++ b/solution.py
@@ -69,8 +69,15 @@
     block_base = row_base // tq
     scal = jnp.array([0, 0, row_base], jnp.int32).at[0].set(first_frame).at[1].set(length)
     kernel = functools.partial(window_kernel, heads=width // HD, scale=HD ** (-0.5))
+    span = tq + 2 * HALF
+    cost = pl.CostEstimate(
+        flops=4 * rows * span * width + 2 * rows * width * out_width,
+        transcendentals=rows * span * (width // HD),
+        bytes_accessed=2 * (rows * width + 2 * keys_wide.size + w_out.size + rows * out_width),
+    )
     return pl.pallas_call(
         kernel,
+        cost_estimate=cost,
         out_shape=jax.ShapeDtypeStruct((rows, out_width), jnp.bfloat16),
         grid_spec=pltpu.PrefetchScalarGridSpec(
             num_scalar_prefetch=1,
@@ -115,8 +122,15 @@
     tl = min(256, latent_count)
     scal = jnp.reshape(valid_count, (1,)).astype(jnp.int32)
     kernel = functools.partial(latent_kernel, heads=heads, scale=HD ** (-0.5))
+    frame_count = keyed.shape[0]
+    cost = pl.CostEstimate(
+        flops=4 * latent_count * frame_count * width,
+        transcendentals=latent_count * frame_count * heads,
+        bytes_accessed=2 * (latent_query.size + 2 * keyed.size) + 4 * latent_count * (width + 128),
+    )
     acc, stat = pl.pallas_call(
         kernel,
+        cost_estimate=cost,
         out_shape=(
             jax.ShapeDtypeStruct((latent_count, width), jnp.float32),
             jax.ShapeDtypeStruct((latent_count, 128), jnp.float32),
@@ -182,24 +196,20 @@
     padded = extended(stacked, (("seq", 0),), HALF)
     keys_wide = padded[:, :head_width]
     values_wide = padded[:, head_width:]
-    chunks = 2 if frame_count % 512 == 0 else 1
-    chunk_rows = frame_count // chunks
-    frame_parts = []
-    for c in range(chunks):
-        terms = window_attention(
-            query, keys_wide, values_wide, w_out, first_frame, length, c * chunk_rows, chunk_rows
-        )
-        if c == 0:
-            terms, keyed, valued = lax.optimization_barrier((terms, keyed, valued))
-        frame_parts.append(lax.psum_scatter(terms, "head", scatter_dimension=1, tiled=True))
-    frames_out = jnp.concatenate(frame_parts, axis=0)
     latent_count = latents.shape[0]
     latent_query = project(latents, w_latent_query)
     valid_count = jnp.clip(length - first_frame, 0, frame_count)
     peaks, totals, local_accum = latent_attention(latent_query, keyed, valued, valid_count)
     rows_here = latent_count // seq_devices
     payload = jnp.concatenate([local_accum, peaks, totals], axis=1)
+    payload, query, keys_wide, values_wide = lax.optimization_barrier(
+        (payload, query, keys_wide, values_wide)
+    )
     parts = shifted_blocks(payload, "seq", rows_here)
+    frame_terms = window_attention(
+        query, keys_wide, values_wide, w_out, first_frame, length, 0, frame_count
+    )
+    frames_out = lax.psum_scatter(frame_terms, "head", scatter_dimension=1, tiled=True)
     part_accum = parts[:, :, :head_width]
     part_peak = parts[:, :, head_width : head_width + heads_here]
     part_total = parts[:, :, head_width + heads_here :]

time: 143 us -> 139 us (0.972)
  the two profiles are of different devices: /device:TPU:0 before, /device:TPU:11 now
where the time goes in v3:
time: 139 us; the launch traced here: 138 us
  waiting for transfers between devices  40.3 us (29%)
  Pallas kernels  39.3 us (28%)
  between operations  14.9 us (11%)
  matrix products  11.4 us (8%)
  starting transfers between devices  11.2 us (8%)
  other arithmetic  10.9 us (8%)
  local copies, waits for them, and re-layouts  10.2 us (7%)
    ppermute x3, waiting for transfers between devices, shifted_blocks(): parts.append(lax.ppermute(block, axis, pairs))  33.7 us
    pallas_call x1, Pallas kernels, window_attention(): pl.pallas_call(kernel, cost_estimate=cost, out_shape=jax.ShapeDtypeStruct...  21.5 us
    pallas_call x1, Pallas kernels, latent_attention(): pl.pallas_call(kernel, cost_estimate=cost, out_shape=(jax.ShapeDtypeStruc...  17.9 us
    dot_general x4, matrix products, project(): jnp.dot(source, weight, preferred_element_type=jnp.float32)  11.1 us
    ppermute x3, waiting for transfers between devices, column_sum(): total = total + lax.ppermute(block, axis, pairs).astype(jnp.float32)  6.56 us
    concatenate x1, other arithmetic, extended(): block = jnp.concatenate([low, block, high], axis=dim)  4.51 us
    ppermute x3, starting transfers between devices, shifted_blocks(): parts.append(lax.ppermute(block, axis, pairs))  3.78 us
    ppermute x1, starting transfers between devices, extended(): lax.ppermute(lax.slice_in_dim(block, block.shape[dim] - width, None, axis...  3.19 us
  transfers between devices with their start and end apart: 9, of which 6 were waited for; matrix products, arithmetic and copies ran while one was open for 14% of the time, Pallas kernels for 13%

profile of v3, /device:TPU:11, one launch (start us, length us, event | category | flops | bytes accessed | tf_op | source)
XLA Modules:
  0.0 138.3 jit_solution(4725783383096135591)
XLA Ops:
  7.2 3.7 %convolution_convert_fusion.1.v_ref = bf16[2048,256]{1,0:T(8,128)(2,1)S(1)} fusion(bf16[2048,1024]{1,0:T(8,128)(2,1)} %param.14, bf16[1024,256]{1,0:T(8,128)(2,1)} %param.19), kind=kOutput, calls=%fused_computation.2 | convolution fusion | flops 1074266112 | bytes 5767168 | tf_op jit(solution)/shard_map/dot_general | solution.py:29
  11.1 1.3 convolution_convert_fusion.2.k_ref
  12.5 0.9 copy-done.4
  13.4 3.2 %collective-permute-start = (bf16[256,512]{1,0:T(8,128)(2,1)S(1)}, bf16[256,512]{1,0:T(8,128)(2,1)S(1)}, u32[]{:S(2)}, u32[]{:S(2)}) collective-permute-start(bf16[256,512]{1,0:T(8,128)(2,1)S(1)} %get-tuple-element.42), channel_id=1, source_target_pairs={{0,4},{4,8},{8,12},{1,5},{5,9},{9,13},{2,6},{6,10},{10,14},{3,7},{... | collective-permute-start | bytes 786440 | tf_op jit(solution)/shard_map/ppermute | solution.py:20
  16.6 2.3 %collective-permute-start.1 = (bf16[256,512]{1,0:T(8,128)(2,1)S(1)}, bf16[256,512]{1,0:T(8,128)(2,1)S(1)}, u32[]{:S(2)}, u32[]{:S(2)}) collective-permute-start(bf16[256,512]{1,0:T(8,128)(2,1)S(1)} %get-tuple-element.43), channel_id=1, source_target_pairs={{4,0},{8,4},{12,8},{5,1},{9,5},{13,9},{6,2},{10,6},{14,10},{7,3},{... | collective-permute-start | bytes 786440 | tf_op jit(solution)/shard_map/ppermute | solution.py:23
  19.5 4.6 %convolution_convert_fusion.q_ref = bf16[2048,256]{1,0:T(8,128)(2,1)} fusion(bf16[2048,1024]{1,0:T(8,128)(2,1)} %param.14, bf16[1024,256]{1,0:T(8,128)(2,1)} %param.17), kind=kOutput, calls=%fused_computation.1 | convolution fusion | flops 1074266112 | bytes 5767168 | tf_op jit(solution)/shard_map/dot_general | solution.py:29
  24.2 1.5 %convolution_convert_fusion.4.q_ref = bf16[1024,256]{1,0:T(8,128)(2,1)} fusion(bf16[1024,1024]{1,0:T(8,128)(2,1)S(1)} %copy-done, bf16[1024,256]{1,0:T(8,128)(2,1)S(1)} %copy-done.10), kind=kOutput, calls=%fused_computation.7 | convolution fusion | flops 537133056 | bytes 3145728 | tf_op jit(solution)/shard_map/dot_general | solution.py:29
  25.7 17.9 %shard_map.113 = (f32[1024,256]{1,0:T(8,128)}, f32[1024,128]{1,0:T(8,128)}) custom-call(s32[1]{0:T(128)} %bitcast.2.scal_ref, bf16[1024,256]{1,0:T(8,128)(2,1)} %convolution_convert_fusion.4.q_ref, bf16[2048,256]{1,0:T(8,128)(2,1)} %copy-done.4, bf16[2048,256]{1,0:T(8,128)(2,1)} %copy-done.2), custom_call_target="tpu_custom_call" | custom-call | flops 2147483648 | bytes 4194304 | tf_op jit(solution)/shard_map/pallas_call | solution.py:131
  43.6 2.8 %pad_maximum_fusion.1 = f32[1024,264]{1,0:T(8,128)} fusion(f32[1024,8]{1,0:T(8,128)} %bitcast.23, f32[1024,256]{1,0:T(8,128)} %get-tuple-element.32), kind=kLoop, calls=%fused_computation.4 | loop fusion | flops 270336 | bytes 2162688 | tf_op jit(solution)/shard_map/concatenate | solution.py:204
  46.4 4.5 %pad_maximum_fusion = bf16[2560,512]{1,0:T(8,128)(2,1)S(1)} fusion(bf16[256,512]{1,0:T(8,128)(2,1)S(1)} %collective-permute-done.1, bf16[2048,256]{1,0:T(8,128)(2,1)S(1)} %copy-done.3, bf16[2048,256]{1,0:T(8,128)(2,1)S(1)} %copy-done.5, bf16[256,512]{1,0:T(8,128)(2,1)S(1)} %collective-permute-done), kind=kLoop, calls=%fused_computation | loop fusion | flops 10485760 | bytes 5242880 | tf_op jit(solution)/shard_map/concatenate | solution.py:24
  50.9 1.7 %fusion.2 = (bf16[2560,256]{1,0:T(8,128)(2,1)}, bf16[2560,256]{1,0:T(8,128)(2,1)}) fusion(bf16[2560,512]{1,0:T(8,128)(2,1)S(1)} %pad_maximum_fusion), kind=kLoop, calls=%fused_computation.26 | loop fusion | bytes 5242880 | tf_op jit(solution)/shard_map/slice | solution.py:198
  52.6 21.5 %shard_map.114 = bf16[2048,1024]{1,0:T(8,128)(2,1)} custom-call(s32[3]{0:T(128)} %copy-done.11, bf16[2048,256]{1,0:T(8,128)(2,1)} %convolution_convert_fusion.q_ref, bf16[2560,256]{1,0:T(8,128)(2,1)} %get-tuple-element.35.k_ref, bf16[2560,256]{1,0:T(8,128)(2,1)} %get-tuple-element.36.v_ref, bf16[256,1024]{1,0:T(8,128)(2,1)} %w_ref.1), custom_call_target="tpu_custom_call" | custom-call | flops 2684354560 | bytes 8388608 | tf_op jit(solution)/shard_map/pallas_call | solution.py:78
  74.2 2.4 %dynamic-slice_bitcast_fusion = (f32[1,256,264]{2,1,0:T(8,128)S(1)}, f32[256,264]{1,0:T(8,128)}, f32[256,264]{1,0:T(8,128)}, f32[256,264]{1,0:T(8,128)}) fusion(f32[1024,264]{1,0:T(8,128)} %pad_maximum_fusion.1, s32[]{:T(128)S(6)} %select_n.51, s32[]{:T(128)S(6)} %select_n.57, s32[]{:T(128)S(6)} %select_n.55, s32[]{:T(128)S(6)} %select_n.53), kind=kLoop, calls=%fused_computation.14 | loop fusion | bytes 2162704 | tf_op jit(solution)/shard_map/stack | solution.py:165
  76.6 1.3 collective-permute-start.2
  77.9 1.0 collective-permute-start.3
  78.9 1.5 %collective-permute-start.4 = (f32[256,264]{1,0:T(8,128)}, f32[256,264]{1,0:T(8,128)}, u32[]{:S(2)}, u32[]{:S(2)}) collective-permute-start(f32[256,264]{1,0:T(8,128)} %get-tuple-element.45), channel_id=1, source_target_pairs={{0,12},{4,0},{8,4},{12,8},{1,13},{5,1},{9,5},{13,9},{2,14},{6,2},{... | collective-permute-start | bytes 811016 | tf_op jit(solution)/shard_map/ppermute | solution.py:164
  80.4 5.8 %collective-permute-done.2 = f32[256,264]{1,0:T(8,128)S(1)} collective-permute-done((f32[256,264]{1,0:T(8,128)}, f32[256,264]{1,0:T(8,128)S(1)}, u32[]{:S(2)}, u32[]{:S(2)}) %collective-permute-start.2) | collective-permute-done | bytes 270368 | tf_op jit(solution)/shard_map/ppermute | solution.py:164
  86.2 24.5 %collective-permute-done.3 = f32[256,264]{1,0:T(8,128)S(1)} collective-permute-done((f32[256,264]{1,0:T(8,128)}, f32[256,264]{1,0:T(8,128)S(1)}, u32[]{:S(2)}, u32[]{:S(2)}) %collective-permute-start.3) | collective-permute-done | bytes 270368 | tf_op jit(solution)/shard_map/ppermute | solution.py:164
  110.7 3.5 %collective-permute-done.4 = f32[256,264]{1,0:T(8,128)} collective-permute-done((f32[256,264]{1,0:T(8,128)}, f32[256,264]{1,0:T(8,128)}, u32[]{:S(2)}, u32[]{:S(2)}) %collective-permute-start.4) | collective-permute-done | bytes 270368 | tf_op jit(solution)/shard_map/ppermute | solution.py:164
  114.1 1.1 pad_maximum_fusion.2
  115.3 1.1 copy-done.1
  116.8 1.1 broadcast_in_dim.7
  117.9 1.6 %copy.21 = f32[4,256,256]{2,1,0:T(8,128)S(1)} copy(f32[4,256,256]{1,2,0:T(8,128)} %bitcast.21) | data formatting | bytes 2097152 | tf_op jit(solution)/shard_map/reshape | solution.py:219
  119.6 0.9 copy.23
  120.4 1.5 %fusion = f32[256,256]{1,0:T(8,128)S(1)} fusion(f32[4,256,256]{2,1,0:T(8,128)S(1)} %copy.21, f32[4,256,264]{2,1,0:T(8,128)} %copy-done.1), kind=kLoop, calls=%fused_computation.9 | loop fusion | flops 458752 | bytes 2359296 | tf_op jit(solution)/shard_map/reduce_sum | solution.py:219
  121.9 0.3 convolution_convert_fusion.3
  122.3 0.7 collective-permute-start.5
  123.0 1.2 collective-permute-start.6
  124.2 1.5 %collective-permute-done.5 = bf16[256,256]{1,0:T(8,128)(2,1)S(1)} collective-permute-done((bf16[256,256]{1,0:T(8,128)(2,1)S(1)}, bf16[256,256]{1,0:T(8,128)(2,1)S(1)}, u32[]{:S(2)}, u32[]{:S(2)}) %collective-permute-start.5) | collective-permute-done | bytes 131104 | tf_op jit(solution)/shard_map/ppermute | solution.py:178
  125.7 4.5 %collective-permute-done.6 = bf16[256,256]{1,0:T(8,128)(2,1)S(1)} collective-permute-done((bf16[256,256]{1,0:T(8,128)(2,1)S(1)}, bf16[256,256]{1,0:T(8,128)(2,1)S(1)}, u32[]{:S(2)}, u32[]{:S(2)}) %collective-permute-start.6) | collective-permute-done | bytes 131104 | tf_op jit(solution)/shard_map/ppermute | solution.py:178
  130.1 0.6 collective-permute-done.7
  130.8 0.7 add_convert_fusion
  (37 shorter events, 0.9 us)
Async XLA Ops:
  7.2 17.0 %copy-start = (bf16[1024,1024]{1,0:T(8,128)(2,1)S(1)}, bf16[1024,1024]{1,0:T(8,128)(2,1)}, u32[]{:S(2)}) copy-start(bf16[1024,1024]{1,0:T(8,128)(2,1)} %param.15) | copy-start | bytes 6291460
  7.2 3.8 %copy-start.9 = (bf16[1024,256]{1,0:T(8,128)(2,1)S(1)}, bf16[1024,256]{1,0:T(8,128)(2,1)}, u32[]{:S(2)}) copy-start(bf16[1024,256]{1,0:T(8,128)(2,1)} %param.18) | copy-start | bytes 1572868
  7.2 124.3 %reduce-scatter.2.cloned.1.call-start = ((), (), s32[]{:S(2)}) async-start(), calls=%async_computation.1 | async-start | bytes 5242880 | tf_op jit(solution)/shard_map/reduce_scatter | solution.py:212
  7.2 3.9 %copy-start.8 = (bf16[2048,1024]{1,0:T(8,128)(2,1)S(1)}, bf16[2048,1024]{1,0:T(8,128)(2,1)}, u32[]{:S(2)}) copy-start(bf16[2048,1024]{1,0:T(8,128)(2,1)} %param.14) | copy-start | bytes 12582916
  11.1 1.3 copy-start.2
  12.4 1.0 copy-start.4
  13.4 33.0 %collective-permute-start = (bf16[256,512]{1,0:T(8,128)(2,1)S(1)}, bf16[256,512]{1,0:T(8,128)(2,1)S(1)}, u32[]{:S(2)}, u32[]{:S(2)}) collective-permute-start(bf16[256,512]{1,0:T(8,128)(2,1)S(1)} %get-tuple-element.42), channel_id=1, source_target_pairs={{0,4},{4,8},{8,12},{1,5},{5,9},{9,13},{2,6},{6,10},{10,14},{3,7},{... | collective-permute-start | bytes 786440 | tf_op jit(solution)/shard_map/ppermute | solution.py:20
  16.6 29.8 %collective-permute-start.1 = (bf16[256,512]{1,0:T(8,128)(2,1)S(1)}, bf16[256,512]{1,0:T(8,128)(2,1)S(1)}, u32[]{:S(2)}, u32[]{:S(2)}) collective-permute-start(bf16[256,512]{1,0:T(8,128)(2,1)S(1)} %get-tuple-element.43), channel_id=1, source_target_pairs={{4,0},{8,4},{12,8},{5,1},{9,5},{13,9},{6,2},{10,6},{14,10},{7,3},{... | collective-permute-start | bytes 786440 | tf_op jit(solution)/shard_map/ppermute | solution.py:23
  19.5 4.6 %copy-start.10 = (bf16[1024,256]{1,0:T(8,128)(2,1)S(1)}, bf16[1024,256]{1,0:T(8,128)(2,1)}, u32[]{:S(2)}) copy-start(bf16[1024,256]{1,0:T(8,128)(2,1)} %param.21) | copy-start | bytes 1572868
  24.2 1.5 %copy-start.11 = (s32[3]{0:T(128)}, s32[3]{0:T(128)S(1)}, u32[]{:S(2)}) copy-start(s32[3]{0:T(128)S(1)} %constant_dynamic-update-slice_fusion.scal_ref) | copy-start | bytes 40
  43.6 2.8 %copy-start.3 = (bf16[2048,256]{1,0:T(8,128)(2,1)S(1)}, bf16[2048,256]{1,0:T(8,128)(2,1)}, u32[]{:S(2)}) copy-start(bf16[2048,256]{1,0:T(8,128)(2,1)} %copy-done.2) | copy-start | bytes 3145732
  43.6 2.8 %copy-start.5 = (bf16[2048,256]{1,0:T(8,128)(2,1)S(1)}, bf16[2048,256]{1,0:T(8,128)(2,1)}, u32[]{:S(2)}) copy-start(bf16[2048,256]{1,0:T(8,128)(2,1)} %copy-done.4) | copy-start | bytes 3145732
  76.6 9.6 %collective-permute-start.2 = (f32[256,264]{1,0:T(8,128)}, f32[256,264]{1,0:T(8,128)S(1)}, u32[]{:S(2)}, u32[]{:S(2)}) collective-permute-start(f32[256,264]{1,0:T(8,128)} %get-tuple-element.47), channel_id=1, source_target_pairs={{0,4},{4,8},{8,12},{12,0},{1,5},{5,9},{9,13},{13,1},{2,6},{6,10},{... | collective-permute-start | bytes 811016 | tf_op jit(solution)/shard_map/ppermute | solution.py:164
  77.9 32.8 %collective-permute-start.3 = (f32[256,264]{1,0:T(8,128)}, f32[256,264]{1,0:T(8,128)S(1)}, u32[]{:S(2)}, u32[]{:S(2)}) collective-permute-start(f32[256,264]{1,0:T(8,128)} %get-tuple-element.46), channel_id=1, source_target_pairs={{0,8},{4,12},{8,0},{12,4},{1,9},{5,13},{9,1},{13,5},{2,10},{6,14},... | collective-permute-start | bytes 811016 | tf_op jit(solution)/shard_map/ppermute | solution.py:164
  78.9 35.2 %collective-permute-start.4 = (f32[256,264]{1,0:T(8,128)}, f32[256,264]{1,0:T(8,128)}, u32[]{:S(2)}, u32[]{:S(2)}) collective-permute-start(f32[256,264]{1,0:T(8,128)} %get-tuple-element.45), channel_id=1, source_target_pairs={{0,12},{4,0},{8,4},{12,8},{1,13},{5,1},{9,5},{13,9},{2,14},{6,2},{... | collective-permute-start | bytes 811016 | tf_op jit(solution)/shard_map/ppermute | solution.py:164
  115.2 1.2 copy-start.1
  120.4 1.5 %copy-start.6 = (f32[256,256]{1,0:T(8,128)S(1)}, f32[256,256]{1,0:T(8,128)}, u32[]{:S(2)}) copy-start(f32[256,256]{1,0:T(8,128)} %copy.23) | copy-start | bytes 786436
  120.4 1.5 %copy-start.7 = (bf16[256,1024]{1,0:T(8,128)(2,1)S(1)}, bf16[256,1024]{1,0:T(8,128)(2,1)}, u32[]{:S(2)}) copy-start(bf16[256,1024]{1,0:T(8,128)(2,1)} %param.22) | copy-start | bytes 1572868
  122.3 3.4 %collective-permute-start.5 = (bf16[256,256]{1,0:T(8,128)(2,1)S(1)}, bf16[256,256]{1,0:T(8,128)(2,1)S(1)}, u32[]{:S(2)}, u32[]{:S(2)}) collective-permute-start(bf16[256,256]{1,0:T(8,128)(2,1)S(1)} %get-tuple-element.48), channel_id=1, source_target_pairs={{0,1},{1,2},{2,3},{3,0},{4,5},{5,6},{6,7},{7,4},{8,9},{9,10},{10,1... | collective-permute-start | bytes 393224 | tf_op jit(solution)/shard_map/ppermute | solution.py:178
  123.0 7.2 %collective-permute-start.6 = (bf16[256,256]{1,0:T(8,128)(2,1)S(1)}, bf16[256,256]{1,0:T(8,128)(2,1)S(1)}, u32[]{:S(2)}, u32[]{:S(2)}) collective-permute-start(bf16[256,256]{1,0:T(8,128)(2,1)S(1)} %get-tuple-element.50), channel_id=1, source_target_pairs={{0,2},{1,3},{2,0},{3,1},{4,6},{5,7},{6,4},{7,5},{8,10},{9,11},{10,... | collective-permute-start | bytes 393224 | tf_op jit(solution)/shard_map/ppermute | solution.py:178
  124.2 6.6 %collective-permute-start.7 = (bf16[256,256]{1,0:T(8,128)(2,1)S(1)}, bf16[256,256]{1,0:T(8,128)(2,1)S(1)}, u32[]{:S(2)}, u32[]{:S(2)}) collective-permute-start(bf16[256,256]{1,0:T(8,128)(2,1)S(1)} %get-tuple-element.49), channel_id=1, source_target_pairs={{0,3},{1,0},{2,1},{3,2},{4,7},{5,4},{6,5},{7,6},{8,11},{9,8},{10,9... | collective-permute-start | bytes 393224 | tf_op jit(solution)/shard_map/ppermute | solution.py:178
Sparse Core Ops, SparseCore 0:
  74.2 45.2 reduce-scatter.1

commit v4 on v3

--- a/solution.py
+++ b/solution.py
@@ -12,26 +12,36 @@
 NEG = -1e30
 
 
-def extended(block, sides, width):
-    for axis, dim in sides:
-        count = lax.axis_size(axis)
-        forward = [(i, i + 1) for i in range(count - 1)]
-        backward = [(target, source) for source, target in forward]
-        low = lax.ppermute(
-            lax.slice_in_dim(block, block.shape[dim] - width, None, axis=dim), axis, forward
-        )
-        high = lax.ppermute(lax.slice_in_dim(block, 0, width, axis=dim), axis, backward)
-        block = jnp.concatenate([low, block, high], axis=dim)
-    return block
+def halos(keyed, valued, axis):
+    count = lax.axis_size(axis)
+    forward = [(i, i + 1) for i in range(count - 1)]
+    backward = [(target, source) for source, target in forward]
+    tail = jnp.concatenate([keyed[-HALF:], valued[-HALF:]], axis=1)
+    head = jnp.concatenate([keyed[:HALF], valued[:HALF]], axis=1)
+    return lax.ppermute(tail, axis, forward), lax.ppermute(head, axis, backward)
 
 
 def project(source, weight):
     return jnp.dot(source, weight, preferred_element_type=jnp.float32).astype(jnp.bfloat16)
 
 
-def window_kernel(scal_ref, q_ref, k_ref, v_ref, w_ref, o_ref, att_ref, *, heads, scale):
+def window_kernel(
+    scal_ref, q_ref, k_ref, v_ref, low_ref, high_ref, w_ref, o_ref, kbuf, vbuf, att_ref, *,
+    heads, scale
+):
     tq = q_ref.shape[0]
+    frame_count, width = k_ref.shape
     span = tq + 2 * HALF
+
+    @pl.when(pl.program_id(0) == 0)
+    def _fill():
+        kbuf[0:HALF, :] = low_ref[:, 0:width]
+        vbuf[0:HALF, :] = low_ref[:, width : 2 * width]
+        kbuf[HALF : HALF + frame_count, :] = k_ref[...]
+        vbuf[HALF : HALF + frame_count, :] = v_ref[...]
+        kbuf[HALF + frame_count :, :] = high_ref[:, 0:width]
+        vbuf[HALF + frame_count :, :] = high_ref[:, width : 2 * width]
+
     start = pl.multiple_of(scal_ref[2] + pl.program_id(0) * tq, tq)
     first = scal_ref[0]
     length = scal_ref[1]
@@ -45,8 +55,8 @@
     for h in range(heads):
         cols = slice(h * HD, (h + 1) * HD)
         q = q_ref[:, cols]
-        k = k_ref[pl.ds(start, span), cols]
-        v = v_ref[pl.ds(start, span), cols]
+        k = kbuf[pl.ds(start, span), cols]
+        v = vbuf[pl.ds(start, span), cols]
         s = lax.dot_general(
             q, k, (((1,), (1,)), ((), ())), preferred_element_type=jnp.float32
         ) * scale
@@ -62,19 +72,20 @@
     ).astype(jnp.bfloat16)
 
 
-def window_attention(query, keys_wide, values_wide, w_out, first_frame, length, row_base, rows):
-    width = query.shape[1]
+def window_attention(query, keyed, valued, low, high, w_out, first_frame, length, row_base, rows):
+    frame_count, width = query.shape
     out_width = w_out.shape[1]
     tq = min(256, rows)
     block_base = row_base // tq
+    span = tq + 2 * HALF
     scal = jnp.array([0, 0, row_base], jnp.int32).at[0].set(first_frame).at[1].set(length)
     kernel = functools.partial(window_kernel, heads=width // HD, scale=HD ** (-0.5))
-    span = tq + 2 * HALF
     cost = pl.CostEstimate(
         flops=4 * rows * span * width + 2 * rows * width * out_width,
         transcendentals=rows * span * (width // HD),
-        bytes_accessed=2 * (rows * width + 2 * keys_wide.size + w_out.size + rows * out_width),
+        bytes_accessed=2 * (2 * query.size + rows * width + 2 * low.size + w_out.size + rows * out_width),
     )
+    full = lambda i, s: (0, 0)
     return pl.pallas_call(
         kernel,
         cost_estimate=cost,
@@ -84,14 +95,21 @@
             grid=(rows // tq,),
             in_specs=[
                 pl.BlockSpec((tq, width), lambda i, s: (i + block_base, 0)),
-                pl.BlockSpec(keys_wide.shape, lambda i, s: (0, 0)),
-                pl.BlockSpec(values_wide.shape, lambda i, s: (0, 0)),
-                pl.BlockSpec(w_out.shape, lambda i, s: (0, 0)),
+                pl.BlockSpec(keyed.shape, full),
+                pl.BlockSpec(valued.shape, full),
+                pl.BlockSpec(low.shape, full),
+                pl.BlockSpec(high.shape, full),
+                pl.BlockSpec(w_out.shape, full),
             ],
             out_specs=pl.BlockSpec((tq, out_width), lambda i, s: (i, 0)),
-            scratch_shapes=[pltpu.VMEM((tq, width), jnp.bfloat16)],
-        ),
-    )(scal, query, keys_wide, values_wide, w_out)
+            scratch_shapes=[
+                pltpu.VMEM((frame_count + 2 * HALF, width), jnp.bfloat16),
+                pltpu.VMEM((frame_count + 2 * HALF, width), jnp.bfloat16),
+                pltpu.VMEM((tq, width), jnp.bfloat16),
+            ],
+        ),
+        compiler_params=pltpu.CompilerParams(dimension_semantics=("arbitrary",)),
+    )(scal, query, keyed, valued, low, high, w_out)
 
 
 def latent_kernel(scal_ref, q_ref, k_ref, v_ref, acc_ref, stat_ref, *, heads, scale):
@@ -179,6 +197,30 @@
     return total.astype(jnp.bfloat16)
 
 
+def paired_column_sum(partial, axis):
+    count = lax.axis_size(axis)
+    if count % 2 != 0:
+        return column_sum(partial, axis)
+    chips = count // 2
+    place = lax.axis_index(axis)
+    core = place % 2
+    chip = place // 2
+    rows = partial.shape[0]
+    width = partial.shape[1] // count
+    grid = partial.reshape(rows, chips, 2, width)
+    mine = lax.dynamic_index_in_dim(grid, core, axis=2, keepdims=False)
+    theirs = lax.dynamic_index_in_dim(grid, 1 - core, axis=2, keepdims=False)
+    swapped = lax.ppermute(theirs, axis, [(i, i ^ 1) for i in range(count)])
+    chip_sum = mine.astype(jnp.float32) + swapped.astype(jnp.float32)
+    total = lax.dynamic_index_in_dim(chip_sum, chip, axis=1, keepdims=False)
+    for shift in range(1, chips):
+        target = (chip + shift) % chips
+        block = lax.dynamic_index_in_dim(chip_sum, target, axis=1, keepdims=False)
+        pairs = [(2 * c + k, 2 * ((c + shift) % chips) + k) for c in range(chips) for k in range(2)]
+        total = total + lax.ppermute(block.astype(jnp.bfloat16), axis, pairs).astype(jnp.float32)
+    return total.astype(jnp.bfloat16)
+
+
 def per_device(
     frames, latents, lengths, w_query, w_key, w_value, w_out, w_latent_query, w_latent_out
 ):
@@ -192,24 +234,24 @@
     query = project(frames, w_query)
     keyed = project(frames, w_key)
     valued = project(frames, w_value)
-    stacked = jnp.concatenate([keyed, valued], axis=1)
-    padded = extended(stacked, (("seq", 0),), HALF)
-    keys_wide = padded[:, :head_width]
-    values_wide = padded[:, head_width:]
+    low, high = halos(keyed, valued, "seq")
+    chunks = 2 if frame_count % 512 == 0 else 1
+    chunk_rows = frame_count // chunks
+    frame_parts = []
+    for c in range(chunks):
+        terms = window_attention(
+            query, keyed, valued, low, high, w_out, first_frame, length, c * chunk_rows, chunk_rows
+        )
+        frame_parts.append(paired_column_sum(terms, "head"))
+    terms, keyed, valued = lax.optimization_barrier((terms, keyed, valued))
+    frames_out = jnp.concatenate(frame_parts, axis=0)
     latent_count = latents.shape[0]
     latent_query = project(latents, w_latent_query)
     valid_count = jnp.clip(length - first_frame, 0, frame_count)
     peaks, totals, local_accum = latent_attention(latent_query, keyed, valued, valid_count)
     rows_here = latent_count // seq_devices
     payload = jnp.concatenate([local_accum, peaks, totals], axis=1)
-    payload, query, keys_wide, values_wide = lax.optimization_barrier(
-        (payload, query, keys_wide, values_wide)
-    )
     parts = shifted_blocks(payload, "seq", rows_here)
-    frame_terms = window_attention(
-        query, keys_wide, values_wide, w_out, first_frame, length, 0, frame_count
-    )
-    frames_out = lax.psum_scatter(frame_terms, "head", scatter_dimension=1, tiled=True)
     part_accum = parts[:, :, :head_width]
     part_peak = parts[:, :, head_width : head_width + heads_here]
     part_total = parts[:, :, head_width + heads_here :]

time: 139 us -> 155 us (1.12)
  the two profiles are of different devices: /device:TPU:11 before, /device:TPU:8 now
where the time goes in v4:
time: 155 us; the launch traced here: 154 us
  Pallas kernels  43.1 us (28%)
  waiting for transfers between devices  34.9 us (23%)
  local copies, waits for them, and re-layouts  33.3 us (21%)
  starting transfers between devices  16 us (10%)
  matrix products  13.4 us (9%)
  other arithmetic  11.9 us (8%)
  between operations  1.71 us (1%)
    pallas_call x2, Pallas kernels, window_attention(): pl.pallas_call(kernel, cost_estimate=cost, out_shape=jax.ShapeDtypeStruct...  25.3 us
    pallas_call x1, Pallas kernels, latent_attention(): pl.pallas_call(kernel, cost_estimate=cost, out_shape=(jax.ShapeDtypeStruc...  17.9 us
    ppermute x3, waiting for transfers between devices, shifted_blocks(): parts.append(lax.ppermute(block, axis, pairs))  17.5 us
    ppermute x2, waiting for transfers between devices, paired_column_sum(): lax.ppermute(block.astype(jnp.bfloat16), axis, pairs).astype(jnp.float32)  17.4 us
    dot_general x4, matrix products, project(): jnp.dot(source, weight, preferred_element_type=jnp.float32)  12.1 us
    dynamic_slice x2, local copies, waits for them, and re-layouts, paired_column_sum(): mine = lax.dynamic_index_in_dim(grid, core, axis=2, keepdims=False)  11.3 us
    reshape x2, local copies, waits for them, and re-layouts, paired_column_sum(): grid = partial.reshape(rows, chips, 2, width)  8.99 us
    unnamed x37, local copies, waits for them, and re-layouts  5.04 us
  transfers between devices with their start and end apart: 12, of which 5 were waited for; matrix products, arithmetic and copies ran while one was open for 23% of the time, Pallas kernels for 0%

profile of v4, /device:TPU:8, one launch (start us, length us, event | category | flops | bytes accessed | tf_op | source)
XLA Modules:
  0.0 154.3 jit_solution(15435580833522227928)
XLA Ops:
  0.7 3.7 %convolution_convert_fusion.1.k_ref = bf16[2048,256]{1,0:T(8,128)(2,1)S(1)} fusion(bf16[2048,1024]{1,0:T(8,128)(2,1)} %param.19, bf16[1024,256]{1,0:T(8,128)(2,1)} %param.23), kind=kOutput, calls=%fused_computation.5 | convolution fusion | flops 1074266112 | bytes 5767168 | tf_op jit(solution)/shard_map/dot_general | solution.py:25
  4.5 1.3 convolution_convert_fusion.v_ref
  6.8 3.5 %collective-permute-start = (bf16[256,512]{1,0:T(8,128)(2,1)S(1)}, bf16[256,512]{1,0:T(8,128)(2,1)S(1)}, u32[]{:S(2)}, u32[]{:S(2)}) collective-permute-start(bf16[256,512]{1,0:T(8,128)(2,1)S(1)} %pad_maximum_fusion.2), channel_id=1, source_target_pairs={{0,4},{4,8},{8,12},{1,5},{5,9},{9,13},{2,6},{6,10},{10,14},{3,7},{... | collective-permute-start | bytes 786440 | tf_op jit(solution)/shard_map/ppermute | solution.py:21
  10.3 2.6 %collective-permute-start.1 = (bf16[256,512]{1,0:T(8,128)(2,1)S(1)}, bf16[256,512]{1,0:T(8,128)(2,1)S(1)}, u32[]{:S(2)}, u32[]{:S(2)}) collective-permute-start(bf16[256,512]{1,0:T(8,128)(2,1)S(1)} %pad_maximum_fusion.3), channel_id=1, source_target_pairs={{4,0},{8,4},{12,8},{5,1},{9,5},{13,9},{6,2},{10,6},{14,10},{7,3},{... | collective-permute-start | bytes 786440 | tf_op jit(solution)/shard_map/ppermute | solution.py:21
  13.8 4.5 %convolution_convert_fusion.2.q_ref = bf16[2048,256]{1,0:T(8,128)(2,1)} fusion(bf16[2048,1024]{1,0:T(8,128)(2,1)} %param.19, bf16[1024,256]{1,0:T(8,128)(2,1)} %param.22), kind=kOutput, calls=%fused_computation.6 | convolution fusion | flops 1074266112 | bytes 5767168 | tf_op jit(solution)/shard_map/dot_general | solution.py:25
  18.3 2.6 %convolution_convert_fusion.4.q_ref = bf16[1024,256]{1,0:T(8,128)(2,1)} fusion(bf16[1024,1024]{1,0:T(8,128)(2,1)S(1)} %copy-done, bf16[1024,256]{1,0:T(8,128)(2,1)} %param.26), kind=kOutput, calls=%fused_computation.15 | convolution fusion | flops 537133056 | bytes 3145728 | tf_op jit(solution)/shard_map/dot_general | solution.py:25
  22.3 12.7 %shard_map.123 = bf16[1024,1024]{1,0:T(8,128)(2,1)} custom-call(s32[3]{0:T(128)} %copy-done.13, bf16[2048,256]{1,0:T(8,128)(2,1)} %convolution_convert_fusion.2.q_ref, bf16[2048,256]{1,0:T(8,128)(2,1)} %copy-done.9, bf16[2048,256]{1,0:T(8,128)(2,1)} %copy-done.10, bf16[256,512]{1,0:T(8,128)(2,1)} %copy-done.11, bf16[256,512]{1,0:T(8,128)(2,1)} %copy-done.12, ...), custom_call_target="tpu_custom_call" | custom-call | flops 1342177280 | bytes 5767168 | tf_op jit(solution)/shard_map/pallas_call | solution.py:89
  35.0 4.5 %reshape.101 = bf16[1024,2,2,256]{3,2,1,0:T(2,128)(2,1)} reshape(bf16[1024,1024]{1,0:T(8,128)(2,1)} %shard_map.123) | data formatting | bytes 4194304 | tf_op jit(solution)/shard_map/reshape | solution.py:210
  39.4 12.6 %shard_map.122 = bf16[1024,1024]{1,0:T(8,128)(2,1)} custom-call(s32[3]{0:T(128)} %copy-done.14, bf16[2048,256]{1,0:T(8,128)(2,1)} %convolution_convert_fusion.2.q_ref, bf16[2048,256]{1,0:T(8,128)(2,1)} %copy-done.9, bf16[2048,256]{1,0:T(8,128)(2,1)} %copy-done.10, bf16[256,512]{1,0:T(8,128)(2,1)} %copy-done.11, bf16[256,512]{1,0:T(8,128)(2,1)} %copy-done.12, ...), custom_call_target="tpu_custom_call" | custom-call | flops 1342177280 | bytes 5767168 | tf_op jit(solution)/shard_map/pallas_call | solution.py:89
  52.1 4.5 %reshape.100 = bf16[1024,2,2,256]{3,2,1,0:T(2,128)(2,1)} reshape(bf16[1024,1024]{1,0:T(8,128)(2,1)} %shard_map.122) | data formatting | bytes 4194304 | tf_op jit(solution)/shard_map/reshape | solution.py:210
  56.6 17.9 %shard_map.124 = (f32[1024,256]{1,0:T(8,128)}, f32[1024,128]{1,0:T(8,128)}) custom-call(s32[1]{0:T(128)} %bitcast.10.scal_ref, bf16[1024,256]{1,0:T(8,128)(2,1)} %convolution_convert_fusion.4.q_ref, bf16[2048,256]{1,0:T(8,128)(2,1)} %copy-done.9, bf16[2048,256]{1,0:T(8,128)(2,1)} %copy-done.10), custom_call_target="tpu_custom_call" | custom-call | flops 2147483648 | bytes 4194304 | tf_op jit(solution)/shard_map/pallas_call | solution.py:149
  74.4 1.6 %fusion.8 = (f32[1,256,264]{2,1,0:T(8,128)S(1)}, f32[256,264]{1,0:T(8,128)S(1)}, f32[256,264]{1,0:T(8,128)S(1)}, f32[256,264]{1,0:T(8,128)S(1)}) fusion(s32[]{:T(128)S(6)} %select_n.93, f32[1024,256]{1,0:T(8,128)} %get-tuple-element.56, f32[1024,8]{1,0:T(8,128)} %bitcast.51, s32[]{:T(128)S(6)} %select_n.95, s32[]{:T(128)S(6)} %select_n.97, s32[]{:T(128)S(6)} %select_n.99), kind=kLoop, calls=%fused_computation.37 | loop fusion | flops 270336 | bytes 2162704 | tf_op jit(solution)/shard_map/stack | solution.py:183
  76.0 1.6 %collective-permute-start.6 = (f32[256,264]{1,0:T(8,128)S(1)}, f32[256,264]{1,0:T(8,128)S(1)}, u32[]{:S(2)}, u32[]{:S(2)}) collective-permute-start(f32[256,264]{1,0:T(8,128)S(1)} %get-tuple-element.65), channel_id=1, source_target_pairs={{0,4},{4,8},{8,12},{12,0},{1,5},{5,9},{9,13},{13,1},{2,6},{6,10},{... | collective-permute-start | bytes 811016 | tf_op jit(solution)/shard_map/ppermute | solution.py:182
  78.7 1.9 %collective-permute-start.8 = (f32[256,264]{1,0:T(8,128)S(1)}, f32[256,264]{1,0:T(8,128)S(1)}, u32[]{:S(2)}, u32[]{:S(2)}) collective-permute-start(f32[256,264]{1,0:T(8,128)S(1)} %get-tuple-element.67), channel_id=1, source_target_pairs={{0,12},{4,0},{8,4},{12,8},{1,13},{5,1},{9,5},{13,9},{2,14},{6,2},{... | collective-permute-start | bytes 811016 | tf_op jit(solution)/shard_map/ppermute | solution.py:182
  80.7 5.6 %constant_dynamic-slice_fusion.3 = (bf16[1024,2,1,256]{3,2,1,0:T(2,128)(2,1)}, bf16[1024,2,1,256]{3,2,1,0:T(2,128)(2,1)S(1)}) fusion(bf16[1024,2,2,256]{3,2,1,0:T(2,128)(2,1)S(1)} %copy-done.2, s32[]{:T(128)S(6)} %select_n.87, s32[]{:T(128)S(6)} %select_n.88), kind=kLoop, calls=%fused_computation.47 | loop fusion | bytes 4194312 | tf_op jit(solution)/shard_map/jit(dynamic_index_in_dim)/dynamic_slice | solution.py:211
  88.3 5.7 %constant_dynamic-slice_fusion.5 = (bf16[1024,2,1,256]{3,2,1,0:T(2,128)(2,1)}, bf16[1024,2,1,256]{3,2,1,0:T(2,128)(2,1)S(1)}) fusion(bf16[1024,2,2,256]{3,2,1,0:T(2,128)(2,1)S(1)} %copy-done.1, s32[]{:T(128)S(6)} %select_n.87, s32[]{:T(128)S(6)} %select_n.88), kind=kLoop, calls=%fused_computation.50 | loop fusion | bytes 4194312 | tf_op jit(solution)/shard_map/jit(dynamic_index_in_dim)/dynamic_slice | solution.py:211
  95.1 9.0 %collective-permute-done.6 = f32[256,264]{1,0:T(8,128)S(1)} collective-permute-done((f32[256,264]{1,0:T(8,128)S(1)}, f32[256,264]{1,0:T(8,128)S(1)}, u32[]{:S(2)}, u32[]{:S(2)}) %collective-permute-start.6) | collective-permute-done | bytes 270368 | tf_op jit(solution)/shard_map/ppermute | solution.py:182
  104.1 6.7 %collective-permute-done.7 = f32[256,264]{1,0:T(8,128)S(1)} collective-permute-done((f32[256,264]{1,0:T(8,128)S(1)}, f32[256,264]{1,0:T(8,128)S(1)}, u32[]{:S(2)}, u32[]{:S(2)}) %collective-permute-start.7) | collective-permute-done | bytes 270368 | tf_op jit(solution)/shard_map/ppermute | solution.py:182
  110.7 1.8 %collective-permute-done.8 = f32[256,264]{1,0:T(8,128)S(1)} collective-permute-done((f32[256,264]{1,0:T(8,128)S(1)}, f32[256,264]{1,0:T(8,128)S(1)}, u32[]{:S(2)}, u32[]{:S(2)}) %collective-permute-start.8) | collective-permute-done | bytes 270368 | tf_op jit(solution)/shard_map/ppermute | solution.py:182
  115.6 1.6 %copy.34 = f32[4,256,256]{2,1,0:T(8,128)S(1)} copy(f32[4,256,256]{1,2,0:T(8,128)} %bitcast.49) | data formatting | bytes 2097152 | tf_op jit(solution)/shard_map/reshape | solution.py:261
  117.1 1.5 fusion
  118.7 1.3 convolution_convert_fusion.3
  120.8 1.7 %collective-permute-start.11 = (bf16[256,256]{1,0:T(8,128)(2,1)S(1)}, bf16[256,256]{1,0:T(8,128)(2,1)}, u32[]{:S(2)}, u32[]{:S(2)}) collective-permute-start(bf16[256,256]{1,0:T(8,128)(2,1)S(1)} %get-tuple-element.73), channel_id=1, source_target_pairs={{0,3},{1,0},{2,1},{3,2},{4,7},{5,4},{6,5},{7,6},{8,11},{9,8},{10,9... | collective-permute-start | bytes 393224 | tf_op jit(solution)/shard_map/ppermute | solution.py:196
  122.5 1.5 collective-permute-start.10
  124.0 1.6 %convert_add_fusion = f32[1024,2,256]{2,0,1:T(8,128)S(1)} fusion(bf16[1024,2,256]{2,0,1:T(8,128)(2,1)} %collective-permute-done.4, bf16[1024,2,1,256]{3,2,1,0:T(2,128)(2,1)S(1)} %copy-done.5), kind=kLoop, calls=%fused_computation.7 | loop fusion | flops 1572864 | bytes 4194304 | tf_op jit(solution)/shard_map/add | solution.py:214
  127.1 1.4 convert_add_fusion.1
  130.0 1.5 collective-permute-start.3
  131.5 1.8 %add_convert_fusion = bf16[256,256]{1,0:T(8,128)(2,1)} fusion(bf16[256,256]{1,0:T(8,128)(2,1)} %collective-permute-done.11, bf16[256,256]{1,0:T(8,128)(2,1)} %collective-permute-done.10, bf16[256,256]{1,0:T(8,128)(2,1)S(1)} %collective-permute-done.9, bf16[256,1024]{1,0:T(8,128)(2,1)S(1)} %convolution_convert_fusion.3, s32[]{:T(128)S(6)} %select_n.100), kind=kLoop, calls=%fused_computation.42 | loop fusion | flops 524288 | bytes 655364 | tf_op jit(solution)/shard_map/convert_element_type | solution.py:197
  133.4 8.9 %collective-permute-done.5 = bf16[1024,256]{1,0:T(8,128)(2,1)S(1)} collective-permute-done((bf16[1024,256]{1,0:T(8,128)(2,1)}, bf16[1024,256]{1,0:T(8,128)(2,1)S(1)}, u32[]{:S(2)}, u32[]{:S(2)}) %collective-permute-start.5) | collective-permute-done | bytes 524320 | tf_op jit(solution)/shard_map/ppermute | solution.py:220
  142.3 1.3 fusion.1
  143.6 8.5 %collective-permute-done.3 = bf16[1024,256]{1,0:T(8,128)(2,1)} collective-permute-done((bf16[1024,256]{1,0:T(8,128)(2,1)}, bf16[1024,256]{1,0:T(8,128)(2,1)}, u32[]{:S(2)}, u32[]{:S(2)}) %collective-permute-start.3) | collective-permute-done | bytes 524320 | tf_op jit(solution)/shard_map/ppermute | solution.py:220
  152.1 1.2 fusion.2
  (70 shorter events, 14.6 us)
Async XLA Ops:
  0.6 17.7 %copy-start = (bf16[1024,1024]{1,0:T(8,128)(2,1)S(1)}, bf16[1024,1024]{1,0:T(8,128)(2,1)}, u32[]{:S(2)}) copy-start(bf16[1024,1024]{1,0:T(8,128)(2,1)} %param.20) | copy-start | bytes 6291460
  0.6 3.8 %copy-start.15 = (bf16[2048,1024]{1,0:T(8,128)(2,1)S(1)}, bf16[2048,1024]{1,0:T(8,128)(2,1)}, u32[]{:S(2)}) copy-start(bf16[2048,1024]{1,0:T(8,128)(2,1)} %param.19) | copy-start | bytes 12582916
  0.7 3.9 %copy-start.16 = (bf16[1024,256]{1,0:T(8,128)(2,1)S(1)}, bf16[1024,256]{1,0:T(8,128)(2,1)}, u32[]{:S(2)}) copy-start(bf16[1024,256]{1,0:T(8,128)(2,1)} %param.24) | copy-start | bytes 1572868
  4.5 1.3 copy-start.9
  5.8 1.0 copy-start.10
  5.8 7.8 %copy-start.17 = (s32[3]{0:T(128)S(1)}, s32[3]{0:T(128)}, u32[]{:S(2)}) copy-start(s32[3]{0:T(128)} %constant.188.clone) | copy-start | bytes 40
  6.8 14.1 %collective-permute-start = (bf16[256,512]{1,0:T(8,128)(2,1)S(1)}, bf16[256,512]{1,0:T(8,128)(2,1)S(1)}, u32[]{:S(2)}, u32[]{:S(2)}) collective-permute-start(bf16[256,512]{1,0:T(8,128)(2,1)S(1)} %pad_maximum_fusion.2), channel_id=1, source_target_pairs={{0,4},{4,8},{8,12},{1,5},{5,9},{9,13},{2,6},{6,10},{10,14},{3,7},{... | collective-permute-start | bytes 786440 | tf_op jit(solution)/shard_map/ppermute | solution.py:21
  10.3 10.6 %collective-permute-start.1 = (bf16[256,512]{1,0:T(8,128)(2,1)S(1)}, bf16[256,512]{1,0:T(8,128)(2,1)S(1)}, u32[]{:S(2)}, u32[]{:S(2)}) collective-permute-start(bf16[256,512]{1,0:T(8,128)(2,1)S(1)} %pad_maximum_fusion.3), channel_id=1, source_target_pairs={{4,0},{8,4},{12,8},{5,1},{9,5},{13,9},{6,2},{10,6},{14,10},{7,3},{... | collective-permute-start | bytes 786440 | tf_op jit(solution)/shard_map/ppermute | solution.py:21
  13.7 4.6 %copy-start.14 = (s32[3]{0:T(128)}, s32[3]{0:T(128)S(1)}, u32[]{:S(2)}) copy-start(s32[3]{0:T(128)S(1)} %constant_dynamic-update-slice_fusion.2.scal_ref) | copy-start | bytes 40
  13.7 4.5 %copy-start.13 = (s32[3]{0:T(128)}, s32[3]{0:T(128)S(1)}, u32[]{:S(2)}) copy-start(s32[3]{0:T(128)S(1)} %constant_dynamic-update-slice_fusion.1.scal_ref) | copy-start | bytes 40
  20.9 0.7 copy-start.11
  21.6 0.7 copy-start.12
  74.4 6.3 %copy-start.2 = (bf16[1024,2,2,256]{3,2,1,0:T(2,128)(2,1)S(1)}, bf16[1024,2,2,256]{3,2,1,0:T(2,128)(2,1)}, u32[]{:S(2)}) copy-start(bf16[1024,2,2,256]{3,2,1,0:T(2,128)(2,1)} %reshape.101) | copy-start | bytes 6291460
  76.0 28.0 %collective-permute-start.6 = (f32[256,264]{1,0:T(8,128)S(1)}, f32[256,264]{1,0:T(8,128)S(1)}, u32[]{:S(2)}, u32[]{:S(2)}) collective-permute-start(f32[256,264]{1,0:T(8,128)S(1)} %get-tuple-element.65), channel_id=1, source_target_pairs={{0,4},{4,8},{8,12},{12,0},{1,5},{5,9},{9,13},{13,1},{2,6},{6,10},{... | collective-permute-start | bytes 811016 | tf_op jit(solution)/shard_map/ppermute | solution.py:182
  77.6 33.1 %collective-permute-start.7 = (f32[256,264]{1,0:T(8,128)S(1)}, f32[256,264]{1,0:T(8,128)S(1)}, u32[]{:S(2)}, u32[]{:S(2)}) collective-permute-start(f32[256,264]{1,0:T(8,128)S(1)} %get-tuple-element.66), channel_id=1, source_target_pairs={{0,8},{4,12},{8,0},{12,4},{1,9},{5,13},{9,1},{13,5},{2,10},{6,14},... | collective-permute-start | bytes 811016 | tf_op jit(solution)/shard_map/ppermute | solution.py:182
  78.7 33.8 %collective-permute-start.8 = (f32[256,264]{1,0:T(8,128)S(1)}, f32[256,264]{1,0:T(8,128)S(1)}, u32[]{:S(2)}, u32[]{:S(2)}) collective-permute-start(f32[256,264]{1,0:T(8,128)S(1)} %get-tuple-element.67), channel_id=1, source_target_pairs={{0,12},{4,0},{8,4},{12,8},{1,13},{5,1},{9,5},{13,9},{2,14},{6,2},{... | collective-permute-start | bytes 811016 | tf_op jit(solution)/shard_map/ppermute | solution.py:182
  86.3 2.0 %copy-start.1 = (bf16[1024,2,2,256]{3,2,1,0:T(2,128)(2,1)S(1)}, bf16[1024,2,2,256]{3,2,1,0:T(2,128)(2,1)}, u32[]{:S(2)}) copy-start(bf16[1024,2,2,256]{3,2,1,0:T(2,128)(2,1)} %reshape.100) | copy-start | bytes 6291460
  87.5 36.5 %collective-permute-start.4 = (bf16[1024,2,256]{2,0,1:T(8,128)(2,1)}, bf16[1024,2,256]{2,0,1:T(8,128)(2,1)}, u32[]{:S(2)}, u32[]{:S(2)}) collective-permute-start(bf16[1024,2,256]{2,0,1:T(8,128)(2,1)} %bitcast.45), channel_id=1, source_target_pairs={{0,1},{1,0},{2,3},{3,2},{4,5},{5,4},{6,7},{7,6},{8,9},{9,8},{10,11... | collective-permute-start | bytes 3145736 | tf_op jit(solution)/shard_map/ppermute | solution.py:213
  95.1 32.0 %collective-permute-start.2 = (bf16[1024,2,256]{2,0,1:T(8,128)(2,1)}, bf16[1024,2,256]{2,0,1:T(8,128)(2,1)}, u32[]{:S(2)}, u32[]{:S(2)}) collective-permute-start(bf16[1024,2,256]{2,0,1:T(8,128)(2,1)} %bitcast.46), channel_id=1, source_target_pairs={{0,1},{1,0},{2,3},{3,2},{4,5},{5,4},{6,7},{7,6},{8,9},{9,8},{10,11... | collective-permute-start | bytes 3145736 | tf_op jit(solution)/shard_map/ppermute | solution.py:213
  112.6 1.2 copy-start.3
  117.1 6.9 %copy-start.5 = (bf16[1024,2,1,256]{3,2,1,0:T(2,128)(2,1)S(1)}, bf16[1024,2,1,256]{3,2,1,0:T(2,128)(2,1)}, u32[]{:S(2)}) copy-start(bf16[1024,2,1,256]{3,2,1,0:T(2,128)(2,1)} %get-tuple-element.62) | copy-start | bytes 3145732
  120.7 10.8 %collective-permute-start.9 = (bf16[256,256]{1,0:T(8,128)(2,1)}, bf16[256,256]{1,0:T(8,128)(2,1)S(1)}, u32[]{:S(2)}, u32[]{:S(2)}) collective-permute-start(bf16[256,256]{1,0:T(8,128)(2,1)} %get-tuple-element.72), channel_id=1, source_target_pairs={{0,1},{1,2},{2,3},{3,0},{4,5},{5,6},{6,7},{7,4},{8,9},{9,10},{10,1... | collective-permute-start | bytes 393224 | tf_op jit(solution)/shard_map/ppermute | solution.py:196
  120.8 10.8 %collective-permute-start.11 = (bf16[256,256]{1,0:T(8,128)(2,1)S(1)}, bf16[256,256]{1,0:T(8,128)(2,1)}, u32[]{:S(2)}, u32[]{:S(2)}) collective-permute-start(bf16[256,256]{1,0:T(8,128)(2,1)S(1)} %get-tuple-element.73), channel_id=1, source_target_pairs={{0,3},{1,0},{2,1},{3,2},{4,7},{5,4},{6,5},{7,6},{8,11},{9,8},{10,9... | collective-permute-start | bytes 393224 | tf_op jit(solution)/shard_map/ppermute | solution.py:196
  122.5 9.0 %collective-permute-start.10 = (bf16[256,256]{1,0:T(8,128)(2,1)S(1)}, bf16[256,256]{1,0:T(8,128)(2,1)}, u32[]{:S(2)}, u32[]{:S(2)}) collective-permute-start(bf16[256,256]{1,0:T(8,128)(2,1)S(1)} %get-tuple-element.74), channel_id=1, source_target_pairs={{0,2},{1,3},{2,0},{3,1},{4,6},{5,7},{6,4},{7,5},{8,10},{9,11},{10,... | collective-permute-start | bytes 393224 | tf_op jit(solution)/shard_map/ppermute | solution.py:196
  124.0 3.1 %copy-start.4 = (bf16[1024,2,1,256]{3,2,1,0:T(2,128)(2,1)S(1)}, bf16[1024,2,1,256]{3,2,1,0:T(2,128)(2,1)}, u32[]{:S(2)}) copy-start(bf16[1024,2,1,256]{3,2,1,0:T(2,128)(2,1)} %get-tuple-element.60) | copy-start | bytes 3145732
  125.6 2.9 %copy-start.6 = (f32[1024,2,256]{2,0,1:T(8,128)}, f32[1024,2,256]{2,0,1:T(8,128)S(1)}, u32[]{:S(2)}) copy-start(f32[1024,2,256]{2,0,1:T(8,128)S(1)} %convert_add_fusion) | copy-start | bytes 6291460
  126.5 15.8 %collective-permute-start.5 = (bf16[1024,256]{1,0:T(8,128)(2,1)}, bf16[1024,256]{1,0:T(8,128)(2,1)S(1)}, u32[]{:S(2)}, u32[]{:S(2)}) collective-permute-start(bf16[1024,256]{1,0:T(8,128)(2,1)} %fusion.4), channel_id=1, source_target_pairs={{0,2},{1,3},{2,0},{3,1},{4,6},{5,7},{6,4},{7,5},{8,10},{9,11},{10,... | collective-permute-start | bytes 1572872 | tf_op jit(solution)/shard_map/ppermute | solution.py:220
  128.5 1.5 copy-start.7
  130.0 22.1 %collective-permute-start.3 = (bf16[1024,256]{1,0:T(8,128)(2,1)}, bf16[1024,256]{1,0:T(8,128)(2,1)}, u32[]{:S(2)}, u32[]{:S(2)}) collective-permute-start(bf16[1024,256]{1,0:T(8,128)(2,1)} %fusion.3), channel_id=1, source_target_pairs={{0,2},{1,3},{2,0},{3,1},{4,6},{5,7},{6,4},{7,5},{8,10},{9,11},{10,... | collective-permute-start | bytes 1572872 | tf_op jit(solution)/shard_map/ppermute | solution.py:220
  131.5 20.6 %copy-start.8 = (f32[1024,2,256]{2,0,1:T(8,128)S(1)}, f32[1024,2,256]{2,0,1:T(8,128)}, u32[]{:S(2)}) copy-start(f32[1024,2,256]{2,0,1:T(8,128)} %copy-done.7) | copy-start | bytes 6291460

commit v5 on v4

--- a/solution.py
+++ b/solution.py
@@ -67,14 +67,18 @@
         blended = jnp.dot(weights.astype(jnp.bfloat16), v, preferred_element_type=jnp.float32)
         divisor = jnp.where(query_valid, denom, 1.0)
         att_ref[:, cols] = jnp.where(query_valid, blended / divisor, 0.0).astype(jnp.bfloat16)
-    o_ref[...] = jnp.dot(
-        att_ref[...], w_ref[...], preferred_element_type=jnp.float32
-    ).astype(jnp.bfloat16)
-
-
-def window_attention(query, keyed, valued, low, high, w_out, first_frame, length, row_base, rows):
+    result = jnp.dot(att_ref[...], w_ref[...], preferred_element_type=jnp.float32)
+    block_width = o_ref.shape[2]
+    for b in range(o_ref.shape[0]):
+        o_ref[b] = result[:, b * block_width : (b + 1) * block_width].astype(jnp.bfloat16)
+
+
+def window_attention(
+    query, keyed, valued, low, high, w_out, first_frame, length, row_base, rows, blocks
+):
     frame_count, width = query.shape
     out_width = w_out.shape[1]
+    block_width = out_width // blocks
     tq = min(256, rows)
     block_base = row_base // tq
     span = tq + 2 * HALF
@@ -89,7 +93,7 @@
     return pl.pallas_call(
         kernel,
         cost_estimate=cost,
-        out_shape=jax.ShapeDtypeStruct((rows, out_width), jnp.bfloat16),
+        out_shape=jax.ShapeDtypeStruct((blocks, rows, block_width), jnp.bfloat16),
         grid_spec=pltpu.PrefetchScalarGridSpec(
             num_scalar_prefetch=1,
             grid=(rows // tq,),
@@ -101,7 +105,7 @@
                 pl.BlockSpec(high.shape, full),
                 pl.BlockSpec(w_out.shape, full),
             ],
-            out_specs=pl.BlockSpec((tq, out_width), lambda i, s: (i, 0)),
+            out_specs=pl.BlockSpec((blocks, tq, block_width), lambda i, s: (0, i, 0)),
             scratch_shapes=[
                 pltpu.VMEM((frame_count + 2 * HALF, width), jnp.bfloat16),
                 pltpu.VMEM((frame_count + 2 * HALF, width), jnp.bfloat16),
@@ -197,27 +201,48 @@
     return total.astype(jnp.bfloat16)
 
 
-def paired_column_sum(partial, axis):
-    count = lax.axis_size(axis)
+def send_order(axis):
+    count = lax.axis_size(axis)
+    place = lax.axis_index(axis)
     if count % 2 != 0:
-        return column_sum(partial, axis)
+        return [(place + j) % count for j in range(count)]
     chips = count // 2
-    place = lax.axis_index(axis)
     core = place % 2
     chip = place // 2
-    rows = partial.shape[0]
-    width = partial.shape[1] // count
-    grid = partial.reshape(rows, chips, 2, width)
-    mine = lax.dynamic_index_in_dim(grid, core, axis=2, keepdims=False)
-    theirs = lax.dynamic_index_in_dim(grid, 1 - core, axis=2, keepdims=False)
-    swapped = lax.ppermute(theirs, axis, [(i, i ^ 1) for i in range(count)])
-    chip_sum = mine.astype(jnp.float32) + swapped.astype(jnp.float32)
-    total = lax.dynamic_index_in_dim(chip_sum, chip, axis=1, keepdims=False)
-    for shift in range(1, chips):
-        target = (chip + shift) % chips
-        block = lax.dynamic_index_in_dim(chip_sum, target, axis=1, keepdims=False)
-        pairs = [(2 * c + k, 2 * ((c + shift) % chips) + k) for c in range(chips) for k in range(2)]
-        total = total + lax.ppermute(block.astype(jnp.bfloat16), axis, pairs).astype(jnp.float32)
+    theirs = [2 * ((chip + d) % chips) + 1 - core for d in range(chips)]
+    mine = [2 * ((chip + d) % chips) + core for d in range(chips)]
+    return theirs + mine
+
+
+def ordered_columns(weight, axis):
+    count = lax.axis_size(axis)
+    width = weight.shape[1] // count
+    return jnp.concatenate(
+        [lax.dynamic_slice_in_dim(weight, b * width, width, 1) for b in send_order(axis)], axis=1
+    )
+
+
+def paired_block_sum(blocks, axis):
+    count = lax.axis_size(axis)
+    if count % 2 != 0:
+        total = blocks[0].astype(jnp.float32)
+        for shift in range(1, count):
+            pairs = [(i, (i + shift) % count) for i in range(count)]
+            total = total + lax.ppermute(blocks[shift], axis, pairs).astype(jnp.float32)
+        return total.astype(jnp.bfloat16)
+    chips = count // 2
+    swap = [(i, i ^ 1) for i in range(count)]
+    chip_sums = [
+        blocks[chips + d].astype(jnp.float32)
+        + lax.ppermute(blocks[d], axis, swap).astype(jnp.float32)
+        for d in range(chips)
+    ]
+    total = chip_sums[0]
+    for d in range(1, chips):
+        pairs = [(2 * c + k, 2 * ((c + d) % chips) + k) for c in range(chips) for k in range(2)]
+        total = total + lax.ppermute(chip_sums[d].astype(jnp.bfloat16), axis, pairs).astype(
+            jnp.float32
+        )
     return total.astype(jnp.bfloat16)
 
 
@@ -237,12 +262,15 @@
     low, high = halos(keyed, valued, "seq")
     chunks = 2 if frame_count % 512 == 0 else 1
     chunk_rows = frame_count // chunks
+    head_devices = lax.axis_size("head")
+    w_ordered = ordered_columns(w_out, "head")
     frame_parts = []
     for c in range(chunks):
         terms = window_attention(
-            query, keyed, valued, low, high, w_out, first_frame, length, c * chunk_rows, chunk_rows
+            query, keyed, valued, low, high, w_ordered, first_frame, length,
+            c * chunk_rows, chunk_rows, head_devices,
         )
-        frame_parts.append(paired_column_sum(terms, "head"))
+        frame_parts.append(paired_block_sum(terms, "head"))
     terms, keyed, valued = lax.optimization_barrier((terms, keyed, valued))
     frames_out = jnp.concatenate(frame_parts, axis=0)
     latent_count = latents.shape[0]

time: 155 us -> 142 us (0.916)
  the two profiles are of different devices: /device:TPU:8 before, /device:TPU:0 now
where the time goes in v5:
time: 142 us; the launch traced here: 141 us
  Pallas kernels  43.2 us (30%)
  waiting for transfers between devices  39.6 us (28%)
  starting transfers between devices  17.1 us (12%)
  other arithmetic  16.1 us (11%)
  local copies, waits for them, and re-layouts  11.8 us (8%)
  matrix products  11.4 us (8%)
  between operations  1.78 us (1%)
    pallas_call x2, Pallas kernels, window_attention(): pl.pallas_call(kernel, cost_estimate=cost, out_shape=jax.ShapeDtypeStruct...  25.3 us
    ppermute x3, waiting for transfers between devices, shifted_blocks(): parts.append(lax.ppermute(block, axis, pairs))  18 us
    pallas_call x1, Pallas kernels, latent_attention(): pl.pallas_call(kernel, cost_estimate=cost, out_shape=(jax.ShapeDtypeStruc...  17.9 us
    ppermute x3, waiting for transfers between devices, column_sum(): total = total + lax.ppermute(block, axis, pairs).astype(jnp.float32)  13.3 us
    dot_general x4, matrix products, project(): jnp.dot(source, weight, preferred_element_type=jnp.float32)  11.1 us
    ppermute x2, waiting for transfers between devices, paired_block_sum(): lax.ppermute(chip_sums[d].astype(jnp.bfloat16), axis, pairs)  7.88 us
    ppermute x3, starting transfers between devices, shifted_blocks(): parts.append(lax.ppermute(block, axis, pairs))  5.65 us
    ppermute x1, starting transfers between devices, halos(): lax.ppermute(tail, axis, forward)  4.95 us
  transfers between devices with their start and end apart: 14, of which 5 were waited for; matrix products, arithmetic and copies ran while one was open for 19% of the time, Pallas kernels for 22%

profile of v5, /device:TPU:0, one launch (start us, length us, event | category | flops | bytes accessed | tf_op | source)
XLA Modules:
  0.0 141.0 jit_solution(428130270490747723)
XLA Ops:
  0.7 3.7 %convolution_convert_fusion.1.k_ref = bf16[2048,256]{1,0:T(8,128)(2,1)S(1)} fusion(bf16[2048,1024]{1,0:T(8,128)(2,1)} %param.19, bf16[1024,256]{1,0:T(8,128)(2,1)} %param.23), kind=kOutput, calls=%fused_computation.5 | convolution fusion | flops 1074266112 | bytes 5767168 | tf_op jit(solution)/shard_map/dot_general | solution.py:25
  4.5 1.3 convolution_convert_fusion.v_ref
  6.8 4.9 %collective-permute-start = (bf16[256,512]{1,0:T(8,128)(2,1)S(1)}, bf16[256,512]{1,0:T(8,128)(2,1)S(1)}, u32[]{:S(2)}, u32[]{:S(2)}) collective-permute-start(bf16[256,512]{1,0:T(8,128)(2,1)S(1)} %pad_maximum_fusion.3), channel_id=1, source_target_pairs={{0,4},{4,8},{8,12},{1,5},{5,9},{9,13},{2,6},{6,10},{10,14},{3,7},{... | collective-permute-start | bytes 786440 | tf_op jit(solution)/shard_map/ppermute | solution.py:21
  12.5 1.3 collective-permute-start.1
  14.7 4.6 %convolution_convert_fusion.2.q_ref = bf16[2048,256]{1,0:T(8,128)(2,1)} fusion(bf16[2048,1024]{1,0:T(8,128)(2,1)} %param.19, bf16[1024,256]{1,0:T(8,128)(2,1)} %param.22), kind=kOutput, calls=%fused_computation.6 | convolution fusion | flops 1074266112 | bytes 5767168 | tf_op jit(solution)/shard_map/dot_general | solution.py:25
  19.5 0.9 pad_maximum_fusion.2.w_ref
  20.4 1.5 %convolution_convert_fusion.4.q_ref = bf16[1024,256]{1,0:T(8,128)(2,1)} fusion(bf16[1024,1024]{1,0:T(8,128)(2,1)S(1)} %copy-done, bf16[1024,256]{1,0:T(8,128)(2,1)S(1)} %copy-done.13), kind=kOutput, calls=%fused_computation.13 | convolution fusion | flops 537133056 | bytes 3145728 | tf_op jit(solution)/shard_map/dot_general | solution.py:25
  23.4 12.7 %shard_map.123 = bf16[4,1024,256]{2,1,0:T(8,128)(2,1)} custom-call(s32[3]{0:T(128)} %copy-done.10, bf16[2048,256]{1,0:T(8,128)(2,1)} %convolution_convert_fusion.2.q_ref, bf16[2048,256]{1,0:T(8,128)(2,1)} %copy-done.2, bf16[2048,256]{1,0:T(8,128)(2,1)} %copy-done.3, bf16[256,512]{1,0:T(8,128)(2,1)} %copy-done.4, bf16[256,512]{1,0:T(8,128)(2,1)} %copy-done.5, ...), custom_call_target="tpu_custom_call" | custom-call | flops 1342177280 | bytes 5767168 | tf_op jit(solution)/shard_map/pallas_call | solution.py:93
  36.0 2.3 %slice_bitcast_fusion.2 = (bf16[1024,256]{1,0:T(8,128)(2,1)}, bf16[1024,256]{1,0:T(8,128)(2,1)}) fusion(bf16[4,1024,256]{2,1,0:T(8,128)(2,1)} %shard_map.123), kind=kLoop, calls=%fused_computation.31 | loop fusion | bytes 2097152 | tf_op jit(solution)/shard_map/squeeze | solution.py:237
  38.9 17.9 %shard_map.124 = (f32[1024,256]{1,0:T(8,128)}, f32[1024,128]{1,0:T(8,128)}) custom-call(s32[1]{0:T(128)} %bitcast.10.scal_ref, bf16[1024,256]{1,0:T(8,128)(2,1)} %convolution_convert_fusion.4.q_ref, bf16[2048,256]{1,0:T(8,128)(2,1)} %copy-done.2, bf16[2048,256]{1,0:T(8,128)(2,1)} %copy-done.3), custom_call_target="tpu_custom_call" | custom-call | flops 2147483648 | bytes 4194304 | tf_op jit(solution)/shard_map/pallas_call | solution.py:153
  56.8 2.4 %fusion.10 = (f32[1,256,264]{2,1,0:T(8,128)S(1)}, f32[256,264]{1,0:T(8,128)}, f32[256,264]{1,0:T(8,128)}, f32[256,264]{1,0:T(8,128)}) fusion(s32[]{:T(128)S(6)} %select_n.91, f32[1024,256]{1,0:T(8,128)} %get-tuple-element.56, f32[1024,8]{1,0:T(8,128)} %bitcast.51, s32[]{:T(128)S(6)} %select_n.93, s32[]{:T(128)S(6)} %select_n.95, s32[]{:T(128)S(6)} %select_n.97), kind=kLoop, calls=%fused_computation.42 | loop fusion | flops 270336 | bytes 2162704 | tf_op jit(solution)/shard_map/stack | solution.py:187
  59.2 4.6 %collective-permute-start.10 = (f32[256,264]{1,0:T(8,128)}, f32[256,264]{1,0:T(8,128)S(1)}, u32[]{:S(2)}, u32[]{:S(2)}) collective-permute-start(f32[256,264]{1,0:T(8,128)} %get-tuple-element.67), channel_id=1, source_target_pairs={{0,12},{4,0},{8,4},{12,8},{1,13},{5,1},{9,5},{13,9},{2,14},{6,2},{... | collective-permute-start | bytes 811016 | tf_op jit(solution)/shard_map/ppermute | solution.py:186
  63.8 1.0 collective-permute-start.8
  64.8 12.7 %shard_map.122 = bf16[4,1024,256]{2,1,0:T(8,128)(2,1)} custom-call(s32[3]{0:T(128)} %copy-done.9, bf16[2048,256]{1,0:T(8,128)(2,1)} %convolution_convert_fusion.2.q_ref, bf16[2048,256]{1,0:T(8,128)(2,1)} %copy-done.2, bf16[2048,256]{1,0:T(8,128)(2,1)} %copy-done.3, bf16[256,512]{1,0:T(8,128)(2,1)} %copy-done.4, bf16[256,512]{1,0:T(8,128)(2,1)} %copy-done.5, ...), custom_call_target="tpu_custom_call" | custom-call | flops 1342177280 | bytes 5767168 | tf_op jit(solution)/shard_map/pallas_call | solution.py:93
  77.5 2.3 %slice_bitcast_fusion.6 = (bf16[1024,256]{1,0:T(8,128)(2,1)}, bf16[1024,256]{1,0:T(8,128)(2,1)}) fusion(bf16[4,1024,256]{2,1,0:T(8,128)(2,1)} %shard_map.122), kind=kLoop, calls=%fused_computation.35 | loop fusion | bytes 2097152 | tf_op jit(solution)/shard_map/squeeze | solution.py:237
  79.8 18.0 %collective-permute-done.9 = f32[256,264]{1,0:T(8,128)S(1)} collective-permute-done((f32[256,264]{1,0:T(8,128)}, f32[256,264]{1,0:T(8,128)S(1)}, u32[]{:S(2)}, u32[]{:S(2)}) %collective-permute-start.9) | collective-permute-done | bytes 270368 | tf_op jit(solution)/shard_map/ppermute | solution.py:186
  97.8 1.1 pad_maximum_fusion
  98.9 1.1 copy-done.1
  100.4 1.1 broadcast_in_dim.7
  101.5 1.6 %copy.22 = f32[4,256,256]{2,1,0:T(8,128)S(1)} copy(f32[4,256,256]{1,2,0:T(8,128)} %bitcast.49) | data formatting | bytes 2097152 | tf_op jit(solution)/shard_map/reshape | solution.py:289
  104.0 1.5 %fusion = f32[256,256]{1,0:T(8,128)S(1)} fusion(f32[4,256,256]{2,1,0:T(8,128)S(1)} %copy.22, f32[4,256,264]{2,1,0:T(8,128)} %copy-done.1), kind=kLoop, calls=%fused_computation.15 | loop fusion | flops 458752 | bytes 2359296 | tf_op jit(solution)/shard_map/reduce_sum | solution.py:289
  105.8 1.3 fusion.1
  107.1 1.6 %collective-permute-start.7 = (bf16[1024,256]{1,0:T(8,128)(2,1)S(1)}, bf16[1024,256]{1,0:T(8,128)(2,1)}, u32[]{:S(2)}, u32[]{:S(2)}) collective-permute-start(bf16[1024,256]{1,0:T(8,128)(2,1)S(1)} %fusion.1), channel_id=1, source_target_pairs={{0,2},{1,3},{2,0},{3,1},{4,6},{5,7},{6,4},{7,5},{8,10},{9,11},{10,... | collective-permute-start | bytes 1572872 | tf_op jit(solution)/shard_map/ppermute | solution.py:243
  109.6 2.1 %fusion.4 = bf16[1024,256]{1,0:T(8,128)(2,1)} fusion(bf16[1024,256]{1,0:T(8,128)(2,1)} %collective-permute-done.3, bf16[4,1024,256]{2,1,0:T(8,128)(2,1)} %shard_map.122), kind=kLoop, calls=%fused_computation.23 | loop fusion | flops 1048576 | bytes 1572864 | tf_op jit(solution)/shard_map/convert_element_type | solution.py:243
  111.7 11.7 %collective-permute-done.13 = bf16[256,256]{1,0:T(8,128)(2,1)S(1)} collective-permute-done((bf16[256,256]{1,0:T(8,128)(2,1)S(1)}, bf16[256,256]{1,0:T(8,128)(2,1)S(1)}, u32[]{:S(2)}, u32[]{:S(2)}) %collective-permute-start.13) | collective-permute-done | bytes 131104 | tf_op jit(solution)/shard_map/ppermute | solution.py:200
  124.2 1.6 %collective-permute-done.12 = bf16[256,256]{1,0:T(8,128)(2,1)S(1)} collective-permute-done((bf16[256,256]{1,0:T(8,128)(2,1)S(1)}, bf16[256,256]{1,0:T(8,128)(2,1)S(1)}, u32[]{:S(2)}, u32[]{:S(2)}) %collective-permute-start.12) | collective-permute-done | bytes 131104 | tf_op jit(solution)/shard_map/ppermute | solution.py:200
  125.8 1.5 %collective-permute-start.4 = (bf16[1024,256]{1,0:T(8,128)(2,1)}, bf16[1024,256]{1,0:T(8,128)(2,1)}, u32[]{:S(2)}, u32[]{:S(2)}) collective-permute-start(bf16[1024,256]{1,0:T(8,128)(2,1)} %fusion.4), channel_id=1, source_target_pairs={{0,2},{1,3},{2,0},{3,1},{4,6},{5,7},{6,4},{7,5},{8,10},{9,11},{10,... | collective-permute-start | bytes 1572872 | tf_op jit(solution)/shard_map/ppermute | solution.py:243
  127.3 1.6 %add_convert_fusion = bf16[256,256]{1,0:T(8,128)(2,1)} fusion(bf16[256,256]{1,0:T(8,128)(2,1)S(1)} %collective-permute-done.13, bf16[256,256]{1,0:T(8,128)(2,1)S(1)} %collective-permute-done.12, bf16[256,256]{1,0:T(8,128)(2,1)} %collective-permute-done.11, bf16[256,1024]{1,0:T(8,128)(2,1)S(1)} %convolution_convert_fusion.3, s32[]{:T(128)S(6)} %select_n.98), kind=kLoop, calls=%fused_computation.47 | loop fusion | flops 524288 | bytes 655364 | tf_op jit(solution)/shard_map/convert_element_type | solution.py:201
  128.9 1.5 %fusion.3 = bf16[1024,256]{1,0:T(8,128)(2,1)S(1)} fusion(bf16[1024,256]{1,0:T(8,128)(2,1)} %collective-permute-done.7, bf16[1024,256]{1,0:T(8,128)(2,1)} %collective-permute-done.5, bf16[4,1024,256]{2,1,0:T(8,128)(2,1)} %shard_map.123), kind=kLoop, calls=%fused_computation.21 | loop fusion | flops 1572864 | bytes 2097152 | tf_op jit(solution)/shard_map/convert_element_type | solution.py:246
  130.5 7.9 %collective-permute-done.4 = bf16[1024,256]{1,0:T(8,128)(2,1)} collective-permute-done((bf16[1024,256]{1,0:T(8,128)(2,1)}, bf16[1024,256]{1,0:T(8,128)(2,1)}, u32[]{:S(2)}, u32[]{:S(2)}) %collective-permute-start.4) | collective-permute-done | bytes 524320 | tf_op jit(solution)/shard_map/ppermute | solution.py:243
  138.4 1.5 %fusion.6 = bf16[1024,256]{1,0:T(8,128)(2,1)S(1)} fusion(bf16[1024,256]{1,0:T(8,128)(2,1)} %collective-permute-done.4, bf16[1024,256]{1,0:T(8,128)(2,1)} %collective-permute-done.2, bf16[4,1024,256]{2,1,0:T(8,128)(2,1)} %shard_map.122), kind=kLoop, calls=%fused_computation.26 | loop fusion | flops 1572864 | bytes 2097152 | tf_op jit(solution)/shard_map/convert_element_type | solution.py:246
  139.9 1.0 pad_maximum_fusion.1
  (64 shorter events, 7.4 us)
Async XLA Ops:
  0.6 19.8 %copy-start = (bf16[1024,1024]{1,0:T(8,128)(2,1)S(1)}, bf16[1024,1024]{1,0:T(8,128)(2,1)}, u32[]{:S(2)}) copy-start(bf16[1024,1024]{1,0:T(8,128)(2,1)} %param.20) | copy-start | bytes 6291460
  0.6 3.8 %copy-start.11 = (bf16[2048,1024]{1,0:T(8,128)(2,1)S(1)}, bf16[2048,1024]{1,0:T(8,128)(2,1)}, u32[]{:S(2)}) copy-start(bf16[2048,1024]{1,0:T(8,128)(2,1)} %param.19) | copy-start | bytes 12582916
  0.7 3.9 %copy-start.12 = (bf16[1024,256]{1,0:T(8,128)(2,1)S(1)}, bf16[1024,256]{1,0:T(8,128)(2,1)}, u32[]{:S(2)}) copy-start(bf16[1024,256]{1,0:T(8,128)(2,1)} %param.24) | copy-start | bytes 1572868
  4.5 1.3 copy-start.2
  5.8 1.0 copy-start.3
  5.8 8.1 %copy-start.14 = (s32[3]{0:T(128)S(1)}, s32[3]{0:T(128)}, u32[]{:S(2)}) copy-start(s32[3]{0:T(128)} %constant.169.clone) | copy-start | bytes 40
  6.8 15.1 %collective-permute-start = (bf16[256,512]{1,0:T(8,128)(2,1)S(1)}, bf16[256,512]{1,0:T(8,128)(2,1)S(1)}, u32[]{:S(2)}, u32[]{:S(2)}) collective-permute-start(bf16[256,512]{1,0:T(8,128)(2,1)S(1)} %pad_maximum_fusion.3), channel_id=1, source_target_pairs={{0,4},{4,8},{8,12},{1,5},{5,9},{9,13},{2,6},{6,10},{10,14},{3,7},{... | collective-permute-start | bytes 786440 | tf_op jit(solution)/shard_map/ppermute | solution.py:21
  12.5 9.9 %collective-permute-start.1 = (bf16[256,512]{1,0:T(8,128)(2,1)}, bf16[256,512]{1,0:T(8,128)(2,1)S(1)}, u32[]{:S(2)}, u32[]{:S(2)}) collective-permute-start(bf16[256,512]{1,0:T(8,128)(2,1)} %pad_maximum_fusion.4), channel_id=1, source_target_pairs={{4,0},{8,4},{12,8},{5,1},{9,5},{13,9},{6,2},{10,6},{14,10},{7,3},{... | collective-permute-start | bytes 786440 | tf_op jit(solution)/shard_map/ppermute | solution.py:21
  14.6 4.7 %copy-start.8 = (bf16[256,1024]{1,0:T(8,128)(2,1)S(1)}, bf16[256,1024]{1,0:T(8,128)(2,1)}, u32[]{:S(2)}) copy-start(bf16[256,1024]{1,0:T(8,128)(2,1)} %param.25) | copy-start | bytes 1572868
  19.3 2.7 %copy-start.10 = (s32[3]{0:T(128)}, s32[3]{0:T(128)S(1)}, u32[]{:S(2)}) copy-start(s32[3]{0:T(128)S(1)} %constant_dynamic-update-slice_fusion.1.scal_ref) | copy-start | bytes 40
  19.3 2.6 %copy-start.9 = (s32[3]{0:T(128)}, s32[3]{0:T(128)S(1)}, u32[]{:S(2)}) copy-start(s32[3]{0:T(128)S(1)} %constant_dynamic-update-slice_fusion.2.scal_ref) | copy-start | bytes 40
  19.4 1.0 copy-start.13
  21.9 0.7 copy-start.4
  22.6 0.7 copy-start.5
  38.4 67.4 %collective-permute-start.6 = (bf16[1024,256]{1,0:T(8,128)(2,1)}, bf16[1024,256]{1,0:T(8,128)(2,1)}, u32[]{:S(2)}, u32[]{:S(2)}) collective-permute-start(bf16[1024,256]{1,0:T(8,128)(2,1)} %get-tuple-element.63), channel_id=1, source_target_pairs={{0,1},{1,0},{2,3},{3,2},{4,5},{5,4},{6,7},{7,6},{8,9},{9,8},{10,11... | collective-permute-start | bytes 1572872 | tf_op jit(solution)/shard_map/ppermute | solution.py:237
  38.4 90.6 %collective-permute-start.5 = (bf16[1024,256]{1,0:T(8,128)(2,1)}, bf16[1024,256]{1,0:T(8,128)(2,1)}, u32[]{:S(2)}, u32[]{:S(2)}) collective-permute-start(bf16[1024,256]{1,0:T(8,128)(2,1)} %get-tuple-element.62), channel_id=1, source_target_pairs={{0,1},{1,0},{2,3},{3,2},{4,5},{5,4},{6,7},{7,6},{8,9},{9,8},{10,11... | collective-permute-start | bytes 1572872 | tf_op jit(solution)/shard_map/ppermute | solution.py:237
  59.2 20.6 %collective-permute-start.10 = (f32[256,264]{1,0:T(8,128)}, f32[256,264]{1,0:T(8,128)S(1)}, u32[]{:S(2)}, u32[]{:S(2)}) collective-permute-start(f32[256,264]{1,0:T(8,128)} %get-tuple-element.67), channel_id=1, source_target_pairs={{0,12},{4,0},{8,4},{12,8},{1,13},{5,1},{9,5},{13,9},{2,14},{6,2},{... | collective-permute-start | bytes 811016 | tf_op jit(solution)/shard_map/ppermute | solution.py:186
  63.8 33.9 %collective-permute-start.9 = (f32[256,264]{1,0:T(8,128)}, f32[256,264]{1,0:T(8,128)S(1)}, u32[]{:S(2)}, u32[]{:S(2)}) collective-permute-start(f32[256,264]{1,0:T(8,128)} %get-tuple-element.66), channel_id=1, source_target_pairs={{0,8},{4,12},{8,0},{12,4},{1,9},{5,13},{9,1},{13,5},{2,10},{6,14},... | collective-permute-start | bytes 811016 | tf_op jit(solution)/shard_map/ppermute | solution.py:186
  63.8 33.9 %collective-permute-start.8 = (f32[256,264]{1,0:T(8,128)}, f32[256,264]{1,0:T(8,128)}, u32[]{:S(2)}, u32[]{:S(2)}) collective-permute-start(f32[256,264]{1,0:T(8,128)} %get-tuple-element.65), channel_id=1, source_target_pairs={{0,4},{4,8},{8,12},{12,0},{1,5},{5,9},{9,13},{13,1},{2,6},{6,10},{... | collective-permute-start | bytes 811016 | tf_op jit(solution)/shard_map/ppermute | solution.py:186
  79.8 29.6 %collective-permute-start.3 = (bf16[1024,256]{1,0:T(8,128)(2,1)}, bf16[1024,256]{1,0:T(8,128)(2,1)}, u32[]{:S(2)}, u32[]{:S(2)}) collective-permute-start(bf16[1024,256]{1,0:T(8,128)(2,1)} %get-tuple-element.61), channel_id=1, source_target_pairs={{0,1},{1,0},{2,3},{3,2},{4,5},{5,4},{6,7},{7,6},{8,9},{9,8},{10,11... | collective-permute-start | bytes 1572872 | tf_op jit(solution)/shard_map/ppermute | solution.py:237
  98.9 1.2 copy-start.1
  104.0 1.5 %copy-start.6 = (f32[256,256]{1,0:T(8,128)S(1)}, f32[256,256]{1,0:T(8,128)}, u32[]{:S(2)}) copy-start(f32[256,256]{1,0:T(8,128)} %copy.24) | copy-start | bytes 786436
  104.0 1.5 %copy-start.7 = (bf16[256,1024]{1,0:T(8,128)(2,1)S(1)}, bf16[256,1024]{1,0:T(8,128)(2,1)}, u32[]{:S(2)}) copy-start(bf16[256,1024]{1,0:T(8,128)(2,1)} %param.27) | copy-start | bytes 1572868
  107.1 21.8 %collective-permute-start.7 = (bf16[1024,256]{1,0:T(8,128)(2,1)S(1)}, bf16[1024,256]{1,0:T(8,128)(2,1)}, u32[]{:S(2)}, u32[]{:S(2)}) collective-permute-start(bf16[1024,256]{1,0:T(8,128)(2,1)S(1)} %fusion.1), channel_id=1, source_target_pairs={{0,2},{1,3},{2,0},{3,1},{4,6},{5,7},{6,4},{7,5},{8,10},{9,11},{10,... | collective-permute-start | bytes 1572872 | tf_op jit(solution)/shard_map/ppermute | solution.py:243
  108.8 14.7 %collective-permute-start.13 = (bf16[256,256]{1,0:T(8,128)(2,1)S(1)}, bf16[256,256]{1,0:T(8,128)(2,1)S(1)}, u32[]{:S(2)}, u32[]{:S(2)}) collective-permute-start(bf16[256,256]{1,0:T(8,128)(2,1)S(1)} %get-tuple-element.73), channel_id=1, source_target_pairs={{0,3},{1,0},{2,1},{3,2},{4,7},{5,4},{6,5},{7,6},{8,11},{9,8},{10,9... | collective-permute-start | bytes 393224 | tf_op jit(solution)/shard_map/ppermute | solution.py:200
  108.8 17.0 %collective-permute-start.12 = (bf16[256,256]{1,0:T(8,128)(2,1)S(1)}, bf16[256,256]{1,0:T(8,128)(2,1)S(1)}, u32[]{:S(2)}, u32[]{:S(2)}) collective-permute-start(bf16[256,256]{1,0:T(8,128)(2,1)S(1)} %get-tuple-element.74), channel_id=1, source_target_pairs={{0,2},{1,3},{2,0},{3,1},{4,6},{5,7},{6,4},{7,5},{8,10},{9,11},{10,... | collective-permute-start | bytes 393224 | tf_op jit(solution)/shard_map/ppermute | solution.py:200
  109.4 17.9 %collective-permute-start.11 = (bf16[256,256]{1,0:T(8,128)(2,1)S(1)}, bf16[256,256]{1,0:T(8,128)(2,1)}, u32[]{:S(2)}, u32[]{:S(2)}) collective-permute-start(bf16[256,256]{1,0:T(8,128)(2,1)S(1)} %get-tuple-element.72), channel_id=1, source_target_pairs={{0,1},{1,2},{2,3},{3,0},{4,5},{5,6},{6,7},{7,4},{8,9},{9,10},{10,1... | collective-permute-start | bytes 393224 | tf_op jit(solution)/shard_map/ppermute | solution.py:200
  123.4 7.1 %collective-permute-start.2 = (bf16[1024,256]{1,0:T(8,128)(2,1)}, bf16[1024,256]{1,0:T(8,128)(2,1)}, u32[]{:S(2)}, u32[]{:S(2)}) collective-permute-start(bf16[1024,256]{1,0:T(8,128)(2,1)} %get-tuple-element.60), channel_id=1, source_target_pairs={{0,1},{1,0},{2,3},{3,2},{4,5},{5,4},{6,7},{7,6},{8,9},{9,8},{10,11... | collective-permute-start | bytes 1572872 | tf_op jit(solution)/shard_map/ppermute | solution.py:237
  125.8 12.6 %collective-permute-start.4 = (bf16[1024,256]{1,0:T(8,128)(2,1)}, bf16[1024,256]{1,0:T(8,128)(2,1)}, u32[]{:S(2)}, u32[]{:S(2)}) collective-permute-start(bf16[1024,256]{1,0:T(8,128)(2,1)} %fusion.4), channel_id=1, source_target_pairs={{0,2},{1,3},{2,0},{3,1},{4,6},{5,7},{6,4},{7,5},{8,10},{9,11},{10,... | collective-permute-start | bytes 1572872 | tf_op jit(solution)/shard_map/ppermute | solution.py:243

commit v6 on v5

--- a/solution.py
+++ b/solution.py
@@ -222,28 +222,53 @@
     )
 
 
-def paired_block_sum(blocks, axis):
-    count = lax.axis_size(axis)
-    if count % 2 != 0:
-        total = blocks[0].astype(jnp.float32)
-        for shift in range(1, count):
-            pairs = [(i, (i + shift) % count) for i in range(count)]
-            total = total + lax.ppermute(blocks[shift], axis, pairs).astype(jnp.float32)
-        return total.astype(jnp.bfloat16)
+def chip_pair_sums(blocks, axis):
+    count = lax.axis_size(axis)
     chips = count // 2
     swap = [(i, i ^ 1) for i in range(count)]
-    chip_sums = [
-        blocks[chips + d].astype(jnp.float32)
-        + lax.ppermute(blocks[d], axis, swap).astype(jnp.float32)
+    return [
+        (
+            blocks[chips + d].astype(jnp.float32)
+            + lax.ppermute(blocks[d], axis, swap).astype(jnp.float32)
+        ).astype(jnp.bfloat16)
         for d in range(chips)
     ]
-    total = chip_sums[0]
+
+
+def cross_chip_sum(chip_sums, axis):
+    count = lax.axis_size(axis)
+    chips = count // 2
+    total = chip_sums[0].astype(jnp.float32)
     for d in range(1, chips):
         pairs = [(2 * c + k, 2 * ((c + d) % chips) + k) for c in range(chips) for k in range(2)]
-        total = total + lax.ppermute(chip_sums[d].astype(jnp.bfloat16), axis, pairs).astype(
-            jnp.float32
-        )
+        total = total + lax.ppermute(chip_sums[d], axis, pairs).astype(jnp.float32)
     return total.astype(jnp.bfloat16)
+
+
+def plain_block_sum(blocks, axis):
+    count = lax.axis_size(axis)
+    total = blocks[0].astype(jnp.float32)
+    for shift in range(1, count):
+        pairs = [(i, (i + shift) % count) for i in range(count)]
+        total = total + lax.ppermute(blocks[shift], axis, pairs).astype(jnp.float32)
+    return total.astype(jnp.bfloat16)
+
+
+def exchange_rows(accum, stats, axis, rows):
+    count = lax.axis_size(axis)
+    place = lax.axis_index(axis)
+    accs = [lax.dynamic_slice_in_dim(accum, place * rows, rows, 0)]
+    stat_parts = [lax.dynamic_slice_in_dim(stats, place * rows, rows, 1)]
+    for shift in range(1, count):
+        target = (place + shift) % count
+        pairs = [(i, (i + shift) % count) for i in range(count)]
+        accs.append(
+            lax.ppermute(lax.dynamic_slice_in_dim(accum, target * rows, rows, 0), axis, pairs)
+        )
+        stat_parts.append(
+            lax.ppermute(lax.dynamic_slice_in_dim(stats, target * rows, rows, 1), axis, pairs)
+        )
+    return jnp.stack(accs).astype(jnp.float32), jnp.stack(stat_parts)
 
 
 def per_device(
@@ -263,30 +288,44 @@
     chunks = 2 if frame_count % 512 == 0 else 1
     chunk_rows = frame_count // chunks
     head_devices = lax.axis_size("head")
+    paired = head_devices % 2 == 0
     w_ordered = ordered_columns(w_out, "head")
-    frame_parts = []
-    for c in range(chunks):
-        terms = window_attention(
+    parts = [
+        window_attention(
             query, keyed, valued, low, high, w_ordered, first_frame, length,
             c * chunk_rows, chunk_rows, head_devices,
         )
-        frame_parts.append(paired_block_sum(terms, "head"))
-    terms, keyed, valued = lax.optimization_barrier((terms, keyed, valued))
-    frames_out = jnp.concatenate(frame_parts, axis=0)
+        for c in range(chunks)
+    ]
     latent_count = latents.shape[0]
     latent_query = project(latents, w_latent_query)
     valid_count = jnp.clip(length - first_frame, 0, frame_count)
+    frame_parts = []
+    if paired:
+        first_sums = chip_pair_sums(parts[0], "head")
+        first_sums, rest, keyed, valued = lax.optimization_barrier(
+            (first_sums, parts[1:], keyed, valued)
+        )
+        frame_parts.append(cross_chip_sum(first_sums, "head"))
+        rest_sums = [chip_pair_sums(blocks, "head") for blocks in rest]
+    else:
+        frame_parts = [plain_block_sum(blocks, "head") for blocks in parts]
     peaks, totals, local_accum = latent_attention(latent_query, keyed, valued, valid_count)
+    stats = jnp.concatenate([peaks, totals], axis=1).T
+    local_accum = local_accum.astype(jnp.bfloat16)
+    if paired:
+        rest_sums, local_accum, stats = lax.optimization_barrier((rest_sums, local_accum, stats))
+        frame_parts.extend(cross_chip_sum(sums, "head") for sums in rest_sums)
+    frames_out = jnp.concatenate(frame_parts, axis=0)
     rows_here = latent_count // seq_devices
-    payload = jnp.concatenate([local_accum, peaks, totals], axis=1)
-    parts = shifted_blocks(payload, "seq", rows_here)
-    part_accum = parts[:, :, :head_width]
-    part_peak = parts[:, :, head_width : head_width + heads_here]
-    part_total = parts[:, :, head_width + heads_here :]
+    part_accum, part_stats = exchange_rows(local_accum, stats, "seq", rows_here)
+    part_peak = part_stats[:, :heads_here, :]
+    part_total = part_stats[:, heads_here:, :]
     joint = jnp.max(part_peak, axis=0)
     factor = jnp.exp(part_peak - joint[None])
-    own_total = jnp.sum(part_total * factor, axis=0)
-    own_accum = jnp.sum(part_accum * jnp.repeat(factor, HD, axis=2), axis=0)
+    own_total = jnp.sum(part_total * factor, axis=0).T
+    factor_rows = jnp.transpose(factor, (0, 2, 1))
+    own_accum = jnp.sum(part_accum * jnp.repeat(factor_rows, HD, axis=2), axis=0)
     summary = (own_accum / jnp.repeat(own_total, HD, axis=1)).astype(jnp.bfloat16)
     latent_terms = jnp.dot(summary, w_latent_out, preferred_element_type=jnp.float32)
     latents_out = column_sum(latent_terms.astype(jnp.bfloat16), "head")

time: 142 us -> 127 us (0.89)
  waiting for transfers between devices: 39.6 us -> 19.7 us
  starting transfers between devices: 17.1 us -> 21.8 us
  local copies, waits for them, and re-layouts: 11.8 us -> 15.4 us
  other arithmetic: 16.1 us -> 14.4 us
    ppermute x9 -> x12, waiting for transfers between devices: 25.9 us -> 9.56 us  [the longest x3 5.45 us: exchange_rows(): lax.ppermute(lax.dynamic_slice_in_dim(stats, target * rows, rows, 1), axi...]
    ppermute x3, waiting for transfers between devices: 13.3 us -> 5.73 us  [column_sum(): total = total + lax.ppermute(block, axis, pairs).astype(jnp.float32)]
    ppermute x1, waiting for transfers between devices: 0.42 us -> 4.44 us  [halos(): lax.ppermute(head, axis, backward)]
    another operation x2 -> x1, other arithmetic: 3.52 us -> 0.01 us  [exchange_rows(): return (jnp.stack(accs).astype(jnp.float32), jnp.stack(stat_parts))]
    ppermute x9 -> x12, starting transfers between devices: 10 us -> 13.4 us  [the longest x3 5.66 us: exchange_rows(): lax.ppermute(lax.dynamic_slice_in_dim(accum, target * rows, rows, 0), axi...]
    another operation x0 -> x3, local copies, waits for them, and re-layouts: none -> 2.88 us  [exchange_rows(): return (jnp.stack(accs).astype(jnp.float32), jnp.stack(stat_parts))]
    convert_element_type x4 -> x6, other arithmetic: 6.55 us -> 9.35 us  [the longest x2 4.88 us: chip_pair_sums(): return [(blocks[chips + d].astype(jnp.float32) + lax.ppermute(blocks[d],...]
    ppermute x0 -> x3, local copies, waits for them, and re-layouts: none -> 2.76 us  [exchange_rows(): lax.ppermute(lax.dynamic_slice_in_dim(accum, target * rows, rows, 0), axi...]
  transfers between devices with their start and end apart: 14 -> 17, of which waited for: 5 -> 6; matrix products, arithmetic and copies ran while one was open for 19% -> 20% of each run, Pallas kernels for 22% -> 24%
where the time goes in v6:
time: 127 us; the launch traced here: 126 us
  Pallas kernels  43.1 us (34%)
  starting transfers between devices  21.8 us (17%)
  waiting for transfers between devices  19.7 us (16%)
  local copies, waits for them, and re-layouts  15.4 us (12%)
  other arithmetic  14.4 us (11%)
  matrix products  10.1 us (8%)
  between operations  1.58 us (1%)
    pallas_call x2, Pallas kernels, window_attention(): pl.pallas_call(kernel, cost_estimate=cost, out_shape=jax.ShapeDtypeStruct...  25.3 us
    pallas_call x1, Pallas kernels, latent_attention(): pl.pallas_call(kernel, cost_estimate=cost, out_shape=(jax.ShapeDtypeStruc...  17.9 us
    dot_general x4, matrix products, project(): jnp.dot(source, weight, preferred_element_type=jnp.float32)  8.77 us
    ppermute x3, waiting for transfers between devices, column_sum(): total = total + lax.ppermute(block, axis, pairs).astype(jnp.float32)  5.73 us
    ppermute x3, starting transfers between devices, exchange_rows(): lax.ppermute(lax.dynamic_slice_in_dim(accum, target * rows, rows, 0), axi...  5.66 us
    ppermute x3, waiting for transfers between devices, exchange_rows(): lax.ppermute(lax.dynamic_slice_in_dim(stats, target * rows, rows, 1), axi...  5.45 us
    ppermute x1, starting transfers between devices, halos(): lax.ppermute(tail, axis, forward)  5.08 us
    convert_element_type x2, other arithmetic, chip_pair_sums(): return [(blocks[chips + d].astype(jnp.float32) + lax.ppermute(blocks[d],...  4.88 us
  transfers between devices with their start and end apart: 17, of which 6 were waited for; matrix products, arithmetic and copies ran while one was open for 20% of the time, Pallas kernels for 24%

profile of v6, /device:TPU:0, one launch (start us, length us, event | category | flops | bytes accessed | tf_op | source)
XLA Modules:
  0.0 126.2 jit_solution(1742890336749837575)
XLA Ops:
  0.7 3.7 %convolution_convert_fusion.1.k_ref = bf16[2048,256]{1,0:T(8,128)(2,1)S(1)} fusion(bf16[2048,1024]{1,0:T(8,128)(2,1)} %param.19, bf16[1024,256]{1,0:T(8,128)(2,1)} %param.23), kind=kOutput, calls=%fused_computation.1 | convolution fusion | flops 1074266112 | bytes 5767168 | tf_op jit(solution)/shard_map/dot_general | solution.py:25
  4.5 1.3 %convolution_convert_fusion.v_ref = bf16[2048,256]{1,0:T(8,128)(2,1)S(1)} fusion(bf16[2048,1024]{1,0:T(8,128)(2,1)S(1)} %copy-done.11, bf16[1024,256]{1,0:T(8,128)(2,1)S(1)} %copy-done.12), kind=kOutput, calls=%fused_computation | convolution fusion | flops 1074266112 | bytes 5767168 | tf_op jit(solution)/shard_map/dot_general | solution.py:25
  5.9 5.1 %collective-permute-start = (bf16[256,512]{1,0:T(8,128)(2,1)S(1)}, bf16[256,512]{1,0:T(8,128)(2,1)S(1)}, u32[]{:S(2)}, u32[]{:S(2)}) collective-permute-start(bf16[256,512]{1,0:T(8,128)(2,1)S(1)} %pad_maximum_fusion.2), channel_id=1, source_target_pairs={{0,4},{4,8},{8,12},{1,5},{5,9},{9,13},{2,6},{6,10},{10,14},{3,7},{... | collective-permute-start | bytes 786440 | tf_op jit(solution)/shard_map/ppermute | solution.py:21
  11.7 1.6 %collective-permute-start.1 = (bf16[256,512]{1,0:T(8,128)(2,1)}, bf16[256,512]{1,0:T(8,128)(2,1)S(1)}, u32[]{:S(2)}, u32[]{:S(2)}) collective-permute-start(bf16[256,512]{1,0:T(8,128)(2,1)} %pad_maximum_fusion.3), channel_id=1, source_target_pairs={{4,0},{8,4},{12,8},{5,1},{9,5},{13,9},{6,2},{10,6},{14,10},{7,3},{... | collective-permute-start | bytes 786440 | tf_op jit(solution)/shard_map/ppermute | solution.py:21
  13.3 2.3 %convolution_convert_fusion.2.q_ref = bf16[2048,256]{1,0:T(8,128)(2,1)} fusion(bf16[2048,1024]{1,0:T(8,128)(2,1)S(1)} %copy-done.11, bf16[1024,256]{1,0:T(8,128)(2,1)S(1)} %copy-done.13), kind=kOutput, calls=%fused_computation.2 | convolution fusion | flops 1074266112 | bytes 5767168 | tf_op jit(solution)/shard_map/dot_general | solution.py:25
  17.3 4.4 %collective-permute-done.1.high_ref = bf16[256,512]{1,0:T(8,128)(2,1)S(1)} collective-permute-done((bf16[256,512]{1,0:T(8,128)(2,1)}, bf16[256,512]{1,0:T(8,128)(2,1)S(1)}, u32[]{:S(2)}, u32[]{:S(2)}) %collective-permute-start.1) | collective-permute-done | bytes 262176 | tf_op jit(solution)/shard_map/ppermute | solution.py:21
  22.4 12.7 %shard_map.122 = bf16[4,1024,256]{2,1,0:T(8,128)(2,1)} custom-call(s32[3]{0:T(128)} %copy-done.9, bf16[2048,256]{1,0:T(8,128)(2,1)} %convolution_convert_fusion.2.q_ref, bf16[2048,256]{1,0:T(8,128)(2,1)} %copy-done.3, bf16[2048,256]{1,0:T(8,128)(2,1)} %copy-done.4, bf16[256,512]{1,0:T(8,128)(2,1)} %copy-done.5, bf16[256,512]{1,0:T(8,128)(2,1)} %copy-done.6, ...), custom_call_target="tpu_custom_call" | custom-call | flops 1342177280 | bytes 5767168 | tf_op jit(solution)/shard_map/pallas_call | solution.py:93
  35.1 2.1 %slice_bitcast_fusion = (bf16[1024,256]{1,0:T(8,128)(2,1)}, bf16[1024,256]{1,0:T(8,128)(2,1)S(1)}) fusion(bf16[4,1024,256]{2,1,0:T(8,128)(2,1)} %shard_map.122), kind=kLoop, calls=%fused_computation.17 | loop fusion | bytes 2097152 | tf_op jit(solution)/shard_map/squeeze | solution.py:232
  38.2 12.6 %shard_map.123 = bf16[4,1024,256]{2,1,0:T(8,128)(2,1)} custom-call(s32[3]{0:T(128)} %copy-done.10, bf16[2048,256]{1,0:T(8,128)(2,1)} %convolution_convert_fusion.2.q_ref, bf16[2048,256]{1,0:T(8,128)(2,1)} %copy-done.3, bf16[2048,256]{1,0:T(8,128)(2,1)} %copy-done.4, bf16[256,512]{1,0:T(8,128)(2,1)} %copy-done.5, bf16[256,512]{1,0:T(8,128)(2,1)} %copy-done.6, ...), custom_call_target="tpu_custom_call" | custom-call | flops 1342177280 | bytes 5767168 | tf_op jit(solution)/shard_map/pallas_call | solution.py:93
  50.9 2.6 %fusion.2 = (bf16[1024,256]{1,0:T(8,128)(2,1)}, bf16[1024,256]{1,0:T(8,128)(2,1)S(1)}) fusion(bf16[1024,256]{1,0:T(8,128)(2,1)S(1)} %collective-permute-done.3, bf16[4,1024,256]{2,1,0:T(8,128)(2,1)} %shard_map.122, bf16[1024,256]{1,0:T(8,128)(2,1)} %collective-permute-done.2), kind=kLoop, calls=%fused_computation.11 | loop fusion | flops 2097152 | bytes 3145728 | tf_op jit(solution)/shard_map/convert_element_type | solution.py:233
  53.5 1.0 slice_bitcast_fusion.5
  55.0 1.5 %convolution_convert_fusion.4.q_ref = bf16[1024,256]{1,0:T(8,128)(2,1)} fusion(bf16[1024,1024]{1,0:T(8,128)(2,1)S(1)} %copy-done, bf16[1024,256]{1,0:T(8,128)(2,1)S(1)} %copy-done.14), kind=kOutput, calls=%fused_computation.4 | convolution fusion | flops 537133056 | bytes 3145728 | tf_op jit(solution)/shard_map/dot_general | solution.py:25
  56.5 17.9 %shard_map.124 = (f32[1024,256]{1,0:T(8,128)}, f32[1024,128]{1,0:T(8,128)}) custom-call(s32[1]{0:T(128)} %bitcast.10.scal_ref, bf16[1024,256]{1,0:T(8,128)(2,1)} %convolution_convert_fusion.4.q_ref, bf16[2048,256]{1,0:T(8,128)(2,1)} %copy-done.3, bf16[2048,256]{1,0:T(8,128)(2,1)} %copy-done.4), custom_call_target="tpu_custom_call" | custom-call | flops 2147483648 | bytes 4194304 | tf_op jit(solution)/shard_map/pallas_call | solution.py:153
  74.4 1.4 %convert_element_type.132 = bf16[1024,256]{1,0:T(8,128)(2,1)S(1)} convert(f32[1024,256]{1,0:T(8,128)} %get-tuple-element.66) | non-fusion elementwise | flops 262144 | bytes 1572864 | tf_op jit(solution)/shard_map/convert_element_type | solution.py:315
  75.8 1.6 %collective-permute-start.4 = (bf16[1024,256]{1,0:T(8,128)(2,1)}, bf16[1024,256]{1,0:T(8,128)(2,1)}, u32[]{:S(2)}, u32[]{:S(2)}) collective-permute-start(bf16[1024,256]{1,0:T(8,128)(2,1)} %get-tuple-element.62), channel_id=1, source_target_pairs={{0,2},{1,3},{2,0},{3,1},{4,6},{5,7},{6,4},{7,5},{8,10},{9,11},{10,... | collective-permute-start | bytes 1572872 | tf_op jit(solution)/shard_map/ppermute | solution.py:244
  77.4 1.1 slice_bitcast_fusion.4
  79.3 2.3 %fusion = (bf16[1024,256]{1,0:T(8,128)(2,1)}, bf16[1024,256]{1,0:T(8,128)(2,1)S(1)}) fusion(bf16[1024,256]{1,0:T(8,128)(2,1)} %copy-done.8, bf16[4,1024,256]{2,1,0:T(8,128)(2,1)S(1)} %copy-done.2, bf16[1024,256]{1,0:T(8,128)(2,1)} %collective-permute-done.5), kind=kLoop, calls=%fused_computation.7 | loop fusion | flops 2097152 | bytes 3145728 | tf_op jit(solution)/shard_map/convert_element_type | solution.py:233
  82.9 1.7 %collective-permute-start.13 = (f32[8,256]{0,1:T(8,128)}, f32[8,256]{0,1:T(8,128)}, u32[]{:S(2)}, u32[]{:S(2)}) collective-permute-start(f32[8,256]{0,1:T(8,128)} %get-tuple-element.88), channel_id=1, source_target_pairs={{0,12},{4,0},{8,4},{12,8},{1,13},{5,1},{9,5},{13,9},{2,14},{6,2},{... | collective-permute-start | bytes 24584 | tf_op jit(solution)/shard_map/ppermute | solution.py:269
  84.5 1.4 %collective-permute-start.12 = (f32[8,256]{0,1:T(8,128)}, f32[8,256]{0,1:T(8,128)}, u32[]{:S(2)}, u32[]{:S(2)}) collective-permute-start(f32[8,256]{0,1:T(8,128)} %get-tuple-element.89), channel_id=1, source_target_pairs={{0,8},{4,12},{8,0},{12,4},{1,9},{5,13},{9,1},{13,5},{2,10},{6,14},... | collective-permute-start | bytes 24584 | tf_op jit(solution)/shard_map/ppermute | solution.py:269
  85.9 1.6 %collective-permute-start.11 = (f32[8,256]{0,1:T(8,128)}, f32[8,256]{0,1:T(8,128)}, u32[]{:S(2)}, u32[]{:S(2)}) collective-permute-start(f32[8,256]{0,1:T(8,128)} %get-tuple-element.90), channel_id=1, source_target_pairs={{0,4},{4,8},{8,12},{12,0},{1,5},{5,9},{9,13},{13,1},{2,6},{6,10},{... | collective-permute-start | bytes 24584 | tf_op jit(solution)/shard_map/ppermute | solution.py:269
  88.9 4.3 %collective-permute-start.10 = (bf16[256,256]{1,0:T(8,128)(2,1)}, bf16[256,256]{1,0:T(8,128)(2,1)S(1)}, u32[]{:S(2)}, u32[]{:S(2)}) collective-permute-start(bf16[256,256]{1,0:T(8,128)(2,1)} %get-tuple-element.92), channel_id=1, source_target_pairs={{0,12},{4,0},{8,4},{12,8},{1,13},{5,1},{9,5},{13,9},{2,14},{6,2},{... | collective-permute-start | bytes 393224 | tf_op jit(solution)/shard_map/ppermute | solution.py:266
  94.1 5.0 %collective-permute-done.12 = f32[8,256]{0,1:T(8,128)} collective-permute-done((f32[8,256]{0,1:T(8,128)}, f32[8,256]{0,1:T(8,128)}, u32[]{:S(2)}, u32[]{:S(2)}) %collective-permute-start.12) | collective-permute-done | bytes 8224 | tf_op jit(solution)/shard_map/ppermute | solution.py:269
  100.1 1.3 %collective-permute-start.8 = (bf16[256,256]{1,0:T(8,128)(2,1)}, bf16[256,256]{1,0:T(8,128)(2,1)}, u32[]{:S(2)}, u32[]{:S(2)}) collective-permute-start(bf16[256,256]{1,0:T(8,128)(2,1)} %get-tuple-element.94), channel_id=1, source_target_pairs={{0,4},{4,8},{8,12},{12,0},{1,5},{5,9},{9,13},{13,1},{2,6},{6,10},{... | collective-permute-start | bytes 393224 | tf_op jit(solution)/shard_map/ppermute | solution.py:266
  104.6 4.1 %collective-permute-done.9 = bf16[256,256]{1,0:T(8,128)(2,1)} collective-permute-done((bf16[256,256]{1,0:T(8,128)(2,1)}, bf16[256,256]{1,0:T(8,128)(2,1)}, u32[]{:S(2)}, u32[]{:S(2)}) %collective-permute-start.9) | collective-permute-done | bytes 131104 | tf_op jit(solution)/shard_map/ppermute | solution.py:266
  109.7 1.7 %copy.36 = bf16[256,256]{0,1:T(8,128)(2,1)} copy(bf16[256,256]{1,0:T(8,128)(2,1)} %collective-permute-done.8) | data formatting | bytes 262144 | tf_op jit(solution)/shard_map/ppermute | solution.py:266
  111.4 1.0 multiply_reduce_fusion
  113.1 1.4 %convolution_convert_fusion.3 = bf16[256,1024]{1,0:T(8,128)(2,1)S(1)} fusion(bf16[256,256]{0,1:T(8,128)(2,1)S(1)} %bitcast.52, bf16[256,1024]{1,0:T(8,128)(2,1)} %param.27), kind=kOutput, calls=%fused_computation.3 | convolution fusion | flops 134479872 | bytes 1179648 | tf_op jit(solution)/shard_map/dot_general | solution.py:330
  114.6 1.6 %collective-permute-start.15 = (bf16[256,256]{1,0:T(8,128)(2,1)S(1)}, bf16[256,256]{1,0:T(8,128)(2,1)S(1)}, u32[]{:S(2)}, u32[]{:S(2)}) collective-permute-start(bf16[256,256]{1,0:T(8,128)(2,1)S(1)} %get-tuple-element.86), channel_id=1, source_target_pairs={{0,2},{1,3},{2,0},{3,1},{4,6},{5,7},{6,4},{7,5},{8,10},{9,11},{10,... | collective-permute-start | bytes 393224 | tf_op jit(solution)/shard_map/ppermute | solution.py:200
  116.4 1.2 add_convert_fusion.1
  117.6 5.6 %collective-permute-done.15 = bf16[256,256]{1,0:T(8,128)(2,1)S(1)} collective-permute-done((bf16[256,256]{1,0:T(8,128)(2,1)S(1)}, bf16[256,256]{1,0:T(8,128)(2,1)S(1)}, u32[]{:S(2)}, u32[]{:S(2)}) %collective-permute-start.15) | collective-permute-done | bytes 131104 | tf_op jit(solution)/shard_map/ppermute | solution.py:200
  124.0 1.2 add_convert_fusion
  125.2 1.0 pad_maximum_fusion
  (80 shorter events, 15.6 us)
Async XLA Ops:
  0.6 54.4 %copy-start = (bf16[1024,1024]{1,0:T(8,128)(2,1)S(1)}, bf16[1024,1024]{1,0:T(8,128)(2,1)}, u32[]{:S(2)}) copy-start(bf16[1024,1024]{1,0:T(8,128)(2,1)} %param.20) | copy-start | bytes 6291460
  0.6 3.8 %copy-start.11 = (bf16[2048,1024]{1,0:T(8,128)(2,1)S(1)}, bf16[2048,1024]{1,0:T(8,128)(2,1)}, u32[]{:S(2)}) copy-start(bf16[2048,1024]{1,0:T(8,128)(2,1)} %param.19) | copy-start | bytes 12582916
  0.7 3.9 %copy-start.12 = (bf16[1024,256]{1,0:T(8,128)(2,1)S(1)}, bf16[1024,256]{1,0:T(8,128)(2,1)}, u32[]{:S(2)}) copy-start(bf16[1024,256]{1,0:T(8,128)(2,1)} %param.24) | copy-start | bytes 1572868
  4.5 1.3 %copy-start.3 = (bf16[2048,256]{1,0:T(8,128)(2,1)}, bf16[2048,256]{1,0:T(8,128)(2,1)S(1)}, u32[]{:S(2)}) copy-start(bf16[2048,256]{1,0:T(8,128)(2,1)S(1)} %convolution_convert_fusion.1.k_ref) | copy-start | bytes 3145732
  5.8 9.8 %copy-start.4 = (bf16[2048,256]{1,0:T(8,128)(2,1)}, bf16[2048,256]{1,0:T(8,128)(2,1)S(1)}, u32[]{:S(2)}) copy-start(bf16[2048,256]{1,0:T(8,128)(2,1)S(1)} %convolution_convert_fusion.v_ref) | copy-start | bytes 3145732
  5.8 7.5 %copy-start.13 = (bf16[1024,256]{1,0:T(8,128)(2,1)S(1)}, bf16[1024,256]{1,0:T(8,128)(2,1)}, u32[]{:S(2)}) copy-start(bf16[1024,256]{1,0:T(8,128)(2,1)} %param.22) | copy-start | bytes 1572868
  5.9 11.3 %collective-permute-start = (bf16[256,512]{1,0:T(8,128)(2,1)S(1)}, bf16[256,512]{1,0:T(8,128)(2,1)S(1)}, u32[]{:S(2)}, u32[]{:S(2)}) collective-permute-start(bf16[256,512]{1,0:T(8,128)(2,1)S(1)} %pad_maximum_fusion.2), channel_id=1, source_target_pairs={{0,4},{4,8},{8,12},{1,5},{5,9},{9,13},{2,6},{6,10},{10,14},{3,7},{... | collective-permute-start | bytes 786440 | tf_op jit(solution)/shard_map/ppermute | solution.py:21
  11.7 4.6 %copy-start.7 = (bf16[256,1024]{1,0:T(8,128)(2,1)S(1)}, bf16[256,1024]{1,0:T(8,128)(2,1)}, u32[]{:S(2)}) copy-start(bf16[256,1024]{1,0:T(8,128)(2,1)} %param.25) | copy-start | bytes 1572868
  11.7 10.0 %collective-permute-start.1 = (bf16[256,512]{1,0:T(8,128)(2,1)}, bf16[256,512]{1,0:T(8,128)(2,1)S(1)}, u32[]{:S(2)}, u32[]{:S(2)}) collective-permute-start(bf16[256,512]{1,0:T(8,128)(2,1)} %pad_maximum_fusion.3), channel_id=1, source_target_pairs={{4,0},{8,4},{12,8},{5,1},{9,5},{13,9},{6,2},{10,6},{14,10},{7,3},{... | collective-permute-start | bytes 786440 | tf_op jit(solution)/shard_map/ppermute | solution.py:21
  16.3 5.5 %copy-start.9 = (s32[3]{0:T(128)}, s32[3]{0:T(128)S(1)}, u32[]{:S(2)}) copy-start(s32[3]{0:T(128)S(1)} %constant_dynamic-update-slice_fusion.2.scal_ref) | copy-start | bytes 40
  17.3 4.4 %copy-start.5 = (bf16[256,512]{1,0:T(8,128)(2,1)}, bf16[256,512]{1,0:T(8,128)(2,1)S(1)}, u32[]{:S(2)}) copy-start(bf16[256,512]{1,0:T(8,128)(2,1)S(1)} %collective-permute-done.low_ref) | copy-start | bytes 786436
  21.7 0.7 copy-start.6
  35.1 2.6 %copy-start.15 = (s32[3]{0:T(128)S(1)}, s32[3]{0:T(128)}, u32[]{:S(2)}) copy-start(s32[3]{0:T(128)} %constant.169.clone) | copy-start | bytes 40
  37.2 13.7 %collective-permute-start.3 = (bf16[1024,256]{1,0:T(8,128)(2,1)}, bf16[1024,256]{1,0:T(8,128)(2,1)S(1)}, u32[]{:S(2)}, u32[]{:S(2)}) collective-permute-start(bf16[1024,256]{1,0:T(8,128)(2,1)} %get-tuple-element.78), channel_id=1, source_target_pairs={{0,1},{1,0},{2,3},{3,2},{4,5},{5,4},{6,7},{7,6},{8,9},{9,8},{10,11... | collective-permute-start | bytes 1572872 | tf_op jit(solution)/shard_map/ppermute | solution.py:232
  37.2 13.7 %collective-permute-start.2 = (bf16[1024,256]{1,0:T(8,128)(2,1)S(1)}, bf16[1024,256]{1,0:T(8,128)(2,1)}, u32[]{:S(2)}, u32[]{:S(2)}) collective-permute-start(bf16[1024,256]{1,0:T(8,128)(2,1)S(1)} %get-tuple-element.79), channel_id=1, source_target_pairs={{0,1},{1,0},{2,3},{3,2},{4,5},{5,4},{6,7},{7,6},{8,9},{9,8},{10,11... | collective-permute-start | bytes 1572872 | tf_op jit(solution)/shard_map/ppermute | solution.py:232
  50.9 2.6 %copy-start.1 = (bf16[4,1024,256]{2,1,0:T(8,128)(2,1)S(1)}, bf16[4,1024,256]{2,1,0:T(8,128)(2,1)}, u32[]{:S(2)}) copy-start(bf16[4,1024,256]{2,1,0:T(8,128)(2,1)} %shard_map.123) | copy-start | bytes 6291460
  50.9 4.2 %copy-start.14 = (bf16[1024,256]{1,0:T(8,128)(2,1)S(1)}, bf16[1024,256]{1,0:T(8,128)(2,1)}, u32[]{:S(2)}) copy-start(bf16[1024,256]{1,0:T(8,128)(2,1)} %param.26) | copy-start | bytes 1572868
  54.5 24.0 %collective-permute-start.6 = (bf16[1024,256]{1,0:T(8,128)(2,1)}, bf16[1024,256]{1,0:T(8,128)(2,1)S(1)}, u32[]{:S(2)}, u32[]{:S(2)}) collective-permute-start(bf16[1024,256]{1,0:T(8,128)(2,1)} %get-tuple-element.74), channel_id=1, source_target_pairs={{0,1},{1,0},{2,3},{3,2},{4,5},{5,4},{6,7},{7,6},{8,9},{9,8},{10,11... | collective-permute-start | bytes 1572872 | tf_op jit(solution)/shard_map/ppermute | solution.py:232
  54.5 24.8 %collective-permute-start.5 = (bf16[1024,256]{1,0:T(8,128)(2,1)}, bf16[1024,256]{1,0:T(8,128)(2,1)}, u32[]{:S(2)}, u32[]{:S(2)}) collective-permute-start(bf16[1024,256]{1,0:T(8,128)(2,1)} %get-tuple-element.75), channel_id=1, source_target_pairs={{0,1},{1,0},{2,3},{3,2},{4,5},{5,4},{6,7},{7,6},{8,9},{9,8},{10,11... | collective-permute-start | bytes 1572872 | tf_op jit(solution)/shard_map/ppermute | solution.py:232
  74.4 4.9 %copy-start.2 = (bf16[4,1024,256]{2,1,0:T(8,128)(2,1)S(1)}, bf16[4,1024,256]{2,1,0:T(8,128)(2,1)}, u32[]{:S(2)}) copy-start(bf16[4,1024,256]{2,1,0:T(8,128)(2,1)} %shard_map.123) | copy-start | bytes 6291460
  75.8 40.5 %collective-permute-start.4 = (bf16[1024,256]{1,0:T(8,128)(2,1)}, bf16[1024,256]{1,0:T(8,128)(2,1)}, u32[]{:S(2)}, u32[]{:S(2)}) collective-permute-start(bf16[1024,256]{1,0:T(8,128)(2,1)} %get-tuple-element.62), channel_id=1, source_target_pairs={{0,2},{1,3},{2,0},{3,1},{4,6},{5,7},{6,4},{7,5},{8,10},{9,11},{10,... | collective-permute-start | bytes 1572872 | tf_op jit(solution)/shard_map/ppermute | solution.py:244
  78.5 0.8 copy-start.8
  81.6 42.4 %collective-permute-start.7 = (bf16[1024,256]{1,0:T(8,128)(2,1)}, bf16[1024,256]{1,0:T(8,128)(2,1)}, u32[]{:S(2)}, u32[]{:S(2)}) collective-permute-start(bf16[1024,256]{1,0:T(8,128)(2,1)} %get-tuple-element.69), channel_id=1, source_target_pairs={{0,2},{1,3},{2,0},{3,1},{4,6},{5,7},{6,4},{7,5},{8,10},{9,11},{10,... | collective-permute-start | bytes 1572872 | tf_op jit(solution)/shard_map/ppermute | solution.py:244
  82.9 6.0 %collective-permute-start.13 = (f32[8,256]{0,1:T(8,128)}, f32[8,256]{0,1:T(8,128)}, u32[]{:S(2)}, u32[]{:S(2)}) collective-permute-start(f32[8,256]{0,1:T(8,128)} %get-tuple-element.88), channel_id=1, source_target_pairs={{0,12},{4,0},{8,4},{12,8},{1,13},{5,1},{9,5},{13,9},{2,14},{6,2},{... | collective-permute-start | bytes 24584 | tf_op jit(solution)/shard_map/ppermute | solution.py:269
  84.5 14.6 %collective-permute-start.12 = (f32[8,256]{0,1:T(8,128)}, f32[8,256]{0,1:T(8,128)}, u32[]{:S(2)}, u32[]{:S(2)}) collective-permute-start(f32[8,256]{0,1:T(8,128)} %get-tuple-element.89), channel_id=1, source_target_pairs={{0,8},{4,12},{8,0},{12,4},{1,9},{5,13},{9,1},{13,5},{2,10},{6,14},... | collective-permute-start | bytes 24584 | tf_op jit(solution)/shard_map/ppermute | solution.py:269
  85.9 14.2 %collective-permute-start.11 = (f32[8,256]{0,1:T(8,128)}, f32[8,256]{0,1:T(8,128)}, u32[]{:S(2)}, u32[]{:S(2)}) collective-permute-start(f32[8,256]{0,1:T(8,128)} %get-tuple-element.90), channel_id=1, source_target_pairs={{0,4},{4,8},{8,12},{12,0},{1,5},{5,9},{9,13},{13,1},{2,6},{6,10},{... | collective-permute-start | bytes 24584 | tf_op jit(solution)/shard_map/ppermute | solution.py:269
  88.9 15.7 %collective-permute-start.10 = (bf16[256,256]{1,0:T(8,128)(2,1)}, bf16[256,256]{1,0:T(8,128)(2,1)S(1)}, u32[]{:S(2)}, u32[]{:S(2)}) collective-permute-start(bf16[256,256]{1,0:T(8,128)(2,1)} %get-tuple-element.92), channel_id=1, source_target_pairs={{0,12},{4,0},{8,4},{12,8},{1,13},{5,1},{9,5},{13,9},{2,14},{6,2},{... | collective-permute-start | bytes 393224 | tf_op jit(solution)/shard_map/ppermute | solution.py:266
  99.1 9.6 %collective-permute-start.9 = (bf16[256,256]{1,0:T(8,128)(2,1)}, bf16[256,256]{1,0:T(8,128)(2,1)}, u32[]{:S(2)}, u32[]{:S(2)}) collective-permute-start(bf16[256,256]{1,0:T(8,128)(2,1)} %get-tuple-element.93), channel_id=1, source_target_pairs={{0,8},{4,12},{8,0},{12,4},{1,9},{5,13},{9,1},{13,5},{2,10},{6,14},... | collective-permute-start | bytes 393224 | tf_op jit(solution)/shard_map/ppermute | solution.py:266
  100.1 9.6 %collective-permute-start.8 = (bf16[256,256]{1,0:T(8,128)(2,1)}, bf16[256,256]{1,0:T(8,128)(2,1)}, u32[]{:S(2)}, u32[]{:S(2)}) collective-permute-start(bf16[256,256]{1,0:T(8,128)(2,1)} %get-tuple-element.94), channel_id=1, source_target_pairs={{0,4},{4,8},{8,12},{12,0},{1,5},{5,9},{9,13},{13,1},{2,6},{6,10},{... | collective-permute-start | bytes 393224 | tf_op jit(solution)/shard_map/ppermute | solution.py:266
  114.6 3.0 %collective-permute-start.16 = (bf16[256,256]{1,0:T(8,128)(2,1)S(1)}, bf16[256,256]{1,0:T(8,128)(2,1)S(1)}, u32[]{:S(2)}, u32[]{:S(2)}) collective-permute-start(bf16[256,256]{1,0:T(8,128)(2,1)S(1)} %get-tuple-element.85), channel_id=1, source_target_pairs={{0,3},{1,0},{2,1},{3,2},{4,7},{5,4},{6,5},{7,6},{8,11},{9,8},{10,9... | collective-permute-start | bytes 393224 | tf_op jit(solution)/shard_map/ppermute | solution.py:200
  114.6 8.6 %collective-permute-start.15 = (bf16[256,256]{1,0:T(8,128)(2,1)S(1)}, bf16[256,256]{1,0:T(8,128)(2,1)S(1)}, u32[]{:S(2)}, u32[]{:S(2)}) collective-permute-start(bf16[256,256]{1,0:T(8,128)(2,1)S(1)} %get-tuple-element.86), channel_id=1, source_target_pairs={{0,2},{1,3},{2,0},{3,1},{4,6},{5,7},{6,4},{7,5},{8,10},{9,11},{10,... | collective-permute-start | bytes 393224 | tf_op jit(solution)/shard_map/ppermute | solution.py:200
  116.2 7.1 %collective-permute-start.14 = (bf16[256,256]{1,0:T(8,128)(2,1)S(1)}, bf16[256,256]{1,0:T(8,128)(2,1)S(1)}, u32[]{:S(2)}, u32[]{:S(2)}) collective-permute-start(bf16[256,256]{1,0:T(8,128)(2,1)S(1)} %get-tuple-element.84), channel_id=1, source_target_pairs={{0,1},{1,2},{2,3},{3,0},{4,5},{5,6},{6,7},{7,4},{8,9},{9,10},{10,1... | collective-permute-start | bytes 393224 | tf_op jit(solution)/shard_map/ppermute | solution.py:200
  (1 other events, 0.5 us)

commit v7 on v6

--- a/solution.py
+++ b/solution.py
@@ -290,6 +290,17 @@
     head_devices = lax.axis_size("head")
     paired = head_devices % 2 == 0
     w_ordered = ordered_columns(w_out, "head")
+    latent_count = latents.shape[0]
+    rows_here = latent_count // seq_devices
+    latent_query = project(latents, w_latent_query)
+    valid_count = jnp.clip(length - first_frame, 0, frame_count)
+    peaks, totals, local_accum = latent_attention(latent_query, keyed, valued, valid_count)
+    stats = jnp.concatenate([peaks, totals], axis=1).T
+    local_accum = local_accum.astype(jnp.bfloat16)
+    local_accum, stats, query, keyed, valued, low, high = lax.optimization_barrier(
+        (local_accum, stats, query, keyed, valued, low, high)
+    )
+    part_accum, part_stats = exchange_rows(local_accum, stats, "seq", rows_here)
     parts = [
         window_attention(
             query, keyed, valued, low, high, w_ordered, first_frame, length,
@@ -297,28 +308,18 @@
         )
         for c in range(chunks)
     ]
-    latent_count = latents.shape[0]
-    latent_query = project(latents, w_latent_query)
-    valid_count = jnp.clip(length - first_frame, 0, frame_count)
-    frame_parts = []
     if paired:
         first_sums = chip_pair_sums(parts[0], "head")
-        first_sums, rest, keyed, valued = lax.optimization_barrier(
-            (first_sums, parts[1:], keyed, valued)
-        )
-        frame_parts.append(cross_chip_sum(first_sums, "head"))
-        rest_sums = [chip_pair_sums(blocks, "head") for blocks in rest]
+        first_sums, rest, part_accum, part_stats = lax.optimization_barrier(
+            (first_sums, parts[1:], part_accum, part_stats)
+        )
+        frame_parts = [cross_chip_sum(first_sums, "head")]
+        frame_parts.extend(
+            cross_chip_sum(chip_pair_sums(blocks, "head"), "head") for blocks in rest
+        )
     else:
         frame_parts = [plain_block_sum(blocks, "head") for blocks in parts]
-    peaks, totals, local_accum = latent_attention(latent_query, keyed, valued, valid_count)
-    stats = jnp.concatenate([peaks, totals], axis=1).T
-    local_accum = local_accum.astype(jnp.bfloat16)
-    if paired:
-        rest_sums, local_accum, stats = lax.optimization_barrier((rest_sums, local_accum, stats))
-        frame_parts.extend(cross_chip_sum(sums, "head") for sums in rest_sums)
     frames_out = jnp.concatenate(frame_parts, axis=0)
-    rows_here = latent_count // seq_devices
-    part_accum, part_stats = exchange_rows(local_accum, stats, "seq", rows_here)
     part_peak = part_stats[:, :heads_here, :]
     part_total = part_stats[:, heads_here:, :]
     joint = jnp.max(part_peak, axis=0)

time: 127 us -> 137 us (1.079)
  starting transfers between devices: 21.8 us -> 27.2 us
  waiting for transfers between devices: 19.7 us -> 23.2 us
  local copies, waits for them, and re-layouts: 15.4 us -> 12.9 us
  other arithmetic: 14.4 us -> 16.7 us
    ppermute x2, waiting for transfers between devices: 0.01 us -> 9.04 us  [cross_chip_sum(): total = total + lax.ppermute(chip_sums[d], axis, pairs).astype(jnp.float32)]
    ppermute x3, starting transfers between devices: 5.66 us -> 10.6 us  [exchange_rows(): lax.ppermute(lax.dynamic_slice_in_dim(accum, target * rows, rows, 0), axi...]
    ppermute x1, waiting for transfers between devices: 4.44 us -> 0.01 us  [halos(): lax.ppermute(head, axis, backward)]
    ppermute x3, waiting for transfers between devices: 4.09 us -> 0.01 us  [exchange_rows(): lax.ppermute(lax.dynamic_slice_in_dim(accum, target * rows, rows, 0), axi...]
    reshape x0 -> x2, local copies, waits for them, and re-layouts: none -> 3.38 us  [the longest x1 2.55 us: per_device(): jnp.repeat(factor_rows, HD, axis=2)]
    ppermute x3 -> x0, local copies, waits for them, and re-layouts: 2.76 us -> none  [exchange_rows(): lax.ppermute(lax.dynamic_slice_in_dim(accum, target * rows, rows, 0), axi...]
    dot_general x4, matrix products: 8.77 us -> 11 us  [project(): jnp.dot(source, weight, preferred_element_type=jnp.float32)]
    another operation x3 -> x4, local copies, waits for them, and re-layouts: 2.88 us -> 0.94 us  [exchange_rows(): return (jnp.stack(accs).astype(jnp.float32), jnp.stack(stat_parts))]
  transfers between devices with their start and end apart: 17 -> 17, of which waited for: 6 -> 5; matrix products, arithmetic and copies ran while one was open for 20% -> 17% of each run, Pallas kernels for 24% -> 22%
where the time goes in v7:
time: 137 us; the launch traced here: 136 us
  Pallas kernels  43.2 us (32%)
  starting transfers between devices  27.2 us (20%)
  waiting for transfers between devices  23.2 us (17%)
  other arithmetic  16.7 us (12%)
  local copies, waits for them, and re-layouts  12.9 us (9%)
  matrix products  11.3 us (8%)
  between operations  1.73 us (1%)
    pallas_call x2, Pallas kernels, window_attention(): pl.pallas_call(kernel, cost_estimate=cost, out_shape=jax.ShapeDtypeStruct...  25.3 us
    pallas_call x1, Pallas kernels, latent_attention(): pl.pallas_call(kernel, cost_estimate=cost, out_shape=(jax.ShapeDtypeStruc...  17.9 us
    dot_general x4, matrix products, project(): jnp.dot(source, weight, preferred_element_type=jnp.float32)  11 us
    ppermute x3, starting transfers between devices, exchange_rows(): lax.ppermute(lax.dynamic_slice_in_dim(accum, target * rows, rows, 0), axi...  10.6 us
    ppermute x2, waiting for transfers between devices, cross_chip_sum(): total = total + lax.ppermute(chip_sums[d], axis, pairs).astype(jnp.float32)  9.04 us
    ppermute x3, waiting for transfers between devices, column_sum(): total = total + lax.ppermute(block, axis, pairs).astype(jnp.float32)  7.59 us
    ppermute x3, waiting for transfers between devices, exchange_rows(): lax.ppermute(lax.dynamic_slice_in_dim(stats, target * rows, rows, 1), axi...  6.56 us
    ppermute x3, starting transfers between devices, exchange_rows(): lax.ppermute(lax.dynamic_slice_in_dim(stats, target * rows, rows, 1), axi...  5.98 us
  transfers between devices with their start and end apart: 17, of which 5 were waited for; matrix products, arithmetic and copies ran while one was open for 17% of the time, Pallas kernels for 22%

profile of v7, /device:TPU:0, one launch (start us, length us, event | category | flops | bytes accessed | tf_op | source)
XLA Modules:
  0.0 136.2 jit_solution(8720587861641480512)
XLA Ops:
  0.7 3.7 %convolution_convert_fusion.2.k_ref = bf16[2048,256]{1,0:T(8,128)(2,1)S(1)} fusion(bf16[2048,1024]{1,0:T(8,128)(2,1)} %param.19, bf16[1024,256]{1,0:T(8,128)(2,1)} %param.23), kind=kOutput, calls=%fused_computation.2 | convolution fusion | flops 1074266112 | bytes 5767168 | tf_op jit(solution)/shard_map/dot_general | solution.py:25
  4.5 1.3 convolution_convert_fusion.1.v_ref
  7.6 4.9 %collective-permute-start = (bf16[256,512]{1,0:T(8,128)(2,1)}, bf16[256,512]{1,0:T(8,128)(2,1)S(1)}, u32[]{:S(2)}, u32[]{:S(2)}) collective-permute-start(bf16[256,512]{1,0:T(8,128)(2,1)} %pad_maximum_fusion.2), channel_id=1, source_target_pairs={{0,4},{4,8},{8,12},{1,5},{5,9},{9,13},{2,6},{6,10},{10,14},{3,7},{... | collective-permute-start | bytes 786440 | tf_op jit(solution)/shard_map/ppermute | solution.py:21
  13.2 1.3 collective-permute-start.1
  15.3 4.5 %convolution_convert_fusion.q_ref = bf16[2048,256]{1,0:T(8,128)(2,1)} fusion(bf16[2048,1024]{1,0:T(8,128)(2,1)} %param.19, bf16[1024,256]{1,0:T(8,128)(2,1)S(1)} %copy-done.15), kind=kOutput, calls=%fused_computation | convolution fusion | flops 1074266112 | bytes 5767168 | tf_op jit(solution)/shard_map/dot_general | solution.py:25
  19.7 1.5 %convolution_convert_fusion.4.q_ref = bf16[1024,256]{1,0:T(8,128)(2,1)} fusion(bf16[1024,1024]{1,0:T(8,128)(2,1)S(1)} %copy-done, bf16[1024,256]{1,0:T(8,128)(2,1)S(1)} %copy-done.16), kind=kOutput, calls=%fused_computation.4 | convolution fusion | flops 537133056 | bytes 3145728 | tf_op jit(solution)/shard_map/dot_general | solution.py:25
  21.2 17.9 %shard_map.122 = (f32[1024,256]{1,0:T(8,128)}, f32[1024,128]{1,0:T(8,128)}) custom-call(s32[1]{0:T(128)} %bitcast.2.scal_ref, bf16[1024,256]{1,0:T(8,128)(2,1)} %convolution_convert_fusion.4.q_ref, bf16[2048,256]{1,0:T(8,128)(2,1)} %copy-done.2, bf16[2048,256]{1,0:T(8,128)(2,1)} %copy-done.3), custom_call_target="tpu_custom_call" | custom-call | flops 2147483648 | bytes 4194304 | tf_op jit(solution)/shard_map/pallas_call | solution.py:153
  40.2 1.3 convert_element_type.108
  41.5 1.1 slice_bitcast_fusion.6
  43.3 12.6 %shard_map.123 = bf16[4,1024,256]{2,1,0:T(8,128)(2,1)} custom-call(s32[3]{0:T(128)} %copy-done.12, bf16[2048,256]{1,0:T(8,128)(2,1)} %convolution_convert_fusion.q_ref, bf16[2048,256]{1,0:T(8,128)(2,1)} %copy-done.2, bf16[2048,256]{1,0:T(8,128)(2,1)} %copy-done.3, bf16[256,512]{1,0:T(8,128)(2,1)} %copy-done.5, ...), custom_call_target="tpu_custom_call" | custom-call | flops 1342177280 | bytes 5767168 | tf_op jit(solution)/shard_map/pallas_call | solution.py:93
  56.0 2.3 %slice_bitcast_fusion = (bf16[1024,256]{1,0:T(8,128)(2,1)}, bf16[1024,256]{1,0:T(8,128)(2,1)}) fusion(bf16[4,1024,256]{2,1,0:T(8,128)(2,1)} %shard_map.123), kind=kLoop, calls=%fused_computation.17 | loop fusion | bytes 2097152 | tf_op jit(solution)/shard_map/squeeze | solution.py:232
  58.8 5.3 %collective-permute-start.9 = (f32[8,256]{0,1:T(8,128)S(1)}, f32[8,256]{0,1:T(8,128)S(1)}, u32[]{:S(2)}, u32[]{:S(2)}) collective-permute-start(f32[8,256]{0,1:T(8,128)S(1)} %get-tuple-element.92), channel_id=1, source_target_pairs={{0,12},{4,0},{8,4},{12,8},{1,13},{5,1},{9,5},{13,9},{2,14},{6,2},{... | collective-permute-start | bytes 24584 | tf_op jit(solution)/shard_map/ppermute | solution.py:269
  65.5 2.6 %collective-permute-done.9 = f32[8,256]{0,1:T(8,128)S(1)} collective-permute-done((f32[8,256]{0,1:T(8,128)S(1)}, f32[8,256]{0,1:T(8,128)S(1)}, u32[]{:S(2)}, u32[]{:S(2)}) %collective-permute-start.9) | collective-permute-done | bytes 8224 | tf_op jit(solution)/shard_map/ppermute | solution.py:269
  68.1 4.3 %collective-permute-start.6 = (bf16[256,256]{1,0:T(8,128)(2,1)}, bf16[256,256]{1,0:T(8,128)(2,1)S(1)}, u32[]{:S(2)}, u32[]{:S(2)}) collective-permute-start(bf16[256,256]{1,0:T(8,128)(2,1)} %get-tuple-element.96), channel_id=1, source_target_pairs={{0,12},{4,0},{8,4},{12,8},{1,13},{5,1},{9,5},{13,9},{2,14},{6,2},{... | collective-permute-start | bytes 393224 | tf_op jit(solution)/shard_map/ppermute | solution.py:266
  72.4 4.0 %collective-permute-done.8 = f32[8,256]{0,1:T(8,128)S(1)} collective-permute-done((f32[8,256]{0,1:T(8,128)S(1)}, f32[8,256]{0,1:T(8,128)S(1)}, u32[]{:S(2)}, u32[]{:S(2)}) %collective-permute-start.8) | collective-permute-done | bytes 8224 | tf_op jit(solution)/shard_map/ppermute | solution.py:269
  76.4 6.3 %collective-permute-start.4 = (bf16[256,256]{1,0:T(8,128)(2,1)S(1)}, bf16[256,256]{1,0:T(8,128)(2,1)S(1)}, u32[]{:S(2)}, u32[]{:S(2)}) collective-permute-start(bf16[256,256]{1,0:T(8,128)(2,1)S(1)} %get-tuple-element.98), channel_id=1, source_target_pairs={{0,4},{4,8},{8,12},{12,0},{1,5},{5,9},{9,13},{13,1},{2,6},{6,10},{... | collective-permute-start | bytes 393224 | tf_op jit(solution)/shard_map/ppermute | solution.py:266
  82.7 12.6 %shard_map.124 = bf16[4,1024,256]{2,1,0:T(8,128)(2,1)} custom-call(s32[3]{0:T(128)} %copy-done.11, bf16[2048,256]{1,0:T(8,128)(2,1)} %convolution_convert_fusion.q_ref, bf16[2048,256]{1,0:T(8,128)(2,1)} %copy-done.2, bf16[2048,256]{1,0:T(8,128)(2,1)} %copy-done.3, bf16[256,512]{1,0:T(8,128)(2,1)} %copy-done.5, ...), custom_call_target="tpu_custom_call" | custom-call | flops 1342177280 | bytes 5767168 | tf_op jit(solution)/shard_map/pallas_call | solution.py:93
  96.3 1.2 maximum_convert_fusion
  97.6 2.8 %fusion.2 = (bf16[1024,256]{1,0:T(8,128)(2,1)}, bf16[1024,256]{1,0:T(8,128)(2,1)}) fusion(bf16[1024,256]{1,0:T(8,128)(2,1)} %collective-permute-done.3, bf16[4,1024,256]{2,1,0:T(8,128)(2,1)} %shard_map.123, bf16[1024,256]{1,0:T(8,128)(2,1)} %collective-permute-done.2), kind=kLoop, calls=%fused_computation.11 | loop fusion | flops 2097152 | bytes 3145728 | tf_op jit(solution)/shard_map/convert_element_type | solution.py:233
  100.4 1.1 slice_bitcast_fusion.5
  102.0 1.5 %collective-permute-start.10 = (bf16[1024,256]{1,0:T(8,128)(2,1)}, bf16[1024,256]{1,0:T(8,128)(2,1)}, u32[]{:S(2)}, u32[]{:S(2)}) collective-permute-start(bf16[1024,256]{1,0:T(8,128)(2,1)} %get-tuple-element.74), channel_id=1, source_target_pairs={{0,2},{1,3},{2,0},{3,1},{4,6},{5,7},{6,4},{7,5},{8,10},{9,11},{10,... | collective-permute-start | bytes 1572872 | tf_op jit(solution)/shard_map/ppermute | solution.py:244
  103.5 1.1 broadcast_in_dim.7
  104.5 2.5 %copy.34 = f32[4,256,256]{2,1,0:T(8,128)} copy(f32[4,256,256]{1,2,0:T(8,128)} %bitcast.53) | data formatting | bytes 2097152 | tf_op jit(solution)/shard_map/reshape | solution.py:329
  108.2 1.5 %multiply_reduce_fusion = f32[256,256]{1,0:T(8,128)S(1)} fusion(f32[4,256,256]{2,1,0:T(8,128)S(1)} %maximum_convert_fusion, f32[4,256,256]{2,1,0:T(8,128)} %copy.34), kind=kLoop, calls=%fused_computation.14 | loop fusion | flops 458752 | bytes 2359296 | tf_op jit(solution)/shard_map/reduce_sum | solution.py:329
  110.1 1.3 collective-permute-start.15
  111.5 2.1 %fusion = bf16[1024,256]{1,0:T(8,128)(2,1)} fusion(bf16[1024,256]{1,0:T(8,128)(2,1)} %collective-permute-done.12, bf16[4,1024,256]{2,1,0:T(8,128)(2,1)} %shard_map.124), kind=kLoop, calls=%fused_computation.7 | loop fusion | flops 1048576 | bytes 1572864 | tf_op jit(solution)/shard_map/convert_element_type | solution.py:233
  113.6 5.2 %collective-permute-done.16 = bf16[256,256]{1,0:T(8,128)(2,1)S(1)} collective-permute-done((bf16[256,256]{1,0:T(8,128)(2,1)S(1)}, bf16[256,256]{1,0:T(8,128)(2,1)S(1)}, u32[]{:S(2)}, u32[]{:S(2)}) %collective-permute-start.16) | collective-permute-done | bytes 131104 | tf_op jit(solution)/shard_map/ppermute | solution.py:200
  119.3 2.4 %collective-permute-done.15 = bf16[256,256]{1,0:T(8,128)(2,1)} collective-permute-done((bf16[256,256]{1,0:T(8,128)(2,1)S(1)}, bf16[256,256]{1,0:T(8,128)(2,1)}, u32[]{:S(2)}, u32[]{:S(2)}) %collective-permute-start.15) | collective-permute-done | bytes 131104 | tf_op jit(solution)/shard_map/ppermute | solution.py:200
  121.7 1.7 %add_convert_fusion.2 = bf16[256,256]{1,0:T(8,128)(2,1)} fusion(bf16[256,256]{1,0:T(8,128)(2,1)S(1)} %collective-permute-done.16, bf16[256,256]{1,0:T(8,128)(2,1)} %collective-permute-done.15, bf16[256,256]{1,0:T(8,128)(2,1)} %collective-permute-done.14, bf16[256,1024]{1,0:T(8,128)(2,1)S(1)} %convolution_convert_fusion.3, s32[]{:T(128)S(6)} %select_n.102), kind=kLoop, calls=%fused_computation.28 | loop fusion | flops 524288 | bytes 655364 | tf_op jit(solution)/shard_map/convert_element_type | solution.py:201
  123.4 1.2 add_convert_fusion.1
  124.6 9.0 %collective-permute-done.13 = bf16[1024,256]{1,0:T(8,128)(2,1)} collective-permute-done((bf16[1024,256]{1,0:T(8,128)(2,1)}, bf16[1024,256]{1,0:T(8,128)(2,1)}, u32[]{:S(2)}, u32[]{:S(2)}) %collective-permute-start.13) | collective-permute-done | bytes 524320 | tf_op jit(solution)/shard_map/ppermute | solution.py:244
  133.6 1.5 %add_convert_fusion = bf16[1024,256]{1,0:T(8,128)(2,1)S(1)} fusion(bf16[1024,256]{1,0:T(8,128)(2,1)} %collective-permute-done.13, bf16[1024,256]{1,0:T(8,128)(2,1)} %collective-permute-done.11, bf16[4,1024,256]{2,1,0:T(8,128)(2,1)} %shard_map.124), kind=kLoop, calls=%fused_computation.15 | loop fusion | flops 2097152 | bytes 2097152 | tf_op jit(solution)/shard_map/convert_element_type | solution.py:245
  (84 shorter events, 10.8 us)
Async XLA Ops:
  0.6 19.1 %copy-start = (bf16[1024,1024]{1,0:T(8,128)(2,1)S(1)}, bf16[1024,1024]{1,0:T(8,128)(2,1)}, u32[]{:S(2)}) copy-start(bf16[1024,1024]{1,0:T(8,128)(2,1)} %param.20) | copy-start | bytes 6291460
  0.6 3.8 %copy-start.13 = (bf16[2048,1024]{1,0:T(8,128)(2,1)S(1)}, bf16[2048,1024]{1,0:T(8,128)(2,1)}, u32[]{:S(2)}) copy-start(bf16[2048,1024]{1,0:T(8,128)(2,1)} %param.19) | copy-start | bytes 12582916
  0.7 3.9 %copy-start.14 = (bf16[1024,256]{1,0:T(8,128)(2,1)S(1)}, bf16[1024,256]{1,0:T(8,128)(2,1)}, u32[]{:S(2)}) copy-start(bf16[1024,256]{1,0:T(8,128)(2,1)} %param.24) | copy-start | bytes 1572868
  4.5 1.3 copy-start.2
  5.8 1.0 copy-start.3
  5.8 9.4 %copy-start.15 = (bf16[1024,256]{1,0:T(8,128)(2,1)S(1)}, bf16[1024,256]{1,0:T(8,128)(2,1)}, u32[]{:S(2)}) copy-start(bf16[1024,256]{1,0:T(8,128)(2,1)} %param.22) | copy-start | bytes 1572868
  7.6 35.1 %collective-permute-start = (bf16[256,512]{1,0:T(8,128)(2,1)}, bf16[256,512]{1,0:T(8,128)(2,1)S(1)}, u32[]{:S(2)}, u32[]{:S(2)}) collective-permute-start(bf16[256,512]{1,0:T(8,128)(2,1)} %pad_maximum_fusion.2), channel_id=1, source_target_pairs={{0,4},{4,8},{8,12},{1,5},{5,9},{9,13},{2,6},{6,10},{10,14},{3,7},{... | collective-permute-start | bytes 786440 | tf_op jit(solution)/shard_map/ppermute | solution.py:21
  13.2 29.4 %collective-permute-start.1 = (bf16[256,512]{1,0:T(8,128)(2,1)}, bf16[256,512]{1,0:T(8,128)(2,1)}, u32[]{:S(2)}, u32[]{:S(2)}) collective-permute-start(bf16[256,512]{1,0:T(8,128)(2,1)} %pad_maximum_fusion.3), channel_id=1, source_target_pairs={{4,0},{8,4},{12,8},{5,1},{9,5},{13,9},{6,2},{10,6},{14,10},{7,3},{... | collective-permute-start | bytes 786440 | tf_op jit(solution)/shard_map/ppermute | solution.py:21
  15.2 4.5 %copy-start.16 = (bf16[1024,256]{1,0:T(8,128)(2,1)S(1)}, bf16[1024,256]{1,0:T(8,128)(2,1)}, u32[]{:S(2)}) copy-start(bf16[1024,256]{1,0:T(8,128)(2,1)} %param.26) | copy-start | bytes 1572868
  21.2 17.9 %copy-start.8 = (bf16[256,1024]{1,0:T(8,128)(2,1)S(1)}, bf16[256,1024]{1,0:T(8,128)(2,1)}, u32[]{:S(2)}) copy-start(bf16[256,1024]{1,0:T(8,128)(2,1)} %param.25) | copy-start | bytes 1572868
  39.2 2.3 %copy-start.17 = (s32[3]{0:T(128)S(1)}, s32[3]{0:T(128)}, u32[]{:S(2)}) copy-start(s32[3]{0:T(128)} %constant.169.clone) | copy-start | bytes 40
  40.2 2.5 %copy-start.12 = (s32[3]{0:T(128)}, s32[3]{0:T(128)S(1)}, u32[]{:S(2)}) copy-start(s32[3]{0:T(128)S(1)} %constant_dynamic-update-slice_fusion.2.scal_ref) | copy-start | bytes 40
  41.5 14.5 %copy-start.11 = (s32[3]{0:T(128)}, s32[3]{0:T(128)S(1)}, u32[]{:S(2)}) copy-start(s32[3]{0:T(128)S(1)} %constant_dynamic-update-slice_fusion.1.scal_ref) | copy-start | bytes 40
  58.3 39.3 %collective-permute-start.3 = (bf16[1024,256]{1,0:T(8,128)(2,1)}, bf16[1024,256]{1,0:T(8,128)(2,1)}, u32[]{:S(2)}, u32[]{:S(2)}) collective-permute-start(bf16[1024,256]{1,0:T(8,128)(2,1)} %get-tuple-element.82), channel_id=1, source_target_pairs={{0,1},{1,0},{2,3},{3,2},{4,5},{5,4},{6,7},{7,6},{8,9},{9,8},{10,11... | collective-permute-start | bytes 1572872 | tf_op jit(solution)/shard_map/ppermute | solution.py:232
  58.3 39.3 %collective-permute-start.2 = (bf16[1024,256]{1,0:T(8,128)(2,1)}, bf16[1024,256]{1,0:T(8,128)(2,1)}, u32[]{:S(2)}, u32[]{:S(2)}) collective-permute-start(bf16[1024,256]{1,0:T(8,128)(2,1)} %get-tuple-element.83), channel_id=1, source_target_pairs={{0,1},{1,0},{2,3},{3,2},{4,5},{5,4},{6,7},{7,6},{8,9},{9,8},{10,11... | collective-permute-start | bytes 1572872 | tf_op jit(solution)/shard_map/ppermute | solution.py:232
  58.8 9.3 %collective-permute-start.9 = (f32[8,256]{0,1:T(8,128)S(1)}, f32[8,256]{0,1:T(8,128)S(1)}, u32[]{:S(2)}, u32[]{:S(2)}) collective-permute-start(f32[8,256]{0,1:T(8,128)S(1)} %get-tuple-element.92), channel_id=1, source_target_pairs={{0,12},{4,0},{8,4},{12,8},{1,13},{5,1},{9,5},{13,9},{2,14},{6,2},{... | collective-permute-start | bytes 24584 | tf_op jit(solution)/shard_map/ppermute | solution.py:269
  64.2 12.3 %collective-permute-start.8 = (f32[8,256]{0,1:T(8,128)S(1)}, f32[8,256]{0,1:T(8,128)S(1)}, u32[]{:S(2)}, u32[]{:S(2)}) collective-permute-start(f32[8,256]{0,1:T(8,128)S(1)} %get-tuple-element.93), channel_id=1, source_target_pairs={{0,8},{4,12},{8,0},{12,4},{1,9},{5,13},{9,1},{13,5},{2,10},{6,14},... | collective-permute-start | bytes 24584 | tf_op jit(solution)/shard_map/ppermute | solution.py:269
  64.2 12.3 %collective-permute-start.7 = (f32[8,256]{0,1:T(8,128)S(1)}, f32[8,256]{0,1:T(8,128)S(1)}, u32[]{:S(2)}, u32[]{:S(2)}) collective-permute-start(f32[8,256]{0,1:T(8,128)S(1)} %get-tuple-element.94), channel_id=1, source_target_pairs={{0,4},{4,8},{8,12},{12,0},{1,5},{5,9},{9,13},{13,1},{2,6},{6,10},{... | collective-permute-start | bytes 24584 | tf_op jit(solution)/shard_map/ppermute | solution.py:269
  68.1 27.5 %collective-permute-start.6 = (bf16[256,256]{1,0:T(8,128)(2,1)}, bf16[256,256]{1,0:T(8,128)(2,1)S(1)}, u32[]{:S(2)}, u32[]{:S(2)}) collective-permute-start(bf16[256,256]{1,0:T(8,128)(2,1)} %get-tuple-element.96), channel_id=1, source_target_pairs={{0,12},{4,0},{8,4},{12,8},{1,13},{5,1},{9,5},{13,9},{2,14},{6,2},{... | collective-permute-start | bytes 393224 | tf_op jit(solution)/shard_map/ppermute | solution.py:266
  76.4 19.2 %collective-permute-start.5 = (bf16[256,256]{1,0:T(8,128)(2,1)}, bf16[256,256]{1,0:T(8,128)(2,1)S(1)}, u32[]{:S(2)}, u32[]{:S(2)}) collective-permute-start(bf16[256,256]{1,0:T(8,128)(2,1)} %get-tuple-element.97), channel_id=1, source_target_pairs={{0,8},{4,12},{8,0},{12,4},{1,9},{5,13},{9,1},{13,5},{2,10},{6,14},... | collective-permute-start | bytes 393224 | tf_op jit(solution)/shard_map/ppermute | solution.py:266
  76.4 19.2 %collective-permute-start.4 = (bf16[256,256]{1,0:T(8,128)(2,1)S(1)}, bf16[256,256]{1,0:T(8,128)(2,1)S(1)}, u32[]{:S(2)}, u32[]{:S(2)}) collective-permute-start(bf16[256,256]{1,0:T(8,128)(2,1)S(1)} %get-tuple-element.98), channel_id=1, source_target_pairs={{0,4},{4,8},{8,12},{12,0},{1,5},{5,9},{9,13},{13,1},{2,6},{6,10},{... | collective-permute-start | bytes 393224 | tf_op jit(solution)/shard_map/ppermute | solution.py:266
  96.3 4.1 %copy-start.1 = (bf16[4,1024,256]{2,1,0:T(8,128)(2,1)S(1)}, bf16[4,1024,256]{2,1,0:T(8,128)(2,1)}, u32[]{:S(2)}) copy-start(bf16[4,1024,256]{2,1,0:T(8,128)(2,1)} %shard_map.124) | copy-start | bytes 6291460
  101.4 10.0 %collective-permute-start.12 = (bf16[1024,256]{1,0:T(8,128)(2,1)}, bf16[1024,256]{1,0:T(8,128)(2,1)}, u32[]{:S(2)}, u32[]{:S(2)}) collective-permute-start(bf16[1024,256]{1,0:T(8,128)(2,1)} %get-tuple-element.79), channel_id=1, source_target_pairs={{0,1},{1,0},{2,3},{3,2},{4,5},{5,4},{6,7},{7,6},{8,9},{9,8},{10,11... | collective-permute-start | bytes 1572872 | tf_op jit(solution)/shard_map/ppermute | solution.py:232
  101.5 23.2 %collective-permute-start.11 = (bf16[1024,256]{1,0:T(8,128)(2,1)}, bf16[1024,256]{1,0:T(8,128)(2,1)}, u32[]{:S(2)}, u32[]{:S(2)}) collective-permute-start(bf16[1024,256]{1,0:T(8,128)(2,1)} %get-tuple-element.78), channel_id=1, source_target_pairs={{0,1},{1,0},{2,3},{3,2},{4,5},{5,4},{6,7},{7,6},{8,9},{9,8},{10,11... | collective-permute-start | bytes 1572872 | tf_op jit(solution)/shard_map/ppermute | solution.py:232
  102.0 21.5 %collective-permute-start.10 = (bf16[1024,256]{1,0:T(8,128)(2,1)}, bf16[1024,256]{1,0:T(8,128)(2,1)}, u32[]{:S(2)}, u32[]{:S(2)}) collective-permute-start(bf16[1024,256]{1,0:T(8,128)(2,1)} %get-tuple-element.74), channel_id=1, source_target_pairs={{0,2},{1,3},{2,0},{3,1},{4,6},{5,7},{6,4},{7,5},{8,10},{9,11},{10,... | collective-permute-start | bytes 1572872 | tf_op jit(solution)/shard_map/ppermute | solution.py:244
  108.2 1.5 %copy-start.6 = (f32[256,256]{1,0:T(8,128)S(1)}, f32[256,256]{1,0:T(8,128)}, u32[]{:S(2)}) copy-start(f32[256,256]{1,0:T(8,128)} %copy.37) | copy-start | bytes 786436
  108.2 1.5 %copy-start.7 = (bf16[256,1024]{1,0:T(8,128)(2,1)S(1)}, bf16[256,1024]{1,0:T(8,128)(2,1)}, u32[]{:S(2)}) copy-start(bf16[256,1024]{1,0:T(8,128)(2,1)} %param.27) | copy-start | bytes 1572868
  109.7 13.8 %copy-start.4 = (bf16[1024,256]{1,0:T(8,128)(2,1)S(1)}, bf16[1024,256]{1,0:T(8,128)(2,1)}, u32[]{:S(2)}) copy-start(bf16[1024,256]{1,0:T(8,128)(2,1)} %get-tuple-element.73) | copy-start | bytes 1572868
  110.1 8.7 %collective-permute-start.16 = (bf16[256,256]{1,0:T(8,128)(2,1)S(1)}, bf16[256,256]{1,0:T(8,128)(2,1)S(1)}, u32[]{:S(2)}, u32[]{:S(2)}) collective-permute-start(bf16[256,256]{1,0:T(8,128)(2,1)S(1)} %get-tuple-element.89), channel_id=1, source_target_pairs={{0,3},{1,0},{2,1},{3,2},{4,7},{5,4},{6,5},{7,6},{8,11},{9,8},{10,9... | collective-permute-start | bytes 393224 | tf_op jit(solution)/shard_map/ppermute | solution.py:200
  110.1 11.6 %collective-permute-start.15 = (bf16[256,256]{1,0:T(8,128)(2,1)S(1)}, bf16[256,256]{1,0:T(8,128)(2,1)}, u32[]{:S(2)}, u32[]{:S(2)}) collective-permute-start(bf16[256,256]{1,0:T(8,128)(2,1)S(1)} %get-tuple-element.90), channel_id=1, source_target_pairs={{0,2},{1,3},{2,0},{3,1},{4,6},{5,7},{6,4},{7,5},{8,10},{9,11},{10,... | collective-permute-start | bytes 393224 | tf_op jit(solution)/shard_map/ppermute | solution.py:200
  111.5 10.3 %collective-permute-start.14 = (bf16[256,256]{1,0:T(8,128)(2,1)S(1)}, bf16[256,256]{1,0:T(8,128)(2,1)}, u32[]{:S(2)}, u32[]{:S(2)}) collective-permute-start(bf16[256,256]{1,0:T(8,128)(2,1)S(1)} %get-tuple-element.88), channel_id=1, source_target_pairs={{0,1},{1,2},{2,3},{3,0},{4,5},{5,6},{6,7},{7,4},{8,9},{9,10},{10,1... | collective-permute-start | bytes 393224 | tf_op jit(solution)/shard_map/ppermute | solution.py:200
  118.8 14.9 %collective-permute-start.13 = (bf16[1024,256]{1,0:T(8,128)(2,1)}, bf16[1024,256]{1,0:T(8,128)(2,1)}, u32[]{:S(2)}, u32[]{:S(2)}) collective-permute-start(bf16[1024,256]{1,0:T(8,128)(2,1)} %fusion), channel_id=1, source_target_pairs={{0,2},{1,3},{2,0},{3,1},{4,6},{5,7},{6,4},{7,5},{8,10},{9,11},{10,... | collective-permute-start | bytes 1572872 | tf_op jit(solution)/shard_map/ppermute | solution.py:244
  (3 other events, 2.0 us)

commit v8 on v6

--- a/solution.py
+++ b/solution.py
@@ -226,11 +226,11 @@
     count = lax.axis_size(axis)
     chips = count // 2
     swap = [(i, i ^ 1) for i in range(count)]
+    received = lax.ppermute(blocks[:chips], axis, swap)
     return [
-        (
-            blocks[chips + d].astype(jnp.float32)
-            + lax.ppermute(blocks[d], axis, swap).astype(jnp.float32)
-        ).astype(jnp.bfloat16)
+        (blocks[chips + d].astype(jnp.float32) + received[d].astype(jnp.float32)).astype(
+            jnp.bfloat16
+        )
         for d in range(chips)
     ]
 
@@ -254,20 +254,48 @@
     return total.astype(jnp.bfloat16)
 
 
+def split_three(values):
+    hi = values.astype(jnp.bfloat16)
+    rest = values - hi.astype(jnp.float32)
+    mid = rest.astype(jnp.bfloat16)
+    lo = (rest - mid.astype(jnp.float32)).astype(jnp.bfloat16)
+    return [hi, mid, lo]
+
+
 def exchange_rows(accum, stats, axis, rows):
     count = lax.axis_size(axis)
     place = lax.axis_index(axis)
-    accs = [lax.dynamic_slice_in_dim(accum, place * rows, rows, 0)]
-    stat_parts = [lax.dynamic_slice_in_dim(stats, place * rows, rows, 1)]
+    width = accum.shape[1]
+    packed = (stats.shape[0] * rows) % width == 0
+
+    def payload(target):
+        acc = lax.dynamic_slice_in_dim(accum, target * rows, rows, 0)
+        stat = lax.dynamic_slice_in_dim(stats, target * rows, rows, 1)
+        if not packed:
+            return acc, stat
+        return jnp.concatenate([acc] + split_three(stat.reshape(-1, width)), axis=0), None
+
+    def unpack(block, stat):
+        if not packed:
+            return block[:rows], stat
+        k = (block.shape[0] - rows) // 3
+        pieces = [block[rows + i * k : rows + (i + 1) * k].astype(jnp.float32) for i in range(3)]
+        return block[:rows], (pieces[0] + pieces[1] + pieces[2]).reshape(stats.shape[0], rows)
+
+    accs, stat_parts = [], []
+    own, own_stat = payload(place)
+    a, b = unpack(own, own_stat)
+    accs.append(a)
+    stat_parts.append(b)
     for shift in range(1, count):
-        target = (place + shift) % count
         pairs = [(i, (i + shift) % count) for i in range(count)]
-        accs.append(
-            lax.ppermute(lax.dynamic_slice_in_dim(accum, target * rows, rows, 0), axis, pairs)
-        )
-        stat_parts.append(
-            lax.ppermute(lax.dynamic_slice_in_dim(stats, target * rows, rows, 1), axis, pairs)
-        )
+        block, stat = payload((place + shift) % count)
+        block = lax.ppermute(block, axis, pairs)
+        if stat is not None:
+            stat = lax.ppermute(stat, axis, pairs)
+        a, b = unpack(block, stat)
+        accs.append(a)
+        stat_parts.append(b)
     return jnp.stack(accs).astype(jnp.float32), jnp.stack(stat_parts)
 
 
@@ -327,8 +355,18 @@
     factor_rows = jnp.transpose(factor, (0, 2, 1))
     own_accum = jnp.sum(part_accum * jnp.repeat(factor_rows, HD, axis=2), axis=0)
     summary = (own_accum / jnp.repeat(own_total, HD, axis=1)).astype(jnp.bfloat16)
-    latent_terms = jnp.dot(summary, w_latent_out, preferred_element_type=jnp.float32)
-    latents_out = column_sum(latent_terms.astype(jnp.bfloat16), "head")
+    if paired:
+        latent_terms = jnp.dot(
+            summary, ordered_columns(w_latent_out, "head"), preferred_element_type=jnp.float32
+        ).astype(jnp.bfloat16)
+        block_width = latent_terms.shape[1] // head_devices
+        latent_blocks = jnp.stack(
+            [latent_terms[:, j * block_width : (j + 1) * block_width] for j in range(head_devices)]
+        )
+        latents_out = cross_chip_sum(chip_pair_sums(latent_blocks, "head"), "head")
+    else:
+        latent_terms = jnp.dot(summary, w_latent_out, preferred_element_type=jnp.float32)
+        latents_out = column_sum(latent_terms.astype(jnp.bfloat16), "head")
     return (frames_out, latents_out)
 
 

time: 127 us -> 124 us (0.976)
  waiting for transfers between devices: 19.7 us -> 6.23 us
  local copies, waits for them, and re-layouts: 15.4 us -> 23.5 us
  other arithmetic: 14.4 us -> 20 us
  starting transfers between devices: 21.8 us -> 16.3 us
  matrix products: 10.1 us -> 12.6 us
    ppermute x13 -> x6, waiting for transfers between devices: 15.3 us -> 2.36 us  [the longest x3 2.02 us: exchange_rows(): block = lax.ppermute(block, axis, pairs)]
    slice x0 -> x8, local copies, waits for them, and re-layouts: none -> 10.2 us  [the longest x6 6.82 us: unpack(): block[:rows]]
    ppermute x13 -> x6, starting transfers between devices: 13.1 us -> 6.12 us  [the longest x3 5.53 us: exchange_rows(): block = lax.ppermute(block, axis, pairs)]
    ppermute x1, waiting for transfers between devices: 4.44 us -> 0.01 us  [halos(): lax.ppermute(head, axis, backward)]
    ppermute x2 -> x3, waiting for transfers between devices: 0.01 us -> 3.86 us  [cross_chip_sum(): total = total + lax.ppermute(chip_sums[d], axis, pairs).astype(jnp.float32)]
    concatenate x0 -> x3, other arithmetic: none -> 3.84 us  [payload(): jnp.concatenate([acc] + split_three(stat.reshape(-1, width)), axis=0)]
    squeeze x2 -> x0, local copies, waits for them, and re-layouts: 3.16 us -> none  [chip_pair_sums(): blocks[d]]
    ppermute x3 -> x0, local copies, waits for them, and re-layouts: 2.76 us -> none  [exchange_rows(): lax.ppermute(lax.dynamic_slice_in_dim(accum, target * rows, rows, 0), axi...]
  transfers between devices with their start and end apart: 17 -> 11, of which waited for: 6 -> 3; matrix products, arithmetic and copies ran while one was open for 20% -> 33% of each run, Pallas kernels for 24% -> 25%
where the time goes in v8:
time: 124 us; the launch traced here: 123 us
  Pallas kernels  43.2 us (35%)
  local copies, waits for them, and re-layouts  23.5 us (19%)
  other arithmetic  20 us (16%)
  starting transfers between devices  16.3 us (13%)
  matrix products  12.6 us (10%)
  waiting for transfers between devices  6.23 us (5%)
  between operations  1.63 us (1%)
    pallas_call x2, Pallas kernels, window_attention(): pl.pallas_call(kernel, cost_estimate=cost, out_shape=jax.ShapeDtypeStruct...  25.4 us
    pallas_call x1, Pallas kernels, latent_attention(): pl.pallas_call(kernel, cost_estimate=cost, out_shape=(jax.ShapeDtypeStruc...  17.9 us
    dot_general x4, matrix products, project(): jnp.dot(source, weight, preferred_element_type=jnp.float32)  11.1 us
    slice x6, local copies, waits for them, and re-layouts, unpack(): block[:rows]  6.82 us
    ppermute x1, starting transfers between devices, halos(): lax.ppermute(tail, axis, forward)  5.74 us
    ppermute x3, starting transfers between devices, exchange_rows(): block = lax.ppermute(block, axis, pairs)  5.53 us
    convert_element_type x3, other arithmetic, chip_pair_sums(): (blocks[chips + d].astype(jnp.float32) + received[d].astype(jnp.float32))...  5.29 us
    ppermute x3, waiting for transfers between devices, cross_chip_sum(): total = total + lax.ppermute(chip_sums[d], axis, pairs).astype(jnp.float32)  3.86 us
  transfers between devices with their start and end apart: 11, of which 3 were waited for; matrix products, arithmetic and copies ran while one was open for 33% of the time, Pallas kernels for 25%

profile of v8, /device:TPU:0, one launch (start us, length us, event | category | flops | bytes accessed | tf_op | source)
XLA Modules:
  0.0 123.4 jit_solution(13968326079599996492)
XLA Ops:
  0.7 3.7 %convolution_convert_fusion.v_ref = bf16[2048,256]{1,0:T(8,128)(2,1)S(1)} fusion(bf16[2048,1024]{1,0:T(8,128)(2,1)} %param.19, bf16[1024,256]{1,0:T(8,128)(2,1)} %param.24), kind=kOutput, calls=%fused_computation | convolution fusion | flops 1074266112 | bytes 5767168 | tf_op jit(solution)/shard_map/dot_general | solution.py:25
  4.5 1.3 %convolution_convert_fusion.1.k_ref = bf16[2048,256]{1,0:T(8,128)(2,1)S(1)} fusion(bf16[2048,1024]{1,0:T(8,128)(2,1)S(1)} %copy-done.12, bf16[1024,256]{1,0:T(8,128)(2,1)S(1)} %copy-done.13), kind=kOutput, calls=%fused_computation.1 | convolution fusion | flops 1074266112 | bytes 5767168 | tf_op jit(solution)/shard_map/dot_general | solution.py:25
  6.9 1.3 %collective-permute-start.1 = (bf16[256,512]{1,0:T(8,128)(2,1)S(1)}, bf16[256,512]{1,0:T(8,128)(2,1)S(1)}, u32[]{:S(2)}, u32[]{:S(2)}) collective-permute-start(bf16[256,512]{1,0:T(8,128)(2,1)S(1)} %pad_maximum_fusion.3), channel_id=1, source_target_pairs={{4,0},{8,4},{12,8},{5,1},{9,5},{13,9},{6,2},{10,6},{14,10},{7,3},{... | collective-permute-start | bytes 786440 | tf_op jit(solution)/shard_map/ppermute | solution.py:21
  8.9 5.7 %collective-permute-start = (bf16[256,512]{1,0:T(8,128)(2,1)}, bf16[256,512]{1,0:T(8,128)(2,1)S(1)}, u32[]{:S(2)}, u32[]{:S(2)}) collective-permute-start(bf16[256,512]{1,0:T(8,128)(2,1)} %pad_maximum_fusion.2), channel_id=1, source_target_pairs={{0,4},{4,8},{8,12},{1,5},{5,9},{9,13},{2,6},{6,10},{10,14},{3,7},{... | collective-permute-start | bytes 786440 | tf_op jit(solution)/shard_map/ppermute | solution.py:21
  15.3 4.6 %convolution_convert_fusion.2.q_ref = bf16[2048,256]{1,0:T(8,128)(2,1)} fusion(bf16[2048,1024]{1,0:T(8,128)(2,1)} %param.19, bf16[1024,256]{1,0:T(8,128)(2,1)} %param.22), kind=kOutput, calls=%fused_computation.2 | convolution fusion | flops 1074266112 | bytes 5767168 | tf_op jit(solution)/shard_map/dot_general | solution.py:25
  20.0 1.9 %constant_dynamic-slice_fusion.2 = (bf16[256,256]{1,0:T(8,128)(2,1)}, bf16[256,256]{1,0:T(8,128)(2,1)}, bf16[256,256]{1,0:T(8,128)(2,1)}, bf16[256,256]{1,0:T(8,...) fusion(bf16[256,1024]{1,0:T(8,128)(2,1)S(1)} %copy-done.8, ...), kind=kLoop, calls=%fused_computation.69 | loop fusion | bytes 2097168 | tf_op jit(solution)/shard_map/dynamic_slice | solution.py:221
  24.3 12.6 %shard_map.122 = bf16[4,1024,256]{2,1,0:T(8,128)(2,1)} custom-call(s32[3]{0:T(128)} %copy-done.10, bf16[2048,256]{1,0:T(8,128)(2,1)} %convolution_convert_fusion.2.q_ref, bf16[2048,256]{1,0:T(8,128)(2,1)} %copy-done.4, bf16[2048,256]{1,0:T(8,128)(2,1)} %copy-done.3, bf16[256,512]{1,0:T(8,128)(2,1)} %copy-done.7, bf16[256,512]{1,0:T(8,128)(2,1)} %copy-done.6, ...), custom_call_target="tpu_custom_call" | custom-call | flops 1342177280 | bytes 5767168 | tf_op jit(solution)/shard_map/pallas_call | solution.py:93
  36.9 2.4 %slice.184 = bf16[2,1024,256]{2,1,0:T(8,128)(2,1)} slice(bf16[4,1024,256]{2,1,0:T(8,128)(2,1)} %shard_map.122), slice={[0:2], [0:1024], [0:256]} | slice | bytes 2097152 | tf_op jit(solution)/shard_map/slice | solution.py:229
  39.8 12.7 %shard_map.123 = bf16[4,1024,256]{2,1,0:T(8,128)(2,1)} custom-call(s32[3]{0:T(128)} %copy-done.11, bf16[2048,256]{1,0:T(8,128)(2,1)} %convolution_convert_fusion.2.q_ref, bf16[2048,256]{1,0:T(8,128)(2,1)} %copy-done.4, bf16[2048,256]{1,0:T(8,128)(2,1)} %copy-done.3, bf16[256,512]{1,0:T(8,128)(2,1)} %copy-done.7, bf16[256,512]{1,0:T(8,128)(2,1)} %copy-done.6, ...), custom_call_target="tpu_custom_call" | custom-call | flops 1342177280 | bytes 5767168 | tf_op jit(solution)/shard_map/pallas_call | solution.py:93
  52.6 2.7 %fusion.1 = (bf16[1024,256]{1,0:T(8,128)(2,1)}, bf16[1024,256]{1,0:T(8,128)(2,1)S(1)}) fusion(bf16[2,1024,256]{2,1,0:T(8,128)(2,1)} %collective-permute-done.2, bf16[4,1024,256]{2,1,0:T(8,128)(2,1)} %shard_map.122), kind=kLoop, calls=%fused_computation.14 | loop fusion | flops 2097152 | bytes 3145728 | tf_op jit(solution)/shard_map/convert_element_type | solution.py:231
  55.3 1.0 slice.155
  56.9 1.5 %convolution_convert_fusion.4.q_ref = bf16[1024,256]{1,0:T(8,128)(2,1)} fusion(bf16[1024,1024]{1,0:T(8,128)(2,1)S(1)} %copy-done, bf16[1024,256]{1,0:T(8,128)(2,1)S(1)} %copy-done.14), kind=kOutput, calls=%fused_computation.4 | convolution fusion | flops 537133056 | bytes 3145728 | tf_op jit(solution)/shard_map/dot_general | solution.py:25
  58.4 17.9 %shard_map.124 = (f32[1024,256]{1,0:T(8,128)}, f32[1024,128]{1,0:T(8,128)}) custom-call(s32[1]{0:T(128)} %bitcast.6.scal_ref, bf16[1024,256]{1,0:T(8,128)(2,1)} %convolution_convert_fusion.4.q_ref, bf16[2048,256]{1,0:T(8,128)(2,1)} %copy-done.4, bf16[2048,256]{1,0:T(8,128)(2,1)} %copy-done.3), custom_call_target="tpu_custom_call" | custom-call | flops 2147483648 | bytes 4194304 | tf_op jit(solution)/shard_map/pallas_call | solution.py:153
  76.3 1.4 %convert_element_type.250 = bf16[1024,256]{1,0:T(8,128)(2,1)S(1)} convert(f32[1024,256]{1,0:T(8,128)} %get-tuple-element.66) | non-fusion elementwise | flops 262144 | bytes 1572864 | tf_op jit(solution)/shard_map/convert_element_type | solution.py:343
  77.7 2.0 %collective-permute-start.3 = (bf16[1024,256]{1,0:T(8,128)(2,1)}, bf16[1024,256]{1,0:T(8,128)(2,1)}, u32[]{:S(2)}, u32[]{:S(2)}) collective-permute-start(bf16[1024,256]{1,0:T(8,128)(2,1)} %get-tuple-element.62), channel_id=1, source_target_pairs={{0,2},{1,3},{2,0},{3,1},{4,6},{5,7},{6,4},{7,5},{8,10},{9,11},{10,... | collective-permute-start | bytes 1572872 | tf_op jit(solution)/shard_map/ppermute | solution.py:244
  79.7 1.1 slice_bitcast_fusion
  80.8 2.5 %fusion.3 = (bf16[1024,256]{1,0:T(8,128)(2,1)}, bf16[1024,256]{1,0:T(8,128)(2,1)}) fusion(bf16[2,1024,256]{2,1,0:T(8,128)(2,1)} %collective-permute-done.4, bf16[4,1024,256]{2,1,0:T(8,128)(2,1)S(1)} %copy-done.2), kind=kLoop, calls=%fused_computation.16 | loop fusion | flops 2097152 | bytes 3145728 | tf_op jit(solution)/shard_map/convert_element_type | solution.py:231
  86.5 1.6 %collective-permute-start.6 = (bf16[280,256]{1,0:T(8,128)(2,1)}, bf16[280,256]{1,0:T(8,128)(2,1)}, u32[]{:S(2)}, u32[]{:S(2)}) collective-permute-start(bf16[280,256]{1,0:T(8,128)(2,1)} %pad_maximum_fusion.5), channel_id=1, source_target_pairs={{0,4},{4,8},{8,12},{12,0},{1,5},{5,9},{9,13},{13,1},{2,6},{6,10},{... | collective-permute-start | bytes 430088 | tf_op jit(solution)/shard_map/ppermute | solution.py:293
  89.9 1.6 %pad_maximum_fusion.6 = bf16[280,256]{1,0:T(8,128)(2,1)} fusion(bf16[8,256]{1,0:T(8,128)(2,1)S(1)} %get-tuple-element.76, bf16[8,256]{1,0:T(8,128)(2,1)S(1)} %get-tuple-element.77, bf16[8,256]{1,0:T(8,128)(2,1)S(1)} %copy.63, bf16[256,256]{1,0:T(8,128)(2,1)} %get-tuple-element.101), kind=kLoop, calls=%fused_computation.39 | loop fusion | flops 573440 | bytes 286720 | tf_op jit(solution)/shard_map/concatenate | solution.py:276
  91.5 1.0 collective-permute-start.7
  93.5 1.6 %pad_maximum_fusion.7 = bf16[280,256]{1,0:T(8,128)(2,1)} fusion(bf16[8,256]{1,0:T(8,128)(2,1)S(1)} %get-tuple-element.80, bf16[8,256]{1,0:T(8,128)(2,1)S(1)} %get-tuple-element.81, bf16[8,256]{1,0:T(8,128)(2,1)S(1)} %copy.67, bf16[256,256]{1,0:T(8,128)(2,1)} %get-tuple-element.100), kind=kLoop, calls=%fused_computation.40 | loop fusion | flops 573440 | bytes 286720 | tf_op jit(solution)/shard_map/concatenate | solution.py:276
  95.1 2.9 %collective-permute-start.8 = (bf16[280,256]{1,0:T(8,128)(2,1)}, bf16[280,256]{1,0:T(8,128)(2,1)S(1)}, u32[]{:S(2)}, u32[]{:S(2)}) collective-permute-start(bf16[280,256]{1,0:T(8,128)(2,1)} %pad_maximum_fusion.7), channel_id=1, source_target_pairs={{0,12},{4,0},{8,4},{12,8},{1,13},{5,1},{9,5},{13,9},{2,14},{6,2},{... | collective-permute-start | bytes 430088 | tf_op jit(solution)/shard_map/ppermute | solution.py:293
  100.1 2.0 %collective-permute-done.7 = bf16[280,256]{1,0:T(8,128)(2,1)} collective-permute-done((bf16[280,256]{1,0:T(8,128)(2,1)}, bf16[280,256]{1,0:T(8,128)(2,1)}, u32[]{:S(2)}, u32[]{:S(2)}) %collective-permute-start.7) | collective-permute-done | bytes 143392 | tf_op jit(solution)/shard_map/ppermute | solution.py:293
  105.2 1.6 %slice.191 = bf16[256,256]{1,0:T(8,128)(2,1)} slice(bf16[280,256]{1,0:T(8,128)(2,1)} %collective-permute-done.7), slice={[0:256], [0:256]} | slice | bytes 262144 | tf_op jit(solution)/shard_map/slice | solution.py:283
  106.8 1.0 copy.64
  107.8 1.6 %slice.192 = bf16[256,256]{1,0:T(8,128)(2,1)} slice(bf16[280,256]{1,0:T(8,128)(2,1)} %copy-done.9), slice={[0:256], [0:256]} | slice | bytes 262144 | tf_op jit(solution)/shard_map/slice | solution.py:283
  109.3 1.7 %copy.68 = bf16[256,256]{0,1:T(8,128)(2,1)} copy(bf16[256,256]{1,0:T(8,128)(2,1)} %slice.192) | data formatting | bytes 262144 | tf_op jit(solution)/shard_map/slice | solution.py:283
  112.8 1.1 multiply_reduce_fusion
  113.9 1.5 %convolution_convert_fusion.3 = bf16[256,1024]{1,0:T(8,128)(2,1)S(1)} fusion(bf16[256,256]{0,1:T(8,128)(2,1)S(1)} %bitcast.58, bf16[256,256]{1,0:T(8,128)(2,1)} %get-tuple-element.96, bf16[256,256]{1,0:T(8,128)(2,1)} %get-tuple-element.97, bf16[256,256]{1,0:T(8,128)(2,1)} %get-tuple-element.95, bf16[256,256]{1,0:T(8,128)(2,1)} %get-tuple-element.94), kind=kOutput, calls=%fused_computation.3 | convolution fusion | flops 136577024 | bytes 1179648 | tf_op jit(solution)/shard_map/dot_general | solution.py:359
  115.5 1.2 add_convert_fusion.3
  117.8 1.0 pad_maximum_fusion
  118.9 3.9 %collective-permute-done.10 = bf16[256,256]{1,0:T(8,128)(2,1)S(1)} collective-permute-done((bf16[256,256]{1,0:T(8,128)(2,1)S(1)}, bf16[256,256]{1,0:T(8,128)(2,1)S(1)}, u32[]{:S(2)}, u32[]{:S(2)}) %collective-permute-start.10) | collective-permute-done | bytes 131104 | tf_op jit(solution)/shard_map/ppermute | solution.py:244
  (85 shorter events, 20.2 us)
Async XLA Ops:
  0.6 56.3 %copy-start = (bf16[1024,1024]{1,0:T(8,128)(2,1)S(1)}, bf16[1024,1024]{1,0:T(8,128)(2,1)}, u32[]{:S(2)}) copy-start(bf16[1024,1024]{1,0:T(8,128)(2,1)} %param.20) | copy-start | bytes 6291460
  0.6 3.8 %copy-start.12 = (bf16[2048,1024]{1,0:T(8,128)(2,1)S(1)}, bf16[2048,1024]{1,0:T(8,128)(2,1)}, u32[]{:S(2)}) copy-start(bf16[2048,1024]{1,0:T(8,128)(2,1)} %param.19) | copy-start | bytes 12582916
  0.7 3.9 %copy-start.13 = (bf16[1024,256]{1,0:T(8,128)(2,1)S(1)}, bf16[1024,256]{1,0:T(8,128)(2,1)}, u32[]{:S(2)}) copy-start(bf16[1024,256]{1,0:T(8,128)(2,1)} %param.23) | copy-start | bytes 1572868
  4.5 1.3 %copy-start.3 = (bf16[2048,256]{1,0:T(8,128)(2,1)}, bf16[2048,256]{1,0:T(8,128)(2,1)S(1)}, u32[]{:S(2)}) copy-start(bf16[2048,256]{1,0:T(8,128)(2,1)S(1)} %convolution_convert_fusion.v_ref) | copy-start | bytes 3145732
  5.8 1.0 copy-start.4
  6.9 16.0 %collective-permute-start.1 = (bf16[256,512]{1,0:T(8,128)(2,1)S(1)}, bf16[256,512]{1,0:T(8,128)(2,1)S(1)}, u32[]{:S(2)}, u32[]{:S(2)}) collective-permute-start(bf16[256,512]{1,0:T(8,128)(2,1)S(1)} %pad_maximum_fusion.3), channel_id=1, source_target_pairs={{4,0},{8,4},{12,8},{5,1},{9,5},{13,9},{6,2},{10,6},{14,10},{7,3},{... | collective-permute-start | bytes 786440 | tf_op jit(solution)/shard_map/ppermute | solution.py:21
  8.9 14.0 %collective-permute-start = (bf16[256,512]{1,0:T(8,128)(2,1)}, bf16[256,512]{1,0:T(8,128)(2,1)S(1)}, u32[]{:S(2)}, u32[]{:S(2)}) collective-permute-start(bf16[256,512]{1,0:T(8,128)(2,1)} %pad_maximum_fusion.2), channel_id=1, source_target_pairs={{0,4},{4,8},{8,12},{1,5},{5,9},{9,13},{2,6},{6,10},{10,14},{3,7},{... | collective-permute-start | bytes 786440 | tf_op jit(solution)/shard_map/ppermute | solution.py:21
  15.3 4.6 %copy-start.8 = (bf16[256,1024]{1,0:T(8,128)(2,1)S(1)}, bf16[256,1024]{1,0:T(8,128)(2,1)}, u32[]{:S(2)}) copy-start(bf16[256,1024]{1,0:T(8,128)(2,1)} %param.27) | copy-start | bytes 1572868
  20.0 2.9 %copy-start.10 = (s32[3]{0:T(128)}, s32[3]{0:T(128)S(1)}, u32[]{:S(2)}) copy-start(s32[3]{0:T(128)S(1)} %constant_dynamic-update-slice_fusion.2.scal_ref) | copy-start | bytes 40
  22.9 0.7 copy-start.6
  23.6 0.7 copy-start.7
  36.9 2.4 %copy-start.15 = (s32[3]{0:T(128)S(1)}, s32[3]{0:T(128)}, u32[]{:S(2)}) copy-start(s32[3]{0:T(128)} %constant.169.clone) | copy-start | bytes 40
  39.3 13.3 %collective-permute-start.2 = (bf16[2,1024,256]{2,1,0:T(8,128)(2,1)}, bf16[2,1024,256]{2,1,0:T(8,128)(2,1)}, u32[]{:S(2)}, u32[]{:S(2)}) collective-permute-start(bf16[2,1024,256]{2,1,0:T(8,128)(2,1)} %slice.184), channel_id=1, source_target_pairs={{0,1},{1,0},{2,3},{3,2},{4,5},{5,4},{6,7},{7,6},{8,9},{9,8},{10,11... | collective-permute-start | bytes 3145736 | tf_op jit(solution)/shard_map/ppermute | solution.py:229
  39.3 0.5 copy-start.11
  52.6 2.8 %copy-start.1 = (bf16[4,1024,256]{2,1,0:T(8,128)(2,1)S(1)}, bf16[4,1024,256]{2,1,0:T(8,128)(2,1)}, u32[]{:S(2)}) copy-start(bf16[4,1024,256]{2,1,0:T(8,128)(2,1)} %shard_map.123) | copy-start | bytes 6291460
  52.6 4.3 %copy-start.14 = (bf16[1024,256]{1,0:T(8,128)(2,1)S(1)}, bf16[1024,256]{1,0:T(8,128)(2,1)}, u32[]{:S(2)}) copy-start(bf16[1024,256]{1,0:T(8,128)(2,1)} %param.26) | copy-start | bytes 1572868
  56.4 24.4 %collective-permute-start.4 = (bf16[2,1024,256]{2,1,0:T(8,128)(2,1)}, bf16[2,1024,256]{2,1,0:T(8,128)(2,1)}, u32[]{:S(2)}, u32[]{:S(2)}) collective-permute-start(bf16[2,1024,256]{2,1,0:T(8,128)(2,1)} %slice.155), channel_id=1, source_target_pairs={{0,1},{1,0},{2,3},{3,2},{4,5},{5,4},{6,7},{7,6},{8,9},{9,8},{10,11... | collective-permute-start | bytes 3145736 | tf_op jit(solution)/shard_map/ppermute | solution.py:229
  76.3 4.5 %copy-start.2 = (bf16[4,1024,256]{2,1,0:T(8,128)(2,1)S(1)}, bf16[4,1024,256]{2,1,0:T(8,128)(2,1)}, u32[]{:S(2)}) copy-start(bf16[4,1024,256]{2,1,0:T(8,128)(2,1)} %shard_map.123) | copy-start | bytes 6291460
  77.7 37.8 %collective-permute-start.3 = (bf16[1024,256]{1,0:T(8,128)(2,1)}, bf16[1024,256]{1,0:T(8,128)(2,1)}, u32[]{:S(2)}, u32[]{:S(2)}) collective-permute-start(bf16[1024,256]{1,0:T(8,128)(2,1)} %get-tuple-element.62), channel_id=1, source_target_pairs={{0,2},{1,3},{2,0},{3,1},{4,6},{5,7},{6,4},{7,5},{8,10},{9,11},{10,... | collective-permute-start | bytes 1572872 | tf_op jit(solution)/shard_map/ppermute | solution.py:244
  86.5 12.9 %collective-permute-start.6 = (bf16[280,256]{1,0:T(8,128)(2,1)}, bf16[280,256]{1,0:T(8,128)(2,1)}, u32[]{:S(2)}, u32[]{:S(2)}) collective-permute-start(bf16[280,256]{1,0:T(8,128)(2,1)} %pad_maximum_fusion.5), channel_id=1, source_target_pairs={{0,4},{4,8},{8,12},{12,0},{1,5},{5,9},{9,13},{13,1},{2,6},{6,10},{... | collective-permute-start | bytes 430088 | tf_op jit(solution)/shard_map/ppermute | solution.py:293
  91.5 10.6 %collective-permute-start.7 = (bf16[280,256]{1,0:T(8,128)(2,1)}, bf16[280,256]{1,0:T(8,128)(2,1)}, u32[]{:S(2)}, u32[]{:S(2)}) collective-permute-start(bf16[280,256]{1,0:T(8,128)(2,1)} %pad_maximum_fusion.6), channel_id=1, source_target_pairs={{0,8},{4,12},{8,0},{12,4},{1,9},{5,13},{9,1},{13,5},{2,10},{6,14},... | collective-permute-start | bytes 430088 | tf_op jit(solution)/shard_map/ppermute | solution.py:293
  95.1 7.7 %collective-permute-start.8 = (bf16[280,256]{1,0:T(8,128)(2,1)}, bf16[280,256]{1,0:T(8,128)(2,1)S(1)}, u32[]{:S(2)}, u32[]{:S(2)}) collective-permute-start(bf16[280,256]{1,0:T(8,128)(2,1)} %pad_maximum_fusion.7), channel_id=1, source_target_pairs={{0,12},{4,0},{8,4},{12,8},{1,13},{5,1},{9,5},{13,9},{2,14},{6,2},{... | collective-permute-start | bytes 430088 | tf_op jit(solution)/shard_map/ppermute | solution.py:293
  98.8 18.9 %collective-permute-start.5 = (bf16[1024,256]{1,0:T(8,128)(2,1)}, bf16[1024,256]{1,0:T(8,128)(2,1)S(1)}, u32[]{:S(2)}, u32[]{:S(2)}) collective-permute-start(bf16[1024,256]{1,0:T(8,128)(2,1)} %get-tuple-element.69), channel_id=1, source_target_pairs={{0,2},{1,3},{2,0},{3,1},{4,6},{5,7},{6,4},{7,5},{8,10},{9,11},{10,... | collective-permute-start | bytes 1572872 | tf_op jit(solution)/shard_map/ppermute | solution.py:244
  102.8 0.8 copy-start.9
  113.9 3.8 %copy-start.5 = (bf16[1024,256]{1,0:T(8,128)(2,1)S(1)}, bf16[1024,256]{1,0:T(8,128)(2,1)}, u32[]{:S(2)}) copy-start(bf16[1024,256]{1,0:T(8,128)(2,1)} %get-tuple-element.68) | copy-start | bytes 1572868
  115.4 1.6 %collective-permute-start.9 = (bf16[2,256,256]{2,1,0:T(8,128)(2,1)S(1)}, bf16[2,256,256]{2,1,0:T(8,128)(2,1)S(1)}, u32[]{:S(2)}, u32[]{:S(2)}) collective-permute-start(bf16[2,256,256]{2,1,0:T(8,128)(2,1)S(1)} %pad_maximum_fusion.4), channel_id=1, source_target_pairs={{0,1},{1,0},{2,3},{3,2},{4,5},{5,4},{6,7},{7,6},{8,9},{9,8},{10,11... | collective-permute-start | bytes 786440 | tf_op jit(solution)/shard_map/ppermute | solution.py:229
  117.1 5.6 %collective-permute-start.10 = (bf16[256,256]{1,0:T(8,128)(2,1)S(1)}, bf16[256,256]{1,0:T(8,128)(2,1)S(1)}, u32[]{:S(2)}, u32[]{:S(2)}) collective-permute-start(bf16[256,256]{1,0:T(8,128)(2,1)S(1)} %fusion.11), channel_id=1, source_target_pairs={{0,2},{1,3},{2,0},{3,1},{4,6},{5,7},{6,4},{7,5},{8,10},{9,11},{10,... | collective-permute-start | bytes 393224 | tf_op jit(solution)/shard_map/ppermute | solution.py:244

commit v9 on v8

--- a/solution.py
+++ b/solution.py
@@ -62,7 +62,7 @@
         ) * scale
         masked = jnp.where(allowed, s, NEG)
         peak = jnp.max(masked, axis=1, keepdims=True)
-        weights = jnp.where(allowed, jnp.exp(masked - peak), 0.0)
+        weights = jnp.exp(masked - peak)
         denom = jnp.sum(weights, axis=1, keepdims=True)
         blended = jnp.dot(weights.astype(jnp.bfloat16), v, preferred_element_type=jnp.float32)
         divisor = jnp.where(query_valid, denom, 1.0)
@@ -129,7 +129,7 @@
         ) * scale
         masked = jnp.where(valid, s, NEG)
         peak = jnp.max(masked, axis=1, keepdims=True)
-        weights = jnp.where(valid, jnp.exp(masked - peak), 0.0)
+        weights = jnp.exp(masked - peak)
         total = jnp.sum(weights, axis=1, keepdims=True)
         acc_ref[:, cols] = jnp.dot(
             weights.astype(jnp.bfloat16), v_ref[:, cols], preferred_element_type=jnp.float32

time: 124 us -> 123 us (level)
  transfers between devices with their start and end apart: 11 -> 11, of which waited for: 3 -> 3; matrix products, arithmetic and copies ran while one was open for 33% -> 34% of each run, Pallas kernels for 25% -> 24%
where the time goes in v9:
time: 123 us; the launch traced here: 122 us
  Pallas kernels  42.1 us (34%)
  local copies, waits for them, and re-layouts  23.5 us (19%)
  other arithmetic  20 us (16%)
  starting transfers between devices  16.3 us (13%)
  matrix products  12.6 us (10%)
  waiting for transfers between devices  6.22 us (5%)
  between operations  1.63 us (1%)
    pallas_call x2, Pallas kernels, window_attention(): pl.pallas_call(kernel, cost_estimate=cost, out_shape=jax.ShapeDtypeStruct...  25.1 us
    pallas_call x1, Pallas kernels, latent_attention(): pl.pallas_call(kernel, cost_estimate=cost, out_shape=(jax.ShapeDtypeStruc...  17 us
    dot_general x4, matrix products, project(): jnp.dot(source, weight, preferred_element_type=jnp.float32)  11.1 us
    slice x6, local copies, waits for them, and re-layouts, unpack(): block[:rows]  6.82 us
    ppermute x1, starting transfers between devices, halos(): lax.ppermute(tail, axis, forward)  5.74 us
    ppermute x3, starting transfers between devices, exchange_rows(): block = lax.ppermute(block, axis, pairs)  5.52 us
    convert_element_type x3, other arithmetic, chip_pair_sums(): (blocks[chips + d].astype(jnp.float32) + received[d].astype(jnp.float32))...  5.29 us
    ppermute x3, waiting for transfers between devices, cross_chip_sum(): total = total + lax.ppermute(chip_sums[d], axis, pairs).astype(jnp.float32)  3.85 us
  transfers between devices with their start and end apart: 11, of which 3 were waited for; matrix products, arithmetic and copies ran while one was open for 34% of the time, Pallas kernels for 24%

profile of v9, /device:TPU:0, one launch (start us, length us, event | category | flops | bytes accessed | tf_op | source)
XLA Modules:
  0.0 122.3 jit_solution(17750042453288305550)
XLA Ops:
  0.7 3.7 %convolution_convert_fusion.v_ref = bf16[2048,256]{1,0:T(8,128)(2,1)S(1)} fusion(bf16[2048,1024]{1,0:T(8,128)(2,1)} %param.19, bf16[1024,256]{1,0:T(8,128)(2,1)} %param.24), kind=kOutput, calls=%fused_computation | convolution fusion | flops 1074266112 | bytes 5767168 | tf_op jit(solution)/shard_map/dot_general | solution.py:25
  4.5 1.3 %convolution_convert_fusion.1.k_ref = bf16[2048,256]{1,0:T(8,128)(2,1)S(1)} fusion(bf16[2048,1024]{1,0:T(8,128)(2,1)S(1)} %copy-done.12, bf16[1024,256]{1,0:T(8,128)(2,1)S(1)} %copy-done.13), kind=kOutput, calls=%fused_computation.1 | convolution fusion | flops 1074266112 | bytes 5767168 | tf_op jit(solution)/shard_map/dot_general | solution.py:25
  6.9 1.3 %collective-permute-start.1 = (bf16[256,512]{1,0:T(8,128)(2,1)S(1)}, bf16[256,512]{1,0:T(8,128)(2,1)S(1)}, u32[]{:S(2)}, u32[]{:S(2)}) collective-permute-start(bf16[256,512]{1,0:T(8,128)(2,1)S(1)} %pad_maximum_fusion.3), channel_id=1, source_target_pairs={{4,0},{8,4},{12,8},{5,1},{9,5},{13,9},{6,2},{10,6},{14,10},{7,3},{... | collective-permute-start | bytes 786440 | tf_op jit(solution)/shard_map/ppermute | solution.py:21
  8.9 5.7 %collective-permute-start = (bf16[256,512]{1,0:T(8,128)(2,1)}, bf16[256,512]{1,0:T(8,128)(2,1)S(1)}, u32[]{:S(2)}, u32[]{:S(2)}) collective-permute-start(bf16[256,512]{1,0:T(8,128)(2,1)} %pad_maximum_fusion.2), channel_id=1, source_target_pairs={{0,4},{4,8},{8,12},{1,5},{5,9},{9,13},{2,6},{6,10},{10,14},{3,7},{... | collective-permute-start | bytes 786440 | tf_op jit(solution)/shard_map/ppermute | solution.py:21
  15.3 4.6 %convolution_convert_fusion.2.q_ref = bf16[2048,256]{1,0:T(8,128)(2,1)} fusion(bf16[2048,1024]{1,0:T(8,128)(2,1)} %param.19, bf16[1024,256]{1,0:T(8,128)(2,1)} %param.22), kind=kOutput, calls=%fused_computation.2 | convolution fusion | flops 1074266112 | bytes 5767168 | tf_op jit(solution)/shard_map/dot_general | solution.py:25
  20.0 1.9 %constant_dynamic-slice_fusion.2 = (bf16[256,256]{1,0:T(8,128)(2,1)}, bf16[256,256]{1,0:T(8,128)(2,1)}, bf16[256,256]{1,0:T(8,128)(2,1)}, bf16[256,256]{1,0:T(8,...) fusion(bf16[256,1024]{1,0:T(8,128)(2,1)S(1)} %copy-done.8, ...), kind=kLoop, calls=%fused_computation.69 | loop fusion | bytes 2097168 | tf_op jit(solution)/shard_map/dynamic_slice | solution.py:221
  24.3 12.5 %shard_map.122 = bf16[4,1024,256]{2,1,0:T(8,128)(2,1)} custom-call(s32[3]{0:T(128)} %copy-done.10, bf16[2048,256]{1,0:T(8,128)(2,1)} %convolution_convert_fusion.2.q_ref, bf16[2048,256]{1,0:T(8,128)(2,1)} %copy-done.4, bf16[2048,256]{1,0:T(8,128)(2,1)} %copy-done.3, bf16[256,512]{1,0:T(8,128)(2,1)} %copy-done.7, bf16[256,512]{1,0:T(8,128)(2,1)} %copy-done.6, ...), custom_call_target="tpu_custom_call" | custom-call | flops 1342177280 | bytes 5767168 | tf_op jit(solution)/shard_map/pallas_call | solution.py:93
  36.8 2.4 %slice.184 = bf16[2,1024,256]{2,1,0:T(8,128)(2,1)} slice(bf16[4,1024,256]{2,1,0:T(8,128)(2,1)} %shard_map.122), slice={[0:2], [0:1024], [0:256]} | slice | bytes 2097152 | tf_op jit(solution)/shard_map/slice | solution.py:229
  39.7 12.6 %shard_map.123 = bf16[4,1024,256]{2,1,0:T(8,128)(2,1)} custom-call(s32[3]{0:T(128)} %copy-done.11, bf16[2048,256]{1,0:T(8,128)(2,1)} %convolution_convert_fusion.2.q_ref, bf16[2048,256]{1,0:T(8,128)(2,1)} %copy-done.4, bf16[2048,256]{1,0:T(8,128)(2,1)} %copy-done.3, bf16[256,512]{1,0:T(8,128)(2,1)} %copy-done.7, bf16[256,512]{1,0:T(8,128)(2,1)} %copy-done.6, ...), custom_call_target="tpu_custom_call" | custom-call | flops 1342177280 | bytes 5767168 | tf_op jit(solution)/shard_map/pallas_call | solution.py:93
  52.3 2.7 %fusion.1 = (bf16[1024,256]{1,0:T(8,128)(2,1)}, bf16[1024,256]{1,0:T(8,128)(2,1)S(1)}) fusion(bf16[2,1024,256]{2,1,0:T(8,128)(2,1)} %collective-permute-done.2, bf16[4,1024,256]{2,1,0:T(8,128)(2,1)} %shard_map.122), kind=kLoop, calls=%fused_computation.14 | loop fusion | flops 2097152 | bytes 3145728 | tf_op jit(solution)/shard_map/convert_element_type | solution.py:231
  55.1 1.0 slice.155
  56.6 1.5 %convolution_convert_fusion.4.q_ref = bf16[1024,256]{1,0:T(8,128)(2,1)} fusion(bf16[1024,1024]{1,0:T(8,128)(2,1)S(1)} %copy-done, bf16[1024,256]{1,0:T(8,128)(2,1)S(1)} %copy-done.14), kind=kOutput, calls=%fused_computation.4 | convolution fusion | flops 537133056 | bytes 3145728 | tf_op jit(solution)/shard_map/dot_general | solution.py:25
  58.1 17.0 %shard_map.124 = (f32[1024,256]{1,0:T(8,128)}, f32[1024,128]{1,0:T(8,128)}) custom-call(s32[1]{0:T(128)} %bitcast.6.scal_ref, bf16[1024,256]{1,0:T(8,128)(2,1)} %convolution_convert_fusion.4.q_ref, bf16[2048,256]{1,0:T(8,128)(2,1)} %copy-done.4, bf16[2048,256]{1,0:T(8,128)(2,1)} %copy-done.3), custom_call_target="tpu_custom_call" | custom-call | flops 2147483648 | bytes 4194304 | tf_op jit(solution)/shard_map/pallas_call | solution.py:153
  75.1 1.4 %convert_element_type.250 = bf16[1024,256]{1,0:T(8,128)(2,1)S(1)} convert(f32[1024,256]{1,0:T(8,128)} %get-tuple-element.66) | non-fusion elementwise | flops 262144 | bytes 1572864 | tf_op jit(solution)/shard_map/convert_element_type | solution.py:343
  76.5 2.0 %collective-permute-start.3 = (bf16[1024,256]{1,0:T(8,128)(2,1)}, bf16[1024,256]{1,0:T(8,128)(2,1)}, u32[]{:S(2)}, u32[]{:S(2)}) collective-permute-start(bf16[1024,256]{1,0:T(8,128)(2,1)} %get-tuple-element.62), channel_id=1, source_target_pairs={{0,2},{1,3},{2,0},{3,1},{4,6},{5,7},{6,4},{7,5},{8,10},{9,11},{10,... | collective-permute-start | bytes 1572872 | tf_op jit(solution)/shard_map/ppermute | solution.py:244
  78.5 1.1 slice_bitcast_fusion
  79.6 2.5 %fusion.3 = (bf16[1024,256]{1,0:T(8,128)(2,1)}, bf16[1024,256]{1,0:T(8,128)(2,1)}) fusion(bf16[2,1024,256]{2,1,0:T(8,128)(2,1)} %collective-permute-done.4, bf16[4,1024,256]{2,1,0:T(8,128)(2,1)S(1)} %copy-done.2), kind=kLoop, calls=%fused_computation.16 | loop fusion | flops 2097152 | bytes 3145728 | tf_op jit(solution)/shard_map/convert_element_type | solution.py:231
  85.3 1.6 %collective-permute-start.6 = (bf16[280,256]{1,0:T(8,128)(2,1)}, bf16[280,256]{1,0:T(8,128)(2,1)}, u32[]{:S(2)}, u32[]{:S(2)}) collective-permute-start(bf16[280,256]{1,0:T(8,128)(2,1)} %pad_maximum_fusion.5), channel_id=1, source_target_pairs={{0,4},{4,8},{8,12},{12,0},{1,5},{5,9},{9,13},{13,1},{2,6},{6,10},{... | collective-permute-start | bytes 430088 | tf_op jit(solution)/shard_map/ppermute | solution.py:293
  88.8 1.6 %pad_maximum_fusion.6 = bf16[280,256]{1,0:T(8,128)(2,1)} fusion(bf16[8,256]{1,0:T(8,128)(2,1)S(1)} %get-tuple-element.76, bf16[8,256]{1,0:T(8,128)(2,1)S(1)} %get-tuple-element.77, bf16[8,256]{1,0:T(8,128)(2,1)S(1)} %copy.63, bf16[256,256]{1,0:T(8,128)(2,1)} %get-tuple-element.101), kind=kLoop, calls=%fused_computation.39 | loop fusion | flops 573440 | bytes 286720 | tf_op jit(solution)/shard_map/concatenate | solution.py:276
  90.3 1.0 collective-permute-start.7
  92.3 1.6 %pad_maximum_fusion.7 = bf16[280,256]{1,0:T(8,128)(2,1)} fusion(bf16[8,256]{1,0:T(8,128)(2,1)S(1)} %get-tuple-element.80, bf16[8,256]{1,0:T(8,128)(2,1)S(1)} %get-tuple-element.81, bf16[8,256]{1,0:T(8,128)(2,1)S(1)} %copy.67, bf16[256,256]{1,0:T(8,128)(2,1)} %get-tuple-element.100), kind=kLoop, calls=%fused_computation.40 | loop fusion | flops 573440 | bytes 286720 | tf_op jit(solution)/shard_map/concatenate | solution.py:276
  93.9 2.9 %collective-permute-start.8 = (bf16[280,256]{1,0:T(8,128)(2,1)}, bf16[280,256]{1,0:T(8,128)(2,1)S(1)}, u32[]{:S(2)}, u32[]{:S(2)}) collective-permute-start(bf16[280,256]{1,0:T(8,128)(2,1)} %pad_maximum_fusion.7), channel_id=1, source_target_pairs={{0,12},{4,0},{8,4},{12,8},{1,13},{5,1},{9,5},{13,9},{2,14},{6,2},{... | collective-permute-start | bytes 430088 | tf_op jit(solution)/shard_map/ppermute | solution.py:293
  98.9 2.0 %collective-permute-done.7 = bf16[280,256]{1,0:T(8,128)(2,1)} collective-permute-done((bf16[280,256]{1,0:T(8,128)(2,1)}, bf16[280,256]{1,0:T(8,128)(2,1)}, u32[]{:S(2)}, u32[]{:S(2)}) %collective-permute-start.7) | collective-permute-done | bytes 143392 | tf_op jit(solution)/shard_map/ppermute | solution.py:293
  104.1 1.6 %slice.191 = bf16[256,256]{1,0:T(8,128)(2,1)} slice(bf16[280,256]{1,0:T(8,128)(2,1)} %collective-permute-done.7), slice={[0:256], [0:256]} | slice | bytes 262144 | tf_op jit(solution)/shard_map/slice | solution.py:283
  105.6 1.0 copy.64
  106.6 1.6 %slice.192 = bf16[256,256]{1,0:T(8,128)(2,1)} slice(bf16[280,256]{1,0:T(8,128)(2,1)} %copy-done.9), slice={[0:256], [0:256]} | slice | bytes 262144 | tf_op jit(solution)/shard_map/slice | solution.py:283
  108.2 1.7 %copy.68 = bf16[256,256]{0,1:T(8,128)(2,1)} copy(bf16[256,256]{1,0:T(8,128)(2,1)} %slice.192) | data formatting | bytes 262144 | tf_op jit(solution)/shard_map/slice | solution.py:283
  111.7 1.1 multiply_reduce_fusion
  112.8 1.5 %convolution_convert_fusion.3 = bf16[256,1024]{1,0:T(8,128)(2,1)S(1)} fusion(bf16[256,256]{0,1:T(8,128)(2,1)S(1)} %bitcast.58, bf16[256,256]{1,0:T(8,128)(2,1)} %get-tuple-element.96, bf16[256,256]{1,0:T(8,128)(2,1)} %get-tuple-element.97, bf16[256,256]{1,0:T(8,128)(2,1)} %get-tuple-element.95, bf16[256,256]{1,0:T(8,128)(2,1)} %get-tuple-element.94), kind=kOutput, calls=%fused_computation.3 | convolution fusion | flops 136577024 | bytes 1179648 | tf_op jit(solution)/shard_map/dot_general | solution.py:359
  114.4 1.2 add_convert_fusion.3
  116.7 1.0 pad_maximum_fusion
  117.7 3.8 %collective-permute-done.10 = bf16[256,256]{1,0:T(8,128)(2,1)S(1)} collective-permute-done((bf16[256,256]{1,0:T(8,128)(2,1)S(1)}, bf16[256,256]{1,0:T(8,128)(2,1)S(1)}, u32[]{:S(2)}, u32[]{:S(2)}) %collective-permute-start.10) | collective-permute-done | bytes 131104 | tf_op jit(solution)/shard_map/ppermute | solution.py:244
  (85 shorter events, 20.2 us)
Async XLA Ops:
  0.6 56.0 %copy-start = (bf16[1024,1024]{1,0:T(8,128)(2,1)S(1)}, bf16[1024,1024]{1,0:T(8,128)(2,1)}, u32[]{:S(2)}) copy-start(bf16[1024,1024]{1,0:T(8,128)(2,1)} %param.20) | copy-start | bytes 6291460
  0.6 3.8 %copy-start.12 = (bf16[2048,1024]{1,0:T(8,128)(2,1)S(1)}, bf16[2048,1024]{1,0:T(8,128)(2,1)}, u32[]{:S(2)}) copy-start(bf16[2048,1024]{1,0:T(8,128)(2,1)} %param.19) | copy-start | bytes 12582916
  0.7 3.9 %copy-start.13 = (bf16[1024,256]{1,0:T(8,128)(2,1)S(1)}, bf16[1024,256]{1,0:T(8,128)(2,1)}, u32[]{:S(2)}) copy-start(bf16[1024,256]{1,0:T(8,128)(2,1)} %param.23) | copy-start | bytes 1572868
  4.5 1.3 %copy-start.3 = (bf16[2048,256]{1,0:T(8,128)(2,1)}, bf16[2048,256]{1,0:T(8,128)(2,1)S(1)}, u32[]{:S(2)}) copy-start(bf16[2048,256]{1,0:T(8,128)(2,1)S(1)} %convolution_convert_fusion.v_ref) | copy-start | bytes 3145732
  5.8 1.0 copy-start.4
  6.9 16.0 %collective-permute-start.1 = (bf16[256,512]{1,0:T(8,128)(2,1)S(1)}, bf16[256,512]{1,0:T(8,128)(2,1)S(1)}, u32[]{:S(2)}, u32[]{:S(2)}) collective-permute-start(bf16[256,512]{1,0:T(8,128)(2,1)S(1)} %pad_maximum_fusion.3), channel_id=1, source_target_pairs={{4,0},{8,4},{12,8},{5,1},{9,5},{13,9},{6,2},{10,6},{14,10},{7,3},{... | collective-permute-start | bytes 786440 | tf_op jit(solution)/shard_map/ppermute | solution.py:21
  8.9 14.0 %collective-permute-start = (bf16[256,512]{1,0:T(8,128)(2,1)}, bf16[256,512]{1,0:T(8,128)(2,1)S(1)}, u32[]{:S(2)}, u32[]{:S(2)}) collective-permute-start(bf16[256,512]{1,0:T(8,128)(2,1)} %pad_maximum_fusion.2), channel_id=1, source_target_pairs={{0,4},{4,8},{8,12},{1,5},{5,9},{9,13},{2,6},{6,10},{10,14},{3,7},{... | collective-permute-start | bytes 786440 | tf_op jit(solution)/shard_map/ppermute | solution.py:21
  15.3 4.6 %copy-start.8 = (bf16[256,1024]{1,0:T(8,128)(2,1)S(1)}, bf16[256,1024]{1,0:T(8,128)(2,1)}, u32[]{:S(2)}) copy-start(bf16[256,1024]{1,0:T(8,128)(2,1)} %param.27) | copy-start | bytes 1572868
  20.0 2.9 %copy-start.10 = (s32[3]{0:T(128)}, s32[3]{0:T(128)S(1)}, u32[]{:S(2)}) copy-start(s32[3]{0:T(128)S(1)} %constant_dynamic-update-slice_fusion.2.scal_ref) | copy-start | bytes 40
  22.9 0.7 copy-start.6
  23.6 0.7 copy-start.7
  36.8 2.4 %copy-start.15 = (s32[3]{0:T(128)S(1)}, s32[3]{0:T(128)}, u32[]{:S(2)}) copy-start(s32[3]{0:T(128)} %constant.169.clone) | copy-start | bytes 40
  39.2 13.1 %collective-permute-start.2 = (bf16[2,1024,256]{2,1,0:T(8,128)(2,1)}, bf16[2,1024,256]{2,1,0:T(8,128)(2,1)}, u32[]{:S(2)}, u32[]{:S(2)}) collective-permute-start(bf16[2,1024,256]{2,1,0:T(8,128)(2,1)} %slice.184), channel_id=1, source_target_pairs={{0,1},{1,0},{2,3},{3,2},{4,5},{5,4},{6,7},{7,6},{8,9},{9,8},{10,11... | collective-permute-start | bytes 3145736 | tf_op jit(solution)/shard_map/ppermute | solution.py:229
  39.2 0.5 copy-start.11
  52.3 2.8 %copy-start.1 = (bf16[4,1024,256]{2,1,0:T(8,128)(2,1)S(1)}, bf16[4,1024,256]{2,1,0:T(8,128)(2,1)}, u32[]{:S(2)}) copy-start(bf16[4,1024,256]{2,1,0:T(8,128)(2,1)} %shard_map.123) | copy-start | bytes 6291460
  52.3 4.3 %copy-start.14 = (bf16[1024,256]{1,0:T(8,128)(2,1)S(1)}, bf16[1024,256]{1,0:T(8,128)(2,1)}, u32[]{:S(2)}) copy-start(bf16[1024,256]{1,0:T(8,128)(2,1)} %param.26) | copy-start | bytes 1572868
  56.1 23.5 %collective-permute-start.4 = (bf16[2,1024,256]{2,1,0:T(8,128)(2,1)}, bf16[2,1024,256]{2,1,0:T(8,128)(2,1)}, u32[]{:S(2)}, u32[]{:S(2)}) collective-permute-start(bf16[2,1024,256]{2,1,0:T(8,128)(2,1)} %slice.155), channel_id=1, source_target_pairs={{0,1},{1,0},{2,3},{3,2},{4,5},{5,4},{6,7},{7,6},{8,9},{9,8},{10,11... | collective-permute-start | bytes 3145736 | tf_op jit(solution)/shard_map/ppermute | solution.py:229
  75.1 4.5 %copy-start.2 = (bf16[4,1024,256]{2,1,0:T(8,128)(2,1)S(1)}, bf16[4,1024,256]{2,1,0:T(8,128)(2,1)}, u32[]{:S(2)}) copy-start(bf16[4,1024,256]{2,1,0:T(8,128)(2,1)} %shard_map.123) | copy-start | bytes 6291460
  76.5 37.8 %collective-permute-start.3 = (bf16[1024,256]{1,0:T(8,128)(2,1)}, bf16[1024,256]{1,0:T(8,128)(2,1)}, u32[]{:S(2)}, u32[]{:S(2)}) collective-permute-start(bf16[1024,256]{1,0:T(8,128)(2,1)} %get-tuple-element.62), channel_id=1, source_target_pairs={{0,2},{1,3},{2,0},{3,1},{4,6},{5,7},{6,4},{7,5},{8,10},{9,11},{10,... | collective-permute-start | bytes 1572872 | tf_op jit(solution)/shard_map/ppermute | solution.py:244
  85.3 12.9 %collective-permute-start.6 = (bf16[280,256]{1,0:T(8,128)(2,1)}, bf16[280,256]{1,0:T(8,128)(2,1)}, u32[]{:S(2)}, u32[]{:S(2)}) collective-permute-start(bf16[280,256]{1,0:T(8,128)(2,1)} %pad_maximum_fusion.5), channel_id=1, source_target_pairs={{0,4},{4,8},{8,12},{12,0},{1,5},{5,9},{9,13},{13,1},{2,6},{6,10},{... | collective-permute-start | bytes 430088 | tf_op jit(solution)/shard_map/ppermute | solution.py:293
  90.3 10.6 %collective-permute-start.7 = (bf16[280,256]{1,0:T(8,128)(2,1)}, bf16[280,256]{1,0:T(8,128)(2,1)}, u32[]{:S(2)}, u32[]{:S(2)}) collective-permute-start(bf16[280,256]{1,0:T(8,128)(2,1)} %pad_maximum_fusion.6), channel_id=1, source_target_pairs={{0,8},{4,12},{8,0},{12,4},{1,9},{5,13},{9,1},{13,5},{2,10},{6,14},... | collective-permute-start | bytes 430088 | tf_op jit(solution)/shard_map/ppermute | solution.py:293
  93.9 7.7 %collective-permute-start.8 = (bf16[280,256]{1,0:T(8,128)(2,1)}, bf16[280,256]{1,0:T(8,128)(2,1)S(1)}, u32[]{:S(2)}, u32[]{:S(2)}) collective-permute-start(bf16[280,256]{1,0:T(8,128)(2,1)} %pad_maximum_fusion.7), channel_id=1, source_target_pairs={{0,12},{4,0},{8,4},{12,8},{1,13},{5,1},{9,5},{13,9},{2,14},{6,2},{... | collective-permute-start | bytes 430088 | tf_op jit(solution)/shard_map/ppermute | solution.py:293
  97.6 18.9 %collective-permute-start.5 = (bf16[1024,256]{1,0:T(8,128)(2,1)}, bf16[1024,256]{1,0:T(8,128)(2,1)S(1)}, u32[]{:S(2)}, u32[]{:S(2)}) collective-permute-start(bf16[1024,256]{1,0:T(8,128)(2,1)} %get-tuple-element.69), channel_id=1, source_target_pairs={{0,2},{1,3},{2,0},{3,1},{4,6},{5,7},{6,4},{7,5},{8,10},{9,11},{10,... | collective-permute-start | bytes 1572872 | tf_op jit(solution)/shard_map/ppermute | solution.py:244
  101.6 0.8 copy-start.9
  112.7 3.8 %copy-start.5 = (bf16[1024,256]{1,0:T(8,128)(2,1)S(1)}, bf16[1024,256]{1,0:T(8,128)(2,1)}, u32[]{:S(2)}) copy-start(bf16[1024,256]{1,0:T(8,128)(2,1)} %get-tuple-element.68) | copy-start | bytes 1572868
  114.3 1.6 %collective-permute-start.9 = (bf16[2,256,256]{2,1,0:T(8,128)(2,1)S(1)}, bf16[2,256,256]{2,1,0:T(8,128)(2,1)S(1)}, u32[]{:S(2)}, u32[]{:S(2)}) collective-permute-start(bf16[2,256,256]{2,1,0:T(8,128)(2,1)S(1)} %pad_maximum_fusion.4), channel_id=1, source_target_pairs={{0,1},{1,0},{2,3},{3,2},{4,5},{5,4},{6,7},{7,6},{8,9},{9,8},{10,11... | collective-permute-start | bytes 786440 | tf_op jit(solution)/shard_map/ppermute | solution.py:229
  115.9 5.6 %collective-permute-start.10 = (bf16[256,256]{1,0:T(8,128)(2,1)S(1)}, bf16[256,256]{1,0:T(8,128)(2,1)S(1)}, u32[]{:S(2)}, u32[]{:S(2)}) collective-permute-start(bf16[256,256]{1,0:T(8,128)(2,1)S(1)} %fusion.11), channel_id=1, source_target_pairs={{0,2},{1,3},{2,0},{3,1},{4,6},{5,7},{6,4},{7,5},{8,10},{9,11},{10,... | collective-permute-start | bytes 393224 | tf_op jit(solution)/shard_map/ppermute | solution.py:244

commit v10 on v9

--- a/solution.py
+++ b/solution.py
@@ -262,41 +262,15 @@
     return [hi, mid, lo]
 
 
-def exchange_rows(accum, stats, axis, rows):
+def exchange_rows(payload, axis, rows):
     count = lax.axis_size(axis)
     place = lax.axis_index(axis)
-    width = accum.shape[1]
-    packed = (stats.shape[0] * rows) % width == 0
-
-    def payload(target):
-        acc = lax.dynamic_slice_in_dim(accum, target * rows, rows, 0)
-        stat = lax.dynamic_slice_in_dim(stats, target * rows, rows, 1)
-        if not packed:
-            return acc, stat
-        return jnp.concatenate([acc] + split_three(stat.reshape(-1, width)), axis=0), None
-
-    def unpack(block, stat):
-        if not packed:
-            return block[:rows], stat
-        k = (block.shape[0] - rows) // 3
-        pieces = [block[rows + i * k : rows + (i + 1) * k].astype(jnp.float32) for i in range(3)]
-        return block[:rows], (pieces[0] + pieces[1] + pieces[2]).reshape(stats.shape[0], rows)
-
-    accs, stat_parts = [], []
-    own, own_stat = payload(place)
-    a, b = unpack(own, own_stat)
-    accs.append(a)
-    stat_parts.append(b)
+    parts = [lax.dynamic_slice_in_dim(payload, place * rows, rows, 0)]
     for shift in range(1, count):
         pairs = [(i, (i + shift) % count) for i in range(count)]
-        block, stat = payload((place + shift) % count)
-        block = lax.ppermute(block, axis, pairs)
-        if stat is not None:
-            stat = lax.ppermute(stat, axis, pairs)
-        a, b = unpack(block, stat)
-        accs.append(a)
-        stat_parts.append(b)
-    return jnp.stack(accs).astype(jnp.float32), jnp.stack(stat_parts)
+        block = lax.dynamic_slice_in_dim(payload, ((place + shift) % count) * rows, rows, 0)
+        parts.append(lax.ppermute(block, axis, pairs))
+    return parts
 
 
 def per_device(
@@ -339,21 +313,39 @@
     else:
         frame_parts = [plain_block_sum(blocks, "head") for blocks in parts]
     peaks, totals, local_accum = latent_attention(latent_query, keyed, valued, valid_count)
-    stats = jnp.concatenate([peaks, totals], axis=1).T
-    local_accum = local_accum.astype(jnp.bfloat16)
+    payload = jnp.concatenate(
+        [local_accum.astype(jnp.bfloat16)] + split_three(jnp.concatenate([peaks, totals], axis=1)),
+        axis=1,
+    )
     if paired:
-        rest_sums, local_accum, stats = lax.optimization_barrier((rest_sums, local_accum, stats))
+        rest_sums, payload = lax.optimization_barrier((rest_sums, payload))
         frame_parts.extend(cross_chip_sum(sums, "head") for sums in rest_sums)
     frames_out = jnp.concatenate(frame_parts, axis=0)
     rows_here = latent_count // seq_devices
-    part_accum, part_stats = exchange_rows(local_accum, stats, "seq", rows_here)
-    part_peak = part_stats[:, :heads_here, :]
-    part_total = part_stats[:, heads_here:, :]
-    joint = jnp.max(part_peak, axis=0)
-    factor = jnp.exp(part_peak - joint[None])
-    own_total = jnp.sum(part_total * factor, axis=0).T
-    factor_rows = jnp.transpose(factor, (0, 2, 1))
-    own_accum = jnp.sum(part_accum * jnp.repeat(factor_rows, HD, axis=2), axis=0)
+    parts = exchange_rows(payload, "seq", rows_here)
+    stat_width = 2 * heads_here
+
+    def stats_of(part):
+        pieces = [
+            part[:, head_width + i * stat_width : head_width + (i + 1) * stat_width].astype(
+                jnp.float32
+            )
+            for i in range(3)
+        ]
+        return pieces[0] + pieces[1] + pieces[2]
+
+    part_stats = [stats_of(part) for part in parts]
+    joint = part_stats[0][:, :heads_here]
+    for stat in part_stats[1:]:
+        joint = jnp.maximum(joint, stat[:, :heads_here])
+    own_total = jnp.zeros_like(joint)
+    own_accum = jnp.zeros((rows_here, head_width), jnp.float32)
+    for part, stat in zip(parts, part_stats):
+        factor = jnp.exp(stat[:, :heads_here] - joint)
+        own_total = own_total + stat[:, heads_here:] * factor
+        own_accum = own_accum + part[:, :head_width].astype(jnp.float32) * jnp.repeat(
+            factor, HD, axis=1
+        )
     summary = (own_accum / jnp.repeat(own_total, HD, axis=1)).astype(jnp.bfloat16)
     if paired:
         latent_terms = jnp.dot(

time: 123 us -> 128 us (1.041)
  waiting for transfers between devices: 6.22 us -> 16.9 us
  other arithmetic: 20 us -> 15.2 us
  matrix products: 12.6 us -> 10.6 us
    ppermute x3, waiting for transfers between devices: 2.02 us -> 12.5 us  [exchange_rows(): parts.append(lax.ppermute(block, axis, pairs))]
    reshape x0 -> x5, local copies, waits for them, and re-layouts: none -> 8.94 us  [the longest x4 7.15 us: per_device(): jnp.repeat(factor, HD, axis=1)]
    slice x6 -> x0, local copies, waits for them, and re-layouts: 6.82 us -> none  [unpack(): block[:rows]]
    exp x0 -> x4, local copies, waits for them, and re-layouts: none -> 3.91 us  [per_device(): factor = jnp.exp(stat[:, :heads_here] - joint)]
    broadcast_in_dim x0 -> x5, local copies, waits for them, and re-layouts: none -> 3.7 us  [the longest x4 2.96 us: per_device(): jnp.repeat(factor, HD, axis=1)]
    concatenate x3 -> x1, other arithmetic: 3.84 us -> 0.26 us  [per_device(): jnp.concatenate([local_accum.astype(jnp.bfloat16)] + split_three(jnp.conc...]
    convert_element_type x3 -> x0, local copies, waits for them, and re-layouts: 2.71 us -> none  [split_three(): hi = values.astype(jnp.bfloat16)]
    add x0 -> x5, other arithmetic: none -> 2.41 us  [the longest x4 1.47 us: stats_of(): return pieces[0] + pieces[1] + pieces[2]]
  transfers between devices with their start and end apart: 11 -> 11, of which waited for: 3 -> 5; matrix products, arithmetic and copies ran while one was open for 34% -> 25% of each run, Pallas kernels for 24% -> 23%
where the time goes in v10:
time: 128 us
  Pallas kernels  42 us (33%)
  local copies, waits for them, and re-layouts  24.6 us (19%)
  waiting for transfers between devices  16.9 us (13%)
  starting transfers between devices  16.6 us (13%)
  other arithmetic  15.2 us (12%)
  matrix products  10.6 us (8%)
  between operations  1.64 us (1%)
    pallas_call x2, Pallas kernels, window_attention(): pl.pallas_call(kernel, cost_estimate=cost, out_shape=jax.ShapeDtypeStruct...  25 us
    pallas_call x1, Pallas kernels, latent_attention(): pl.pallas_call(kernel, cost_estimate=cost, out_shape=(jax.ShapeDtypeStruc...  17 us
    ppermute x3, waiting for transfers between devices, exchange_rows(): parts.append(lax.ppermute(block, axis, pairs))  12.5 us
    dot_general x4, matrix products, project(): jnp.dot(source, weight, preferred_element_type=jnp.float32)  8.75 us
    reshape x4, local copies, waits for them, and re-layouts, per_device(): jnp.repeat(factor, HD, axis=1)  7.15 us
    ppermute x1, starting transfers between devices, halos(): lax.ppermute(tail, axis, forward)  5.87 us
    ppermute x3, starting transfers between devices, exchange_rows(): parts.append(lax.ppermute(block, axis, pairs))  5.57 us
    convert_element_type x3, other arithmetic, chip_pair_sums(): (blocks[chips + d].astype(jnp.float32) + received[d].astype(jnp.float32))...  5.29 us
  transfers between devices with their start and end apart: 11, of which 5 were waited for; matrix products, arithmetic and copies ran while one was open for 25% of the time, Pallas kernels for 23%

profile of v10, /device:TPU:0, one launch (start us, length us, event | category | flops | bytes accessed | tf_op | source)
XLA Modules:
  0.0 127.6 jit_solution(2291906735430234606)
XLA Ops:
  0.7 3.7 %convolution_convert_fusion.v_ref = bf16[2048,256]{1,0:T(8,128)(2,1)S(1)} fusion(bf16[2048,1024]{1,0:T(8,128)(2,1)} %param.19, bf16[1024,256]{1,0:T(8,128)(2,1)} %param.24), kind=kOutput, calls=%fused_computation | convolution fusion | flops 1074266112 | bytes 5767168 | tf_op jit(solution)/shard_map/dot_general | solution.py:25
  4.5 1.3 %convolution_convert_fusion.1.k_ref = bf16[2048,256]{1,0:T(8,128)(2,1)S(1)} fusion(bf16[2048,1024]{1,0:T(8,128)(2,1)S(1)} %copy-done.15, bf16[1024,256]{1,0:T(8,128)(2,1)S(1)} %copy-done.16), kind=kOutput, calls=%fused_computation.1 | convolution fusion | flops 1074266112 | bytes 5767168 | tf_op jit(solution)/shard_map/dot_general | solution.py:25
  5.9 1.4 %collective-permute-start.1 = (bf16[256,512]{1,0:T(8,128)(2,1)S(1)}, bf16[256,512]{1,0:T(8,128)(2,1)S(1)}, u32[]{:S(2)}, u32[]{:S(2)}) collective-permute-start(bf16[256,512]{1,0:T(8,128)(2,1)S(1)} %pad_maximum_fusion.4), channel_id=1, source_target_pairs={{4,0},{8,4},{12,8},{5,1},{9,5},{13,9},{6,2},{10,6},{14,10},{7,3},{... | collective-permute-start | bytes 786440 | tf_op jit(solution)/shard_map/ppermute | solution.py:21
  8.1 5.9 %collective-permute-start = (bf16[256,512]{1,0:T(8,128)(2,1)}, bf16[256,512]{1,0:T(8,128)(2,1)S(1)}, u32[]{:S(2)}, u32[]{:S(2)}) collective-permute-start(bf16[256,512]{1,0:T(8,128)(2,1)} %pad_maximum_fusion.3), channel_id=1, source_target_pairs={{0,4},{4,8},{8,12},{1,5},{5,9},{9,13},{2,6},{6,10},{10,14},{3,7},{... | collective-permute-start | bytes 786440 | tf_op jit(solution)/shard_map/ppermute | solution.py:21
  14.0 2.3 %convolution_convert_fusion.2.q_ref = bf16[2048,256]{1,0:T(8,128)(2,1)} fusion(bf16[2048,1024]{1,0:T(8,128)(2,1)S(1)} %copy-done.15, bf16[1024,256]{1,0:T(8,128)(2,1)S(1)} %copy-done.17), kind=kOutput, calls=%fused_computation.2 | convolution fusion | flops 1074266112 | bytes 5767168 | tf_op jit(solution)/shard_map/dot_general | solution.py:25
  17.9 1.7 %collective-permute-done.low_ref = bf16[256,512]{1,0:T(8,128)(2,1)S(1)} collective-permute-done((bf16[256,512]{1,0:T(8,128)(2,1)}, bf16[256,512]{1,0:T(8,128)(2,1)S(1)}, u32[]{:S(2)}, u32[]{:S(2)}) %collective-permute-start) | collective-permute-done | bytes 262176 | tf_op jit(solution)/shard_map/ppermute | solution.py:21
  20.3 12.5 %shard_map.122 = bf16[4,1024,256]{2,1,0:T(8,128)(2,1)} custom-call(s32[3]{0:T(128)} %copy-done.13, bf16[2048,256]{1,0:T(8,128)(2,1)} %convolution_convert_fusion.2.q_ref, bf16[2048,256]{1,0:T(8,128)(2,1)} %copy-done.4, bf16[2048,256]{1,0:T(8,128)(2,1)} %copy-done.3, bf16[256,512]{1,0:T(8,128)(2,1)} %copy-done.8, bf16[256,512]{1,0:T(8,128)(2,1)} %copy-done.7, ...), custom_call_target="tpu_custom_call" | custom-call | flops 1342177280 | bytes 5767168 | tf_op jit(solution)/shard_map/pallas_call | solution.py:93
  32.8 1.3 %slice.228 = bf16[2,1024,256]{2,1,0:T(8,128)(2,1)S(1)} slice(bf16[4,1024,256]{2,1,0:T(8,128)(2,1)} %shard_map.122), slice={[0:2], [0:1024], [0:256]} | slice | bytes 2097152 | tf_op jit(solution)/shard_map/slice | solution.py:229
  34.8 12.5 %shard_map.123 = bf16[4,1024,256]{2,1,0:T(8,128)(2,1)} custom-call(s32[3]{0:T(128)} %copy-done.14, bf16[2048,256]{1,0:T(8,128)(2,1)} %convolution_convert_fusion.2.q_ref, bf16[2048,256]{1,0:T(8,128)(2,1)} %copy-done.4, bf16[2048,256]{1,0:T(8,128)(2,1)} %copy-done.3, bf16[256,512]{1,0:T(8,128)(2,1)} %copy-done.8, bf16[256,512]{1,0:T(8,128)(2,1)} %copy-done.7, ...), custom_call_target="tpu_custom_call" | custom-call | flops 1342177280 | bytes 5767168 | tf_op jit(solution)/shard_map/pallas_call | solution.py:93
  47.3 2.8 %fusion.1 = (bf16[1024,256]{1,0:T(8,128)(2,1)}, bf16[1024,256]{1,0:T(8,128)(2,1)S(1)}) fusion(bf16[2,1024,256]{2,1,0:T(8,128)(2,1)} %collective-permute-done.2, bf16[4,1024,256]{2,1,0:T(8,128)(2,1)} %shard_map.122), kind=kLoop, calls=%fused_computation.14 | loop fusion | flops 2097152 | bytes 3145728 | tf_op jit(solution)/shard_map/convert_element_type | solution.py:231
  50.1 1.0 slice.189
  51.6 1.5 %convolution_convert_fusion.4.q_ref = bf16[1024,256]{1,0:T(8,128)(2,1)} fusion(bf16[1024,1024]{1,0:T(8,128)(2,1)S(1)} %copy-done, bf16[1024,256]{1,0:T(8,128)(2,1)S(1)} %copy-done.18), kind=kOutput, calls=%fused_computation.4 | convolution fusion | flops 537133056 | bytes 3145728 | tf_op jit(solution)/shard_map/dot_general | solution.py:25
  53.1 17.0 %shard_map.124 = (f32[1024,256]{1,0:T(8,128)}, f32[1024,128]{1,0:T(8,128)}) custom-call(s32[1]{0:T(128)} %bitcast.6.scal_ref, bf16[1024,256]{1,0:T(8,128)(2,1)} %convolution_convert_fusion.4.q_ref, bf16[2048,256]{1,0:T(8,128)(2,1)} %copy-done.4, bf16[2048,256]{1,0:T(8,128)(2,1)} %copy-done.3), custom_call_target="tpu_custom_call" | custom-call | flops 2147483648 | bytes 4194304 | tf_op jit(solution)/shard_map/pallas_call | solution.py:153
  70.1 1.3 %convert_element_type.214 = bf16[1024,256]{1,0:T(8,128)(2,1)S(1)} convert(f32[1024,256]{1,0:T(8,128)} %get-tuple-element.65) | non-fusion elementwise | flops 262144 | bytes 1572864 | tf_op jit(solution)/shard_map/convert_element_type | solution.py:317
  71.9 1.2 copy-done.2
  73.1 2.5 %fusion.3 = (bf16[1024,256]{1,0:T(8,128)(2,1)}, bf16[1024,256]{1,0:T(8,128)(2,1)}) fusion(bf16[2,1024,256]{2,1,0:T(8,128)(2,1)} %collective-permute-done.4, bf16[4,1024,256]{2,1,0:T(8,128)(2,1)S(1)} %copy-done.2), kind=kLoop, calls=%fused_computation.16 | loop fusion | flops 2097152 | bytes 3145728 | tf_op jit(solution)/shard_map/convert_element_type | solution.py:231
  76.4 4.6 %collective-permute-start.8 = (bf16[256,280]{1,0:T(8,128)(2,1)}, bf16[256,280]{1,0:T(8,128)(2,1)}, u32[]{:S(2)}, u32[]{:S(2)}) collective-permute-start(bf16[256,280]{1,0:T(8,128)(2,1)} %get-tuple-element.87), channel_id=1, source_target_pairs={{0,12},{4,0},{8,4},{12,8},{1,13},{5,1},{9,5},{13,9},{2,14},{6,2},{... | collective-permute-start | bytes 430088 | tf_op jit(solution)/shard_map/ppermute | solution.py:272
  81.8 1.5 %collective-permute-start.3 = (bf16[1024,256]{1,0:T(8,128)(2,1)}, bf16[1024,256]{1,0:T(8,128)(2,1)}, u32[]{:S(2)}, u32[]{:S(2)}) collective-permute-start(bf16[1024,256]{1,0:T(8,128)(2,1)} %get-tuple-element.61), channel_id=1, source_target_pairs={{0,2},{1,3},{2,0},{3,1},{4,6},{5,7},{6,4},{7,5},{8,10},{9,11},{10,... | collective-permute-start | bytes 1572872 | tf_op jit(solution)/shard_map/ppermute | solution.py:244
  84.9 1.7 %collective-permute-done.8 = bf16[256,280]{1,0:T(8,128)(2,1)} collective-permute-done((bf16[256,280]{1,0:T(8,128)(2,1)}, bf16[256,280]{1,0:T(8,128)(2,1)}, u32[]{:S(2)}, u32[]{:S(2)}) %collective-permute-start.8) | collective-permute-done | bytes 143392 | tf_op jit(solution)/shard_map/ppermute | solution.py:272
  86.6 1.2 convert_add_fusion.2
  87.8 10.8 %collective-permute-done.7 = bf16[256,280]{1,0:T(8,128)(2,1)S(1)} collective-permute-done((bf16[256,280]{1,0:T(8,128)(2,1)}, bf16[256,280]{1,0:T(8,128)(2,1)S(1)}, u32[]{:S(2)}, u32[]{:S(2)}) %collective-permute-start.7) | collective-permute-done | bytes 143392 | tf_op jit(solution)/shard_map/ppermute | solution.py:272
  102.7 1.8 %copy.30 = f32[256,256]{1,0:T(8,128)} copy(f32[256,256]{0,1:T(8,128)} %bitcast.39) | data formatting | bytes 524288 | tf_op jit(solution)/shard_map/reshape | solution.py:346
  106.2 1.8 %copy.32 = f32[256,256]{1,0:T(8,128)} copy(f32[256,256]{0,1:T(8,128)} %bitcast.40) | data formatting | bytes 524288 | tf_op jit(solution)/shard_map/reshape | solution.py:346
  109.7 1.8 %copy.34 = f32[256,256]{1,0:T(8,128)} copy(f32[256,256]{0,1:T(8,128)} %bitcast.41) | data formatting | bytes 524288 | tf_op jit(solution)/shard_map/reshape | solution.py:346
  113.2 1.8 %copy.36 = f32[256,256]{1,0:T(8,128)} copy(f32[256,256]{0,1:T(8,128)} %bitcast.42) | data formatting | bytes 524288 | tf_op jit(solution)/shard_map/reshape | solution.py:346
  115.8 1.8 %copy.38 = f32[256,256]{1,0:T(8,128)} copy(f32[256,256]{0,1:T(8,128)} %bitcast.43) | data formatting | bytes 524288 | tf_op jit(solution)/shard_map/reshape | solution.py:349
  117.6 1.9 %convolution_convert_fusion.3 = bf16[256,1024]{1,0:T(8,128)(2,1)S(1)} fusion(bf16[256,256]{1,0:T(8,128)(2,1)} %get-tuple-element.93, bf16[256,256]{1,0:T(8,128)(2,1)} %get-tuple-element.94, bf16[256,256]{1,0:T(8,128)(2,1)} %get-tuple-element.92, bf16[256,256]{1,0:T(8,128)(2,1)} %get-tuple-element.91, f32[256,256]{1,0:T(8,128)} %copy.38, ...), kind=kOutput, calls=%fused_computation.3 | convolution fusion | flops 137428992 | bytes 2883588 | tf_op jit(solution)/shard_map/dot_general | solution.py:351
  119.7 1.2 add_convert_fusion.3
  121.2 1.1 collective-permute-start.10
  122.3 1.2 add_convert_fusion
  123.5 1.0 pad_maximum_fusion
  124.5 2.3 %collective-permute-done.10 = bf16[256,256]{1,0:T(8,128)(2,1)S(1)} collective-permute-done((bf16[256,256]{1,0:T(8,128)(2,1)S(1)}, bf16[256,256]{1,0:T(8,128)(2,1)S(1)}, u32[]{:S(2)}, u32[]{:S(2)}) %collective-permute-start.10) | collective-permute-done | bytes 131104 | tf_op jit(solution)/shard_map/ppermute | solution.py:244
  (84 shorter events, 18.7 us)
Async XLA Ops:
  0.6 51.0 %copy-start = (bf16[1024,1024]{1,0:T(8,128)(2,1)S(1)}, bf16[1024,1024]{1,0:T(8,128)(2,1)}, u32[]{:S(2)}) copy-start(bf16[1024,1024]{1,0:T(8,128)(2,1)} %param.20) | copy-start | bytes 6291460
  0.6 3.8 %copy-start.15 = (bf16[2048,1024]{1,0:T(8,128)(2,1)S(1)}, bf16[2048,1024]{1,0:T(8,128)(2,1)}, u32[]{:S(2)}) copy-start(bf16[2048,1024]{1,0:T(8,128)(2,1)} %param.19) | copy-start | bytes 12582916
  0.7 3.9 %copy-start.16 = (bf16[1024,256]{1,0:T(8,128)(2,1)S(1)}, bf16[1024,256]{1,0:T(8,128)(2,1)}, u32[]{:S(2)}) copy-start(bf16[1024,256]{1,0:T(8,128)(2,1)} %param.23) | copy-start | bytes 1572868
  4.5 1.3 %copy-start.3 = (bf16[2048,256]{1,0:T(8,128)(2,1)}, bf16[2048,256]{1,0:T(8,128)(2,1)S(1)}, u32[]{:S(2)}) copy-start(bf16[2048,256]{1,0:T(8,128)(2,1)S(1)} %convolution_convert_fusion.v_ref) | copy-start | bytes 3145732
  5.8 10.4 %copy-start.4 = (bf16[2048,256]{1,0:T(8,128)(2,1)}, bf16[2048,256]{1,0:T(8,128)(2,1)S(1)}, u32[]{:S(2)}) copy-start(bf16[2048,256]{1,0:T(8,128)(2,1)S(1)} %convolution_convert_fusion.1.k_ref) | copy-start | bytes 3145732
  5.8 8.1 %copy-start.17 = (bf16[1024,256]{1,0:T(8,128)(2,1)S(1)}, bf16[1024,256]{1,0:T(8,128)(2,1)}, u32[]{:S(2)}) copy-start(bf16[1024,256]{1,0:T(8,128)(2,1)} %param.22) | copy-start | bytes 1572868
  5.9 12.0 %collective-permute-start.1 = (bf16[256,512]{1,0:T(8,128)(2,1)S(1)}, bf16[256,512]{1,0:T(8,128)(2,1)S(1)}, u32[]{:S(2)}, u32[]{:S(2)}) collective-permute-start(bf16[256,512]{1,0:T(8,128)(2,1)S(1)} %pad_maximum_fusion.4), channel_id=1, source_target_pairs={{4,0},{8,4},{12,8},{5,1},{9,5},{13,9},{6,2},{10,6},{14,10},{7,3},{... | collective-permute-start | bytes 786440 | tf_op jit(solution)/shard_map/ppermute | solution.py:21
  8.1 8.9 %copy-start.9 = (bf16[256,1024]{1,0:T(8,128)(2,1)S(1)}, bf16[256,1024]{1,0:T(8,128)(2,1)}, u32[]{:S(2)}) copy-start(bf16[256,1024]{1,0:T(8,128)(2,1)} %param.25) | copy-start | bytes 1572868
  8.1 11.5 %collective-permute-start = (bf16[256,512]{1,0:T(8,128)(2,1)}, bf16[256,512]{1,0:T(8,128)(2,1)S(1)}, u32[]{:S(2)}, u32[]{:S(2)}) collective-permute-start(bf16[256,512]{1,0:T(8,128)(2,1)} %pad_maximum_fusion.3), channel_id=1, source_target_pairs={{0,4},{4,8},{8,12},{1,5},{5,9},{9,13},{2,6},{6,10},{10,14},{3,7},{... | collective-permute-start | bytes 786440 | tf_op jit(solution)/shard_map/ppermute | solution.py:21
  16.9 2.7 %copy-start.13 = (s32[3]{0:T(128)}, s32[3]{0:T(128)S(1)}, u32[]{:S(2)}) copy-start(s32[3]{0:T(128)S(1)} %constant_dynamic-update-slice_fusion.2.scal_ref) | copy-start | bytes 40
  17.9 1.7 %copy-start.7 = (bf16[256,512]{1,0:T(8,128)(2,1)}, bf16[256,512]{1,0:T(8,128)(2,1)S(1)}, u32[]{:S(2)}) copy-start(bf16[256,512]{1,0:T(8,128)(2,1)S(1)} %collective-permute-done.1.high_ref) | copy-start | bytes 786436
  19.6 0.7 copy-start.8
  32.8 1.4 %copy-start.19 = (s32[3]{0:T(128)S(1)}, s32[3]{0:T(128)}, u32[]{:S(2)}) copy-start(s32[3]{0:T(128)} %constant.165.clone) | copy-start | bytes 40
  34.2 13.1 %collective-permute-start.2 = (bf16[2,1024,256]{2,1,0:T(8,128)(2,1)S(1)}, bf16[2,1024,256]{2,1,0:T(8,128)(2,1)}, u32[]{:S(2)}, u32[]{:S(2)}) collective-permute-start(bf16[2,1024,256]{2,1,0:T(8,128)(2,1)S(1)} %slice.228), channel_id=1, source_target_pairs={{0,1},{1,0},{2,3},{3,2},{4,5},{5,4},{6,7},{7,6},{8,9},{9,8},{10,11... | collective-permute-start | bytes 3145736 | tf_op jit(solution)/shard_map/ppermute | solution.py:229
  34.3 0.5 copy-start.14
  47.3 2.8 %copy-start.1 = (bf16[4,1024,256]{2,1,0:T(8,128)(2,1)S(1)}, bf16[4,1024,256]{2,1,0:T(8,128)(2,1)}, u32[]{:S(2)}) copy-start(bf16[4,1024,256]{2,1,0:T(8,128)(2,1)} %shard_map.123) | copy-start | bytes 6291460
  47.3 4.3 %copy-start.18 = (bf16[1024,256]{1,0:T(8,128)(2,1)S(1)}, bf16[1024,256]{1,0:T(8,128)(2,1)}, u32[]{:S(2)}) copy-start(bf16[1024,256]{1,0:T(8,128)(2,1)} %param.26) | copy-start | bytes 1572868
  51.1 20.8 %collective-permute-start.4 = (bf16[2,1024,256]{2,1,0:T(8,128)(2,1)}, bf16[2,1024,256]{2,1,0:T(8,128)(2,1)}, u32[]{:S(2)}, u32[]{:S(2)}) collective-permute-start(bf16[2,1024,256]{2,1,0:T(8,128)(2,1)} %slice.189), channel_id=1, source_target_pairs={{0,1},{1,0},{2,3},{3,2},{4,5},{5,4},{6,7},{7,6},{8,9},{9,8},{10,11... | collective-permute-start | bytes 3145736 | tf_op jit(solution)/shard_map/ppermute | solution.py:229
  70.1 1.4 %copy-start.6 = (f32[1024,128]{1,0:T(8,128)S(1)}, f32[1024,128]{1,0:T(8,128)}, u32[]{:S(2)}) copy-start(f32[1024,128]{1,0:T(8,128)} %get-tuple-element.66) | copy-start | bytes 1572868
  71.5 1.6 %copy-start.2 = (bf16[4,1024,256]{2,1,0:T(8,128)(2,1)S(1)}, bf16[4,1024,256]{2,1,0:T(8,128)(2,1)}, u32[]{:S(2)}) copy-start(bf16[4,1024,256]{2,1,0:T(8,128)(2,1)} %shard_map.123) | copy-start | bytes 6291460
  71.9 9.1 %copy-start.10 = (bf16[256,1024]{1,0:T(8,128)(2,1)S(1)}, bf16[256,1024]{1,0:T(8,128)(2,1)}, u32[]{:S(2)}) copy-start(bf16[256,1024]{1,0:T(8,128)(2,1)} %param.27) | copy-start | bytes 1572868
  76.4 10.2 %collective-permute-start.8 = (bf16[256,280]{1,0:T(8,128)(2,1)}, bf16[256,280]{1,0:T(8,128)(2,1)}, u32[]{:S(2)}, u32[]{:S(2)}) collective-permute-start(bf16[256,280]{1,0:T(8,128)(2,1)} %get-tuple-element.87), channel_id=1, source_target_pairs={{0,12},{4,0},{8,4},{12,8},{1,13},{5,1},{9,5},{13,9},{2,14},{6,2},{... | collective-permute-start | bytes 430088 | tf_op jit(solution)/shard_map/ppermute | solution.py:272
  81.8 37.9 %collective-permute-start.3 = (bf16[1024,256]{1,0:T(8,128)(2,1)}, bf16[1024,256]{1,0:T(8,128)(2,1)}, u32[]{:S(2)}, u32[]{:S(2)}) collective-permute-start(bf16[1024,256]{1,0:T(8,128)(2,1)} %get-tuple-element.61), channel_id=1, source_target_pairs={{0,2},{1,3},{2,0},{3,1},{4,6},{5,7},{6,4},{7,5},{8,10},{9,11},{10,... | collective-permute-start | bytes 1572872 | tf_op jit(solution)/shard_map/ppermute | solution.py:244
  83.3 15.3 %collective-permute-start.7 = (bf16[256,280]{1,0:T(8,128)(2,1)}, bf16[256,280]{1,0:T(8,128)(2,1)S(1)}, u32[]{:S(2)}, u32[]{:S(2)}) collective-permute-start(bf16[256,280]{1,0:T(8,128)(2,1)} %get-tuple-element.88), channel_id=1, source_target_pairs={{0,8},{4,12},{8,0},{12,4},{1,9},{5,13},{9,1},{13,5},{2,10},{6,14},... | collective-permute-start | bytes 430088 | tf_op jit(solution)/shard_map/ppermute | solution.py:272
  83.3 15.4 %collective-permute-start.6 = (bf16[256,280]{1,0:T(8,128)(2,1)}, bf16[256,280]{1,0:T(8,128)(2,1)S(1)}, u32[]{:S(2)}, u32[]{:S(2)}) collective-permute-start(bf16[256,280]{1,0:T(8,128)(2,1)} %get-tuple-element.86), channel_id=1, source_target_pairs={{0,4},{4,8},{8,12},{12,0},{1,5},{5,9},{9,13},{13,1},{2,6},{6,10},{... | collective-permute-start | bytes 430088 | tf_op jit(solution)/shard_map/ppermute | solution.py:272
  84.3 38.0 %collective-permute-start.5 = (bf16[1024,256]{1,0:T(8,128)(2,1)}, bf16[1024,256]{1,0:T(8,128)(2,1)}, u32[]{:S(2)}, u32[]{:S(2)}) collective-permute-start(bf16[1024,256]{1,0:T(8,128)(2,1)} %get-tuple-element.68), channel_id=1, source_target_pairs={{0,2},{1,3},{2,0},{3,1},{4,6},{5,7},{6,4},{7,5},{8,10},{9,11},{10,... | collective-permute-start | bytes 1572872 | tf_op jit(solution)/shard_map/ppermute | solution.py:244
  98.6 0.7 copy-start.11
  99.3 0.7 copy-start.12
  119.5 2.8 %copy-start.5 = (bf16[1024,256]{1,0:T(8,128)(2,1)S(1)}, bf16[1024,256]{1,0:T(8,128)(2,1)}, u32[]{:S(2)}) copy-start(bf16[1024,256]{1,0:T(8,128)(2,1)} %get-tuple-element.67) | copy-start | bytes 1572868
  119.6 1.6 %collective-permute-start.9 = (bf16[2,256,256]{2,1,0:T(8,128)(2,1)S(1)}, bf16[2,256,256]{2,1,0:T(8,128)(2,1)S(1)}, u32[]{:S(2)}, u32[]{:S(2)}) collective-permute-start(bf16[2,256,256]{2,1,0:T(8,128)(2,1)S(1)} %pad_maximum_fusion.5), channel_id=1, source_target_pairs={{0,1},{1,0},{2,3},{3,2},{4,5},{5,4},{6,7},{7,6},{8,9},{9,8},{10,11... | collective-permute-start | bytes 786440 | tf_op jit(solution)/shard_map/ppermute | solution.py:229
  121.2 5.6 %collective-permute-start.10 = (bf16[256,256]{1,0:T(8,128)(2,1)S(1)}, bf16[256,256]{1,0:T(8,128)(2,1)S(1)}, u32[]{:S(2)}, u32[]{:S(2)}) collective-permute-start(bf16[256,256]{1,0:T(8,128)(2,1)S(1)} %fusion.12), channel_id=1, source_target_pairs={{0,2},{1,3},{2,0},{3,1},{4,6},{5,7},{6,4},{7,5},{8,10},{9,11},{10,... | collective-permute-start | bytes 393224 | tf_op jit(solution)/shard_map/ppermute | solution.py:244

commit v11 on v10

--- a/solution.py
+++ b/solution.py
@@ -273,6 +273,42 @@
     return parts
 
 
+def merge_kernel(*refs, heads):
+    part_refs, out_ref = refs[:-1], refs[-1]
+    width = out_ref.shape[1]
+    stat_width = 2 * heads
+
+    def column(ref, c):
+        pieces = [
+            ref[:, width + i * stat_width + c : width + i * stat_width + c + 1].astype(jnp.float32)
+            for i in range(3)
+        ]
+        return pieces[0] + pieces[1] + pieces[2]
+
+    for h in range(heads):
+        peaks = [column(ref, h) for ref in part_refs]
+        joint = peaks[0]
+        for peak in peaks[1:]:
+            joint = jnp.maximum(joint, peak)
+        total = jnp.zeros_like(joint)
+        accum = jnp.zeros((out_ref.shape[0], HD), jnp.float32)
+        for ref, peak in zip(part_refs, peaks):
+            factor = jnp.exp(peak - joint)
+            total = total + column(ref, heads + h) * factor
+            accum = accum + ref[:, h * HD : (h + 1) * HD].astype(jnp.float32) * factor
+        out_ref[:, h * HD : (h + 1) * HD] = (accum / total).astype(jnp.bfloat16)
+
+
+def merge_parts(parts, width, heads):
+    rows = parts[0].shape[0]
+    return pl.pallas_call(
+        functools.partial(merge_kernel, heads=heads),
+        out_shape=jax.ShapeDtypeStruct((rows, width), jnp.bfloat16),
+        in_specs=[pl.BlockSpec(memory_space=pltpu.VMEM)] * len(parts),
+        out_specs=pl.BlockSpec(memory_space=pltpu.VMEM),
+    )(*parts)
+
+
 def per_device(
     frames, latents, lengths, w_query, w_key, w_value, w_out, w_latent_query, w_latent_out
 ):
@@ -323,30 +359,7 @@
     frames_out = jnp.concatenate(frame_parts, axis=0)
     rows_here = latent_count // seq_devices
     parts = exchange_rows(payload, "seq", rows_here)
-    stat_width = 2 * heads_here
-
-    def stats_of(part):
-        pieces = [
-            part[:, head_width + i * stat_width : head_width + (i + 1) * stat_width].astype(
-                jnp.float32
-            )
-            for i in range(3)
-        ]
-        return pieces[0] + pieces[1] + pieces[2]
-
-    part_stats = [stats_of(part) for part in parts]
-    joint = part_stats[0][:, :heads_here]
-    for stat in part_stats[1:]:
-        joint = jnp.maximum(joint, stat[:, :heads_here])
-    own_total = jnp.zeros_like(joint)
-    own_accum = jnp.zeros((rows_here, head_width), jnp.float32)
-    for part, stat in zip(parts, part_stats):
-        factor = jnp.exp(stat[:, :heads_here] - joint)
-        own_total = own_total + stat[:, heads_here:] * factor
-        own_accum = own_accum + part[:, :head_width].astype(jnp.float32) * jnp.repeat(
-            factor, HD, axis=1
-        )
-    summary = (own_accum / jnp.repeat(own_total, HD, axis=1)).astype(jnp.bfloat16)
+    summary = merge_parts(parts, head_width, heads_here)
     if paired:
         latent_terms = jnp.dot(
             summary, ordered_columns(w_latent_out, "head"), preferred_element_type=jnp.float32

time: 128 us -> 113 us (0.88)
  local copies, waits for them, and re-layouts: 24.6 us -> 7.46 us
  Pallas kernels: 42 us -> 46.1 us
  other arithmetic: 15.2 us -> 12.6 us
  starting transfers between devices: 16.6 us -> 18 us
    reshape x5 -> x0, local copies, waits for them, and re-layouts: 8.94 us -> none  [the longest x4 7.15 us: per_device(): jnp.repeat(factor, HD, axis=1)]
    pallas_call x0 -> x1, Pallas kernels: none -> 4.09 us  [merge_parts(): pl.pallas_call(functools.partial(merge_kernel, heads=heads), out_shape=ja...]
    exp x4 -> x0, local copies, waits for them, and re-layouts: 3.91 us -> none  [per_device(): factor = jnp.exp(stat[:, :heads_here] - joint)]
    broadcast_in_dim x5 -> x0, local copies, waits for them, and re-layouts: 3.7 us -> none  [the longest x4 2.96 us: per_device(): jnp.repeat(factor, HD, axis=1)]
    ppermute x3, waiting for transfers between devices: 12.5 us -> 8.88 us  [exchange_rows(): parts.append(lax.ppermute(block, axis, pairs))]
    ppermute x3, waiting for transfers between devices: 2.34 us -> 5.46 us  [cross_chip_sum(): total = total + lax.ppermute(chip_sums[d], axis, pairs).astype(jnp.float32)]
    add x5 -> x0, other arithmetic: 2.41 us -> none  [the longest x4 1.47 us: stats_of(): return pieces[0] + pieces[1] + pieces[2]]
  transfers between devices with their start and end apart: 11 -> 11, of which waited for: 5 -> 5; matrix products, arithmetic and copies ran while one was open for 25% -> 12% of each run, Pallas kernels for 23% -> 30%
where the time goes in v11:
time: 113 us; the launch traced here: 112 us
  Pallas kernels  46.1 us (41%)
  starting transfers between devices  18 us (16%)
  waiting for transfers between devices  16.4 us (15%)
  other arithmetic  12.6 us (11%)
  matrix products  10.2 us (9%)
  local copies, waits for them, and re-layouts  7.46 us (7%)
  between operations  1.6 us (1%)
    pallas_call x2, Pallas kernels, window_attention(): pl.pallas_call(kernel, cost_estimate=cost, out_shape=jax.ShapeDtypeStruct...  25 us
    pallas_call x1, Pallas kernels, latent_attention(): pl.pallas_call(kernel, cost_estimate=cost, out_shape=(jax.ShapeDtypeStruc...  17 us
    ppermute x3, waiting for transfers between devices, exchange_rows(): parts.append(lax.ppermute(block, axis, pairs))  8.88 us
    dot_general x4, matrix products, project(): jnp.dot(source, weight, preferred_element_type=jnp.float32)  8.74 us
    ppermute x3, starting transfers between devices, exchange_rows(): parts.append(lax.ppermute(block, axis, pairs))  6.48 us
    ppermute x1, starting transfers between devices, halos(): lax.ppermute(tail, axis, forward)  5.87 us
    ppermute x3, waiting for transfers between devices, cross_chip_sum(): total = total + lax.ppermute(chip_sums[d], axis, pairs).astype(jnp.float32)  5.46 us
    convert_element_type x3, other arithmetic, chip_pair_sums(): (blocks[chips + d].astype(jnp.float32) + received[d].astype(jnp.float32))...  5.1 us
  transfers between devices with their start and end apart: 11, of which 5 were waited for; matrix products, arithmetic and copies ran while one was open for 12% of the time, Pallas kernels for 30%

profile of v11, /device:TPU:0, one launch (start us, length us, event | category | flops | bytes accessed | tf_op | source)
XLA Modules:
  0.0 112.3 jit_solution(5598931070112789609)
XLA Ops:
  0.7 3.7 %convolution_convert_fusion.v_ref = bf16[2048,256]{1,0:T(8,128)(2,1)S(1)} fusion(bf16[2048,1024]{1,0:T(8,128)(2,1)} %param.19, bf16[1024,256]{1,0:T(8,128)(2,1)} %param.24), kind=kOutput, calls=%fused_computation | convolution fusion | flops 1074266112 | bytes 5767168 | tf_op jit(solution)/shard_map/dot_general | solution.py:25
  4.5 1.3 %convolution_convert_fusion.1.k_ref = bf16[2048,256]{1,0:T(8,128)(2,1)S(1)} fusion(bf16[2048,1024]{1,0:T(8,128)(2,1)S(1)} %copy-done.15, bf16[1024,256]{1,0:T(8,128)(2,1)S(1)} %copy-done.16), kind=kOutput, calls=%fused_computation.1 | convolution fusion | flops 1074266112 | bytes 5767168 | tf_op jit(solution)/shard_map/dot_general | solution.py:25
  5.9 1.4 %collective-permute-start.1 = (bf16[256,512]{1,0:T(8,128)(2,1)S(1)}, bf16[256,512]{1,0:T(8,128)(2,1)S(1)}, u32[]{:S(2)}, u32[]{:S(2)}) collective-permute-start(bf16[256,512]{1,0:T(8,128)(2,1)S(1)} %pad_maximum_fusion.4), channel_id=1, source_target_pairs={{4,0},{8,4},{12,8},{5,1},{9,5},{13,9},{6,2},{10,6},{14,10},{7,3},{... | collective-permute-start | bytes 786440 | tf_op jit(solution)/shard_map/ppermute | solution.py:21
  8.1 5.9 %collective-permute-start = (bf16[256,512]{1,0:T(8,128)(2,1)}, bf16[256,512]{1,0:T(8,128)(2,1)S(1)}, u32[]{:S(2)}, u32[]{:S(2)}) collective-permute-start(bf16[256,512]{1,0:T(8,128)(2,1)} %pad_maximum_fusion.3), channel_id=1, source_target_pairs={{0,4},{4,8},{8,12},{1,5},{5,9},{9,13},{2,6},{6,10},{10,14},{3,7},{... | collective-permute-start | bytes 786440 | tf_op jit(solution)/shard_map/ppermute | solution.py:21
  14.0 2.3 %convolution_convert_fusion.2.q_ref = bf16[2048,256]{1,0:T(8,128)(2,1)} fusion(bf16[2048,1024]{1,0:T(8,128)(2,1)S(1)} %copy-done.15, bf16[1024,256]{1,0:T(8,128)(2,1)S(1)} %copy-done.17), kind=kOutput, calls=%fused_computation.2 | convolution fusion | flops 1074266112 | bytes 5767168 | tf_op jit(solution)/shard_map/dot_general | solution.py:25
  17.0 0.9 pad_maximum_fusion.2.w_ref
  17.9 1.7 %collective-permute-done.low_ref = bf16[256,512]{1,0:T(8,128)(2,1)S(1)} collective-permute-done((bf16[256,512]{1,0:T(8,128)(2,1)}, bf16[256,512]{1,0:T(8,128)(2,1)S(1)}, u32[]{:S(2)}, u32[]{:S(2)}) %collective-permute-start) | collective-permute-done | bytes 262176 | tf_op jit(solution)/shard_map/ppermute | solution.py:21
  20.3 12.5 %shard_map.122 = bf16[4,1024,256]{2,1,0:T(8,128)(2,1)} custom-call(s32[3]{0:T(128)} %copy-done.13, bf16[2048,256]{1,0:T(8,128)(2,1)} %convolution_convert_fusion.2.q_ref, bf16[2048,256]{1,0:T(8,128)(2,1)} %copy-done.4, bf16[2048,256]{1,0:T(8,128)(2,1)} %copy-done.3, bf16[256,512]{1,0:T(8,128)(2,1)} %copy-done.7, bf16[256,512]{1,0:T(8,128)(2,1)} %copy-done.6, ...), custom_call_target="tpu_custom_call" | custom-call | flops 1342177280 | bytes 5767168 | tf_op jit(solution)/shard_map/pallas_call | solution.py:93
  32.9 1.3 %slice.128 = bf16[2,1024,256]{2,1,0:T(8,128)(2,1)S(1)} slice(bf16[4,1024,256]{2,1,0:T(8,128)(2,1)} %shard_map.122), slice={[0:2], [0:1024], [0:256]} | slice | bytes 2097152 | tf_op jit(solution)/shard_map/slice | solution.py:229
  34.8 12.5 %shard_map.123 = bf16[4,1024,256]{2,1,0:T(8,128)(2,1)} custom-call(s32[3]{0:T(128)} %copy-done.14, bf16[2048,256]{1,0:T(8,128)(2,1)} %convolution_convert_fusion.2.q_ref, bf16[2048,256]{1,0:T(8,128)(2,1)} %copy-done.4, bf16[2048,256]{1,0:T(8,128)(2,1)} %copy-done.3, bf16[256,512]{1,0:T(8,128)(2,1)} %copy-done.7, bf16[256,512]{1,0:T(8,128)(2,1)} %copy-done.6, ...), custom_call_target="tpu_custom_call" | custom-call | flops 1342177280 | bytes 5767168 | tf_op jit(solution)/shard_map/pallas_call | solution.py:93
  47.3 2.8 %fusion.1 = (bf16[1024,256]{1,0:T(8,128)(2,1)}, bf16[1024,256]{1,0:T(8,128)(2,1)S(1)}) fusion(bf16[2,1024,256]{2,1,0:T(8,128)(2,1)} %collective-permute-done.2, bf16[4,1024,256]{2,1,0:T(8,128)(2,1)} %shard_map.122), kind=kLoop, calls=%fused_computation.14 | loop fusion | flops 2097152 | bytes 3145728 | tf_op jit(solution)/shard_map/convert_element_type | solution.py:231
  50.1 1.0 slice.113
  51.6 1.5 %convolution_convert_fusion.4.q_ref = bf16[1024,256]{1,0:T(8,128)(2,1)} fusion(bf16[1024,1024]{1,0:T(8,128)(2,1)S(1)} %copy-done, bf16[1024,256]{1,0:T(8,128)(2,1)S(1)} %copy-done.18), kind=kOutput, calls=%fused_computation.4 | convolution fusion | flops 537133056 | bytes 3145728 | tf_op jit(solution)/shard_map/dot_general | solution.py:25
  53.1 17.0 %shard_map.124 = (f32[1024,256]{1,0:T(8,128)}, f32[1024,128]{1,0:T(8,128)}) custom-call(s32[1]{0:T(128)} %bitcast.6.scal_ref, bf16[1024,256]{1,0:T(8,128)(2,1)} %convolution_convert_fusion.4.q_ref, bf16[2048,256]{1,0:T(8,128)(2,1)} %copy-done.4, bf16[2048,256]{1,0:T(8,128)(2,1)} %copy-done.3), custom_call_target="tpu_custom_call" | custom-call | flops 2147483648 | bytes 4194304 | tf_op jit(solution)/shard_map/pallas_call | solution.py:153
  70.1 1.3 %convert_element_type.163 = bf16[1024,256]{1,0:T(8,128)(2,1)S(1)} convert(f32[1024,256]{1,0:T(8,128)} %get-tuple-element.65) | non-fusion elementwise | flops 262144 | bytes 1572864 | tf_op jit(solution)/shard_map/convert_element_type | solution.py:353
  71.9 1.2 %copy-done.2 = bf16[4,1024,256]{2,1,0:T(8,128)(2,1)S(1)} copy-done((bf16[4,1024,256]{2,1,0:T(8,128)(2,1)S(1)}, bf16[4,1024,256]{2,1,0:T(8,128)(2,1)}, u32[]{:S(2)}) %copy-start.2) | copy-done | bytes 2097176
  73.0 2.3 %fusion.3 = (bf16[1024,256]{1,0:T(8,128)(2,1)}, bf16[1024,256]{1,0:T(8,128)(2,1)S(1)}) fusion(bf16[2,1024,256]{2,1,0:T(8,128)(2,1)} %collective-permute-done.4, bf16[4,1024,256]{2,1,0:T(8,128)(2,1)S(1)} %copy-done.2), kind=kLoop, calls=%fused_computation.16 | loop fusion | flops 2097152 | bytes 3145728 | tf_op jit(solution)/shard_map/convert_element_type | solution.py:231
  75.3 0.8 constant_dynamic-slice_fusion.3
  76.1 2.4 %collective-permute-start.6 = (bf16[256,280]{1,0:T(8,128)(2,1)S(1)}, bf16[256,280]{1,0:T(8,128)(2,1)S(1)}, u32[]{:S(2)}, u32[]{:S(2)}) collective-permute-start(bf16[256,280]{1,0:T(8,128)(2,1)S(1)} %get-tuple-element.83), channel_id=1, source_target_pairs={{0,4},{4,8},{8,12},{12,0},{1,5},{5,9},{9,13},{13,1},{2,6},{6,10},{... | collective-permute-start | bytes 430088 | tf_op jit(solution)/shard_map/ppermute | solution.py:272
  78.5 2.8 %collective-permute-start.7 = (bf16[256,280]{1,0:T(8,128)(2,1)S(1)}, bf16[256,280]{1,0:T(8,128)(2,1)S(1)}, u32[]{:S(2)}, u32[]{:S(2)}) collective-permute-start(bf16[256,280]{1,0:T(8,128)(2,1)S(1)} %get-tuple-element.82), channel_id=1, source_target_pairs={{0,8},{4,12},{8,0},{12,4},{1,9},{5,13},{9,1},{13,5},{2,10},{6,14},... | collective-permute-start | bytes 430088 | tf_op jit(solution)/shard_map/ppermute | solution.py:272
  81.2 1.3 %collective-permute-start.8 = (bf16[256,280]{1,0:T(8,128)(2,1)S(1)}, bf16[256,280]{1,0:T(8,128)(2,1)S(1)}, u32[]{:S(2)}, u32[]{:S(2)}) collective-permute-start(bf16[256,280]{1,0:T(8,128)(2,1)S(1)} %get-tuple-element.81), channel_id=1, source_target_pairs={{0,12},{4,0},{8,4},{12,8},{1,13},{5,1},{9,5},{13,9},{2,14},{6,2},{... | collective-permute-start | bytes 430088 | tf_op jit(solution)/shard_map/ppermute | solution.py:272
  82.6 0.8 constant_dynamic-slice_fusion.2
  83.4 1.5 %collective-permute-start.3 = (bf16[1024,256]{1,0:T(8,128)(2,1)}, bf16[1024,256]{1,0:T(8,128)(2,1)}, u32[]{:S(2)}, u32[]{:S(2)}) collective-permute-start(bf16[1024,256]{1,0:T(8,128)(2,1)} %get-tuple-element.61), channel_id=1, source_target_pairs={{0,2},{1,3},{2,0},{3,1},{4,6},{5,7},{6,4},{7,5},{8,10},{9,11},{10,... | collective-permute-start | bytes 1572872 | tf_op jit(solution)/shard_map/ppermute | solution.py:244
  85.5 1.1 collective-permute-done.6.refs_1_
  86.5 7.8 %collective-permute-done.7.refs_2_ = bf16[256,280]{1,0:T(8,128)(2,1)S(1)} collective-permute-done((bf16[256,280]{1,0:T(8,128)(2,1)S(1)}, bf16[256,280]{1,0:T(8,128)(2,1)S(1)}, u32[]{:S(2)}, u32[]{:S(2)}) %collective-permute-start.7) | collective-permute-done | bytes 143392 | tf_op jit(solution)/shard_map/ppermute | solution.py:272
  95.1 4.1 %shard_map.125 = bf16[256,256]{1,0:T(8,128)(2,1)} custom-call(bf16[256,280]{1,0:T(8,128)(2,1)} %get-tuple-element.84.refs_0_, bf16[256,280]{1,0:T(8,128)(2,1)} %copy-done.10, bf16[256,280]{1,0:T(8,128)(2,1)} %copy-done.11, bf16[256,280]{1,0:T(8,128)(2,1)} %copy-done.12), custom_call_target="tpu_custom_call" | custom-call | tf_op jit(solution)/shard_map/pallas_call | solution.py:304
  99.2 1.5 %convolution_convert_fusion.3 = bf16[256,1024]{1,0:T(8,128)(2,1)S(1)} fusion(bf16[256,256]{1,0:T(8,128)(2,1)} %shard_map.125, bf16[256,256]{1,0:T(8,128)(2,1)} %get-tuple-element.89, bf16[256,256]{1,0:T(8,128)(2,1)} %get-tuple-element.90, bf16[256,256]{1,0:T(8,128)(2,1)} %get-tuple-element.88, bf16[256,256]{1,0:T(8,128)(2,1)} %get-tuple-element.87), kind=kOutput, calls=%fused_computation.3 | convolution fusion | flops 136577024 | bytes 1179648 | tf_op jit(solution)/shard_map/dot_general | solution.py:364
  100.8 1.2 %add_convert_fusion.3 = bf16[1024,256]{1,0:T(8,128)(2,1)S(1)} fusion(bf16[1024,256]{1,0:T(8,128)(2,1)} %collective-permute-done.3, bf16[1024,256]{1,0:T(8,128)(2,1)S(1)} %get-tuple-element.60), kind=kLoop, calls=%fused_computation.9 | loop fusion | flops 1048576 | bytes 1572864 | tf_op jit(solution)/shard_map/convert_element_type | solution.py:245
  102.4 1.6 %collective-permute-start.10 = (bf16[256,256]{1,0:T(8,128)(2,1)S(1)}, bf16[256,256]{1,0:T(8,128)(2,1)S(1)}, u32[]{:S(2)}, u32[]{:S(2)}) collective-permute-start(bf16[256,256]{1,0:T(8,128)(2,1)S(1)} %fusion.12), channel_id=1, source_target_pairs={{0,2},{1,3},{2,0},{3,1},{4,6},{5,7},{6,4},{7,5},{8,10},{9,11},{10,... | collective-permute-start | bytes 393224 | tf_op jit(solution)/shard_map/ppermute | solution.py:244
  103.9 5.5 %collective-permute-done.5 = bf16[1024,256]{1,0:T(8,128)(2,1)} collective-permute-done((bf16[1024,256]{1,0:T(8,128)(2,1)}, bf16[1024,256]{1,0:T(8,128)(2,1)}, u32[]{:S(2)}, u32[]{:S(2)}) %collective-permute-start.5) | collective-permute-done | bytes 524320 | tf_op jit(solution)/shard_map/ppermute | solution.py:244
  109.4 1.2 %add_convert_fusion = bf16[1024,256]{1,0:T(8,128)(2,1)S(1)} fusion(bf16[1024,256]{1,0:T(8,128)(2,1)} %collective-permute-done.5, bf16[1024,256]{1,0:T(8,128)(2,1)S(1)} %get-tuple-element.67), kind=kLoop, calls=%fused_computation.6 | loop fusion | flops 1048576 | bytes 1572864 | tf_op jit(solution)/shard_map/convert_element_type | solution.py:245
  110.5 1.0 pad_maximum_fusion
  (65 shorter events, 5.8 us)
Async XLA Ops:
  0.6 51.0 %copy-start = (bf16[1024,1024]{1,0:T(8,128)(2,1)S(1)}, bf16[1024,1024]{1,0:T(8,128)(2,1)}, u32[]{:S(2)}) copy-start(bf16[1024,1024]{1,0:T(8,128)(2,1)} %param.20) | copy-start | bytes 6291460
  0.6 3.8 %copy-start.15 = (bf16[2048,1024]{1,0:T(8,128)(2,1)S(1)}, bf16[2048,1024]{1,0:T(8,128)(2,1)}, u32[]{:S(2)}) copy-start(bf16[2048,1024]{1,0:T(8,128)(2,1)} %param.19) | copy-start | bytes 12582916
  0.7 3.9 %copy-start.16 = (bf16[1024,256]{1,0:T(8,128)(2,1)S(1)}, bf16[1024,256]{1,0:T(8,128)(2,1)}, u32[]{:S(2)}) copy-start(bf16[1024,256]{1,0:T(8,128)(2,1)} %param.23) | copy-start | bytes 1572868
  4.5 1.3 %copy-start.3 = (bf16[2048,256]{1,0:T(8,128)(2,1)}, bf16[2048,256]{1,0:T(8,128)(2,1)S(1)}, u32[]{:S(2)}) copy-start(bf16[2048,256]{1,0:T(8,128)(2,1)S(1)} %convolution_convert_fusion.v_ref) | copy-start | bytes 3145732
  5.8 10.4 %copy-start.4 = (bf16[2048,256]{1,0:T(8,128)(2,1)}, bf16[2048,256]{1,0:T(8,128)(2,1)S(1)}, u32[]{:S(2)}) copy-start(bf16[2048,256]{1,0:T(8,128)(2,1)S(1)} %convolution_convert_fusion.1.k_ref) | copy-start | bytes 3145732
  5.8 8.1 %copy-start.17 = (bf16[1024,256]{1,0:T(8,128)(2,1)S(1)}, bf16[1024,256]{1,0:T(8,128)(2,1)}, u32[]{:S(2)}) copy-start(bf16[1024,256]{1,0:T(8,128)(2,1)} %param.22) | copy-start | bytes 1572868
  5.9 12.0 %collective-permute-start.1 = (bf16[256,512]{1,0:T(8,128)(2,1)S(1)}, bf16[256,512]{1,0:T(8,128)(2,1)S(1)}, u32[]{:S(2)}, u32[]{:S(2)}) collective-permute-start(bf16[256,512]{1,0:T(8,128)(2,1)S(1)} %pad_maximum_fusion.4), channel_id=1, source_target_pairs={{4,0},{8,4},{12,8},{5,1},{9,5},{13,9},{6,2},{10,6},{14,10},{7,3},{... | collective-permute-start | bytes 786440 | tf_op jit(solution)/shard_map/ppermute | solution.py:21
  8.1 8.8 %copy-start.8 = (bf16[256,1024]{1,0:T(8,128)(2,1)S(1)}, bf16[256,1024]{1,0:T(8,128)(2,1)}, u32[]{:S(2)}) copy-start(bf16[256,1024]{1,0:T(8,128)(2,1)} %param.25) | copy-start | bytes 1572868
  8.1 11.5 %collective-permute-start = (bf16[256,512]{1,0:T(8,128)(2,1)}, bf16[256,512]{1,0:T(8,128)(2,1)S(1)}, u32[]{:S(2)}, u32[]{:S(2)}) collective-permute-start(bf16[256,512]{1,0:T(8,128)(2,1)} %pad_maximum_fusion.3), channel_id=1, source_target_pairs={{0,4},{4,8},{8,12},{1,5},{5,9},{9,13},{2,6},{6,10},{10,14},{3,7},{... | collective-permute-start | bytes 786440 | tf_op jit(solution)/shard_map/ppermute | solution.py:21
  16.9 2.7 %copy-start.13 = (s32[3]{0:T(128)}, s32[3]{0:T(128)S(1)}, u32[]{:S(2)}) copy-start(s32[3]{0:T(128)S(1)} %constant_dynamic-update-slice_fusion.2.scal_ref) | copy-start | bytes 40
  17.9 1.7 %copy-start.6 = (bf16[256,512]{1,0:T(8,128)(2,1)}, bf16[256,512]{1,0:T(8,128)(2,1)S(1)}, u32[]{:S(2)}) copy-start(bf16[256,512]{1,0:T(8,128)(2,1)S(1)} %collective-permute-done.1.high_ref) | copy-start | bytes 786436
  19.6 0.7 copy-start.7
  32.9 1.4 %copy-start.19 = (s32[3]{0:T(128)S(1)}, s32[3]{0:T(128)}, u32[]{:S(2)}) copy-start(s32[3]{0:T(128)} %constant.165.clone) | copy-start | bytes 40
  34.2 13.1 %collective-permute-start.2 = (bf16[2,1024,256]{2,1,0:T(8,128)(2,1)S(1)}, bf16[2,1024,256]{2,1,0:T(8,128)(2,1)}, u32[]{:S(2)}, u32[]{:S(2)}) collective-permute-start(bf16[2,1024,256]{2,1,0:T(8,128)(2,1)S(1)} %slice.128), channel_id=1, source_target_pairs={{0,1},{1,0},{2,3},{3,2},{4,5},{5,4},{6,7},{7,6},{8,9},{9,8},{10,11... | collective-permute-start | bytes 3145736 | tf_op jit(solution)/shard_map/ppermute | solution.py:229
  34.3 0.5 copy-start.14
  47.3 2.8 %copy-start.1 = (bf16[4,1024,256]{2,1,0:T(8,128)(2,1)S(1)}, bf16[4,1024,256]{2,1,0:T(8,128)(2,1)}, u32[]{:S(2)}) copy-start(bf16[4,1024,256]{2,1,0:T(8,128)(2,1)} %shard_map.123) | copy-start | bytes 6291460
  47.3 4.3 %copy-start.18 = (bf16[1024,256]{1,0:T(8,128)(2,1)S(1)}, bf16[1024,256]{1,0:T(8,128)(2,1)}, u32[]{:S(2)}) copy-start(bf16[1024,256]{1,0:T(8,128)(2,1)} %param.26) | copy-start | bytes 1572868
  51.1 20.7 %collective-permute-start.4 = (bf16[2,1024,256]{2,1,0:T(8,128)(2,1)}, bf16[2,1024,256]{2,1,0:T(8,128)(2,1)}, u32[]{:S(2)}, u32[]{:S(2)}) collective-permute-start(bf16[2,1024,256]{2,1,0:T(8,128)(2,1)} %slice.113), channel_id=1, source_target_pairs={{0,1},{1,0},{2,3},{3,2},{4,5},{5,4},{6,7},{7,6},{8,9},{9,8},{10,11... | collective-permute-start | bytes 3145736 | tf_op jit(solution)/shard_map/ppermute | solution.py:229
  70.1 1.4 %copy-start.5 = (f32[1024,128]{1,0:T(8,128)S(1)}, f32[1024,128]{1,0:T(8,128)}, u32[]{:S(2)}) copy-start(f32[1024,128]{1,0:T(8,128)} %get-tuple-element.66) | copy-start | bytes 1572868
  71.4 1.6 %copy-start.2 = (bf16[4,1024,256]{2,1,0:T(8,128)(2,1)S(1)}, bf16[4,1024,256]{2,1,0:T(8,128)(2,1)}, u32[]{:S(2)}) copy-start(bf16[4,1024,256]{2,1,0:T(8,128)(2,1)} %shard_map.123) | copy-start | bytes 6291460
  71.8 10.7 %copy-start.9 = (bf16[256,1024]{1,0:T(8,128)(2,1)S(1)}, bf16[256,1024]{1,0:T(8,128)(2,1)}, u32[]{:S(2)}) copy-start(bf16[256,1024]{1,0:T(8,128)(2,1)} %param.27) | copy-start | bytes 1572868
  76.1 10.4 %collective-permute-start.6 = (bf16[256,280]{1,0:T(8,128)(2,1)S(1)}, bf16[256,280]{1,0:T(8,128)(2,1)S(1)}, u32[]{:S(2)}, u32[]{:S(2)}) collective-permute-start(bf16[256,280]{1,0:T(8,128)(2,1)S(1)} %get-tuple-element.83), channel_id=1, source_target_pairs={{0,4},{4,8},{8,12},{12,0},{1,5},{5,9},{9,13},{13,1},{2,6},{6,10},{... | collective-permute-start | bytes 430088 | tf_op jit(solution)/shard_map/ppermute | solution.py:272
  78.5 15.9 %collective-permute-start.7 = (bf16[256,280]{1,0:T(8,128)(2,1)S(1)}, bf16[256,280]{1,0:T(8,128)(2,1)S(1)}, u32[]{:S(2)}, u32[]{:S(2)}) collective-permute-start(bf16[256,280]{1,0:T(8,128)(2,1)S(1)} %get-tuple-element.82), channel_id=1, source_target_pairs={{0,8},{4,12},{8,0},{12,4},{1,9},{5,13},{9,1},{13,5},{2,10},{6,14},... | collective-permute-start | bytes 430088 | tf_op jit(solution)/shard_map/ppermute | solution.py:272
  81.2 13.1 %collective-permute-start.8 = (bf16[256,280]{1,0:T(8,128)(2,1)S(1)}, bf16[256,280]{1,0:T(8,128)(2,1)S(1)}, u32[]{:S(2)}, u32[]{:S(2)}) collective-permute-start(bf16[256,280]{1,0:T(8,128)(2,1)S(1)} %get-tuple-element.81), channel_id=1, source_target_pairs={{0,12},{4,0},{8,4},{12,8},{1,13},{5,1},{9,5},{13,9},{2,14},{6,2},{... | collective-permute-start | bytes 430088 | tf_op jit(solution)/shard_map/ppermute | solution.py:272
  83.4 17.4 %collective-permute-start.3 = (bf16[1024,256]{1,0:T(8,128)(2,1)}, bf16[1024,256]{1,0:T(8,128)(2,1)}, u32[]{:S(2)}, u32[]{:S(2)}) collective-permute-start(bf16[1024,256]{1,0:T(8,128)(2,1)} %get-tuple-element.61), channel_id=1, source_target_pairs={{0,2},{1,3},{2,0},{3,1},{4,6},{5,7},{6,4},{7,5},{8,10},{9,11},{10,... | collective-permute-start | bytes 1572872 | tf_op jit(solution)/shard_map/ppermute | solution.py:244
  84.9 24.5 %collective-permute-start.5 = (bf16[1024,256]{1,0:T(8,128)(2,1)}, bf16[1024,256]{1,0:T(8,128)(2,1)}, u32[]{:S(2)}, u32[]{:S(2)}) collective-permute-start(bf16[1024,256]{1,0:T(8,128)(2,1)} %get-tuple-element.68), channel_id=1, source_target_pairs={{0,2},{1,3},{2,0},{3,1},{4,6},{5,7},{6,4},{7,5},{8,10},{9,11},{10,... | collective-permute-start | bytes 1572872 | tf_op jit(solution)/shard_map/ppermute | solution.py:244
  86.5 8.5 %copy-start.10 = (bf16[256,280]{1,0:T(8,128)(2,1)}, bf16[256,280]{1,0:T(8,128)(2,1)S(1)}, u32[]{:S(2)}) copy-start(bf16[256,280]{1,0:T(8,128)(2,1)S(1)} %collective-permute-done.6.refs_1_) | copy-start | bytes 430084
  94.3 0.8 copy-start.11
  94.3 0.7 copy-start.12
  100.7 1.6 %collective-permute-start.9 = (bf16[2,256,256]{2,1,0:T(8,128)(2,1)S(1)}, bf16[2,256,256]{2,1,0:T(8,128)(2,1)S(1)}, u32[]{:S(2)}, u32[]{:S(2)}) collective-permute-start(bf16[2,256,256]{2,1,0:T(8,128)(2,1)S(1)} %pad_maximum_fusion.5), channel_id=1, source_target_pairs={{0,1},{1,0},{2,3},{3,2},{4,5},{5,4},{6,7},{7,6},{8,9},{9,8},{10,11... | collective-permute-start | bytes 786440 | tf_op jit(solution)/shard_map/ppermute | solution.py:229
  102.4 9.2 %collective-permute-start.10 = (bf16[256,256]{1,0:T(8,128)(2,1)S(1)}, bf16[256,256]{1,0:T(8,128)(2,1)S(1)}, u32[]{:S(2)}, u32[]{:S(2)}) collective-permute-start(bf16[256,256]{1,0:T(8,128)(2,1)S(1)} %fusion.12), channel_id=1, source_target_pairs={{0,2},{1,3},{2,0},{3,1},{4,6},{5,7},{6,4},{7,5},{8,10},{9,11},{10,... | collective-permute-start | bytes 393224 | tf_op jit(solution)/shard_map/ppermute | solution.py:244

commit v12 on v11

--- a/solution.py
+++ b/solution.py
@@ -328,26 +328,33 @@
     head_devices = lax.axis_size("head")
     paired = head_devices % 2 == 0
     w_ordered = ordered_columns(w_out, "head")
-    parts = [
-        window_attention(
+    def window_chunk(c, query, keyed, valued, low, high):
+        return window_attention(
             query, keyed, valued, low, high, w_ordered, first_frame, length,
             c * chunk_rows, chunk_rows, head_devices,
         )
-        for c in range(chunks)
-    ]
+
     latent_count = latents.shape[0]
     latent_query = project(latents, w_latent_query)
     valid_count = jnp.clip(length - first_frame, 0, frame_count)
-    frame_parts = []
-    if paired:
-        first_sums = chip_pair_sums(parts[0], "head")
-        first_sums, rest, keyed, valued = lax.optimization_barrier(
-            (first_sums, parts[1:], keyed, valued)
+    if paired and chunks == 2:
+        first = window_chunk(0, query, keyed, valued, low, high)
+        first_sums = chip_pair_sums(first, "head")
+        first_sums, query, keyed, valued, low, high = lax.optimization_barrier(
+            (first_sums, query, keyed, valued, low, high)
         )
-        frame_parts.append(cross_chip_sum(first_sums, "head"))
-        rest_sums = [chip_pair_sums(blocks, "head") for blocks in rest]
+        first_out = cross_chip_sum(first_sums, "head")
+        second = window_chunk(1, query, keyed, valued, low, high)
+        rest_sums = [chip_pair_sums(second, "head")]
+        first_out, keyed, valued = lax.optimization_barrier((first_out, keyed, valued))
+        frame_parts = [first_out]
     else:
-        frame_parts = [plain_block_sum(blocks, "head") for blocks in parts]
+        parts = [window_chunk(c, query, keyed, valued, low, high) for c in range(chunks)]
+        if paired:
+            rest_sums = [chip_pair_sums(blocks, "head") for blocks in parts]
+            frame_parts = []
+        else:
+            frame_parts = [plain_block_sum(blocks, "head") for blocks in parts]
     peaks, totals, local_accum = latent_attention(latent_query, keyed, valued, valid_count)
     payload = jnp.concatenate(
         [local_accum.astype(jnp.bfloat16)] + split_three(jnp.concatenate([peaks, totals], axis=1)),

time: 113 us -> 115 us (1.018); the launches traced: 112 us -> 113 us
  waiting for transfers between devices: 16.4 us -> 19.5 us
  other arithmetic: 12.6 us -> 10 us
  starting transfers between devices: 18 us -> 16.6 us
  local copies, waits for them, and re-layouts: 7.46 us -> 8.83 us
    ppermute x3, waiting for transfers between devices: 0.34 us -> 4.17 us  [chip_pair_sums(): received = lax.ppermute(blocks[:chips], axis, swap)]
    ppermute x3, waiting for transfers between devices: 5.46 us -> 2.8 us  [cross_chip_sum(): total = total + lax.ppermute(chip_sums[d], axis, pairs).astype(jnp.float32)]
    convert_element_type x3, other arithmetic: 5.1 us -> 2.61 us  [chip_pair_sums(): (blocks[chips + d].astype(jnp.float32) + received[d].astype(jnp.float32))...]
    ppermute x3, waiting for transfers between devices: 8.88 us -> 10.8 us  [exchange_rows(): parts.append(lax.ppermute(block, axis, pairs))]
    slice x2, local copies, waits for them, and re-layouts: 2.34 us -> 3.76 us  [chip_pair_sums(): received = lax.ppermute(blocks[:chips], axis, swap)]
  transfers between devices with their start and end apart: 11 -> 11, of which waited for: 5 -> 6; matrix products, arithmetic and copies ran while one was open for 12% -> 14% of each run, Pallas kernels for 30% -> 30%
where the time goes in v12:
time: 115 us; the launch traced here: 113 us
  Pallas kernels  46.1 us (40%)
  waiting for transfers between devices  19.5 us (17%)
  starting transfers between devices  16.6 us (14%)
  matrix products  10.2 us (9%)
  other arithmetic  10 us (9%)
  local copies, waits for them, and re-layouts  8.83 us (8%)
  between operations  1.59 us (1%)
    pallas_call x2, Pallas kernels, window_attention(): pl.pallas_call(kernel, cost_estimate=cost, out_shape=jax.ShapeDtypeStruct...  25 us
    pallas_call x1, Pallas kernels, latent_attention(): pl.pallas_call(kernel, cost_estimate=cost, out_shape=(jax.ShapeDtypeStruc...  17 us
    ppermute x3, waiting for transfers between devices, exchange_rows(): parts.append(lax.ppermute(block, axis, pairs))  10.8 us
    dot_general x4, matrix products, project(): jnp.dot(source, weight, preferred_element_type=jnp.float32)  8.74 us
    ppermute x3, starting transfers between devices, exchange_rows(): parts.append(lax.ppermute(block, axis, pairs))  6.31 us
    ppermute x1, starting transfers between devices, halos(): lax.ppermute(tail, axis, forward)  5.87 us
    ppermute x3, waiting for transfers between devices, chip_pair_sums(): received = lax.ppermute(blocks[:chips], axis, swap)  4.17 us
    pallas_call x1, Pallas kernels, merge_parts(): pl.pallas_call(functools.partial(merge_kernel, heads=heads), out_shape=ja...  4.09 us
  transfers between devices with their start and end apart: 11, of which 6 were waited for; matrix products, arithmetic and copies ran while one was open for 14% of the time, Pallas kernels for 30%

profile of v12, /device:TPU:0, one launch (start us, length us, event | category | flops | bytes accessed | tf_op | source)
XLA Modules:
  0.0 112.9 jit_solution(17563065628111140416)
XLA Ops:
  0.7 3.7 %convolution_convert_fusion.v_ref = bf16[2048,256]{1,0:T(8,128)(2,1)S(1)} fusion(bf16[2048,1024]{1,0:T(8,128)(2,1)} %param.19, bf16[1024,256]{1,0:T(8,128)(2,1)} %param.24), kind=kOutput, calls=%fused_computation | convolution fusion | flops 1074266112 | bytes 5767168 | tf_op jit(solution)/shard_map/dot_general | solution.py:25
  4.5 1.3 %convolution_convert_fusion.1.k_ref = bf16[2048,256]{1,0:T(8,128)(2,1)S(1)} fusion(bf16[2048,1024]{1,0:T(8,128)(2,1)S(1)} %copy-done.15, bf16[1024,256]{1,0:T(8,128)(2,1)S(1)} %copy-done.16), kind=kOutput, calls=%fused_computation.1 | convolution fusion | flops 1074266112 | bytes 5767168 | tf_op jit(solution)/shard_map/dot_general | solution.py:25
  5.9 1.4 %collective-permute-start.1 = (bf16[256,512]{1,0:T(8,128)(2,1)S(1)}, bf16[256,512]{1,0:T(8,128)(2,1)S(1)}, u32[]{:S(2)}, u32[]{:S(2)}) collective-permute-start(bf16[256,512]{1,0:T(8,128)(2,1)S(1)} %pad_maximum_fusion.4), channel_id=1, source_target_pairs={{4,0},{8,4},{12,8},{5,1},{9,5},{13,9},{6,2},{10,6},{14,10},{7,3},{... | collective-permute-start | bytes 786440 | tf_op jit(solution)/shard_map/ppermute | solution.py:21
  8.1 5.9 %collective-permute-start = (bf16[256,512]{1,0:T(8,128)(2,1)}, bf16[256,512]{1,0:T(8,128)(2,1)S(1)}, u32[]{:S(2)}, u32[]{:S(2)}) collective-permute-start(bf16[256,512]{1,0:T(8,128)(2,1)} %pad_maximum_fusion.3), channel_id=1, source_target_pairs={{0,4},{4,8},{8,12},{1,5},{5,9},{9,13},{2,6},{6,10},{10,14},{3,7},{... | collective-permute-start | bytes 786440 | tf_op jit(solution)/shard_map/ppermute | solution.py:21
  13.9 2.3 %convolution_convert_fusion.2.q_ref = bf16[2048,256]{1,0:T(8,128)(2,1)} fusion(bf16[2048,1024]{1,0:T(8,128)(2,1)S(1)} %copy-done.15, bf16[1024,256]{1,0:T(8,128)(2,1)S(1)} %copy-done.17), kind=kOutput, calls=%fused_computation.2 | convolution fusion | flops 1074266112 | bytes 5767168 | tf_op jit(solution)/shard_map/dot_general | solution.py:25
  17.0 0.9 pad_maximum_fusion.2.w_ref
  17.9 1.7 %collective-permute-done.low_ref = bf16[256,512]{1,0:T(8,128)(2,1)S(1)} collective-permute-done((bf16[256,512]{1,0:T(8,128)(2,1)}, bf16[256,512]{1,0:T(8,128)(2,1)S(1)}, u32[]{:S(2)}, u32[]{:S(2)}) %collective-permute-start) | collective-permute-done | bytes 262176 | tf_op jit(solution)/shard_map/ppermute | solution.py:21
  20.3 12.5 %shard_map.122 = bf16[4,1024,256]{2,1,0:T(8,128)(2,1)} custom-call(s32[3]{0:T(128)} %copy-done.13, bf16[2048,256]{1,0:T(8,128)(2,1)} %convolution_convert_fusion.2.q_ref, bf16[2048,256]{1,0:T(8,128)(2,1)} %copy-done.4, bf16[2048,256]{1,0:T(8,128)(2,1)} %copy-done.3, bf16[256,512]{1,0:T(8,128)(2,1)} %copy-done.7, bf16[256,512]{1,0:T(8,128)(2,1)} %copy-done.6, ...), custom_call_target="tpu_custom_call" | custom-call | flops 1342177280 | bytes 5767168 | tf_op jit(solution)/shard_map/pallas_call | solution.py:93
  32.8 1.4 %slice.128 = bf16[2,1024,256]{2,1,0:T(8,128)(2,1)S(1)} slice(bf16[4,1024,256]{2,1,0:T(8,128)(2,1)} %shard_map.122), slice={[0:2], [0:1024], [0:256]} | slice | bytes 2097152 | tf_op jit(solution)/shard_map/slice | solution.py:229
  34.3 2.6 %collective-permute-done.2 = bf16[2,1024,256]{2,1,0:T(8,128)(2,1)S(1)} collective-permute-done((bf16[2,1024,256]{2,1,0:T(8,128)(2,1)S(1)}, bf16[2,1024,256]{2,1,0:T(8,128)(2,1)S(1)}, u32[]{:S(2)}, u32[]{:S(2)}) %collective-permute-start.2) | collective-permute-done | bytes 1048608 | tf_op jit(solution)/shard_map/ppermute | solution.py:229
  37.3 1.7 %collective-permute-start.3 = (bf16[1024,256]{1,0:T(8,128)(2,1)S(1)}, bf16[1024,256]{1,0:T(8,128)(2,1)}, u32[]{:S(2)}, u32[]{:S(2)}) collective-permute-start(bf16[1024,256]{1,0:T(8,128)(2,1)S(1)} %get-tuple-element.66), channel_id=1, source_target_pairs={{0,2},{1,3},{2,0},{3,1},{4,6},{5,7},{6,4},{7,5},{8,10},{9,11},{10,... | collective-permute-start | bytes 1572872 | tf_op jit(solution)/shard_map/ppermute | solution.py:244
  39.5 12.5 %shard_map.123 = bf16[4,1024,256]{2,1,0:T(8,128)(2,1)} custom-call(s32[3]{0:T(128)} %copy-done.14, bf16[2048,256]{1,0:T(8,128)(2,1)} %convolution_convert_fusion.2.q_ref, bf16[2048,256]{1,0:T(8,128)(2,1)} %copy-done.4, bf16[2048,256]{1,0:T(8,128)(2,1)} %copy-done.3, bf16[256,512]{1,0:T(8,128)(2,1)} %copy-done.7, bf16[256,512]{1,0:T(8,128)(2,1)} %copy-done.6, ...), custom_call_target="tpu_custom_call" | custom-call | flops 1342177280 | bytes 5767168 | tf_op jit(solution)/shard_map/pallas_call | solution.py:93
  52.1 2.3 %slice.133 = bf16[2,1024,256]{2,1,0:T(8,128)(2,1)} slice(bf16[4,1024,256]{2,1,0:T(8,128)(2,1)} %shard_map.123), slice={[0:2], [0:1024], [0:256]} | slice | bytes 2097152 | tf_op jit(solution)/shard_map/slice | solution.py:229
  54.4 1.5 %convolution_convert_fusion.4.q_ref = bf16[1024,256]{1,0:T(8,128)(2,1)} fusion(bf16[1024,1024]{1,0:T(8,128)(2,1)S(1)} %copy-done, bf16[1024,256]{1,0:T(8,128)(2,1)S(1)} %copy-done.18), kind=kOutput, calls=%fused_computation.4 | convolution fusion | flops 537133056 | bytes 3145728 | tf_op jit(solution)/shard_map/dot_general | solution.py:25
  55.9 1.2 %add_convert_fusion.3 = bf16[1024,256]{1,0:T(8,128)(2,1)S(1)} fusion(bf16[1024,256]{1,0:T(8,128)(2,1)} %collective-permute-done.3, bf16[1024,256]{1,0:T(8,128)(2,1)S(1)} %get-tuple-element.65), kind=kLoop, calls=%fused_computation.9 | loop fusion | flops 1048576 | bytes 1572864 | tf_op jit(solution)/shard_map/convert_element_type | solution.py:245
  57.1 17.0 %shard_map.124 = (f32[1024,256]{1,0:T(8,128)}, f32[1024,128]{1,0:T(8,128)}) custom-call(s32[1]{0:T(128)} %bitcast.6.scal_ref, bf16[1024,256]{1,0:T(8,128)(2,1)} %convolution_convert_fusion.4.q_ref, bf16[2048,256]{1,0:T(8,128)(2,1)} %copy-done.4, bf16[2048,256]{1,0:T(8,128)(2,1)} %copy-done.3), custom_call_target="tpu_custom_call" | custom-call | flops 2147483648 | bytes 4194304 | tf_op jit(solution)/shard_map/pallas_call | solution.py:153
  74.1 1.3 %convert_element_type.163 = bf16[1024,256]{1,0:T(8,128)(2,1)S(1)} convert(f32[1024,256]{1,0:T(8,128)} %get-tuple-element.75) | non-fusion elementwise | flops 262144 | bytes 1572864 | tf_op jit(solution)/shard_map/convert_element_type | solution.py:360
  75.8 1.2 %copy-done.1 = bf16[4,1024,256]{2,1,0:T(8,128)(2,1)S(1)} copy-done((bf16[4,1024,256]{2,1,0:T(8,128)(2,1)S(1)}, bf16[4,1024,256]{2,1,0:T(8,128)(2,1)}, u32[]{:S(2)}) %copy-start.1) | copy-done | bytes 2097176
  77.0 2.3 %fusion.3 = (bf16[1024,256]{1,0:T(8,128)(2,1)}, bf16[1024,256]{1,0:T(8,128)(2,1)S(1)}) fusion(bf16[2,1024,256]{2,1,0:T(8,128)(2,1)} %collective-permute-done.4, bf16[4,1024,256]{2,1,0:T(8,128)(2,1)S(1)} %copy-done.1), kind=kLoop, calls=%fused_computation.16 | loop fusion | flops 2097152 | bytes 3145728 | tf_op jit(solution)/shard_map/convert_element_type | solution.py:231
  79.3 0.8 constant_dynamic-slice_fusion.3
  80.1 2.4 %collective-permute-start.6 = (bf16[256,280]{1,0:T(8,128)(2,1)S(1)}, bf16[256,280]{1,0:T(8,128)(2,1)S(1)}, u32[]{:S(2)}, u32[]{:S(2)}) collective-permute-start(bf16[256,280]{1,0:T(8,128)(2,1)S(1)} %get-tuple-element.93), channel_id=1, source_target_pairs={{0,4},{4,8},{8,12},{12,0},{1,5},{5,9},{9,13},{13,1},{2,6},{6,10},{... | collective-permute-start | bytes 430088 | tf_op jit(solution)/shard_map/ppermute | solution.py:272
  82.4 2.6 %collective-permute-start.7 = (bf16[256,280]{1,0:T(8,128)(2,1)S(1)}, bf16[256,280]{1,0:T(8,128)(2,1)S(1)}, u32[]{:S(2)}, u32[]{:S(2)}) collective-permute-start(bf16[256,280]{1,0:T(8,128)(2,1)S(1)} %get-tuple-element.92), channel_id=1, source_target_pairs={{0,8},{4,12},{8,0},{12,4},{1,9},{5,13},{9,1},{13,5},{2,10},{6,14},... | collective-permute-start | bytes 430088 | tf_op jit(solution)/shard_map/ppermute | solution.py:272
  85.0 1.3 %collective-permute-start.8 = (bf16[256,280]{1,0:T(8,128)(2,1)S(1)}, bf16[256,280]{1,0:T(8,128)(2,1)S(1)}, u32[]{:S(2)}, u32[]{:S(2)}) collective-permute-start(bf16[256,280]{1,0:T(8,128)(2,1)S(1)} %get-tuple-element.91), channel_id=1, source_target_pairs={{0,12},{4,0},{8,4},{12,8},{1,13},{5,1},{9,5},{13,9},{2,14},{6,2},{... | collective-permute-start | bytes 430088 | tf_op jit(solution)/shard_map/ppermute | solution.py:272
  86.4 0.8 constant_dynamic-slice_fusion.2
  87.7 2.6 %collective-permute-done.6.refs_1_ = bf16[256,280]{1,0:T(8,128)(2,1)S(1)} collective-permute-done((bf16[256,280]{1,0:T(8,128)(2,1)S(1)}, bf16[256,280]{1,0:T(8,128)(2,1)S(1)}, u32[]{:S(2)}, u32[]{:S(2)}) %collective-permute-start.6) | collective-permute-done | bytes 143392 | tf_op jit(solution)/shard_map/ppermute | solution.py:272
  90.4 8.2 %collective-permute-done.7.refs_2_ = bf16[256,280]{1,0:T(8,128)(2,1)S(1)} collective-permute-done((bf16[256,280]{1,0:T(8,128)(2,1)S(1)}, bf16[256,280]{1,0:T(8,128)(2,1)S(1)}, u32[]{:S(2)}, u32[]{:S(2)}) %collective-permute-start.7) | collective-permute-done | bytes 143392 | tf_op jit(solution)/shard_map/ppermute | solution.py:272
  99.3 4.1 %shard_map.125 = bf16[256,256]{1,0:T(8,128)(2,1)} custom-call(bf16[256,280]{1,0:T(8,128)(2,1)} %get-tuple-element.94.refs_0_, bf16[256,280]{1,0:T(8,128)(2,1)} %copy-done.10, bf16[256,280]{1,0:T(8,128)(2,1)} %copy-done.11, bf16[256,280]{1,0:T(8,128)(2,1)} %copy-done.12), custom_call_target="tpu_custom_call" | custom-call | tf_op jit(solution)/shard_map/pallas_call | solution.py:304
  103.4 1.5 %convolution_convert_fusion.3 = bf16[256,1024]{1,0:T(8,128)(2,1)S(1)} fusion(bf16[256,256]{1,0:T(8,128)(2,1)} %shard_map.125, bf16[256,256]{1,0:T(8,128)(2,1)} %get-tuple-element.99, bf16[256,256]{1,0:T(8,128)(2,1)} %get-tuple-element.100, bf16[256,256]{1,0:T(8,128)(2,1)} %get-tuple-element.98, bf16[256,256]{1,0:T(8,128)(2,1)} %get-tuple-element.97), kind=kOutput, calls=%fused_computation.3 | convolution fusion | flops 136577024 | bytes 1179648 | tf_op jit(solution)/shard_map/dot_general | solution.py:371
  105.0 1.5 %collective-permute-done.9 = bf16[2,256,256]{2,1,0:T(8,128)(2,1)S(1)} collective-permute-done((bf16[2,256,256]{2,1,0:T(8,128)(2,1)S(1)}, bf16[2,256,256]{2,1,0:T(8,128)(2,1)S(1)}, u32[]{:S(2)}, u32[]{:S(2)}) %collective-permute-start.9) | collective-permute-done | bytes 262176 | tf_op jit(solution)/shard_map/ppermute | solution.py:229
  107.2 1.2 %add_convert_fusion = bf16[1024,256]{1,0:T(8,128)(2,1)S(1)} fusion(bf16[1024,256]{1,0:T(8,128)(2,1)} %collective-permute-done.5, bf16[1024,256]{1,0:T(8,128)(2,1)S(1)} %get-tuple-element.77), kind=kLoop, calls=%fused_computation.6 | loop fusion | flops 1048576 | bytes 1572864 | tf_op jit(solution)/shard_map/convert_element_type | solution.py:245
  108.3 1.0 pad_maximum_fusion
  109.4 2.8 %collective-permute-done.10 = bf16[256,256]{1,0:T(8,128)(2,1)S(1)} collective-permute-done((bf16[256,256]{1,0:T(8,128)(2,1)S(1)}, bf16[256,256]{1,0:T(8,128)(2,1)S(1)}, u32[]{:S(2)}, u32[]{:S(2)}) %collective-permute-start.10) | collective-permute-done | bytes 131104 | tf_op jit(solution)/shard_map/ppermute | solution.py:244
  (65 shorter events, 5.8 us)
Async XLA Ops:
  0.6 53.8 %copy-start = (bf16[1024,1024]{1,0:T(8,128)(2,1)S(1)}, bf16[1024,1024]{1,0:T(8,128)(2,1)}, u32[]{:S(2)}) copy-start(bf16[1024,1024]{1,0:T(8,128)(2,1)} %param.20) | copy-start | bytes 6291460
  0.6 3.8 %copy-start.15 = (bf16[2048,1024]{1,0:T(8,128)(2,1)S(1)}, bf16[2048,1024]{1,0:T(8,128)(2,1)}, u32[]{:S(2)}) copy-start(bf16[2048,1024]{1,0:T(8,128)(2,1)} %param.19) | copy-start | bytes 12582916
  0.7 3.9 %copy-start.16 = (bf16[1024,256]{1,0:T(8,128)(2,1)S(1)}, bf16[1024,256]{1,0:T(8,128)(2,1)}, u32[]{:S(2)}) copy-start(bf16[1024,256]{1,0:T(8,128)(2,1)} %param.23) | copy-start | bytes 1572868
  4.5 1.3 %copy-start.3 = (bf16[2048,256]{1,0:T(8,128)(2,1)}, bf16[2048,256]{1,0:T(8,128)(2,1)S(1)}, u32[]{:S(2)}) copy-start(bf16[2048,256]{1,0:T(8,128)(2,1)S(1)} %convolution_convert_fusion.v_ref) | copy-start | bytes 3145732
  5.8 10.4 %copy-start.4 = (bf16[2048,256]{1,0:T(8,128)(2,1)}, bf16[2048,256]{1,0:T(8,128)(2,1)S(1)}, u32[]{:S(2)}) copy-start(bf16[2048,256]{1,0:T(8,128)(2,1)S(1)} %convolution_convert_fusion.1.k_ref) | copy-start | bytes 3145732
  5.8 8.1 %copy-start.17 = (bf16[1024,256]{1,0:T(8,128)(2,1)S(1)}, bf16[1024,256]{1,0:T(8,128)(2,1)}, u32[]{:S(2)}) copy-start(bf16[1024,256]{1,0:T(8,128)(2,1)} %param.22) | copy-start | bytes 1572868
  5.9 12.0 %collective-permute-start.1 = (bf16[256,512]{1,0:T(8,128)(2,1)S(1)}, bf16[256,512]{1,0:T(8,128)(2,1)S(1)}, u32[]{:S(2)}, u32[]{:S(2)}) collective-permute-start(bf16[256,512]{1,0:T(8,128)(2,1)S(1)} %pad_maximum_fusion.4), channel_id=1, source_target_pairs={{4,0},{8,4},{12,8},{5,1},{9,5},{13,9},{6,2},{10,6},{14,10},{7,3},{... | collective-permute-start | bytes 786440 | tf_op jit(solution)/shard_map/ppermute | solution.py:21
  8.1 8.8 %copy-start.8 = (bf16[256,1024]{1,0:T(8,128)(2,1)S(1)}, bf16[256,1024]{1,0:T(8,128)(2,1)}, u32[]{:S(2)}) copy-start(bf16[256,1024]{1,0:T(8,128)(2,1)} %param.25) | copy-start | bytes 1572868
  8.1 11.5 %collective-permute-start = (bf16[256,512]{1,0:T(8,128)(2,1)}, bf16[256,512]{1,0:T(8,128)(2,1)S(1)}, u32[]{:S(2)}, u32[]{:S(2)}) collective-permute-start(bf16[256,512]{1,0:T(8,128)(2,1)} %pad_maximum_fusion.3), channel_id=1, source_target_pairs={{0,4},{4,8},{8,12},{1,5},{5,9},{9,13},{2,6},{6,10},{10,14},{3,7},{... | collective-permute-start | bytes 786440 | tf_op jit(solution)/shard_map/ppermute | solution.py:21
  16.9 2.7 %copy-start.13 = (s32[3]{0:T(128)}, s32[3]{0:T(128)S(1)}, u32[]{:S(2)}) copy-start(s32[3]{0:T(128)S(1)} %constant_dynamic-update-slice_fusion.2.scal_ref) | copy-start | bytes 40
  17.9 1.7 %copy-start.6 = (bf16[256,512]{1,0:T(8,128)(2,1)}, bf16[256,512]{1,0:T(8,128)(2,1)S(1)}, u32[]{:S(2)}) copy-start(bf16[256,512]{1,0:T(8,128)(2,1)S(1)} %collective-permute-done.1.high_ref) | copy-start | bytes 786436
  19.6 0.7 copy-start.7
  32.8 4.2 %copy-start.2 = (bf16[4,1024,256]{2,1,0:T(8,128)(2,1)S(1)}, bf16[4,1024,256]{2,1,0:T(8,128)(2,1)}, u32[]{:S(2)}) copy-start(bf16[4,1024,256]{2,1,0:T(8,128)(2,1)} %shard_map.122) | copy-start | bytes 6291460
  34.3 4.7 %copy-start.19 = (s32[3]{0:T(128)S(1)}, s32[3]{0:T(128)}, u32[]{:S(2)}) copy-start(s32[3]{0:T(128)} %constant.165.clone) | copy-start | bytes 40
  34.3 2.7 %collective-permute-start.2 = (bf16[2,1024,256]{2,1,0:T(8,128)(2,1)S(1)}, bf16[2,1024,256]{2,1,0:T(8,128)(2,1)S(1)}, u32[]{:S(2)}, u32[]{:S(2)}) collective-permute-start(bf16[2,1024,256]{2,1,0:T(8,128)(2,1)S(1)} %slice.128), channel_id=1, source_target_pairs={{0,1},{1,0},{2,3},{3,2},{4,5},{5,4},{6,7},{7,6},{8,9},{9,8},{10,11... | collective-permute-start | bytes 3145736 | tf_op jit(solution)/shard_map/ppermute | solution.py:229
  37.3 18.6 %collective-permute-start.3 = (bf16[1024,256]{1,0:T(8,128)(2,1)S(1)}, bf16[1024,256]{1,0:T(8,128)(2,1)}, u32[]{:S(2)}, u32[]{:S(2)}) collective-permute-start(bf16[1024,256]{1,0:T(8,128)(2,1)S(1)} %get-tuple-element.66), channel_id=1, source_target_pairs={{0,2},{1,3},{2,0},{3,1},{4,6},{5,7},{6,4},{7,5},{8,10},{9,11},{10,... | collective-permute-start | bytes 1572872 | tf_op jit(solution)/shard_map/ppermute | solution.py:244
  39.0 0.5 copy-start.14
  52.1 2.3 %copy-start.18 = (bf16[1024,256]{1,0:T(8,128)(2,1)S(1)}, bf16[1024,256]{1,0:T(8,128)(2,1)}, u32[]{:S(2)}) copy-start(bf16[1024,256]{1,0:T(8,128)(2,1)} %param.26) | copy-start | bytes 1572868
  54.4 21.5 %collective-permute-start.4 = (bf16[2,1024,256]{2,1,0:T(8,128)(2,1)}, bf16[2,1024,256]{2,1,0:T(8,128)(2,1)}, u32[]{:S(2)}, u32[]{:S(2)}) collective-permute-start(bf16[2,1024,256]{2,1,0:T(8,128)(2,1)} %slice.133), channel_id=1, source_target_pairs={{0,1},{1,0},{2,3},{3,2},{4,5},{5,4},{6,7},{7,6},{8,9},{9,8},{10,11... | collective-permute-start | bytes 3145736 | tf_op jit(solution)/shard_map/ppermute | solution.py:229
  74.1 1.4 %copy-start.5 = (f32[1024,128]{1,0:T(8,128)S(1)}, f32[1024,128]{1,0:T(8,128)}, u32[]{:S(2)}) copy-start(f32[1024,128]{1,0:T(8,128)} %get-tuple-element.76) | copy-start | bytes 1572868
  75.4 1.6 %copy-start.1 = (bf16[4,1024,256]{2,1,0:T(8,128)(2,1)S(1)}, bf16[4,1024,256]{2,1,0:T(8,128)(2,1)}, u32[]{:S(2)}) copy-start(bf16[4,1024,256]{2,1,0:T(8,128)(2,1)} %shard_map.123) | copy-start | bytes 6291460
  75.8 10.6 %copy-start.9 = (bf16[256,1024]{1,0:T(8,128)(2,1)S(1)}, bf16[256,1024]{1,0:T(8,128)(2,1)}, u32[]{:S(2)}) copy-start(bf16[256,1024]{1,0:T(8,128)(2,1)} %param.27) | copy-start | bytes 1572868
  80.1 10.3 %collective-permute-start.6 = (bf16[256,280]{1,0:T(8,128)(2,1)S(1)}, bf16[256,280]{1,0:T(8,128)(2,1)S(1)}, u32[]{:S(2)}, u32[]{:S(2)}) collective-permute-start(bf16[256,280]{1,0:T(8,128)(2,1)S(1)} %get-tuple-element.93), channel_id=1, source_target_pairs={{0,4},{4,8},{8,12},{12,0},{1,5},{5,9},{9,13},{13,1},{2,6},{6,10},{... | collective-permute-start | bytes 430088 | tf_op jit(solution)/shard_map/ppermute | solution.py:272
  82.4 16.1 %collective-permute-start.7 = (bf16[256,280]{1,0:T(8,128)(2,1)S(1)}, bf16[256,280]{1,0:T(8,128)(2,1)S(1)}, u32[]{:S(2)}, u32[]{:S(2)}) collective-permute-start(bf16[256,280]{1,0:T(8,128)(2,1)S(1)} %get-tuple-element.92), channel_id=1, source_target_pairs={{0,8},{4,12},{8,0},{12,4},{1,9},{5,13},{9,1},{13,5},{2,10},{6,14},... | collective-permute-start | bytes 430088 | tf_op jit(solution)/shard_map/ppermute | solution.py:272
  85.0 13.5 %collective-permute-start.8 = (bf16[256,280]{1,0:T(8,128)(2,1)S(1)}, bf16[256,280]{1,0:T(8,128)(2,1)S(1)}, u32[]{:S(2)}, u32[]{:S(2)}) collective-permute-start(bf16[256,280]{1,0:T(8,128)(2,1)S(1)} %get-tuple-element.91), channel_id=1, source_target_pairs={{0,12},{4,0},{8,4},{12,8},{1,13},{5,1},{9,5},{13,9},{2,14},{6,2},{... | collective-permute-start | bytes 430088 | tf_op jit(solution)/shard_map/ppermute | solution.py:272
  87.2 20.0 %collective-permute-start.5 = (bf16[1024,256]{1,0:T(8,128)(2,1)}, bf16[1024,256]{1,0:T(8,128)(2,1)}, u32[]{:S(2)}, u32[]{:S(2)}) collective-permute-start(bf16[1024,256]{1,0:T(8,128)(2,1)} %get-tuple-element.78), channel_id=1, source_target_pairs={{0,2},{1,3},{2,0},{3,1},{4,6},{5,7},{6,4},{7,5},{8,10},{9,11},{10,... | collective-permute-start | bytes 1572872 | tf_op jit(solution)/shard_map/ppermute | solution.py:244
  90.4 8.9 %copy-start.10 = (bf16[256,280]{1,0:T(8,128)(2,1)}, bf16[256,280]{1,0:T(8,128)(2,1)S(1)}, u32[]{:S(2)}) copy-start(bf16[256,280]{1,0:T(8,128)(2,1)S(1)} %collective-permute-done.6.refs_1_) | copy-start | bytes 430084
  98.6 0.7 copy-start.11
  98.6 0.7 copy-start.12
  104.9 1.6 %collective-permute-start.9 = (bf16[2,256,256]{2,1,0:T(8,128)(2,1)S(1)}, bf16[2,256,256]{2,1,0:T(8,128)(2,1)S(1)}, u32[]{:S(2)}, u32[]{:S(2)}) collective-permute-start(bf16[2,256,256]{2,1,0:T(8,128)(2,1)S(1)} %pad_maximum_fusion.5), channel_id=1, source_target_pairs={{0,1},{1,0},{2,3},{3,2},{4,5},{5,4},{6,7},{7,6},{8,9},{9,8},{10,11... | collective-permute-start | bytes 786440 | tf_op jit(solution)/shard_map/ppermute | solution.py:229
  106.6 5.6 %collective-permute-start.10 = (bf16[256,256]{1,0:T(8,128)(2,1)S(1)}, bf16[256,256]{1,0:T(8,128)(2,1)S(1)}, u32[]{:S(2)}, u32[]{:S(2)}) collective-permute-start(bf16[256,256]{1,0:T(8,128)(2,1)S(1)} %fusion.12), channel_id=1, source_target_pairs={{0,2},{1,3},{2,0},{3,1},{4,6},{5,7},{6,4},{7,5},{8,10},{9,11},{10,... | collective-permute-start | bytes 393224 | tf_op jit(solution)/shard_map/ppermute | solution.py:244

commit v13 on v11

--- a/solution.py
+++ b/solution.py
@@ -79,7 +79,7 @@
     frame_count, width = query.shape
     out_width = w_out.shape[1]
     block_width = out_width // blocks
-    tq = min(256, rows)
+    tq = min(128, rows)
     block_base = row_base // tq
     span = tq + 2 * HALF
     scal = jnp.array([0, 0, row_base], jnp.int32).at[0].set(first_frame).at[1].set(length)
@@ -278,23 +278,28 @@
     width = out_ref.shape[1]
     stat_width = 2 * heads
 
-    def column(ref, c):
-        pieces = [
-            ref[:, width + i * stat_width + c : width + i * stat_width + c + 1].astype(jnp.float32)
-            for i in range(3)
-        ]
-        return pieces[0] + pieces[1] + pieces[2]
+    stat_blocks = []
+    for ref in part_refs:
+        raw = ref[:, width : width + 3 * stat_width].astype(jnp.float32)
+        stat_blocks.append(
+            raw[:, 0:stat_width]
+            + raw[:, stat_width : 2 * stat_width]
+            + raw[:, 2 * stat_width : 3 * stat_width]
+        )
+
+    def column(k, c):
+        return stat_blocks[k][:, c : c + 1]
 
     for h in range(heads):
-        peaks = [column(ref, h) for ref in part_refs]
+        peaks = [column(k, h) for k in range(len(part_refs))]
         joint = peaks[0]
         for peak in peaks[1:]:
             joint = jnp.maximum(joint, peak)
         total = jnp.zeros_like(joint)
         accum = jnp.zeros((out_ref.shape[0], HD), jnp.float32)
-        for ref, peak in zip(part_refs, peaks):
+        for k, (ref, peak) in enumerate(zip(part_refs, peaks)):
             factor = jnp.exp(peak - joint)
-            total = total + column(ref, heads + h) * factor
+            total = total + column(k, heads + h) * factor
             accum = accum + ref[:, h * HD : (h + 1) * HD].astype(jnp.float32) * factor
         out_ref[:, h * HD : (h + 1) * HD] = (accum / total).astype(jnp.bfloat16)
 

time: 113 us -> 124 us (1.097)
  Pallas kernels: 46.1 us -> 56.5 us
    pallas_call x2, Pallas kernels: 25 us -> 36.5 us  [window_attention(): pl.pallas_call(kernel, cost_estimate=cost, out_shape=jax.ShapeDtypeStruct...]
  transfers between devices with their start and end apart: 11 -> 11, of which waited for: 5 -> 5; matrix products, arithmetic and copies ran while one was open for 12% -> 10% of each run, Pallas kernels for 30% -> 31%
where the time goes in v13:
time: 124 us
  Pallas kernels  56.5 us (46%)
  starting transfers between devices  18 us (15%)
  waiting for transfers between devices  17.5 us (14%)
  other arithmetic  12.6 us (10%)
  matrix products  10.2 us (8%)
  local copies, waits for them, and re-layouts  7.46 us (6%)
  between operations  1.6 us (1%)
    pallas_call x2, Pallas kernels, window_attention(): pl.pallas_call(kernel, cost_estimate=cost, out_shape=jax.ShapeDtypeStruct...  36.5 us
    pallas_call x1, Pallas kernels, latent_attention(): pl.pallas_call(kernel, cost_estimate=cost, out_shape=(jax.ShapeDtypeStruc...  17 us
    ppermute x3, waiting for transfers between devices, exchange_rows(): parts.append(lax.ppermute(block, axis, pairs))  8.92 us
    dot_general x4, matrix products, project(): jnp.dot(source, weight, preferred_element_type=jnp.float32)  8.74 us
    ppermute x3, waiting for transfers between devices, cross_chip_sum(): total = total + lax.ppermute(chip_sums[d], axis, pairs).astype(jnp.float32)  6.54 us
    ppermute x3, starting transfers between devices, exchange_rows(): parts.append(lax.ppermute(block, axis, pairs))  6.47 us
    ppermute x1, starting transfers between devices, halos(): lax.ppermute(tail, axis, forward)  5.87 us
    convert_element_type x3, other arithmetic, chip_pair_sums(): (blocks[chips + d].astype(jnp.float32) + received[d].astype(jnp.float32))...  5.1 us
  transfers between devices with their start and end apart: 11, of which 5 were waited for; matrix products, arithmetic and copies ran while one was open for 10% of the time, Pallas kernels for 31%

profile of v13, /device:TPU:0, one launch (start us, length us, event | category | flops | bytes accessed | tf_op | source)
XLA Modules:
  0.0 123.8 jit_solution(11072289073003336676)
XLA Ops:
  0.7 3.7 %convolution_convert_fusion.v_ref = bf16[2048,256]{1,0:T(8,128)(2,1)S(1)} fusion(bf16[2048,1024]{1,0:T(8,128)(2,1)} %param.19, bf16[1024,256]{1,0:T(8,128)(2,1)} %param.24), kind=kOutput, calls=%fused_computation | convolution fusion | flops 1074266112 | bytes 5767168 | tf_op jit(solution)/shard_map/dot_general | solution.py:25
  4.5 1.3 %convolution_convert_fusion.1.k_ref = bf16[2048,256]{1,0:T(8,128)(2,1)S(1)} fusion(bf16[2048,1024]{1,0:T(8,128)(2,1)S(1)} %copy-done.15, bf16[1024,256]{1,0:T(8,128)(2,1)S(1)} %copy-done.16), kind=kOutput, calls=%fused_computation.1 | convolution fusion | flops 1074266112 | bytes 5767168 | tf_op jit(solution)/shard_map/dot_general | solution.py:25
  5.9 1.4 %collective-permute-start.1 = (bf16[256,512]{1,0:T(8,128)(2,1)S(1)}, bf16[256,512]{1,0:T(8,128)(2,1)S(1)}, u32[]{:S(2)}, u32[]{:S(2)}) collective-permute-start(bf16[256,512]{1,0:T(8,128)(2,1)S(1)} %pad_maximum_fusion.4), channel_id=1, source_target_pairs={{4,0},{8,4},{12,8},{5,1},{9,5},{13,9},{6,2},{10,6},{14,10},{7,3},{... | collective-permute-start | bytes 786440 | tf_op jit(solution)/shard_map/ppermute | solution.py:21
  8.1 5.9 %collective-permute-start = (bf16[256,512]{1,0:T(8,128)(2,1)}, bf16[256,512]{1,0:T(8,128)(2,1)S(1)}, u32[]{:S(2)}, u32[]{:S(2)}) collective-permute-start(bf16[256,512]{1,0:T(8,128)(2,1)} %pad_maximum_fusion.3), channel_id=1, source_target_pairs={{0,4},{4,8},{8,12},{1,5},{5,9},{9,13},{2,6},{6,10},{10,14},{3,7},{... | collective-permute-start | bytes 786440 | tf_op jit(solution)/shard_map/ppermute | solution.py:21
  14.0 2.3 %convolution_convert_fusion.2.q_ref = bf16[2048,256]{1,0:T(8,128)(2,1)} fusion(bf16[2048,1024]{1,0:T(8,128)(2,1)S(1)} %copy-done.15, bf16[1024,256]{1,0:T(8,128)(2,1)S(1)} %copy-done.17), kind=kOutput, calls=%fused_computation.2 | convolution fusion | flops 1074266112 | bytes 5767168 | tf_op jit(solution)/shard_map/dot_general | solution.py:25
  17.0 0.9 pad_maximum_fusion.2.w_ref
  17.9 1.7 %collective-permute-done.low_ref = bf16[256,512]{1,0:T(8,128)(2,1)S(1)} collective-permute-done((bf16[256,512]{1,0:T(8,128)(2,1)}, bf16[256,512]{1,0:T(8,128)(2,1)S(1)}, u32[]{:S(2)}, u32[]{:S(2)}) %collective-permute-start) | collective-permute-done | bytes 262176 | tf_op jit(solution)/shard_map/ppermute | solution.py:21
  20.3 18.2 %shard_map.122 = bf16[4,1024,256]{2,1,0:T(8,128)(2,1)} custom-call(s32[3]{0:T(128)} %copy-done.13, bf16[2048,256]{1,0:T(8,128)(2,1)} %convolution_convert_fusion.2.q_ref, bf16[2048,256]{1,0:T(8,128)(2,1)} %copy-done.4, bf16[2048,256]{1,0:T(8,128)(2,1)} %copy-done.3, bf16[256,512]{1,0:T(8,128)(2,1)} %copy-done.7, bf16[256,512]{1,0:T(8,128)(2,1)} %copy-done.6, ...), custom_call_target="tpu_custom_call" | custom-call | flops 1207959552 | bytes 5767168 | tf_op jit(solution)/shard_map/pallas_call | solution.py:93
  38.6 1.3 %slice.128 = bf16[2,1024,256]{2,1,0:T(8,128)(2,1)S(1)} slice(bf16[4,1024,256]{2,1,0:T(8,128)(2,1)} %shard_map.122), slice={[0:2], [0:1024], [0:256]} | slice | bytes 2097152 | tf_op jit(solution)/shard_map/slice | solution.py:229
  40.5 18.3 %shard_map.123 = bf16[4,1024,256]{2,1,0:T(8,128)(2,1)} custom-call(s32[3]{0:T(128)} %copy-done.14, bf16[2048,256]{1,0:T(8,128)(2,1)} %convolution_convert_fusion.2.q_ref, bf16[2048,256]{1,0:T(8,128)(2,1)} %copy-done.4, bf16[2048,256]{1,0:T(8,128)(2,1)} %copy-done.3, bf16[256,512]{1,0:T(8,128)(2,1)} %copy-done.7, bf16[256,512]{1,0:T(8,128)(2,1)} %copy-done.6, ...), custom_call_target="tpu_custom_call" | custom-call | flops 1207959552 | bytes 5767168 | tf_op jit(solution)/shard_map/pallas_call | solution.py:93
  58.8 2.8 %fusion.1 = (bf16[1024,256]{1,0:T(8,128)(2,1)}, bf16[1024,256]{1,0:T(8,128)(2,1)S(1)}) fusion(bf16[2,1024,256]{2,1,0:T(8,128)(2,1)} %collective-permute-done.2, bf16[4,1024,256]{2,1,0:T(8,128)(2,1)} %shard_map.122), kind=kLoop, calls=%fused_computation.14 | loop fusion | flops 2097152 | bytes 3145728 | tf_op jit(solution)/shard_map/convert_element_type | solution.py:231
  61.6 1.0 slice.113
  63.1 1.5 %convolution_convert_fusion.4.q_ref = bf16[1024,256]{1,0:T(8,128)(2,1)} fusion(bf16[1024,1024]{1,0:T(8,128)(2,1)S(1)} %copy-done, bf16[1024,256]{1,0:T(8,128)(2,1)S(1)} %copy-done.18), kind=kOutput, calls=%fused_computation.4 | convolution fusion | flops 537133056 | bytes 3145728 | tf_op jit(solution)/shard_map/dot_general | solution.py:25
  64.6 17.0 %shard_map.124 = (f32[1024,256]{1,0:T(8,128)}, f32[1024,128]{1,0:T(8,128)}) custom-call(s32[1]{0:T(128)} %bitcast.6.scal_ref, bf16[1024,256]{1,0:T(8,128)(2,1)} %convolution_convert_fusion.4.q_ref, bf16[2048,256]{1,0:T(8,128)(2,1)} %copy-done.4, bf16[2048,256]{1,0:T(8,128)(2,1)} %copy-done.3), custom_call_target="tpu_custom_call" | custom-call | flops 2147483648 | bytes 4194304 | tf_op jit(solution)/shard_map/pallas_call | solution.py:153
  81.6 1.3 %convert_element_type.163 = bf16[1024,256]{1,0:T(8,128)(2,1)S(1)} convert(f32[1024,256]{1,0:T(8,128)} %get-tuple-element.65) | non-fusion elementwise | flops 262144 | bytes 1572864 | tf_op jit(solution)/shard_map/convert_element_type | solution.py:358
  83.4 1.2 copy-done.2
  84.5 2.3 %fusion.3 = (bf16[1024,256]{1,0:T(8,128)(2,1)}, bf16[1024,256]{1,0:T(8,128)(2,1)S(1)}) fusion(bf16[2,1024,256]{2,1,0:T(8,128)(2,1)} %collective-permute-done.4, bf16[4,1024,256]{2,1,0:T(8,128)(2,1)S(1)} %copy-done.2), kind=kLoop, calls=%fused_computation.16 | loop fusion | flops 2097152 | bytes 3145728 | tf_op jit(solution)/shard_map/convert_element_type | solution.py:231
  86.8 0.8 constant_dynamic-slice_fusion.3
  87.6 2.4 %collective-permute-start.6 = (bf16[256,280]{1,0:T(8,128)(2,1)S(1)}, bf16[256,280]{1,0:T(8,128)(2,1)S(1)}, u32[]{:S(2)}, u32[]{:S(2)}) collective-permute-start(bf16[256,280]{1,0:T(8,128)(2,1)S(1)} %get-tuple-element.83), channel_id=1, source_target_pairs={{0,4},{4,8},{8,12},{12,0},{1,5},{5,9},{9,13},{13,1},{2,6},{6,10},{... | collective-permute-start | bytes 430088 | tf_op jit(solution)/shard_map/ppermute | solution.py:272
  90.0 2.8 %collective-permute-start.7 = (bf16[256,280]{1,0:T(8,128)(2,1)S(1)}, bf16[256,280]{1,0:T(8,128)(2,1)S(1)}, u32[]{:S(2)}, u32[]{:S(2)}) collective-permute-start(bf16[256,280]{1,0:T(8,128)(2,1)S(1)} %get-tuple-element.82), channel_id=1, source_target_pairs={{0,8},{4,12},{8,0},{12,4},{1,9},{5,13},{9,1},{13,5},{2,10},{6,14},... | collective-permute-start | bytes 430088 | tf_op jit(solution)/shard_map/ppermute | solution.py:272
  92.7 1.3 %collective-permute-start.8 = (bf16[256,280]{1,0:T(8,128)(2,1)S(1)}, bf16[256,280]{1,0:T(8,128)(2,1)S(1)}, u32[]{:S(2)}, u32[]{:S(2)}) collective-permute-start(bf16[256,280]{1,0:T(8,128)(2,1)S(1)} %get-tuple-element.81), channel_id=1, source_target_pairs={{0,12},{4,0},{8,4},{12,8},{1,13},{5,1},{9,5},{13,9},{2,14},{6,2},{... | collective-permute-start | bytes 430088 | tf_op jit(solution)/shard_map/ppermute | solution.py:272
  94.1 0.8 constant_dynamic-slice_fusion.2
  94.9 1.5 %collective-permute-start.3 = (bf16[1024,256]{1,0:T(8,128)(2,1)}, bf16[1024,256]{1,0:T(8,128)(2,1)}, u32[]{:S(2)}, u32[]{:S(2)}) collective-permute-start(bf16[1024,256]{1,0:T(8,128)(2,1)} %get-tuple-element.61), channel_id=1, source_target_pairs={{0,2},{1,3},{2,0},{3,1},{4,6},{5,7},{6,4},{7,5},{8,10},{9,11},{10,... | collective-permute-start | bytes 1572872 | tf_op jit(solution)/shard_map/ppermute | solution.py:244
  96.9 1.1 collective-permute-done.6.refs_1_
  98.0 7.8 %collective-permute-done.7.refs_2_ = bf16[256,280]{1,0:T(8,128)(2,1)S(1)} collective-permute-done((bf16[256,280]{1,0:T(8,128)(2,1)S(1)}, bf16[256,280]{1,0:T(8,128)(2,1)S(1)}, u32[]{:S(2)}, u32[]{:S(2)}) %collective-permute-start.7) | collective-permute-done | bytes 143392 | tf_op jit(solution)/shard_map/ppermute | solution.py:272
  106.6 3.0 %shard_map.125 = bf16[256,256]{1,0:T(8,128)(2,1)} custom-call(bf16[256,280]{1,0:T(8,128)(2,1)} %get-tuple-element.84.refs_0_, bf16[256,280]{1,0:T(8,128)(2,1)} %copy-done.10, bf16[256,280]{1,0:T(8,128)(2,1)} %copy-done.11, bf16[256,280]{1,0:T(8,128)(2,1)} %copy-done.12), custom_call_target="tpu_custom_call" | custom-call | tf_op jit(solution)/shard_map/pallas_call | solution.py:309
  109.6 1.5 %convolution_convert_fusion.3 = bf16[256,1024]{1,0:T(8,128)(2,1)S(1)} fusion(bf16[256,256]{1,0:T(8,128)(2,1)} %shard_map.125, bf16[256,256]{1,0:T(8,128)(2,1)} %get-tuple-element.89, bf16[256,256]{1,0:T(8,128)(2,1)} %get-tuple-element.90, bf16[256,256]{1,0:T(8,128)(2,1)} %get-tuple-element.88, bf16[256,256]{1,0:T(8,128)(2,1)} %get-tuple-element.87), kind=kOutput, calls=%fused_computation.3 | convolution fusion | flops 136577024 | bytes 1179648 | tf_op jit(solution)/shard_map/dot_general | solution.py:369
  111.2 1.2 add_convert_fusion.3
  112.8 1.6 %collective-permute-start.10 = (bf16[256,256]{1,0:T(8,128)(2,1)S(1)}, bf16[256,256]{1,0:T(8,128)(2,1)S(1)}, u32[]{:S(2)}, u32[]{:S(2)}) collective-permute-start(bf16[256,256]{1,0:T(8,128)(2,1)S(1)} %fusion.12), channel_id=1, source_target_pairs={{0,2},{1,3},{2,0},{3,1},{4,6},{5,7},{6,4},{7,5},{8,10},{9,11},{10,... | collective-permute-start | bytes 393224 | tf_op jit(solution)/shard_map/ppermute | solution.py:244
  114.3 6.5 %collective-permute-done.5 = bf16[1024,256]{1,0:T(8,128)(2,1)} collective-permute-done((bf16[1024,256]{1,0:T(8,128)(2,1)}, bf16[1024,256]{1,0:T(8,128)(2,1)}, u32[]{:S(2)}, u32[]{:S(2)}) %collective-permute-start.5) | collective-permute-done | bytes 524320 | tf_op jit(solution)/shard_map/ppermute | solution.py:244
  120.9 1.2 add_convert_fusion
  122.0 1.0 pad_maximum_fusion
  (65 shorter events, 5.8 us)
Async XLA Ops:
  0.6 62.5 %copy-start = (bf16[1024,1024]{1,0:T(8,128)(2,1)S(1)}, bf16[1024,1024]{1,0:T(8,128)(2,1)}, u32[]{:S(2)}) copy-start(bf16[1024,1024]{1,0:T(8,128)(2,1)} %param.20) | copy-start | bytes 6291460
  0.6 3.8 %copy-start.15 = (bf16[2048,1024]{1,0:T(8,128)(2,1)S(1)}, bf16[2048,1024]{1,0:T(8,128)(2,1)}, u32[]{:S(2)}) copy-start(bf16[2048,1024]{1,0:T(8,128)(2,1)} %param.19) | copy-start | bytes 12582916
  0.7 3.9 %copy-start.16 = (bf16[1024,256]{1,0:T(8,128)(2,1)S(1)}, bf16[1024,256]{1,0:T(8,128)(2,1)}, u32[]{:S(2)}) copy-start(bf16[1024,256]{1,0:T(8,128)(2,1)} %param.23) | copy-start | bytes 1572868
  4.5 1.3 %copy-start.3 = (bf16[2048,256]{1,0:T(8,128)(2,1)}, bf16[2048,256]{1,0:T(8,128)(2,1)S(1)}, u32[]{:S(2)}) copy-start(bf16[2048,256]{1,0:T(8,128)(2,1)S(1)} %convolution_convert_fusion.v_ref) | copy-start | bytes 3145732
  5.8 10.4 %copy-start.4 = (bf16[2048,256]{1,0:T(8,128)(2,1)}, bf16[2048,256]{1,0:T(8,128)(2,1)S(1)}, u32[]{:S(2)}) copy-start(bf16[2048,256]{1,0:T(8,128)(2,1)S(1)} %convolution_convert_fusion.1.k_ref) | copy-start | bytes 3145732
  5.8 8.1 %copy-start.17 = (bf16[1024,256]{1,0:T(8,128)(2,1)S(1)}, bf16[1024,256]{1,0:T(8,128)(2,1)}, u32[]{:S(2)}) copy-start(bf16[1024,256]{1,0:T(8,128)(2,1)} %param.22) | copy-start | bytes 1572868
  5.9 12.0 %collective-permute-start.1 = (bf16[256,512]{1,0:T(8,128)(2,1)S(1)}, bf16[256,512]{1,0:T(8,128)(2,1)S(1)}, u32[]{:S(2)}, u32[]{:S(2)}) collective-permute-start(bf16[256,512]{1,0:T(8,128)(2,1)S(1)} %pad_maximum_fusion.4), channel_id=1, source_target_pairs={{4,0},{8,4},{12,8},{5,1},{9,5},{13,9},{6,2},{10,6},{14,10},{7,3},{... | collective-permute-start | bytes 786440 | tf_op jit(solution)/shard_map/ppermute | solution.py:21
  8.1 8.8 %copy-start.8 = (bf16[256,1024]{1,0:T(8,128)(2,1)S(1)}, bf16[256,1024]{1,0:T(8,128)(2,1)}, u32[]{:S(2)}) copy-start(bf16[256,1024]{1,0:T(8,128)(2,1)} %param.25) | copy-start | bytes 1572868
  8.1 11.5 %collective-permute-start = (bf16[256,512]{1,0:T(8,128)(2,1)}, bf16[256,512]{1,0:T(8,128)(2,1)S(1)}, u32[]{:S(2)}, u32[]{:S(2)}) collective-permute-start(bf16[256,512]{1,0:T(8,128)(2,1)} %pad_maximum_fusion.3), channel_id=1, source_target_pairs={{0,4},{4,8},{8,12},{1,5},{5,9},{9,13},{2,6},{6,10},{10,14},{3,7},{... | collective-permute-start | bytes 786440 | tf_op jit(solution)/shard_map/ppermute | solution.py:21
  16.9 2.7 %copy-start.13 = (s32[3]{0:T(128)}, s32[3]{0:T(128)S(1)}, u32[]{:S(2)}) copy-start(s32[3]{0:T(128)S(1)} %constant_dynamic-update-slice_fusion.2.scal_ref) | copy-start | bytes 40
  17.9 1.7 %copy-start.6 = (bf16[256,512]{1,0:T(8,128)(2,1)}, bf16[256,512]{1,0:T(8,128)(2,1)S(1)}, u32[]{:S(2)}) copy-start(bf16[256,512]{1,0:T(8,128)(2,1)S(1)} %collective-permute-done.1.high_ref) | copy-start | bytes 786436
  19.6 0.7 copy-start.7
  38.6 1.4 %copy-start.19 = (s32[3]{0:T(128)S(1)}, s32[3]{0:T(128)}, u32[]{:S(2)}) copy-start(s32[3]{0:T(128)} %constant.165.clone) | copy-start | bytes 40
  39.9 18.9 %collective-permute-start.2 = (bf16[2,1024,256]{2,1,0:T(8,128)(2,1)S(1)}, bf16[2,1024,256]{2,1,0:T(8,128)(2,1)}, u32[]{:S(2)}, u32[]{:S(2)}) collective-permute-start(bf16[2,1024,256]{2,1,0:T(8,128)(2,1)S(1)} %slice.128), channel_id=1, source_target_pairs={{0,1},{1,0},{2,3},{3,2},{4,5},{5,4},{6,7},{7,6},{8,9},{9,8},{10,11... | collective-permute-start | bytes 3145736 | tf_op jit(solution)/shard_map/ppermute | solution.py:229
  40.0 0.5 copy-start.14
  58.8 2.8 %copy-start.1 = (bf16[4,1024,256]{2,1,0:T(8,128)(2,1)S(1)}, bf16[4,1024,256]{2,1,0:T(8,128)(2,1)}, u32[]{:S(2)}) copy-start(bf16[4,1024,256]{2,1,0:T(8,128)(2,1)} %shard_map.123) | copy-start | bytes 6291460
  58.8 4.3 %copy-start.18 = (bf16[1024,256]{1,0:T(8,128)(2,1)S(1)}, bf16[1024,256]{1,0:T(8,128)(2,1)}, u32[]{:S(2)}) copy-start(bf16[1024,256]{1,0:T(8,128)(2,1)} %param.26) | copy-start | bytes 1572868
  62.6 20.7 %collective-permute-start.4 = (bf16[2,1024,256]{2,1,0:T(8,128)(2,1)}, bf16[2,1024,256]{2,1,0:T(8,128)(2,1)}, u32[]{:S(2)}, u32[]{:S(2)}) collective-permute-start(bf16[2,1024,256]{2,1,0:T(8,128)(2,1)} %slice.113), channel_id=1, source_target_pairs={{0,1},{1,0},{2,3},{3,2},{4,5},{5,4},{6,7},{7,6},{8,9},{9,8},{10,11... | collective-permute-start | bytes 3145736 | tf_op jit(solution)/shard_map/ppermute | solution.py:229
  81.6 1.4 %copy-start.5 = (f32[1024,128]{1,0:T(8,128)S(1)}, f32[1024,128]{1,0:T(8,128)}, u32[]{:S(2)}) copy-start(f32[1024,128]{1,0:T(8,128)} %get-tuple-element.66) | copy-start | bytes 1572868
  82.9 1.6 %copy-start.2 = (bf16[4,1024,256]{2,1,0:T(8,128)(2,1)S(1)}, bf16[4,1024,256]{2,1,0:T(8,128)(2,1)}, u32[]{:S(2)}) copy-start(bf16[4,1024,256]{2,1,0:T(8,128)(2,1)} %shard_map.123) | copy-start | bytes 6291460
  83.3 10.7 %copy-start.9 = (bf16[256,1024]{1,0:T(8,128)(2,1)S(1)}, bf16[256,1024]{1,0:T(8,128)(2,1)}, u32[]{:S(2)}) copy-start(bf16[256,1024]{1,0:T(8,128)(2,1)} %param.27) | copy-start | bytes 1572868
  87.6 10.4 %collective-permute-start.6 = (bf16[256,280]{1,0:T(8,128)(2,1)S(1)}, bf16[256,280]{1,0:T(8,128)(2,1)S(1)}, u32[]{:S(2)}, u32[]{:S(2)}) collective-permute-start(bf16[256,280]{1,0:T(8,128)(2,1)S(1)} %get-tuple-element.83), channel_id=1, source_target_pairs={{0,4},{4,8},{8,12},{12,0},{1,5},{5,9},{9,13},{13,1},{2,6},{6,10},{... | collective-permute-start | bytes 430088 | tf_op jit(solution)/shard_map/ppermute | solution.py:272
  90.0 15.9 %collective-permute-start.7 = (bf16[256,280]{1,0:T(8,128)(2,1)S(1)}, bf16[256,280]{1,0:T(8,128)(2,1)S(1)}, u32[]{:S(2)}, u32[]{:S(2)}) collective-permute-start(bf16[256,280]{1,0:T(8,128)(2,1)S(1)} %get-tuple-element.82), channel_id=1, source_target_pairs={{0,8},{4,12},{8,0},{12,4},{1,9},{5,13},{9,1},{13,5},{2,10},{6,14},... | collective-permute-start | bytes 430088 | tf_op jit(solution)/shard_map/ppermute | solution.py:272
  92.7 13.1 %collective-permute-start.8 = (bf16[256,280]{1,0:T(8,128)(2,1)S(1)}, bf16[256,280]{1,0:T(8,128)(2,1)S(1)}, u32[]{:S(2)}, u32[]{:S(2)}) collective-permute-start(bf16[256,280]{1,0:T(8,128)(2,1)S(1)} %get-tuple-element.81), channel_id=1, source_target_pairs={{0,12},{4,0},{8,4},{12,8},{1,13},{5,1},{9,5},{13,9},{2,14},{6,2},{... | collective-permute-start | bytes 430088 | tf_op jit(solution)/shard_map/ppermute | solution.py:272
  94.9 16.3 %collective-permute-start.3 = (bf16[1024,256]{1,0:T(8,128)(2,1)}, bf16[1024,256]{1,0:T(8,128)(2,1)}, u32[]{:S(2)}, u32[]{:S(2)}) collective-permute-start(bf16[1024,256]{1,0:T(8,128)(2,1)} %get-tuple-element.61), channel_id=1, source_target_pairs={{0,2},{1,3},{2,0},{3,1},{4,6},{5,7},{6,4},{7,5},{8,10},{9,11},{10,... | collective-permute-start | bytes 1572872 | tf_op jit(solution)/shard_map/ppermute | solution.py:244
  96.4 24.5 %collective-permute-start.5 = (bf16[1024,256]{1,0:T(8,128)(2,1)}, bf16[1024,256]{1,0:T(8,128)(2,1)}, u32[]{:S(2)}, u32[]{:S(2)}) collective-permute-start(bf16[1024,256]{1,0:T(8,128)(2,1)} %get-tuple-element.68), channel_id=1, source_target_pairs={{0,2},{1,3},{2,0},{3,1},{4,6},{5,7},{6,4},{7,5},{8,10},{9,11},{10,... | collective-permute-start | bytes 1572872 | tf_op jit(solution)/shard_map/ppermute | solution.py:244
  98.0 8.5 %copy-start.10 = (bf16[256,280]{1,0:T(8,128)(2,1)}, bf16[256,280]{1,0:T(8,128)(2,1)S(1)}, u32[]{:S(2)}) copy-start(bf16[256,280]{1,0:T(8,128)(2,1)S(1)} %collective-permute-done.6.refs_1_) | copy-start | bytes 430084
  105.8 0.8 copy-start.11
  105.8 0.7 copy-start.12
  111.1 1.6 %collective-permute-start.9 = (bf16[2,256,256]{2,1,0:T(8,128)(2,1)S(1)}, bf16[2,256,256]{2,1,0:T(8,128)(2,1)S(1)}, u32[]{:S(2)}, u32[]{:S(2)}) collective-permute-start(bf16[2,256,256]{2,1,0:T(8,128)(2,1)S(1)} %pad_maximum_fusion.5), channel_id=1, source_target_pairs={{0,1},{1,0},{2,3},{3,2},{4,5},{5,4},{6,7},{7,6},{8,9},{9,8},{10,11... | collective-permute-start | bytes 786440 | tf_op jit(solution)/shard_map/ppermute | solution.py:229
  112.8 10.3 %collective-permute-start.10 = (bf16[256,256]{1,0:T(8,128)(2,1)S(1)}, bf16[256,256]{1,0:T(8,128)(2,1)S(1)}, u32[]{:S(2)}, u32[]{:S(2)}) collective-permute-start(bf16[256,256]{1,0:T(8,128)(2,1)S(1)} %fusion.12), channel_id=1, source_target_pairs={{0,2},{1,3},{2,0},{3,1},{4,6},{5,7},{6,4},{7,5},{8,10},{9,11},{10,... | collective-permute-start | bytes 393224 | tf_op jit(solution)/shard_map/ppermute | solution.py:244

commit v14 on v13

--- a/solution.py
+++ b/solution.py
@@ -79,7 +79,7 @@
     frame_count, width = query.shape
     out_width = w_out.shape[1]
     block_width = out_width // blocks
-    tq = min(128, rows)
+    tq = min(256, rows)
     block_base = row_base // tq
     span = tq + 2 * HALF
     scal = jnp.array([0, 0, row_base], jnp.int32).at[0].set(first_frame).at[1].set(length)

time: 124 us -> 113 us (0.911)
  Pallas kernels: 56.5 us -> 45 us
    pallas_call x2, Pallas kernels: 36.5 us -> 25 us  [window_attention(): pl.pallas_call(kernel, cost_estimate=cost, out_shape=jax.ShapeDtypeStruct...]
  transfers between devices with their start and end apart: 11 -> 11, of which waited for: 5 -> 5; matrix products, arithmetic and copies ran while one was open for 10% -> 12% of each run, Pallas kernels for 31% -> 29%
where the time goes in v14:
time: 113 us; the launch traced here: 112 us
  Pallas kernels  45 us (40%)
  starting transfers between devices  18 us (16%)
  waiting for transfers between devices  17.4 us (15%)
  other arithmetic  12.6 us (11%)
  matrix products  10.2 us (9%)
  local copies, waits for them, and re-layouts  7.46 us (7%)
  between operations  1.6 us (1%)
    pallas_call x2, Pallas kernels, window_attention(): pl.pallas_call(kernel, cost_estimate=cost, out_shape=jax.ShapeDtypeStruct...  25 us
    pallas_call x1, Pallas kernels, latent_attention(): pl.pallas_call(kernel, cost_estimate=cost, out_shape=(jax.ShapeDtypeStruc...  17 us
    ppermute x3, waiting for transfers between devices, exchange_rows(): parts.append(lax.ppermute(block, axis, pairs))  8.88 us
    dot_general x4, matrix products, project(): jnp.dot(source, weight, preferred_element_type=jnp.float32)  8.74 us
    ppermute x3, waiting for transfers between devices, cross_chip_sum(): total = total + lax.ppermute(chip_sums[d], axis, pairs).astype(jnp.float32)  6.54 us
    ppermute x3, starting transfers between devices, exchange_rows(): parts.append(lax.ppermute(block, axis, pairs))  6.48 us
    ppermute x1, starting transfers between devices, halos(): lax.ppermute(tail, axis, forward)  5.87 us
    convert_element_type x3, other arithmetic, chip_pair_sums(): (blocks[chips + d].astype(jnp.float32) + received[d].astype(jnp.float32))...  5.1 us
  transfers between devices with their start and end apart: 11, of which 5 were waited for; matrix products, arithmetic and copies ran while one was open for 12% of the time, Pallas kernels for 29%

profile of v14, /device:TPU:0, one launch (start us, length us, event | category | flops | bytes accessed | tf_op | source)
XLA Modules:
  0.0 112.3 jit_solution(13940734163799504811)
XLA Ops:
  0.7 3.7 %convolution_convert_fusion.v_ref = bf16[2048,256]{1,0:T(8,128)(2,1)S(1)} fusion(bf16[2048,1024]{1,0:T(8,128)(2,1)} %param.19, bf16[1024,256]{1,0:T(8,128)(2,1)} %param.24), kind=kOutput, calls=%fused_computation | convolution fusion | flops 1074266112 | bytes 5767168 | tf_op jit(solution)/shard_map/dot_general | solution.py:25
  4.5 1.3 %convolution_convert_fusion.1.k_ref = bf16[2048,256]{1,0:T(8,128)(2,1)S(1)} fusion(bf16[2048,1024]{1,0:T(8,128)(2,1)S(1)} %copy-done.15, bf16[1024,256]{1,0:T(8,128)(2,1)S(1)} %copy-done.16), kind=kOutput, calls=%fused_computation.1 | convolution fusion | flops 1074266112 | bytes 5767168 | tf_op jit(solution)/shard_map/dot_general | solution.py:25
  5.9 1.4 %collective-permute-start.1 = (bf16[256,512]{1,0:T(8,128)(2,1)S(1)}, bf16[256,512]{1,0:T(8,128)(2,1)S(1)}, u32[]{:S(2)}, u32[]{:S(2)}) collective-permute-start(bf16[256,512]{1,0:T(8,128)(2,1)S(1)} %pad_maximum_fusion.4), channel_id=1, source_target_pairs={{4,0},{8,4},{12,8},{5,1},{9,5},{13,9},{6,2},{10,6},{14,10},{7,3},{... | collective-permute-start | bytes 786440 | tf_op jit(solution)/shard_map/ppermute | solution.py:21
  8.1 5.9 %collective-permute-start = (bf16[256,512]{1,0:T(8,128)(2,1)}, bf16[256,512]{1,0:T(8,128)(2,1)S(1)}, u32[]{:S(2)}, u32[]{:S(2)}) collective-permute-start(bf16[256,512]{1,0:T(8,128)(2,1)} %pad_maximum_fusion.3), channel_id=1, source_target_pairs={{0,4},{4,8},{8,12},{1,5},{5,9},{9,13},{2,6},{6,10},{10,14},{3,7},{... | collective-permute-start | bytes 786440 | tf_op jit(solution)/shard_map/ppermute | solution.py:21
  14.0 2.3 %convolution_convert_fusion.2.q_ref = bf16[2048,256]{1,0:T(8,128)(2,1)} fusion(bf16[2048,1024]{1,0:T(8,128)(2,1)S(1)} %copy-done.15, bf16[1024,256]{1,0:T(8,128)(2,1)S(1)} %copy-done.17), kind=kOutput, calls=%fused_computation.2 | convolution fusion | flops 1074266112 | bytes 5767168 | tf_op jit(solution)/shard_map/dot_general | solution.py:25
  17.0 0.9 pad_maximum_fusion.2.w_ref
  17.9 1.7 %collective-permute-done.low_ref = bf16[256,512]{1,0:T(8,128)(2,1)S(1)} collective-permute-done((bf16[256,512]{1,0:T(8,128)(2,1)}, bf16[256,512]{1,0:T(8,128)(2,1)S(1)}, u32[]{:S(2)}, u32[]{:S(2)}) %collective-permute-start) | collective-permute-done | bytes 262176 | tf_op jit(solution)/shard_map/ppermute | solution.py:21
  20.3 12.5 %shard_map.122 = bf16[4,1024,256]{2,1,0:T(8,128)(2,1)} custom-call(s32[3]{0:T(128)} %copy-done.13, bf16[2048,256]{1,0:T(8,128)(2,1)} %convolution_convert_fusion.2.q_ref, bf16[2048,256]{1,0:T(8,128)(2,1)} %copy-done.4, bf16[2048,256]{1,0:T(8,128)(2,1)} %copy-done.3, bf16[256,512]{1,0:T(8,128)(2,1)} %copy-done.7, bf16[256,512]{1,0:T(8,128)(2,1)} %copy-done.6, ...), custom_call_target="tpu_custom_call" | custom-call | flops 1342177280 | bytes 5767168 | tf_op jit(solution)/shard_map/pallas_call | solution.py:93
  32.9 1.3 %slice.128 = bf16[2,1024,256]{2,1,0:T(8,128)(2,1)S(1)} slice(bf16[4,1024,256]{2,1,0:T(8,128)(2,1)} %shard_map.122), slice={[0:2], [0:1024], [0:256]} | slice | bytes 2097152 | tf_op jit(solution)/shard_map/slice | solution.py:229
  34.8 12.5 %shard_map.123 = bf16[4,1024,256]{2,1,0:T(8,128)(2,1)} custom-call(s32[3]{0:T(128)} %copy-done.14, bf16[2048,256]{1,0:T(8,128)(2,1)} %convolution_convert_fusion.2.q_ref, bf16[2048,256]{1,0:T(8,128)(2,1)} %copy-done.4, bf16[2048,256]{1,0:T(8,128)(2,1)} %copy-done.3, bf16[256,512]{1,0:T(8,128)(2,1)} %copy-done.7, bf16[256,512]{1,0:T(8,128)(2,1)} %copy-done.6, ...), custom_call_target="tpu_custom_call" | custom-call | flops 1342177280 | bytes 5767168 | tf_op jit(solution)/shard_map/pallas_call | solution.py:93
  47.3 2.8 %fusion.1 = (bf16[1024,256]{1,0:T(8,128)(2,1)}, bf16[1024,256]{1,0:T(8,128)(2,1)S(1)}) fusion(bf16[2,1024,256]{2,1,0:T(8,128)(2,1)} %collective-permute-done.2, bf16[4,1024,256]{2,1,0:T(8,128)(2,1)} %shard_map.122), kind=kLoop, calls=%fused_computation.14 | loop fusion | flops 2097152 | bytes 3145728 | tf_op jit(solution)/shard_map/convert_element_type | solution.py:231
  50.1 1.0 slice.113
  51.6 1.5 %convolution_convert_fusion.4.q_ref = bf16[1024,256]{1,0:T(8,128)(2,1)} fusion(bf16[1024,1024]{1,0:T(8,128)(2,1)S(1)} %copy-done, bf16[1024,256]{1,0:T(8,128)(2,1)S(1)} %copy-done.18), kind=kOutput, calls=%fused_computation.4 | convolution fusion | flops 537133056 | bytes 3145728 | tf_op jit(solution)/shard_map/dot_general | solution.py:25
  53.1 17.0 %shard_map.124 = (f32[1024,256]{1,0:T(8,128)}, f32[1024,128]{1,0:T(8,128)}) custom-call(s32[1]{0:T(128)} %bitcast.6.scal_ref, bf16[1024,256]{1,0:T(8,128)(2,1)} %convolution_convert_fusion.4.q_ref, bf16[2048,256]{1,0:T(8,128)(2,1)} %copy-done.4, bf16[2048,256]{1,0:T(8,128)(2,1)} %copy-done.3), custom_call_target="tpu_custom_call" | custom-call | flops 2147483648 | bytes 4194304 | tf_op jit(solution)/shard_map/pallas_call | solution.py:153
  70.1 1.3 %convert_element_type.163 = bf16[1024,256]{1,0:T(8,128)(2,1)S(1)} convert(f32[1024,256]{1,0:T(8,128)} %get-tuple-element.65) | non-fusion elementwise | flops 262144 | bytes 1572864 | tf_op jit(solution)/shard_map/convert_element_type | solution.py:358
  71.9 1.2 %copy-done.2 = bf16[4,1024,256]{2,1,0:T(8,128)(2,1)S(1)} copy-done((bf16[4,1024,256]{2,1,0:T(8,128)(2,1)S(1)}, bf16[4,1024,256]{2,1,0:T(8,128)(2,1)}, u32[]{:S(2)}) %copy-start.2) | copy-done | bytes 2097176
  73.0 2.3 %fusion.3 = (bf16[1024,256]{1,0:T(8,128)(2,1)}, bf16[1024,256]{1,0:T(8,128)(2,1)S(1)}) fusion(bf16[2,1024,256]{2,1,0:T(8,128)(2,1)} %collective-permute-done.4, bf16[4,1024,256]{2,1,0:T(8,128)(2,1)S(1)} %copy-done.2), kind=kLoop, calls=%fused_computation.16 | loop fusion | flops 2097152 | bytes 3145728 | tf_op jit(solution)/shard_map/convert_element_type | solution.py:231
  75.3 0.8 constant_dynamic-slice_fusion.3
  76.1 2.4 %collective-permute-start.6 = (bf16[256,280]{1,0:T(8,128)(2,1)S(1)}, bf16[256,280]{1,0:T(8,128)(2,1)S(1)}, u32[]{:S(2)}, u32[]{:S(2)}) collective-permute-start(bf16[256,280]{1,0:T(8,128)(2,1)S(1)} %get-tuple-element.83), channel_id=1, source_target_pairs={{0,4},{4,8},{8,12},{12,0},{1,5},{5,9},{9,13},{13,1},{2,6},{6,10},{... | collective-permute-start | bytes 430088 | tf_op jit(solution)/shard_map/ppermute | solution.py:272
  78.5 2.8 %collective-permute-start.7 = (bf16[256,280]{1,0:T(8,128)(2,1)S(1)}, bf16[256,280]{1,0:T(8,128)(2,1)S(1)}, u32[]{:S(2)}, u32[]{:S(2)}) collective-permute-start(bf16[256,280]{1,0:T(8,128)(2,1)S(1)} %get-tuple-element.82), channel_id=1, source_target_pairs={{0,8},{4,12},{8,0},{12,4},{1,9},{5,13},{9,1},{13,5},{2,10},{6,14},... | collective-permute-start | bytes 430088 | tf_op jit(solution)/shard_map/ppermute | solution.py:272
  81.2 1.3 %collective-permute-start.8 = (bf16[256,280]{1,0:T(8,128)(2,1)S(1)}, bf16[256,280]{1,0:T(8,128)(2,1)S(1)}, u32[]{:S(2)}, u32[]{:S(2)}) collective-permute-start(bf16[256,280]{1,0:T(8,128)(2,1)S(1)} %get-tuple-element.81), channel_id=1, source_target_pairs={{0,12},{4,0},{8,4},{12,8},{1,13},{5,1},{9,5},{13,9},{2,14},{6,2},{... | collective-permute-start | bytes 430088 | tf_op jit(solution)/shard_map/ppermute | solution.py:272
  82.6 0.8 constant_dynamic-slice_fusion.2
  83.4 1.5 %collective-permute-start.3 = (bf16[1024,256]{1,0:T(8,128)(2,1)}, bf16[1024,256]{1,0:T(8,128)(2,1)}, u32[]{:S(2)}, u32[]{:S(2)}) collective-permute-start(bf16[1024,256]{1,0:T(8,128)(2,1)} %get-tuple-element.61), channel_id=1, source_target_pairs={{0,2},{1,3},{2,0},{3,1},{4,6},{5,7},{6,4},{7,5},{8,10},{9,11},{10,... | collective-permute-start | bytes 1572872 | tf_op jit(solution)/shard_map/ppermute | solution.py:244
  85.5 1.1 collective-permute-done.6.refs_1_
  86.5 7.8 %collective-permute-done.7.refs_2_ = bf16[256,280]{1,0:T(8,128)(2,1)S(1)} collective-permute-done((bf16[256,280]{1,0:T(8,128)(2,1)S(1)}, bf16[256,280]{1,0:T(8,128)(2,1)S(1)}, u32[]{:S(2)}, u32[]{:S(2)}) %collective-permute-start.7) | collective-permute-done | bytes 143392 | tf_op jit(solution)/shard_map/ppermute | solution.py:272
  95.1 3.0 %shard_map.125 = bf16[256,256]{1,0:T(8,128)(2,1)} custom-call(bf16[256,280]{1,0:T(8,128)(2,1)} %get-tuple-element.84.refs_0_, bf16[256,280]{1,0:T(8,128)(2,1)} %copy-done.10, bf16[256,280]{1,0:T(8,128)(2,1)} %copy-done.11, bf16[256,280]{1,0:T(8,128)(2,1)} %copy-done.12), custom_call_target="tpu_custom_call" | custom-call | tf_op jit(solution)/shard_map/pallas_call | solution.py:309
  98.1 1.5 %convolution_convert_fusion.3 = bf16[256,1024]{1,0:T(8,128)(2,1)S(1)} fusion(bf16[256,256]{1,0:T(8,128)(2,1)} %shard_map.125, bf16[256,256]{1,0:T(8,128)(2,1)} %get-tuple-element.89, bf16[256,256]{1,0:T(8,128)(2,1)} %get-tuple-element.90, bf16[256,256]{1,0:T(8,128)(2,1)} %get-tuple-element.88, bf16[256,256]{1,0:T(8,128)(2,1)} %get-tuple-element.87), kind=kOutput, calls=%fused_computation.3 | convolution fusion | flops 136577024 | bytes 1179648 | tf_op jit(solution)/shard_map/dot_general | solution.py:369
  99.7 1.2 %add_convert_fusion.3 = bf16[1024,256]{1,0:T(8,128)(2,1)S(1)} fusion(bf16[1024,256]{1,0:T(8,128)(2,1)} %collective-permute-done.3, bf16[1024,256]{1,0:T(8,128)(2,1)S(1)} %get-tuple-element.60), kind=kLoop, calls=%fused_computation.9 | loop fusion | flops 1048576 | bytes 1572864 | tf_op jit(solution)/shard_map/convert_element_type | solution.py:245
  101.3 1.6 %collective-permute-start.10 = (bf16[256,256]{1,0:T(8,128)(2,1)S(1)}, bf16[256,256]{1,0:T(8,128)(2,1)S(1)}, u32[]{:S(2)}, u32[]{:S(2)}) collective-permute-start(bf16[256,256]{1,0:T(8,128)(2,1)S(1)} %fusion.12), channel_id=1, source_target_pairs={{0,2},{1,3},{2,0},{3,1},{4,6},{5,7},{6,4},{7,5},{8,10},{9,11},{10,... | collective-permute-start | bytes 393224 | tf_op jit(solution)/shard_map/ppermute | solution.py:244
  102.8 6.5 %collective-permute-done.5 = bf16[1024,256]{1,0:T(8,128)(2,1)} collective-permute-done((bf16[1024,256]{1,0:T(8,128)(2,1)}, bf16[1024,256]{1,0:T(8,128)(2,1)}, u32[]{:S(2)}, u32[]{:S(2)}) %collective-permute-start.5) | collective-permute-done | bytes 524320 | tf_op jit(solution)/shard_map/ppermute | solution.py:244
  109.4 1.2 %add_convert_fusion = bf16[1024,256]{1,0:T(8,128)(2,1)S(1)} fusion(bf16[1024,256]{1,0:T(8,128)(2,1)} %collective-permute-done.5, bf16[1024,256]{1,0:T(8,128)(2,1)S(1)} %get-tuple-element.67), kind=kLoop, calls=%fused_computation.6 | loop fusion | flops 1048576 | bytes 1572864 | tf_op jit(solution)/shard_map/convert_element_type | solution.py:245
  110.5 1.0 pad_maximum_fusion
  (65 shorter events, 5.8 us)
Async XLA Ops:
  0.6 51.0 %copy-start = (bf16[1024,1024]{1,0:T(8,128)(2,1)S(1)}, bf16[1024,1024]{1,0:T(8,128)(2,1)}, u32[]{:S(2)}) copy-start(bf16[1024,1024]{1,0:T(8,128)(2,1)} %param.20) | copy-start | bytes 6291460
  0.6 3.8 %copy-start.15 = (bf16[2048,1024]{1,0:T(8,128)(2,1)S(1)}, bf16[2048,1024]{1,0:T(8,128)(2,1)}, u32[]{:S(2)}) copy-start(bf16[2048,1024]{1,0:T(8,128)(2,1)} %param.19) | copy-start | bytes 12582916
  0.7 3.9 %copy-start.16 = (bf16[1024,256]{1,0:T(8,128)(2,1)S(1)}, bf16[1024,256]{1,0:T(8,128)(2,1)}, u32[]{:S(2)}) copy-start(bf16[1024,256]{1,0:T(8,128)(2,1)} %param.23) | copy-start | bytes 1572868
  4.5 1.3 %copy-start.3 = (bf16[2048,256]{1,0:T(8,128)(2,1)}, bf16[2048,256]{1,0:T(8,128)(2,1)S(1)}, u32[]{:S(2)}) copy-start(bf16[2048,256]{1,0:T(8,128)(2,1)S(1)} %convolution_convert_fusion.v_ref) | copy-start | bytes 3145732
  5.8 10.4 %copy-start.4 = (bf16[2048,256]{1,0:T(8,128)(2,1)}, bf16[2048,256]{1,0:T(8,128)(2,1)S(1)}, u32[]{:S(2)}) copy-start(bf16[2048,256]{1,0:T(8,128)(2,1)S(1)} %convolution_convert_fusion.1.k_ref) | copy-start | bytes 3145732
  5.8 8.1 %copy-start.17 = (bf16[1024,256]{1,0:T(8,128)(2,1)S(1)}, bf16[1024,256]{1,0:T(8,128)(2,1)}, u32[]{:S(2)}) copy-start(bf16[1024,256]{1,0:T(8,128)(2,1)} %param.22) | copy-start | bytes 1572868
  5.9 12.0 %collective-permute-start.1 = (bf16[256,512]{1,0:T(8,128)(2,1)S(1)}, bf16[256,512]{1,0:T(8,128)(2,1)S(1)}, u32[]{:S(2)}, u32[]{:S(2)}) collective-permute-start(bf16[256,512]{1,0:T(8,128)(2,1)S(1)} %pad_maximum_fusion.4), channel_id=1, source_target_pairs={{4,0},{8,4},{12,8},{5,1},{9,5},{13,9},{6,2},{10,6},{14,10},{7,3},{... | collective-permute-start | bytes 786440 | tf_op jit(solution)/shard_map/ppermute | solution.py:21
  8.1 8.8 %copy-start.8 = (bf16[256,1024]{1,0:T(8,128)(2,1)S(1)}, bf16[256,1024]{1,0:T(8,128)(2,1)}, u32[]{:S(2)}) copy-start(bf16[256,1024]{1,0:T(8,128)(2,1)} %param.25) | copy-start | bytes 1572868
  8.1 11.5 %collective-permute-start = (bf16[256,512]{1,0:T(8,128)(2,1)}, bf16[256,512]{1,0:T(8,128)(2,1)S(1)}, u32[]{:S(2)}, u32[]{:S(2)}) collective-permute-start(bf16[256,512]{1,0:T(8,128)(2,1)} %pad_maximum_fusion.3), channel_id=1, source_target_pairs={{0,4},{4,8},{8,12},{1,5},{5,9},{9,13},{2,6},{6,10},{10,14},{3,7},{... | collective-permute-start | bytes 786440 | tf_op jit(solution)/shard_map/ppermute | solution.py:21
  16.9 2.7 %copy-start.13 = (s32[3]{0:T(128)}, s32[3]{0:T(128)S(1)}, u32[]{:S(2)}) copy-start(s32[3]{0:T(128)S(1)} %constant_dynamic-update-slice_fusion.2.scal_ref) | copy-start | bytes 40
  17.9 1.7 %copy-start.6 = (bf16[256,512]{1,0:T(8,128)(2,1)}, bf16[256,512]{1,0:T(8,128)(2,1)S(1)}, u32[]{:S(2)}) copy-start(bf16[256,512]{1,0:T(8,128)(2,1)S(1)} %collective-permute-done.1.high_ref) | copy-start | bytes 786436
  19.6 0.7 copy-start.7
  32.9 1.4 %copy-start.19 = (s32[3]{0:T(128)S(1)}, s32[3]{0:T(128)}, u32[]{:S(2)}) copy-start(s32[3]{0:T(128)} %constant.165.clone) | copy-start | bytes 40
  34.2 13.1 %collective-permute-start.2 = (bf16[2,1024,256]{2,1,0:T(8,128)(2,1)S(1)}, bf16[2,1024,256]{2,1,0:T(8,128)(2,1)}, u32[]{:S(2)}, u32[]{:S(2)}) collective-permute-start(bf16[2,1024,256]{2,1,0:T(8,128)(2,1)S(1)} %slice.128), channel_id=1, source_target_pairs={{0,1},{1,0},{2,3},{3,2},{4,5},{5,4},{6,7},{7,6},{8,9},{9,8},{10,11... | collective-permute-start | bytes 3145736 | tf_op jit(solution)/shard_map/ppermute | solution.py:229
  34.3 0.5 copy-start.14
  47.3 2.8 %copy-start.1 = (bf16[4,1024,256]{2,1,0:T(8,128)(2,1)S(1)}, bf16[4,1024,256]{2,1,0:T(8,128)(2,1)}, u32[]{:S(2)}) copy-start(bf16[4,1024,256]{2,1,0:T(8,128)(2,1)} %shard_map.123) | copy-start | bytes 6291460
  47.3 4.3 %copy-start.18 = (bf16[1024,256]{1,0:T(8,128)(2,1)S(1)}, bf16[1024,256]{1,0:T(8,128)(2,1)}, u32[]{:S(2)}) copy-start(bf16[1024,256]{1,0:T(8,128)(2,1)} %param.26) | copy-start | bytes 1572868
  51.1 20.7 %collective-permute-start.4 = (bf16[2,1024,256]{2,1,0:T(8,128)(2,1)}, bf16[2,1024,256]{2,1,0:T(8,128)(2,1)}, u32[]{:S(2)}, u32[]{:S(2)}) collective-permute-start(bf16[2,1024,256]{2,1,0:T(8,128)(2,1)} %slice.113), channel_id=1, source_target_pairs={{0,1},{1,0},{2,3},{3,2},{4,5},{5,4},{6,7},{7,6},{8,9},{9,8},{10,11... | collective-permute-start | bytes 3145736 | tf_op jit(solution)/shard_map/ppermute | solution.py:229
  70.1 1.4 %copy-start.5 = (f32[1024,128]{1,0:T(8,128)S(1)}, f32[1024,128]{1,0:T(8,128)}, u32[]{:S(2)}) copy-start(f32[1024,128]{1,0:T(8,128)} %get-tuple-element.66) | copy-start | bytes 1572868
  71.4 1.6 %copy-start.2 = (bf16[4,1024,256]{2,1,0:T(8,128)(2,1)S(1)}, bf16[4,1024,256]{2,1,0:T(8,128)(2,1)}, u32[]{:S(2)}) copy-start(bf16[4,1024,256]{2,1,0:T(8,128)(2,1)} %shard_map.123) | copy-start | bytes 6291460
  71.8 10.7 %copy-start.9 = (bf16[256,1024]{1,0:T(8,128)(2,1)S(1)}, bf16[256,1024]{1,0:T(8,128)(2,1)}, u32[]{:S(2)}) copy-start(bf16[256,1024]{1,0:T(8,128)(2,1)} %param.27) | copy-start | bytes 1572868
  76.1 10.4 %collective-permute-start.6 = (bf16[256,280]{1,0:T(8,128)(2,1)S(1)}, bf16[256,280]{1,0:T(8,128)(2,1)S(1)}, u32[]{:S(2)}, u32[]{:S(2)}) collective-permute-start(bf16[256,280]{1,0:T(8,128)(2,1)S(1)} %get-tuple-element.83), channel_id=1, source_target_pairs={{0,4},{4,8},{8,12},{12,0},{1,5},{5,9},{9,13},{13,1},{2,6},{6,10},{... | collective-permute-start | bytes 430088 | tf_op jit(solution)/shard_map/ppermute | solution.py:272
  78.5 15.9 %collective-permute-start.7 = (bf16[256,280]{1,0:T(8,128)(2,1)S(1)}, bf16[256,280]{1,0:T(8,128)(2,1)S(1)}, u32[]{:S(2)}, u32[]{:S(2)}) collective-permute-start(bf16[256,280]{1,0:T(8,128)(2,1)S(1)} %get-tuple-element.82), channel_id=1, source_target_pairs={{0,8},{4,12},{8,0},{12,4},{1,9},{5,13},{9,1},{13,5},{2,10},{6,14},... | collective-permute-start | bytes 430088 | tf_op jit(solution)/shard_map/ppermute | solution.py:272
  81.2 13.1 %collective-permute-start.8 = (bf16[256,280]{1,0:T(8,128)(2,1)S(1)}, bf16[256,280]{1,0:T(8,128)(2,1)S(1)}, u32[]{:S(2)}, u32[]{:S(2)}) collective-permute-start(bf16[256,280]{1,0:T(8,128)(2,1)S(1)} %get-tuple-element.81), channel_id=1, source_target_pairs={{0,12},{4,0},{8,4},{12,8},{1,13},{5,1},{9,5},{13,9},{2,14},{6,2},{... | collective-permute-start | bytes 430088 | tf_op jit(solution)/shard_map/ppermute | solution.py:272
  83.4 16.3 %collective-permute-start.3 = (bf16[1024,256]{1,0:T(8,128)(2,1)}, bf16[1024,256]{1,0:T(8,128)(2,1)}, u32[]{:S(2)}, u32[]{:S(2)}) collective-permute-start(bf16[1024,256]{1,0:T(8,128)(2,1)} %get-tuple-element.61), channel_id=1, source_target_pairs={{0,2},{1,3},{2,0},{3,1},{4,6},{5,7},{6,4},{7,5},{8,10},{9,11},{10,... | collective-permute-start | bytes 1572872 | tf_op jit(solution)/shard_map/ppermute | solution.py:244
  84.9 24.5 %collective-permute-start.5 = (bf16[1024,256]{1,0:T(8,128)(2,1)}, bf16[1024,256]{1,0:T(8,128)(2,1)}, u32[]{:S(2)}, u32[]{:S(2)}) collective-permute-start(bf16[1024,256]{1,0:T(8,128)(2,1)} %get-tuple-element.68), channel_id=1, source_target_pairs={{0,2},{1,3},{2,0},{3,1},{4,6},{5,7},{6,4},{7,5},{8,10},{9,11},{10,... | collective-permute-start | bytes 1572872 | tf_op jit(solution)/shard_map/ppermute | solution.py:244
  86.5 8.5 %copy-start.10 = (bf16[256,280]{1,0:T(8,128)(2,1)}, bf16[256,280]{1,0:T(8,128)(2,1)S(1)}, u32[]{:S(2)}) copy-start(bf16[256,280]{1,0:T(8,128)(2,1)S(1)} %collective-permute-done.6.refs_1_) | copy-start | bytes 430084
  94.3 0.8 copy-start.11
  94.3 0.7 copy-start.12
  99.6 1.6 %collective-permute-start.9 = (bf16[2,256,256]{2,1,0:T(8,128)(2,1)S(1)}, bf16[2,256,256]{2,1,0:T(8,128)(2,1)S(1)}, u32[]{:S(2)}, u32[]{:S(2)}) collective-permute-start(bf16[2,256,256]{2,1,0:T(8,128)(2,1)S(1)} %pad_maximum_fusion.5), channel_id=1, source_target_pairs={{0,1},{1,0},{2,3},{3,2},{4,5},{5,4},{6,7},{7,6},{8,9},{9,8},{10,11... | collective-permute-start | bytes 786440 | tf_op jit(solution)/shard_map/ppermute | solution.py:229
  101.3 10.3 %collective-permute-start.10 = (bf16[256,256]{1,0:T(8,128)(2,1)S(1)}, bf16[256,256]{1,0:T(8,128)(2,1)S(1)}, u32[]{:S(2)}, u32[]{:S(2)}) collective-permute-start(bf16[256,256]{1,0:T(8,128)(2,1)S(1)} %fusion.12), channel_id=1, source_target_pairs={{0,2},{1,3},{2,0},{3,1},{4,6},{5,7},{6,4},{7,5},{8,10},{9,11},{10,... | collective-permute-start | bytes 393224 | tf_op jit(solution)/shard_map/ppermute | solution.py:244

commit v15 on v14

--- a/solution.py
+++ b/solution.py
@@ -79,7 +79,7 @@
     frame_count, width = query.shape
     out_width = w_out.shape[1]
     block_width = out_width // blocks
-    tq = min(256, rows)
+    tq = min(512, rows)
     block_base = row_base // tq
     span = tq + 2 * HALF
     scal = jnp.array([0, 0, row_base], jnp.int32).at[0].set(first_frame).at[1].set(length)

time: 113 us -> 111 us (0.982)
    unnamed x41 -> x39, local copies, waits for them, and re-layouts: 3.35 us -> 2.74 us
  transfers between devices with their start and end apart: 11 -> 11, of which waited for: 5 -> 5; matrix products, arithmetic and copies ran while one was open for 12% -> 11% of each run, Pallas kernels for 29% -> 29%
where the time goes in v15:
time: 111 us; the launch traced here: 110 us
  Pallas kernels  44.5 us (40%)
  starting transfers between devices  18.7 us (17%)
  waiting for transfers between devices  16.6 us (15%)
  other arithmetic  11.9 us (11%)
  matrix products  10.2 us (9%)
  local copies, waits for them, and re-layouts  6.85 us (6%)
  between operations  1.6 us (1%)
    pallas_call x2, Pallas kernels, window_attention(): pl.pallas_call(kernel, cost_estimate=cost, out_shape=jax.ShapeDtypeStruct...  24.5 us
    pallas_call x1, Pallas kernels, latent_attention(): pl.pallas_call(kernel, cost_estimate=cost, out_shape=(jax.ShapeDtypeStruc...  17 us
    ppermute x3, waiting for transfers between devices, exchange_rows(): parts.append(lax.ppermute(block, axis, pairs))  8.91 us
    dot_general x4, matrix products, project(): jnp.dot(source, weight, preferred_element_type=jnp.float32)  8.76 us
    ppermute x3, starting transfers between devices, exchange_rows(): parts.append(lax.ppermute(block, axis, pairs))  6.68 us
    ppermute x3, waiting for transfers between devices, cross_chip_sum(): total = total + lax.ppermute(chip_sums[d], axis, pairs).astype(jnp.float32)  6.53 us
    ppermute x1, starting transfers between devices, halos(): lax.ppermute(tail, axis, forward)  6.42 us
    convert_element_type x3, other arithmetic, chip_pair_sums(): (blocks[chips + d].astype(jnp.float32) + received[d].astype(jnp.float32))...  5.1 us
  transfers between devices with their start and end apart: 11, of which 5 were waited for; matrix products, arithmetic and copies ran while one was open for 11% of the time, Pallas kernels for 29%

profile of v15, /device:TPU:0, one launch (start us, length us, event | category | flops | bytes accessed | tf_op | source)
XLA Modules:
  0.0 110.4 jit_solution(2913404722379840895)
XLA Ops:
  0.7 3.7 %convolution_convert_fusion.v_ref = bf16[2048,256]{1,0:T(8,128)(2,1)S(1)} fusion(bf16[2048,1024]{1,0:T(8,128)(2,1)} %param.19, bf16[1024,256]{1,0:T(8,128)(2,1)} %param.24), kind=kOutput, calls=%fused_computation | convolution fusion | flops 1074266112 | bytes 5767168 | tf_op jit(solution)/shard_map/dot_general | solution.py:25
  4.5 1.3 %convolution_convert_fusion.1.k_ref = bf16[2048,256]{1,0:T(8,128)(2,1)S(1)} fusion(bf16[2048,1024]{1,0:T(8,128)(2,1)S(1)} %copy-done.11, bf16[1024,256]{1,0:T(8,128)(2,1)S(1)} %copy-done.12), kind=kOutput, calls=%fused_computation.1 | convolution fusion | flops 1074266112 | bytes 5767168 | tf_op jit(solution)/shard_map/dot_general | solution.py:25
  5.9 1.4 %collective-permute-start.1 = (bf16[256,512]{1,0:T(8,128)(2,1)S(1)}, bf16[256,512]{1,0:T(8,128)(2,1)S(1)}, u32[]{:S(2)}, u32[]{:S(2)}) collective-permute-start(bf16[256,512]{1,0:T(8,128)(2,1)S(1)} %pad_maximum_fusion.4), channel_id=1, source_target_pairs={{4,0},{8,4},{12,8},{5,1},{9,5},{13,9},{6,2},{10,6},{14,10},{7,3},{... | collective-permute-start | bytes 786440 | tf_op jit(solution)/shard_map/ppermute | solution.py:21
  7.4 6.4 %collective-permute-start = (bf16[256,512]{1,0:T(8,128)(2,1)S(1)}, bf16[256,512]{1,0:T(8,128)(2,1)}, u32[]{:S(2)}, u32[]{:S(2)}) collective-permute-start(bf16[256,512]{1,0:T(8,128)(2,1)S(1)} %pad_maximum_fusion.3), channel_id=1, source_target_pairs={{0,4},{4,8},{8,12},{1,5},{5,9},{9,13},{2,6},{6,10},{10,14},{3,7},{... | collective-permute-start | bytes 786440 | tf_op jit(solution)/shard_map/ppermute | solution.py:21
  13.8 2.2 %convolution_convert_fusion.2.q_ref = bf16[2048,256]{1,0:T(8,128)(2,1)} fusion(bf16[2048,1024]{1,0:T(8,128)(2,1)S(1)} %copy-done.11, bf16[1024,256]{1,0:T(8,128)(2,1)S(1)} %copy-done.13), kind=kOutput, calls=%fused_computation.2 | convolution fusion | flops 1074266112 | bytes 5767168 | tf_op jit(solution)/shard_map/dot_general | solution.py:25
  16.9 0.9 pad_maximum_fusion.2.w_ref
  17.8 0.8 collective-permute-done.low_ref
  18.6 12.3 %shard_map.122 = bf16[4,1024,256]{2,1,0:T(8,128)(2,1)} custom-call(s32[3]{0:T(128)} %copy-done.16, bf16[2048,256]{1,0:T(8,128)(2,1)} %convolution_convert_fusion.2.q_ref, bf16[2048,256]{1,0:T(8,128)(2,1)} %copy-done.10, bf16[2048,256]{1,0:T(8,128)(2,1)} %copy-done.9, bf16[256,512]{1,0:T(8,128)(2,1)} %collective-permute-done.low_ref, ...), custom_call_target="tpu_custom_call" | custom-call | flops 1610612736 | bytes 5767168 | tf_op jit(solution)/shard_map/pallas_call | solution.py:93
  30.9 1.3 %slice.128 = bf16[2,1024,256]{2,1,0:T(8,128)(2,1)S(1)} slice(bf16[4,1024,256]{2,1,0:T(8,128)(2,1)} %shard_map.122), slice={[0:2], [0:1024], [0:256]} | slice | bytes 2097152 | tf_op jit(solution)/shard_map/slice | solution.py:229
  32.9 12.2 %shard_map.123 = bf16[4,1024,256]{2,1,0:T(8,128)(2,1)} custom-call(s32[3]{0:T(128)} %copy-done.18, bf16[2048,256]{1,0:T(8,128)(2,1)} %convolution_convert_fusion.2.q_ref, bf16[2048,256]{1,0:T(8,128)(2,1)} %copy-done.10, bf16[2048,256]{1,0:T(8,128)(2,1)} %copy-done.9, bf16[256,512]{1,0:T(8,128)(2,1)} %collective-permute-done.low_ref, ...), custom_call_target="tpu_custom_call" | custom-call | flops 1610612736 | bytes 5767168 | tf_op jit(solution)/shard_map/pallas_call | solution.py:93
  45.2 2.8 %fusion.1 = (bf16[1024,256]{1,0:T(8,128)(2,1)}, bf16[1024,256]{1,0:T(8,128)(2,1)S(1)}) fusion(bf16[2,1024,256]{2,1,0:T(8,128)(2,1)} %collective-permute-done.2, bf16[4,1024,256]{2,1,0:T(8,128)(2,1)} %shard_map.122), kind=kLoop, calls=%fused_computation.14 | loop fusion | flops 2097152 | bytes 3145728 | tf_op jit(solution)/shard_map/convert_element_type | solution.py:231
  48.0 1.0 slice.113
  49.5 1.5 %convolution_convert_fusion.4.q_ref = bf16[1024,256]{1,0:T(8,128)(2,1)} fusion(bf16[1024,1024]{1,0:T(8,128)(2,1)S(1)} %copy-done, bf16[1024,256]{1,0:T(8,128)(2,1)S(1)} %copy-done.14), kind=kOutput, calls=%fused_computation.4 | convolution fusion | flops 537133056 | bytes 3145728 | tf_op jit(solution)/shard_map/dot_general | solution.py:25
  51.0 17.0 %shard_map.124 = (f32[1024,256]{1,0:T(8,128)}, f32[1024,128]{1,0:T(8,128)}) custom-call(s32[1]{0:T(128)} %bitcast.6.scal_ref, bf16[1024,256]{1,0:T(8,128)(2,1)} %convolution_convert_fusion.4.q_ref, bf16[2048,256]{1,0:T(8,128)(2,1)} %copy-done.10, bf16[2048,256]{1,0:T(8,128)(2,1)} %copy-done.9), custom_call_target="tpu_custom_call" | custom-call | flops 2147483648 | bytes 4194304 | tf_op jit(solution)/shard_map/pallas_call | solution.py:153
  68.0 1.3 %convert_element_type.163 = bf16[1024,256]{1,0:T(8,128)(2,1)S(1)} convert(f32[1024,256]{1,0:T(8,128)} %get-tuple-element.65) | non-fusion elementwise | flops 262144 | bytes 1572864 | tf_op jit(solution)/shard_map/convert_element_type | solution.py:358
  69.8 1.2 %copy-done.2 = bf16[4,1024,256]{2,1,0:T(8,128)(2,1)S(1)} copy-done((bf16[4,1024,256]{2,1,0:T(8,128)(2,1)S(1)}, bf16[4,1024,256]{2,1,0:T(8,128)(2,1)}, u32[]{:S(2)}) %copy-start.2) | copy-done | bytes 2097176
  70.9 2.3 %fusion.3 = (bf16[1024,256]{1,0:T(8,128)(2,1)}, bf16[1024,256]{1,0:T(8,128)(2,1)S(1)}) fusion(bf16[2,1024,256]{2,1,0:T(8,128)(2,1)} %collective-permute-done.4, bf16[4,1024,256]{2,1,0:T(8,128)(2,1)S(1)} %copy-done.2), kind=kLoop, calls=%fused_computation.16 | loop fusion | flops 2097152 | bytes 3145728 | tf_op jit(solution)/shard_map/convert_element_type | solution.py:231
  73.2 0.8 constant_dynamic-slice_fusion.3
  74.0 2.6 %collective-permute-start.6 = (bf16[256,280]{1,0:T(8,128)(2,1)S(1)}, bf16[256,280]{1,0:T(8,128)(2,1)S(1)}, u32[]{:S(2)}, u32[]{:S(2)}) collective-permute-start(bf16[256,280]{1,0:T(8,128)(2,1)S(1)} %get-tuple-element.83), channel_id=1, source_target_pairs={{0,4},{4,8},{8,12},{12,0},{1,5},{5,9},{9,13},{13,1},{2,6},{6,10},{... | collective-permute-start | bytes 430088 | tf_op jit(solution)/shard_map/ppermute | solution.py:272
  76.6 2.8 %collective-permute-start.7 = (bf16[256,280]{1,0:T(8,128)(2,1)S(1)}, bf16[256,280]{1,0:T(8,128)(2,1)S(1)}, u32[]{:S(2)}, u32[]{:S(2)}) collective-permute-start(bf16[256,280]{1,0:T(8,128)(2,1)S(1)} %get-tuple-element.82), channel_id=1, source_target_pairs={{0,8},{4,12},{8,0},{12,4},{1,9},{5,13},{9,1},{13,5},{2,10},{6,14},... | collective-permute-start | bytes 430088 | tf_op jit(solution)/shard_map/ppermute | solution.py:272
  79.3 1.3 %collective-permute-start.8 = (bf16[256,280]{1,0:T(8,128)(2,1)S(1)}, bf16[256,280]{1,0:T(8,128)(2,1)S(1)}, u32[]{:S(2)}, u32[]{:S(2)}) collective-permute-start(bf16[256,280]{1,0:T(8,128)(2,1)S(1)} %get-tuple-element.81), channel_id=1, source_target_pairs={{0,12},{4,0},{8,4},{12,8},{1,13},{5,1},{9,5},{13,9},{2,14},{6,2},{... | collective-permute-start | bytes 430088 | tf_op jit(solution)/shard_map/ppermute | solution.py:272
  80.7 0.8 constant_dynamic-slice_fusion.2
  81.5 1.5 %collective-permute-start.3 = (bf16[1024,256]{1,0:T(8,128)(2,1)}, bf16[1024,256]{1,0:T(8,128)(2,1)}, u32[]{:S(2)}, u32[]{:S(2)}) collective-permute-start(bf16[1024,256]{1,0:T(8,128)(2,1)} %get-tuple-element.61), channel_id=1, source_target_pairs={{0,2},{1,3},{2,0},{3,1},{4,6},{5,7},{6,4},{7,5},{8,10},{9,11},{10,... | collective-permute-start | bytes 1572872 | tf_op jit(solution)/shard_map/ppermute | solution.py:244
  83.5 1.1 collective-permute-done.6.refs_1_
  84.6 7.8 %collective-permute-done.7.refs_2_ = bf16[256,280]{1,0:T(8,128)(2,1)S(1)} collective-permute-done((bf16[256,280]{1,0:T(8,128)(2,1)S(1)}, bf16[256,280]{1,0:T(8,128)(2,1)S(1)}, u32[]{:S(2)}, u32[]{:S(2)}) %collective-permute-start.7) | collective-permute-done | bytes 143392 | tf_op jit(solution)/shard_map/ppermute | solution.py:272
  93.2 3.0 %shard_map.125 = bf16[256,256]{1,0:T(8,128)(2,1)} custom-call(bf16[256,280]{1,0:T(8,128)(2,1)} %get-tuple-element.84.refs_0_, bf16[256,280]{1,0:T(8,128)(2,1)} %copy-done.6, bf16[256,280]{1,0:T(8,128)(2,1)} %copy-done.7, bf16[256,280]{1,0:T(8,128)(2,1)} %copy-done.8), custom_call_target="tpu_custom_call" | custom-call | tf_op jit(solution)/shard_map/pallas_call | solution.py:309
  96.2 1.5 %convolution_convert_fusion.3 = bf16[256,1024]{1,0:T(8,128)(2,1)S(1)} fusion(bf16[256,256]{1,0:T(8,128)(2,1)} %shard_map.125, bf16[256,256]{1,0:T(8,128)(2,1)} %get-tuple-element.89, bf16[256,256]{1,0:T(8,128)(2,1)} %get-tuple-element.90, bf16[256,256]{1,0:T(8,128)(2,1)} %get-tuple-element.88, bf16[256,256]{1,0:T(8,128)(2,1)} %get-tuple-element.87), kind=kOutput, calls=%fused_computation.3 | convolution fusion | flops 136577024 | bytes 1179648 | tf_op jit(solution)/shard_map/dot_general | solution.py:369
  97.8 1.2 %add_convert_fusion.3 = bf16[1024,256]{1,0:T(8,128)(2,1)S(1)} fusion(bf16[1024,256]{1,0:T(8,128)(2,1)} %collective-permute-done.3, bf16[1024,256]{1,0:T(8,128)(2,1)S(1)} %get-tuple-element.60), kind=kLoop, calls=%fused_computation.9 | loop fusion | flops 1048576 | bytes 1572864 | tf_op jit(solution)/shard_map/convert_element_type | solution.py:245
  99.4 1.6 %collective-permute-start.10 = (bf16[256,256]{1,0:T(8,128)(2,1)S(1)}, bf16[256,256]{1,0:T(8,128)(2,1)S(1)}, u32[]{:S(2)}, u32[]{:S(2)}) collective-permute-start(bf16[256,256]{1,0:T(8,128)(2,1)S(1)} %fusion.12), channel_id=1, source_target_pairs={{0,2},{1,3},{2,0},{3,1},{4,6},{5,7},{6,4},{7,5},{8,10},{9,11},{10,... | collective-permute-start | bytes 393224 | tf_op jit(solution)/shard_map/ppermute | solution.py:244
  100.9 6.5 %collective-permute-done.5 = bf16[1024,256]{1,0:T(8,128)(2,1)} collective-permute-done((bf16[1024,256]{1,0:T(8,128)(2,1)}, bf16[1024,256]{1,0:T(8,128)(2,1)}, u32[]{:S(2)}, u32[]{:S(2)}) %collective-permute-start.5) | collective-permute-done | bytes 524320 | tf_op jit(solution)/shard_map/ppermute | solution.py:244
  107.5 1.2 %add_convert_fusion = bf16[1024,256]{1,0:T(8,128)(2,1)S(1)} fusion(bf16[1024,256]{1,0:T(8,128)(2,1)} %collective-permute-done.5, bf16[1024,256]{1,0:T(8,128)(2,1)S(1)} %get-tuple-element.67), kind=kLoop, calls=%fused_computation.6 | loop fusion | flops 1048576 | bytes 1572864 | tf_op jit(solution)/shard_map/convert_element_type | solution.py:245
  108.6 1.0 pad_maximum_fusion
  (63 shorter events, 4.5 us)
Async XLA Ops:
  0.6 48.8 %copy-start = (bf16[1024,1024]{1,0:T(8,128)(2,1)S(1)}, bf16[1024,1024]{1,0:T(8,128)(2,1)}, u32[]{:S(2)}) copy-start(bf16[1024,1024]{1,0:T(8,128)(2,1)} %param.20) | copy-start | bytes 6291460
  0.6 3.8 %copy-start.11 = (bf16[2048,1024]{1,0:T(8,128)(2,1)S(1)}, bf16[2048,1024]{1,0:T(8,128)(2,1)}, u32[]{:S(2)}) copy-start(bf16[2048,1024]{1,0:T(8,128)(2,1)} %param.19) | copy-start | bytes 12582916
  0.7 3.9 %copy-start.12 = (bf16[1024,256]{1,0:T(8,128)(2,1)S(1)}, bf16[1024,256]{1,0:T(8,128)(2,1)}, u32[]{:S(2)}) copy-start(bf16[1024,256]{1,0:T(8,128)(2,1)} %param.23) | copy-start | bytes 1572868
  4.5 1.3 %copy-start.9 = (bf16[2048,256]{1,0:T(8,128)(2,1)}, bf16[2048,256]{1,0:T(8,128)(2,1)S(1)}, u32[]{:S(2)}) copy-start(bf16[2048,256]{1,0:T(8,128)(2,1)S(1)} %convolution_convert_fusion.v_ref) | copy-start | bytes 3145732
  5.8 10.2 %copy-start.10 = (bf16[2048,256]{1,0:T(8,128)(2,1)}, bf16[2048,256]{1,0:T(8,128)(2,1)S(1)}, u32[]{:S(2)}) copy-start(bf16[2048,256]{1,0:T(8,128)(2,1)S(1)} %convolution_convert_fusion.1.k_ref) | copy-start | bytes 3145732
  5.8 8.0 %copy-start.13 = (bf16[1024,256]{1,0:T(8,128)(2,1)S(1)}, bf16[1024,256]{1,0:T(8,128)(2,1)}, u32[]{:S(2)}) copy-start(bf16[1024,256]{1,0:T(8,128)(2,1)} %param.22) | copy-start | bytes 1572868
  5.9 11.9 %collective-permute-start.1 = (bf16[256,512]{1,0:T(8,128)(2,1)S(1)}, bf16[256,512]{1,0:T(8,128)(2,1)S(1)}, u32[]{:S(2)}, u32[]{:S(2)}) collective-permute-start(bf16[256,512]{1,0:T(8,128)(2,1)S(1)} %pad_maximum_fusion.4), channel_id=1, source_target_pairs={{4,0},{8,4},{12,8},{5,1},{9,5},{13,9},{6,2},{10,6},{14,10},{7,3},{... | collective-permute-start | bytes 786440 | tf_op jit(solution)/shard_map/ppermute | solution.py:21
  7.4 9.4 %copy-start.4 = (bf16[256,1024]{1,0:T(8,128)(2,1)S(1)}, bf16[256,1024]{1,0:T(8,128)(2,1)}, u32[]{:S(2)}) copy-start(bf16[256,1024]{1,0:T(8,128)(2,1)} %param.25) | copy-start | bytes 1572868
  7.4 11.2 %collective-permute-start = (bf16[256,512]{1,0:T(8,128)(2,1)S(1)}, bf16[256,512]{1,0:T(8,128)(2,1)}, u32[]{:S(2)}, u32[]{:S(2)}) collective-permute-start(bf16[256,512]{1,0:T(8,128)(2,1)S(1)} %pad_maximum_fusion.3), channel_id=1, source_target_pairs={{0,4},{4,8},{8,12},{1,5},{5,9},{9,13},{2,6},{6,10},{10,14},{3,7},{... | collective-permute-start | bytes 786440 | tf_op jit(solution)/shard_map/ppermute | solution.py:21
  16.8 1.9 %copy-start.16 = (s32[3]{0:T(128)}, s32[3]{0:T(128)S(1)}, u32[]{:S(2)}) copy-start(s32[3]{0:T(128)S(1)} %constant_dynamic-update-slice_fusion.2.scal_ref) | copy-start | bytes 40
  17.8 0.8 copy-start.15
  30.9 1.4 %copy-start.17 = (s32[3]{0:T(128)S(1)}, s32[3]{0:T(128)}, u32[]{:S(2)}) copy-start(s32[3]{0:T(128)} %constant.165.clone) | copy-start | bytes 40
  32.2 13.0 %collective-permute-start.2 = (bf16[2,1024,256]{2,1,0:T(8,128)(2,1)S(1)}, bf16[2,1024,256]{2,1,0:T(8,128)(2,1)}, u32[]{:S(2)}, u32[]{:S(2)}) collective-permute-start(bf16[2,1024,256]{2,1,0:T(8,128)(2,1)S(1)} %slice.128), channel_id=1, source_target_pairs={{0,1},{1,0},{2,3},{3,2},{4,5},{5,4},{6,7},{7,6},{8,9},{9,8},{10,11... | collective-permute-start | bytes 3145736 | tf_op jit(solution)/shard_map/ppermute | solution.py:229
  32.3 0.6 copy-start.18
  45.2 2.8 %copy-start.1 = (bf16[4,1024,256]{2,1,0:T(8,128)(2,1)S(1)}, bf16[4,1024,256]{2,1,0:T(8,128)(2,1)}, u32[]{:S(2)}) copy-start(bf16[4,1024,256]{2,1,0:T(8,128)(2,1)} %shard_map.123) | copy-start | bytes 6291460
  45.2 4.3 %copy-start.14 = (bf16[1024,256]{1,0:T(8,128)(2,1)S(1)}, bf16[1024,256]{1,0:T(8,128)(2,1)}, u32[]{:S(2)}) copy-start(bf16[1024,256]{1,0:T(8,128)(2,1)} %param.26) | copy-start | bytes 1572868
  49.0 20.8 %collective-permute-start.4 = (bf16[2,1024,256]{2,1,0:T(8,128)(2,1)}, bf16[2,1024,256]{2,1,0:T(8,128)(2,1)}, u32[]{:S(2)}, u32[]{:S(2)}) collective-permute-start(bf16[2,1024,256]{2,1,0:T(8,128)(2,1)} %slice.113), channel_id=1, source_target_pairs={{0,1},{1,0},{2,3},{3,2},{4,5},{5,4},{6,7},{7,6},{8,9},{9,8},{10,11... | collective-permute-start | bytes 3145736 | tf_op jit(solution)/shard_map/ppermute | solution.py:229
  68.0 1.4 %copy-start.3 = (f32[1024,128]{1,0:T(8,128)S(1)}, f32[1024,128]{1,0:T(8,128)}, u32[]{:S(2)}) copy-start(f32[1024,128]{1,0:T(8,128)} %get-tuple-element.66) | copy-start | bytes 1572868
  69.3 1.6 %copy-start.2 = (bf16[4,1024,256]{2,1,0:T(8,128)(2,1)S(1)}, bf16[4,1024,256]{2,1,0:T(8,128)(2,1)}, u32[]{:S(2)}) copy-start(bf16[4,1024,256]{2,1,0:T(8,128)(2,1)} %shard_map.123) | copy-start | bytes 6291460
  69.7 10.9 %copy-start.5 = (bf16[256,1024]{1,0:T(8,128)(2,1)S(1)}, bf16[256,1024]{1,0:T(8,128)(2,1)}, u32[]{:S(2)}) copy-start(bf16[256,1024]{1,0:T(8,128)(2,1)} %param.27) | copy-start | bytes 1572868
  74.0 10.6 %collective-permute-start.6 = (bf16[256,280]{1,0:T(8,128)(2,1)S(1)}, bf16[256,280]{1,0:T(8,128)(2,1)S(1)}, u32[]{:S(2)}, u32[]{:S(2)}) collective-permute-start(bf16[256,280]{1,0:T(8,128)(2,1)S(1)} %get-tuple-element.83), channel_id=1, source_target_pairs={{0,4},{4,8},{8,12},{12,0},{1,5},{5,9},{9,13},{13,1},{2,6},{6,10},{... | collective-permute-start | bytes 430088 | tf_op jit(solution)/shard_map/ppermute | solution.py:272
  76.6 15.9 %collective-permute-start.7 = (bf16[256,280]{1,0:T(8,128)(2,1)S(1)}, bf16[256,280]{1,0:T(8,128)(2,1)S(1)}, u32[]{:S(2)}, u32[]{:S(2)}) collective-permute-start(bf16[256,280]{1,0:T(8,128)(2,1)S(1)} %get-tuple-element.82), channel_id=1, source_target_pairs={{0,8},{4,12},{8,0},{12,4},{1,9},{5,13},{9,1},{13,5},{2,10},{6,14},... | collective-permute-start | bytes 430088 | tf_op jit(solution)/shard_map/ppermute | solution.py:272
  79.3 13.1 %collective-permute-start.8 = (bf16[256,280]{1,0:T(8,128)(2,1)S(1)}, bf16[256,280]{1,0:T(8,128)(2,1)S(1)}, u32[]{:S(2)}, u32[]{:S(2)}) collective-permute-start(bf16[256,280]{1,0:T(8,128)(2,1)S(1)} %get-tuple-element.81), channel_id=1, source_target_pairs={{0,12},{4,0},{8,4},{12,8},{1,13},{5,1},{9,5},{13,9},{2,14},{6,2},{... | collective-permute-start | bytes 430088 | tf_op jit(solution)/shard_map/ppermute | solution.py:272
  81.5 16.3 %collective-permute-start.3 = (bf16[1024,256]{1,0:T(8,128)(2,1)}, bf16[1024,256]{1,0:T(8,128)(2,1)}, u32[]{:S(2)}, u32[]{:S(2)}) collective-permute-start(bf16[1024,256]{1,0:T(8,128)(2,1)} %get-tuple-element.61), channel_id=1, source_target_pairs={{0,2},{1,3},{2,0},{3,1},{4,6},{5,7},{6,4},{7,5},{8,10},{9,11},{10,... | collective-permute-start | bytes 1572872 | tf_op jit(solution)/shard_map/ppermute | solution.py:244
  83.0 24.5 %collective-permute-start.5 = (bf16[1024,256]{1,0:T(8,128)(2,1)}, bf16[1024,256]{1,0:T(8,128)(2,1)}, u32[]{:S(2)}, u32[]{:S(2)}) collective-permute-start(bf16[1024,256]{1,0:T(8,128)(2,1)} %get-tuple-element.68), channel_id=1, source_target_pairs={{0,2},{1,3},{2,0},{3,1},{4,6},{5,7},{6,4},{7,5},{8,10},{9,11},{10,... | collective-permute-start | bytes 1572872 | tf_op jit(solution)/shard_map/ppermute | solution.py:244
  84.6 8.5 %copy-start.6 = (bf16[256,280]{1,0:T(8,128)(2,1)}, bf16[256,280]{1,0:T(8,128)(2,1)S(1)}, u32[]{:S(2)}) copy-start(bf16[256,280]{1,0:T(8,128)(2,1)S(1)} %collective-permute-done.6.refs_1_) | copy-start | bytes 430084
  92.4 0.8 copy-start.7
  92.4 0.7 copy-start.8
  97.7 1.6 %collective-permute-start.9 = (bf16[2,256,256]{2,1,0:T(8,128)(2,1)S(1)}, bf16[2,256,256]{2,1,0:T(8,128)(2,1)S(1)}, u32[]{:S(2)}, u32[]{:S(2)}) collective-permute-start(bf16[2,256,256]{2,1,0:T(8,128)(2,1)S(1)} %pad_maximum_fusion.5), channel_id=1, source_target_pairs={{0,1},{1,0},{2,3},{3,2},{4,5},{5,4},{6,7},{7,6},{8,9},{9,8},{10,11... | collective-permute-start | bytes 786440 | tf_op jit(solution)/shard_map/ppermute | solution.py:229
  99.4 10.3 %collective-permute-start.10 = (bf16[256,256]{1,0:T(8,128)(2,1)S(1)}, bf16[256,256]{1,0:T(8,128)(2,1)S(1)}, u32[]{:S(2)}, u32[]{:S(2)}) collective-permute-start(bf16[256,256]{1,0:T(8,128)(2,1)S(1)} %fusion.12), channel_id=1, source_target_pairs={{0,2},{1,3},{2,0},{3,1},{4,6},{5,7},{6,4},{7,5},{8,10},{9,11},{10,... | collective-permute-start | bytes 393224 | tf_op jit(solution)/shard_map/ppermute | solution.py:244

commit v16 on v15

--- a/solution.py
+++ b/solution.py
@@ -141,7 +141,7 @@
 def latent_attention(latent_query, keyed, valued, valid_count):
     latent_count, width = latent_query.shape
     heads = width // HD
-    tl = min(256, latent_count)
+    tl = min(512, latent_count)
     scal = jnp.reshape(valid_count, (1,)).astype(jnp.int32)
     kernel = functools.partial(latent_kernel, heads=heads, scale=HD ** (-0.5))
     frame_count = keyed.shape[0]

time: 111 us -> 111 us (level)
  no operation moved by 1% of the time
where the time goes in v16:
time: 111 us
  Pallas kernels  44.6 us (40%)
  starting transfers between devices  18.7 us (17%)
  waiting for transfers between devices  16.6 us (15%)
  other arithmetic  11.9 us (11%)
  matrix products  10.2 us (9%)
  local copies, waits for them, and re-layouts  6.85 us (6%)
  between operations  1.6 us (1%)
    pallas_call x2, Pallas kernels, window_attention(): pl.pallas_call(kernel, cost_estimate=cost, out_shape=jax.ShapeDtypeStruct...  24.5 us
    pallas_call x1, Pallas kernels, latent_attention(): pl.pallas_call(kernel, cost_estimate=cost, out_shape=(jax.ShapeDtypeStruc...  17.1 us
    ppermute x3, waiting for transfers between devices, exchange_rows(): parts.append(lax.ppermute(block, axis, pairs))  8.91 us
    dot_general x4, matrix products, project(): jnp.dot(source, weight, preferred_element_type=jnp.float32)  8.76 us
    ppermute x3, starting transfers between devices, exchange_rows(): parts.append(lax.ppermute(block, axis, pairs))  6.68 us
    ppermute x3, waiting for transfers between devices, cross_chip_sum(): total = total + lax.ppermute(chip_sums[d], axis, pairs).astype(jnp.float32)  6.53 us
    ppermute x1, starting transfers between devices, halos(): lax.ppermute(tail, axis, forward)  6.42 us
    convert_element_type x3, other arithmetic, chip_pair_sums(): (blocks[chips + d].astype(jnp.float32) + received[d].astype(jnp.float32))...  5.1 us
  transfers between devices with their start and end apart: 11, of which 5 were waited for; matrix products, arithmetic and copies ran while one was open for 11% of the time, Pallas kernels for 29%

profile of v16, /device:TPU:0, one launch (start us, length us, event | category | flops | bytes accessed | tf_op | source)
XLA Modules:
  0.0 110.5 jit_solution(16971090604502542581)
XLA Ops:
  0.7 3.7 %convolution_convert_fusion.v_ref = bf16[2048,256]{1,0:T(8,128)(2,1)S(1)} fusion(bf16[2048,1024]{1,0:T(8,128)(2,1)} %param.19, bf16[1024,256]{1,0:T(8,128)(2,1)} %param.24), kind=kOutput, calls=%fused_computation | convolution fusion | flops 1074266112 | bytes 5767168 | tf_op jit(solution)/shard_map/dot_general | solution.py:25
  4.5 1.3 %convolution_convert_fusion.1.k_ref = bf16[2048,256]{1,0:T(8,128)(2,1)S(1)} fusion(bf16[2048,1024]{1,0:T(8,128)(2,1)S(1)} %copy-done.11, bf16[1024,256]{1,0:T(8,128)(2,1)S(1)} %copy-done.12), kind=kOutput, calls=%fused_computation.1 | convolution fusion | flops 1074266112 | bytes 5767168 | tf_op jit(solution)/shard_map/dot_general | solution.py:25
  5.9 1.4 %collective-permute-start.1 = (bf16[256,512]{1,0:T(8,128)(2,1)S(1)}, bf16[256,512]{1,0:T(8,128)(2,1)S(1)}, u32[]{:S(2)}, u32[]{:S(2)}) collective-permute-start(bf16[256,512]{1,0:T(8,128)(2,1)S(1)} %pad_maximum_fusion.4), channel_id=1, source_target_pairs={{4,0},{8,4},{12,8},{5,1},{9,5},{13,9},{6,2},{10,6},{14,10},{7,3},{... | collective-permute-start | bytes 786440 | tf_op jit(solution)/shard_map/ppermute | solution.py:21
  7.4 6.4 %collective-permute-start = (bf16[256,512]{1,0:T(8,128)(2,1)S(1)}, bf16[256,512]{1,0:T(8,128)(2,1)}, u32[]{:S(2)}, u32[]{:S(2)}) collective-permute-start(bf16[256,512]{1,0:T(8,128)(2,1)S(1)} %pad_maximum_fusion.3), channel_id=1, source_target_pairs={{0,4},{4,8},{8,12},{1,5},{5,9},{9,13},{2,6},{6,10},{10,14},{3,7},{... | collective-permute-start | bytes 786440 | tf_op jit(solution)/shard_map/ppermute | solution.py:21
  13.8 2.2 %convolution_convert_fusion.2.q_ref = bf16[2048,256]{1,0:T(8,128)(2,1)} fusion(bf16[2048,1024]{1,0:T(8,128)(2,1)S(1)} %copy-done.11, bf16[1024,256]{1,0:T(8,128)(2,1)S(1)} %copy-done.13), kind=kOutput, calls=%fused_computation.2 | convolution fusion | flops 1074266112 | bytes 5767168 | tf_op jit(solution)/shard_map/dot_general | solution.py:25
  16.9 0.9 pad_maximum_fusion.2.w_ref
  17.8 0.8 collective-permute-done.low_ref
  18.6 12.3 %shard_map.122 = bf16[4,1024,256]{2,1,0:T(8,128)(2,1)} custom-call(s32[3]{0:T(128)} %copy-done.16, bf16[2048,256]{1,0:T(8,128)(2,1)} %convolution_convert_fusion.2.q_ref, bf16[2048,256]{1,0:T(8,128)(2,1)} %copy-done.10, bf16[2048,256]{1,0:T(8,128)(2,1)} %copy-done.9, bf16[256,512]{1,0:T(8,128)(2,1)} %collective-permute-done.low_ref, ...), custom_call_target="tpu_custom_call" | custom-call | flops 1610612736 | bytes 5767168 | tf_op jit(solution)/shard_map/pallas_call | solution.py:93
  30.9 1.3 %slice.128 = bf16[2,1024,256]{2,1,0:T(8,128)(2,1)S(1)} slice(bf16[4,1024,256]{2,1,0:T(8,128)(2,1)} %shard_map.122), slice={[0:2], [0:1024], [0:256]} | slice | bytes 2097152 | tf_op jit(solution)/shard_map/slice | solution.py:229
  32.9 12.2 %shard_map.123 = bf16[4,1024,256]{2,1,0:T(8,128)(2,1)} custom-call(s32[3]{0:T(128)} %copy-done.18, bf16[2048,256]{1,0:T(8,128)(2,1)} %convolution_convert_fusion.2.q_ref, bf16[2048,256]{1,0:T(8,128)(2,1)} %copy-done.10, bf16[2048,256]{1,0:T(8,128)(2,1)} %copy-done.9, bf16[256,512]{1,0:T(8,128)(2,1)} %collective-permute-done.low_ref, ...), custom_call_target="tpu_custom_call" | custom-call | flops 1610612736 | bytes 5767168 | tf_op jit(solution)/shard_map/pallas_call | solution.py:93
  45.2 2.8 %fusion.1 = (bf16[1024,256]{1,0:T(8,128)(2,1)}, bf16[1024,256]{1,0:T(8,128)(2,1)S(1)}) fusion(bf16[2,1024,256]{2,1,0:T(8,128)(2,1)} %collective-permute-done.2, bf16[4,1024,256]{2,1,0:T(8,128)(2,1)} %shard_map.122), kind=kLoop, calls=%fused_computation.14 | loop fusion | flops 2097152 | bytes 3145728 | tf_op jit(solution)/shard_map/convert_element_type | solution.py:231
  48.0 1.0 slice.113
  49.5 1.5 %convolution_convert_fusion.4.q_ref = bf16[1024,256]{1,0:T(8,128)(2,1)} fusion(bf16[1024,1024]{1,0:T(8,128)(2,1)S(1)} %copy-done, bf16[1024,256]{1,0:T(8,128)(2,1)S(1)} %copy-done.14), kind=kOutput, calls=%fused_computation.4 | convolution fusion | flops 537133056 | bytes 3145728 | tf_op jit(solution)/shard_map/dot_general | solution.py:25
  51.0 17.1 %shard_map.124 = (f32[1024,256]{1,0:T(8,128)}, f32[1024,128]{1,0:T(8,128)}) custom-call(s32[1]{0:T(128)} %bitcast.6.scal_ref, bf16[1024,256]{1,0:T(8,128)(2,1)} %convolution_convert_fusion.4.q_ref, bf16[2048,256]{1,0:T(8,128)(2,1)} %copy-done.10, bf16[2048,256]{1,0:T(8,128)(2,1)} %copy-done.9), custom_call_target="tpu_custom_call" | custom-call | flops 2147483648 | bytes 4194304 | tf_op jit(solution)/shard_map/pallas_call | solution.py:153
  68.1 1.3 %convert_element_type.163 = bf16[1024,256]{1,0:T(8,128)(2,1)S(1)} convert(f32[1024,256]{1,0:T(8,128)} %get-tuple-element.65) | non-fusion elementwise | flops 262144 | bytes 1572864 | tf_op jit(solution)/shard_map/convert_element_type | solution.py:358
  69.9 1.2 %copy-done.2 = bf16[4,1024,256]{2,1,0:T(8,128)(2,1)S(1)} copy-done((bf16[4,1024,256]{2,1,0:T(8,128)(2,1)S(1)}, bf16[4,1024,256]{2,1,0:T(8,128)(2,1)}, u32[]{:S(2)}) %copy-start.2) | copy-done | bytes 2097176
  71.0 2.3 %fusion.3 = (bf16[1024,256]{1,0:T(8,128)(2,1)}, bf16[1024,256]{1,0:T(8,128)(2,1)S(1)}) fusion(bf16[2,1024,256]{2,1,0:T(8,128)(2,1)} %collective-permute-done.4, bf16[4,1024,256]{2,1,0:T(8,128)(2,1)S(1)} %copy-done.2), kind=kLoop, calls=%fused_computation.16 | loop fusion | flops 2097152 | bytes 3145728 | tf_op jit(solution)/shard_map/convert_element_type | solution.py:231
  73.3 0.8 constant_dynamic-slice_fusion.3
  74.1 2.6 %collective-permute-start.6 = (bf16[256,280]{1,0:T(8,128)(2,1)S(1)}, bf16[256,280]{1,0:T(8,128)(2,1)S(1)}, u32[]{:S(2)}, u32[]{:S(2)}) collective-permute-start(bf16[256,280]{1,0:T(8,128)(2,1)S(1)} %get-tuple-element.83), channel_id=1, source_target_pairs={{0,4},{4,8},{8,12},{12,0},{1,5},{5,9},{9,13},{13,1},{2,6},{6,10},{... | collective-permute-start | bytes 430088 | tf_op jit(solution)/shard_map/ppermute | solution.py:272
  76.7 2.8 %collective-permute-start.7 = (bf16[256,280]{1,0:T(8,128)(2,1)S(1)}, bf16[256,280]{1,0:T(8,128)(2,1)S(1)}, u32[]{:S(2)}, u32[]{:S(2)}) collective-permute-start(bf16[256,280]{1,0:T(8,128)(2,1)S(1)} %get-tuple-element.82), channel_id=1, source_target_pairs={{0,8},{4,12},{8,0},{12,4},{1,9},{5,13},{9,1},{13,5},{2,10},{6,14},... | collective-permute-start | bytes 430088 | tf_op jit(solution)/shard_map/ppermute | solution.py:272
  79.4 1.3 %collective-permute-start.8 = (bf16[256,280]{1,0:T(8,128)(2,1)S(1)}, bf16[256,280]{1,0:T(8,128)(2,1)S(1)}, u32[]{:S(2)}, u32[]{:S(2)}) collective-permute-start(bf16[256,280]{1,0:T(8,128)(2,1)S(1)} %get-tuple-element.81), channel_id=1, source_target_pairs={{0,12},{4,0},{8,4},{12,8},{1,13},{5,1},{9,5},{13,9},{2,14},{6,2},{... | collective-permute-start | bytes 430088 | tf_op jit(solution)/shard_map/ppermute | solution.py:272
  80.8 0.8 constant_dynamic-slice_fusion.2
  81.6 1.5 %collective-permute-start.3 = (bf16[1024,256]{1,0:T(8,128)(2,1)}, bf16[1024,256]{1,0:T(8,128)(2,1)}, u32[]{:S(2)}, u32[]{:S(2)}) collective-permute-start(bf16[1024,256]{1,0:T(8,128)(2,1)} %get-tuple-element.61), channel_id=1, source_target_pairs={{0,2},{1,3},{2,0},{3,1},{4,6},{5,7},{6,4},{7,5},{8,10},{9,11},{10,... | collective-permute-start | bytes 1572872 | tf_op jit(solution)/shard_map/ppermute | solution.py:244
  83.6 1.1 collective-permute-done.6.refs_1_
  84.7 7.8 %collective-permute-done.7.refs_2_ = bf16[256,280]{1,0:T(8,128)(2,1)S(1)} collective-permute-done((bf16[256,280]{1,0:T(8,128)(2,1)S(1)}, bf16[256,280]{1,0:T(8,128)(2,1)S(1)}, u32[]{:S(2)}, u32[]{:S(2)}) %collective-permute-start.7) | collective-permute-done | bytes 143392 | tf_op jit(solution)/shard_map/ppermute | solution.py:272
  93.3 3.0 %shard_map.125 = bf16[256,256]{1,0:T(8,128)(2,1)} custom-call(bf16[256,280]{1,0:T(8,128)(2,1)} %get-tuple-element.84.refs_0_, bf16[256,280]{1,0:T(8,128)(2,1)} %copy-done.6, bf16[256,280]{1,0:T(8,128)(2,1)} %copy-done.7, bf16[256,280]{1,0:T(8,128)(2,1)} %copy-done.8), custom_call_target="tpu_custom_call" | custom-call | tf_op jit(solution)/shard_map/pallas_call | solution.py:309
  96.3 1.5 %convolution_convert_fusion.3 = bf16[256,1024]{1,0:T(8,128)(2,1)S(1)} fusion(bf16[256,256]{1,0:T(8,128)(2,1)} %shard_map.125, bf16[256,256]{1,0:T(8,128)(2,1)} %get-tuple-element.89, bf16[256,256]{1,0:T(8,128)(2,1)} %get-tuple-element.90, bf16[256,256]{1,0:T(8,128)(2,1)} %get-tuple-element.88, bf16[256,256]{1,0:T(8,128)(2,1)} %get-tuple-element.87), kind=kOutput, calls=%fused_computation.3 | convolution fusion | flops 136577024 | bytes 1179648 | tf_op jit(solution)/shard_map/dot_general | solution.py:369
  97.9 1.2 %add_convert_fusion.3 = bf16[1024,256]{1,0:T(8,128)(2,1)S(1)} fusion(bf16[1024,256]{1,0:T(8,128)(2,1)} %collective-permute-done.3, bf16[1024,256]{1,0:T(8,128)(2,1)S(1)} %get-tuple-element.60), kind=kLoop, calls=%fused_computation.9 | loop fusion | flops 1048576 | bytes 1572864 | tf_op jit(solution)/shard_map/convert_element_type | solution.py:245
  99.5 1.6 %collective-permute-start.10 = (bf16[256,256]{1,0:T(8,128)(2,1)S(1)}, bf16[256,256]{1,0:T(8,128)(2,1)S(1)}, u32[]{:S(2)}, u32[]{:S(2)}) collective-permute-start(bf16[256,256]{1,0:T(8,128)(2,1)S(1)} %fusion.12), channel_id=1, source_target_pairs={{0,2},{1,3},{2,0},{3,1},{4,6},{5,7},{6,4},{7,5},{8,10},{9,11},{10,... | collective-permute-start | bytes 393224 | tf_op jit(solution)/shard_map/ppermute | solution.py:244
  101.1 6.5 %collective-permute-done.5 = bf16[1024,256]{1,0:T(8,128)(2,1)} collective-permute-done((bf16[1024,256]{1,0:T(8,128)(2,1)}, bf16[1024,256]{1,0:T(8,128)(2,1)}, u32[]{:S(2)}, u32[]{:S(2)}) %collective-permute-start.5) | collective-permute-done | bytes 524320 | tf_op jit(solution)/shard_map/ppermute | solution.py:244
  107.6 1.2 %add_convert_fusion = bf16[1024,256]{1,0:T(8,128)(2,1)S(1)} fusion(bf16[1024,256]{1,0:T(8,128)(2,1)} %collective-permute-done.5, bf16[1024,256]{1,0:T(8,128)(2,1)S(1)} %get-tuple-element.67), kind=kLoop, calls=%fused_computation.6 | loop fusion | flops 1048576 | bytes 1572864 | tf_op jit(solution)/shard_map/convert_element_type | solution.py:245
  108.8 1.0 pad_maximum_fusion
  (63 shorter events, 4.5 us)
Async XLA Ops:
  0.6 48.8 %copy-start = (bf16[1024,1024]{1,0:T(8,128)(2,1)S(1)}, bf16[1024,1024]{1,0:T(8,128)(2,1)}, u32[]{:S(2)}) copy-start(bf16[1024,1024]{1,0:T(8,128)(2,1)} %param.20) | copy-start | bytes 6291460
  0.6 3.8 %copy-start.11 = (bf16[2048,1024]{1,0:T(8,128)(2,1)S(1)}, bf16[2048,1024]{1,0:T(8,128)(2,1)}, u32[]{:S(2)}) copy-start(bf16[2048,1024]{1,0:T(8,128)(2,1)} %param.19) | copy-start | bytes 12582916
  0.7 3.9 %copy-start.12 = (bf16[1024,256]{1,0:T(8,128)(2,1)S(1)}, bf16[1024,256]{1,0:T(8,128)(2,1)}, u32[]{:S(2)}) copy-start(bf16[1024,256]{1,0:T(8,128)(2,1)} %param.23) | copy-start | bytes 1572868
  4.5 1.3 %copy-start.9 = (bf16[2048,256]{1,0:T(8,128)(2,1)}, bf16[2048,256]{1,0:T(8,128)(2,1)S(1)}, u32[]{:S(2)}) copy-start(bf16[2048,256]{1,0:T(8,128)(2,1)S(1)} %convolution_convert_fusion.v_ref) | copy-start | bytes 3145732
  5.8 10.2 %copy-start.10 = (bf16[2048,256]{1,0:T(8,128)(2,1)}, bf16[2048,256]{1,0:T(8,128)(2,1)S(1)}, u32[]{:S(2)}) copy-start(bf16[2048,256]{1,0:T(8,128)(2,1)S(1)} %convolution_convert_fusion.1.k_ref) | copy-start | bytes 3145732
  5.8 8.0 %copy-start.13 = (bf16[1024,256]{1,0:T(8,128)(2,1)S(1)}, bf16[1024,256]{1,0:T(8,128)(2,1)}, u32[]{:S(2)}) copy-start(bf16[1024,256]{1,0:T(8,128)(2,1)} %param.22) | copy-start | bytes 1572868
  5.9 11.9 %collective-permute-start.1 = (bf16[256,512]{1,0:T(8,128)(2,1)S(1)}, bf16[256,512]{1,0:T(8,128)(2,1)S(1)}, u32[]{:S(2)}, u32[]{:S(2)}) collective-permute-start(bf16[256,512]{1,0:T(8,128)(2,1)S(1)} %pad_maximum_fusion.4), channel_id=1, source_target_pairs={{4,0},{8,4},{12,8},{5,1},{9,5},{13,9},{6,2},{10,6},{14,10},{7,3},{... | collective-permute-start | bytes 786440 | tf_op jit(solution)/shard_map/ppermute | solution.py:21
  7.4 9.4 %copy-start.4 = (bf16[256,1024]{1,0:T(8,128)(2,1)S(1)}, bf16[256,1024]{1,0:T(8,128)(2,1)}, u32[]{:S(2)}) copy-start(bf16[256,1024]{1,0:T(8,128)(2,1)} %param.25) | copy-start | bytes 1572868
  7.4 11.2 %collective-permute-start = (bf16[256,512]{1,0:T(8,128)(2,1)S(1)}, bf16[256,512]{1,0:T(8,128)(2,1)}, u32[]{:S(2)}, u32[]{:S(2)}) collective-permute-start(bf16[256,512]{1,0:T(8,128)(2,1)S(1)} %pad_maximum_fusion.3), channel_id=1, source_target_pairs={{0,4},{4,8},{8,12},{1,5},{5,9},{9,13},{2,6},{6,10},{10,14},{3,7},{... | collective-permute-start | bytes 786440 | tf_op jit(solution)/shard_map/ppermute | solution.py:21
  16.8 1.9 %copy-start.16 = (s32[3]{0:T(128)}, s32[3]{0:T(128)S(1)}, u32[]{:S(2)}) copy-start(s32[3]{0:T(128)S(1)} %constant_dynamic-update-slice_fusion.2.scal_ref) | copy-start | bytes 40
  17.8 0.8 copy-start.15
  30.9 1.4 %copy-start.17 = (s32[3]{0:T(128)S(1)}, s32[3]{0:T(128)}, u32[]{:S(2)}) copy-start(s32[3]{0:T(128)} %constant.165.clone) | copy-start | bytes 40
  32.2 13.0 %collective-permute-start.2 = (bf16[2,1024,256]{2,1,0:T(8,128)(2,1)S(1)}, bf16[2,1024,256]{2,1,0:T(8,128)(2,1)}, u32[]{:S(2)}, u32[]{:S(2)}) collective-permute-start(bf16[2,1024,256]{2,1,0:T(8,128)(2,1)S(1)} %slice.128), channel_id=1, source_target_pairs={{0,1},{1,0},{2,3},{3,2},{4,5},{5,4},{6,7},{7,6},{8,9},{9,8},{10,11... | collective-permute-start | bytes 3145736 | tf_op jit(solution)/shard_map/ppermute | solution.py:229
  32.3 0.6 copy-start.18
  45.2 2.8 %copy-start.1 = (bf16[4,1024,256]{2,1,0:T(8,128)(2,1)S(1)}, bf16[4,1024,256]{2,1,0:T(8,128)(2,1)}, u32[]{:S(2)}) copy-start(bf16[4,1024,256]{2,1,0:T(8,128)(2,1)} %shard_map.123) | copy-start | bytes 6291460
  45.2 4.3 %copy-start.14 = (bf16[1024,256]{1,0:T(8,128)(2,1)S(1)}, bf16[1024,256]{1,0:T(8,128)(2,1)}, u32[]{:S(2)}) copy-start(bf16[1024,256]{1,0:T(8,128)(2,1)} %param.26) | copy-start | bytes 1572868
  49.0 20.9 %collective-permute-start.4 = (bf16[2,1024,256]{2,1,0:T(8,128)(2,1)}, bf16[2,1024,256]{2,1,0:T(8,128)(2,1)}, u32[]{:S(2)}, u32[]{:S(2)}) collective-permute-start(bf16[2,1024,256]{2,1,0:T(8,128)(2,1)} %slice.113), channel_id=1, source_target_pairs={{0,1},{1,0},{2,3},{3,2},{4,5},{5,4},{6,7},{7,6},{8,9},{9,8},{10,11... | collective-permute-start | bytes 3145736 | tf_op jit(solution)/shard_map/ppermute | solution.py:229
  68.1 1.4 %copy-start.3 = (f32[1024,128]{1,0:T(8,128)S(1)}, f32[1024,128]{1,0:T(8,128)}, u32[]{:S(2)}) copy-start(f32[1024,128]{1,0:T(8,128)} %get-tuple-element.66) | copy-start | bytes 1572868
  69.4 1.6 %copy-start.2 = (bf16[4,1024,256]{2,1,0:T(8,128)(2,1)S(1)}, bf16[4,1024,256]{2,1,0:T(8,128)(2,1)}, u32[]{:S(2)}) copy-start(bf16[4,1024,256]{2,1,0:T(8,128)(2,1)} %shard_map.123) | copy-start | bytes 6291460
  69.8 10.9 %copy-start.5 = (bf16[256,1024]{1,0:T(8,128)(2,1)S(1)}, bf16[256,1024]{1,0:T(8,128)(2,1)}, u32[]{:S(2)}) copy-start(bf16[256,1024]{1,0:T(8,128)(2,1)} %param.27) | copy-start | bytes 1572868
  74.1 10.6 %collective-permute-start.6 = (bf16[256,280]{1,0:T(8,128)(2,1)S(1)}, bf16[256,280]{1,0:T(8,128)(2,1)S(1)}, u32[]{:S(2)}, u32[]{:S(2)}) collective-permute-start(bf16[256,280]{1,0:T(8,128)(2,1)S(1)} %get-tuple-element.83), channel_id=1, source_target_pairs={{0,4},{4,8},{8,12},{12,0},{1,5},{5,9},{9,13},{13,1},{2,6},{6,10},{... | collective-permute-start | bytes 430088 | tf_op jit(solution)/shard_map/ppermute | solution.py:272
  76.7 15.9 %collective-permute-start.7 = (bf16[256,280]{1,0:T(8,128)(2,1)S(1)}, bf16[256,280]{1,0:T(8,128)(2,1)S(1)}, u32[]{:S(2)}, u32[]{:S(2)}) collective-permute-start(bf16[256,280]{1,0:T(8,128)(2,1)S(1)} %get-tuple-element.82), channel_id=1, source_target_pairs={{0,8},{4,12},{8,0},{12,4},{1,9},{5,13},{9,1},{13,5},{2,10},{6,14},... | collective-permute-start | bytes 430088 | tf_op jit(solution)/shard_map/ppermute | solution.py:272
  79.4 13.1 %collective-permute-start.8 = (bf16[256,280]{1,0:T(8,128)(2,1)S(1)}, bf16[256,280]{1,0:T(8,128)(2,1)S(1)}, u32[]{:S(2)}, u32[]{:S(2)}) collective-permute-start(bf16[256,280]{1,0:T(8,128)(2,1)S(1)} %get-tuple-element.81), channel_id=1, source_target_pairs={{0,12},{4,0},{8,4},{12,8},{1,13},{5,1},{9,5},{13,9},{2,14},{6,2},{... | collective-permute-start | bytes 430088 | tf_op jit(solution)/shard_map/ppermute | solution.py:272
  81.6 16.3 %collective-permute-start.3 = (bf16[1024,256]{1,0:T(8,128)(2,1)}, bf16[1024,256]{1,0:T(8,128)(2,1)}, u32[]{:S(2)}, u32[]{:S(2)}) collective-permute-start(bf16[1024,256]{1,0:T(8,128)(2,1)} %get-tuple-element.61), channel_id=1, source_target_pairs={{0,2},{1,3},{2,0},{3,1},{4,6},{5,7},{6,4},{7,5},{8,10},{9,11},{10,... | collective-permute-start | bytes 1572872 | tf_op jit(solution)/shard_map/ppermute | solution.py:244
  83.1 24.5 %collective-permute-start.5 = (bf16[1024,256]{1,0:T(8,128)(2,1)}, bf16[1024,256]{1,0:T(8,128)(2,1)}, u32[]{:S(2)}, u32[]{:S(2)}) collective-permute-start(bf16[1024,256]{1,0:T(8,128)(2,1)} %get-tuple-element.68), channel_id=1, source_target_pairs={{0,2},{1,3},{2,0},{3,1},{4,6},{5,7},{6,4},{7,5},{8,10},{9,11},{10,... | collective-permute-start | bytes 1572872 | tf_op jit(solution)/shard_map/ppermute | solution.py:244
  84.7 8.5 %copy-start.6 = (bf16[256,280]{1,0:T(8,128)(2,1)}, bf16[256,280]{1,0:T(8,128)(2,1)S(1)}, u32[]{:S(2)}) copy-start(bf16[256,280]{1,0:T(8,128)(2,1)S(1)} %collective-permute-done.6.refs_1_) | copy-start | bytes 430084
  92.5 0.8 copy-start.7
  92.5 0.7 copy-start.8
  97.9 1.6 %collective-permute-start.9 = (bf16[2,256,256]{2,1,0:T(8,128)(2,1)S(1)}, bf16[2,256,256]{2,1,0:T(8,128)(2,1)S(1)}, u32[]{:S(2)}, u32[]{:S(2)}) collective-permute-start(bf16[2,256,256]{2,1,0:T(8,128)(2,1)S(1)} %pad_maximum_fusion.5), channel_id=1, source_target_pairs={{0,1},{1,0},{2,3},{3,2},{4,5},{5,4},{6,7},{7,6},{8,9},{9,8},{10,11... | collective-permute-start | bytes 786440 | tf_op jit(solution)/shard_map/ppermute | solution.py:229
  99.5 10.3 %collective-permute-start.10 = (bf16[256,256]{1,0:T(8,128)(2,1)S(1)}, bf16[256,256]{1,0:T(8,128)(2,1)S(1)}, u32[]{:S(2)}, u32[]{:S(2)}) collective-permute-start(bf16[256,256]{1,0:T(8,128)(2,1)S(1)} %fusion.12), channel_id=1, source_target_pairs={{0,2},{1,3},{2,0},{3,1},{4,6},{5,7},{6,4},{7,5},{8,10},{9,11},{10,... | collective-permute-start | bytes 393224 | tf_op jit(solution)/shard_map/ppermute | solution.py:244

commit v17 on v15

--- a/solution.py
+++ b/solution.py
@@ -76,7 +76,8 @@
 def window_attention(
     query, keyed, valued, low, high, w_out, first_frame, length, row_base, rows, blocks
 ):
-    frame_count, width = query.shape
+    frame_count = query.shape[0]
+    width = low.shape[1] // 2
     out_width = w_out.shape[1]
     block_width = out_width // blocks
     tq = min(512, rows)
@@ -99,8 +100,8 @@
             grid=(rows // tq,),
             in_specs=[
                 pl.BlockSpec((tq, width), lambda i, s: (i + block_base, 0)),
-                pl.BlockSpec(keyed.shape, full),
-                pl.BlockSpec(valued.shape, full),
+                pl.BlockSpec((frame_count, width), lambda i, s: (0, 1)),
+                pl.BlockSpec((frame_count, width), lambda i, s: (0, 2)),
                 pl.BlockSpec(low.shape, full),
                 pl.BlockSpec(high.shape, full),
                 pl.BlockSpec(w_out.shape, full),
@@ -162,8 +163,8 @@
             grid=(latent_count // tl,),
             in_specs=[
                 pl.BlockSpec((tl, width), lambda i, s: (i, 0)),
-                pl.BlockSpec(keyed.shape, lambda i, s: (0, 0)),
-                pl.BlockSpec(valued.shape, lambda i, s: (0, 0)),
+                pl.BlockSpec((frame_count, width), lambda i, s: (0, 1)),
+                pl.BlockSpec((frame_count, width), lambda i, s: (0, 2)),
             ],
             out_specs=[
                 pl.BlockSpec((tl, width), lambda i, s: (i, 0)),
@@ -324,9 +325,9 @@
     seq_place = lax.axis_index("seq")
     first_frame = seq_place * frame_count
     length = lengths[0]
-    query = project(frames, w_query)
-    keyed = project(frames, w_key)
-    valued = project(frames, w_value)
+    qkv = project(frames, jnp.concatenate([w_query, w_key, w_value], axis=1))
+    keyed = qkv[:, head_width : 2 * head_width]
+    valued = qkv[:, 2 * head_width :]
     low, high = halos(keyed, valued, "seq")
     chunks = 2 if frame_count % 512 == 0 else 1
     chunk_rows = frame_count // chunks
@@ -335,7 +336,7 @@
     w_ordered = ordered_columns(w_out, "head")
     parts = [
         window_attention(
-            query, keyed, valued, low, high, w_ordered, first_frame, length,
+            qkv, qkv, qkv, low, high, w_ordered, first_frame, length,
             c * chunk_rows, chunk_rows, head_devices,
         )
         for c in range(chunks)
@@ -346,14 +347,12 @@
     frame_parts = []
     if paired:
         first_sums = chip_pair_sums(parts[0], "head")
-        first_sums, rest, keyed, valued = lax.optimization_barrier(
-            (first_sums, parts[1:], keyed, valued)
-        )
+        first_sums, rest, qkv = lax.optimization_barrier((first_sums, parts[1:], qkv))
         frame_parts.append(cross_chip_sum(first_sums, "head"))
         rest_sums = [chip_pair_sums(blocks, "head") for blocks in rest]
     else:
         frame_parts = [plain_block_sum(blocks, "head") for blocks in parts]
-    peaks, totals, local_accum = latent_attention(latent_query, keyed, valued, valid_count)
+    peaks, totals, local_accum = latent_attention(latent_query, qkv, qkv, valid_count)
     payload = jnp.concatenate(
         [local_accum.astype(jnp.bfloat16)] + split_three(jnp.concatenate([peaks, totals], axis=1)),
         axis=1,

time: 111 us -> 116 us (1.045)
  waiting for transfers between devices: 16.6 us -> 22.2 us
  local copies, waits for them, and re-layouts: 6.85 us -> 9.68 us
  starting transfers between devices: 18.7 us -> 16.1 us
    ppermute x1, waiting for transfers between devices: 0.01 us -> 3.81 us  [halos(): lax.ppermute(head, axis, backward)]
    unnamed x39 -> x33, local copies, waits for them, and re-layouts: 2.74 us -> 4.87 us
    ppermute x1, waiting for transfers between devices: 0.84 us -> 2.63 us  [halos(): lax.ppermute(tail, axis, forward)]
    ppermute x1, starting transfers between devices: 6.42 us -> 4.93 us  [halos(): lax.ppermute(tail, axis, forward)]
    ppermute x3, starting transfers between devices: 6.68 us -> 5.51 us  [exchange_rows(): parts.append(lax.ppermute(block, axis, pairs))]
    dot_general x4 -> x2, matrix products: 8.76 us -> 7.76 us  [project(): jnp.dot(source, weight, preferred_element_type=jnp.float32)]
  transfers between devices with their start and end apart: 11 -> 11, of which waited for: 5 -> 6; matrix products, arithmetic and copies ran while one was open for 11% -> 9% of each run, Pallas kernels for 29% -> 28%
where the time goes in v17:
time: 116 us; the launch traced here: 115 us
  Pallas kernels  44.6 us (38%)
  waiting for transfers between devices  22.2 us (19%)
  starting transfers between devices  16.1 us (14%)
  other arithmetic  11.8 us (10%)
  local copies, waits for them, and re-layouts  9.68 us (8%)
  matrix products  9.22 us (8%)
  between operations  1.61 us (1%)
    pallas_call x2, Pallas kernels, window_attention(): pl.pallas_call(kernel, cost_estimate=cost, out_shape=jax.ShapeDtypeStruct...  24.6 us
    pallas_call x1, Pallas kernels, latent_attention(): pl.pallas_call(kernel, cost_estimate=cost, out_shape=(jax.ShapeDtypeStruc...  17 us
    ppermute x3, waiting for transfers between devices, exchange_rows(): parts.append(lax.ppermute(block, axis, pairs))  8.83 us
    dot_general x2, matrix products, project(): jnp.dot(source, weight, preferred_element_type=jnp.float32)  7.76 us
    ppermute x3, waiting for transfers between devices, cross_chip_sum(): total = total + lax.ppermute(chip_sums[d], axis, pairs).astype(jnp.float32)  6.59 us
    ppermute x3, starting transfers between devices, exchange_rows(): parts.append(lax.ppermute(block, axis, pairs))  5.51 us
    convert_element_type x3, other arithmetic, chip_pair_sums(): (blocks[chips + d].astype(jnp.float32) + received[d].astype(jnp.float32))...  5.11 us
    ppermute x1, starting transfers between devices, halos(): lax.ppermute(tail, axis, forward)  4.93 us
  transfers between devices with their start and end apart: 11, of which 6 were waited for; matrix products, arithmetic and copies ran while one was open for 9% of the time, Pallas kernels for 28%

profile of v17, /device:TPU:0, one launch (start us, length us, event | category | flops | bytes accessed | tf_op | source)
XLA Modules:
  0.0 115.3 jit_solution(16931597726928899513)
XLA Ops:
  0.7 6.2 %fusion.q_ref.k_ref.v_ref = bf16[2048,768]{1,0:T(8,128)(2,1)S(1)} fusion(bf16[2048,1024]{1,0:T(8,128)(2,1)} %param.19, bf16[1024,256]{1,0:T(8,128)(2,1)} %param.24, bf16[1024,256]{1,0:T(8,128)(2,1)} %param.23, bf16[1024,256]{1,0:T(8,128)(2,1)} %param.22), kind=kOutput, calls=%fused_computation.1 | convolution fusion | flops 3227516928 | bytes 8912896 | tf_op jit(solution)/shard_map/dot_general | solution.py:25
  6.9 1.6 %copy-done.1 = bf16[2048,768]{1,0:T(8,128)(2,1)} copy-done((bf16[2048,768]{1,0:T(8,128)(2,1)}, bf16[2048,768]{1,0:T(8,128)(2,1)S(1)}, u32[]{:S(2)}) %copy-start.1) | copy-done | bytes 3145752
  9.2 4.9 %collective-permute-start = (bf16[256,512]{1,0:T(8,128)(2,1)}, bf16[256,512]{1,0:T(8,128)(2,1)S(1)}, u32[]{:S(2)}, u32[]{:S(2)}) collective-permute-start(bf16[256,512]{1,0:T(8,128)(2,1)} %get-tuple-element.76), channel_id=1, source_target_pairs={{0,4},{4,8},{8,12},{1,5},{5,9},{9,13},{2,6},{6,10},{10,14},{3,7},{... | collective-permute-start | bytes 786440 | tf_op jit(solution)/shard_map/ppermute | solution.py:21
  14.2 1.5 %collective-permute-start.1 = (bf16[256,512]{1,0:T(8,128)(2,1)S(1)}, bf16[256,512]{1,0:T(8,128)(2,1)S(1)}, u32[]{:S(2)}, u32[]{:S(2)}) collective-permute-start(bf16[256,512]{1,0:T(8,128)(2,1)S(1)} %get-tuple-element.75), channel_id=1, source_target_pairs={{4,0},{8,4},{12,8},{5,1},{9,5},{13,9},{6,2},{10,6},{14,10},{7,3},{... | collective-permute-start | bytes 786440 | tf_op jit(solution)/shard_map/ppermute | solution.py:21
  16.5 0.9 pad_maximum_fusion.2.w_ref
  17.4 2.6 %collective-permute-done.low_ref = bf16[256,512]{1,0:T(8,128)(2,1)S(1)} collective-permute-done((bf16[256,512]{1,0:T(8,128)(2,1)}, bf16[256,512]{1,0:T(8,128)(2,1)S(1)}, u32[]{:S(2)}, u32[]{:S(2)}) %collective-permute-start) | collective-permute-done | bytes 262176 | tf_op jit(solution)/shard_map/ppermute | solution.py:21
  20.0 3.8 %collective-permute-done.1.high_ref = bf16[256,512]{1,0:T(8,128)(2,1)S(1)} collective-permute-done((bf16[256,512]{1,0:T(8,128)(2,1)S(1)}, bf16[256,512]{1,0:T(8,128)(2,1)S(1)}, u32[]{:S(2)}, u32[]{:S(2)}) %collective-permute-start.1) | collective-permute-done | bytes 262176 | tf_op jit(solution)/shard_map/ppermute | solution.py:21
  24.6 12.3 %shard_map.122 = bf16[4,1024,256]{2,1,0:T(8,128)(2,1)} custom-call(s32[3]{0:T(128)} %copy-done.12, bf16[2048,768]{1,0:T(8,128)(2,1)} %copy-done.1, bf16[2048,768]{1,0:T(8,128)(2,1)} %copy-done.1, bf16[2048,768]{1,0:T(8,128)(2,1)} %copy-done.1, bf16[256,512]{1,0:T(8,128)(2,1)} %copy-done.5, bf16[256,512]{1,0:T(8,128)(2,1)} %copy-done.6, ...), custom_call_target="tpu_custom_call" | custom-call | flops 1610612736 | bytes 9961472 | tf_op jit(solution)/shard_map/pallas_call | solution.py:94
  36.9 1.3 %slice.120 = bf16[2,1024,256]{2,1,0:T(8,128)(2,1)S(1)} slice(bf16[4,1024,256]{2,1,0:T(8,128)(2,1)} %shard_map.122), slice={[0:2], [0:1024], [0:256]} | slice | bytes 2097152 | tf_op jit(solution)/shard_map/slice | solution.py:230
  38.9 12.3 %shard_map.123 = bf16[4,1024,256]{2,1,0:T(8,128)(2,1)} custom-call(s32[3]{0:T(128)} %copy-done.13, bf16[2048,768]{1,0:T(8,128)(2,1)} %copy-done.1, bf16[2048,768]{1,0:T(8,128)(2,1)} %copy-done.1, bf16[2048,768]{1,0:T(8,128)(2,1)} %copy-done.1, bf16[256,512]{1,0:T(8,128)(2,1)} %copy-done.5, bf16[256,512]{1,0:T(8,128)(2,1)} %copy-done.6, ...), custom_call_target="tpu_custom_call" | custom-call | flops 1610612736 | bytes 9961472 | tf_op jit(solution)/shard_map/pallas_call | solution.py:94
  51.2 2.8 %fusion.7 = (bf16[1024,256]{1,0:T(8,128)(2,1)}, bf16[1024,256]{1,0:T(8,128)(2,1)S(1)}) fusion(bf16[2,1024,256]{2,1,0:T(8,128)(2,1)} %collective-permute-done.2, bf16[4,1024,256]{2,1,0:T(8,128)(2,1)} %shard_map.122), kind=kLoop, calls=%fused_computation.18 | loop fusion | flops 2097152 | bytes 3145728 | tf_op jit(solution)/shard_map/convert_element_type | solution.py:232
  54.0 1.0 slice.109
  55.5 1.5 %convolution_convert_fusion.2.q_ref = bf16[1024,256]{1,0:T(8,128)(2,1)} fusion(bf16[1024,1024]{1,0:T(8,128)(2,1)S(1)} %copy-done, bf16[1024,256]{1,0:T(8,128)(2,1)S(1)} %copy-done.14), kind=kOutput, calls=%fused_computation.8 | convolution fusion | flops 537133056 | bytes 3145728 | tf_op jit(solution)/shard_map/dot_general | solution.py:25
  57.0 17.0 %shard_map.124 = (f32[1024,256]{1,0:T(8,128)}, f32[1024,128]{1,0:T(8,128)}) custom-call(s32[1]{0:T(128)} %bitcast.7.scal_ref, bf16[1024,256]{1,0:T(8,128)(2,1)} %convolution_convert_fusion.2.q_ref, bf16[2048,768]{1,0:T(8,128)(2,1)} %copy-done.1, bf16[2048,768]{1,0:T(8,128)(2,1)} %copy-done.1), custom_call_target="tpu_custom_call" | custom-call | flops 2147483648 | bytes 8388608 | tf_op jit(solution)/shard_map/pallas_call | solution.py:154
  74.0 1.3 %convert_element_type.158 = bf16[1024,256]{1,0:T(8,128)(2,1)S(1)} convert(f32[1024,256]{1,0:T(8,128)} %get-tuple-element.63) | non-fusion elementwise | flops 262144 | bytes 1572864 | tf_op jit(solution)/shard_map/convert_element_type | solution.py:357
  75.8 1.2 %copy-done.3 = bf16[4,1024,256]{2,1,0:T(8,128)(2,1)S(1)} copy-done((bf16[4,1024,256]{2,1,0:T(8,128)(2,1)S(1)}, bf16[4,1024,256]{2,1,0:T(8,128)(2,1)}, u32[]{:S(2)}) %copy-start.3) | copy-done | bytes 2097176
  77.0 2.3 %fusion.9 = (bf16[1024,256]{1,0:T(8,128)(2,1)}, bf16[1024,256]{1,0:T(8,128)(2,1)S(1)}) fusion(bf16[2,1024,256]{2,1,0:T(8,128)(2,1)} %collective-permute-done.4, bf16[4,1024,256]{2,1,0:T(8,128)(2,1)S(1)} %copy-done.3), kind=kLoop, calls=%fused_computation.20 | loop fusion | flops 2097152 | bytes 3145728 | tf_op jit(solution)/shard_map/convert_element_type | solution.py:232
  79.3 0.8 constant_dynamic-slice_fusion.3
  80.0 1.6 %collective-permute-start.6 = (bf16[256,280]{1,0:T(8,128)(2,1)S(1)}, bf16[256,280]{1,0:T(8,128)(2,1)S(1)}, u32[]{:S(2)}, u32[]{:S(2)}) collective-permute-start(bf16[256,280]{1,0:T(8,128)(2,1)S(1)} %get-tuple-element.79), channel_id=1, source_target_pairs={{0,4},{4,8},{8,12},{12,0},{1,5},{5,9},{9,13},{13,1},{2,6},{6,10},{... | collective-permute-start | bytes 430088 | tf_op jit(solution)/shard_map/ppermute | solution.py:273
  81.6 1.0 collective-permute-start.7
  82.6 2.9 %collective-permute-start.8 = (bf16[256,280]{1,0:T(8,128)(2,1)S(1)}, bf16[256,280]{1,0:T(8,128)(2,1)S(1)}, u32[]{:S(2)}, u32[]{:S(2)}) collective-permute-start(bf16[256,280]{1,0:T(8,128)(2,1)S(1)} %get-tuple-element.77), channel_id=1, source_target_pairs={{0,12},{4,0},{8,4},{12,8},{1,13},{5,1},{9,5},{13,9},{2,14},{6,2},{... | collective-permute-start | bytes 430088 | tf_op jit(solution)/shard_map/ppermute | solution.py:273
  85.5 0.8 constant_dynamic-slice_fusion.2
  86.4 1.5 %collective-permute-start.3 = (bf16[1024,256]{1,0:T(8,128)(2,1)}, bf16[1024,256]{1,0:T(8,128)(2,1)}, u32[]{:S(2)}, u32[]{:S(2)}) collective-permute-start(bf16[1024,256]{1,0:T(8,128)(2,1)} %get-tuple-element.60), channel_id=1, source_target_pairs={{0,2},{1,3},{2,0},{3,1},{4,6},{5,7},{6,4},{7,5},{8,10},{9,11},{10,... | collective-permute-start | bytes 1572872 | tf_op jit(solution)/shard_map/ppermute | solution.py:245
  88.4 1.3 %collective-permute-done.6.refs_1_ = bf16[256,280]{1,0:T(8,128)(2,1)S(1)} collective-permute-done((bf16[256,280]{1,0:T(8,128)(2,1)S(1)}, bf16[256,280]{1,0:T(8,128)(2,1)S(1)}, u32[]{:S(2)}, u32[]{:S(2)}) %collective-permute-start.6) | collective-permute-done | bytes 143392 | tf_op jit(solution)/shard_map/ppermute | solution.py:273
  89.7 7.5 %collective-permute-done.7.refs_2_ = bf16[256,280]{1,0:T(8,128)(2,1)S(1)} collective-permute-done((bf16[256,280]{1,0:T(8,128)(2,1)S(1)}, bf16[256,280]{1,0:T(8,128)(2,1)S(1)}, u32[]{:S(2)}, u32[]{:S(2)}) %collective-permute-start.7) | collective-permute-done | bytes 143392 | tf_op jit(solution)/shard_map/ppermute | solution.py:273
  98.0 3.0 %shard_map.125 = bf16[256,256]{1,0:T(8,128)(2,1)} custom-call(bf16[256,280]{1,0:T(8,128)(2,1)} %get-tuple-element.80.refs_0_, bf16[256,280]{1,0:T(8,128)(2,1)} %copy-done.9, bf16[256,280]{1,0:T(8,128)(2,1)} %copy-done.10, bf16[256,280]{1,0:T(8,128)(2,1)} %copy-done.11), custom_call_target="tpu_custom_call" | custom-call | tf_op jit(solution)/shard_map/pallas_call | solution.py:310
  101.0 1.5 %convolution_convert_fusion.1 = bf16[256,1024]{1,0:T(8,128)(2,1)S(1)} fusion(bf16[256,256]{1,0:T(8,128)(2,1)} %shard_map.125, bf16[256,256]{1,0:T(8,128)(2,1)} %get-tuple-element.85, bf16[256,256]{1,0:T(8,128)(2,1)} %get-tuple-element.86, bf16[256,256]{1,0:T(8,128)(2,1)} %get-tuple-element.84, bf16[256,256]{1,0:T(8,128)(2,1)} %get-tuple-element.83), kind=kOutput, calls=%fused_computation.7 | convolution fusion | flops 136577024 | bytes 1179648 | tf_op jit(solution)/shard_map/dot_general | solution.py:368
  102.6 1.2 %add_convert_fusion.3 = bf16[1024,256]{1,0:T(8,128)(2,1)S(1)} fusion(bf16[1024,256]{1,0:T(8,128)(2,1)} %collective-permute-done.3, bf16[1024,256]{1,0:T(8,128)(2,1)S(1)} %get-tuple-element.59), kind=kLoop, calls=%fused_computation.13 | loop fusion | flops 1048576 | bytes 1572864 | tf_op jit(solution)/shard_map/convert_element_type | solution.py:246
  104.2 1.6 %collective-permute-start.10 = (bf16[256,256]{1,0:T(8,128)(2,1)S(1)}, bf16[256,256]{1,0:T(8,128)(2,1)S(1)}, u32[]{:S(2)}, u32[]{:S(2)}) collective-permute-start(bf16[256,256]{1,0:T(8,128)(2,1)S(1)} %fusion.18), channel_id=1, source_target_pairs={{0,2},{1,3},{2,0},{3,1},{4,6},{5,7},{6,4},{7,5},{8,10},{9,11},{10,... | collective-permute-start | bytes 393224 | tf_op jit(solution)/shard_map/ppermute | solution.py:245
  105.7 6.6 %collective-permute-done.5 = bf16[1024,256]{1,0:T(8,128)(2,1)} collective-permute-done((bf16[1024,256]{1,0:T(8,128)(2,1)}, bf16[1024,256]{1,0:T(8,128)(2,1)}, u32[]{:S(2)}, u32[]{:S(2)}) %collective-permute-start.5) | collective-permute-done | bytes 524320 | tf_op jit(solution)/shard_map/ppermute | solution.py:245
  112.3 1.2 %add_convert_fusion = bf16[1024,256]{1,0:T(8,128)(2,1)S(1)} fusion(bf16[1024,256]{1,0:T(8,128)(2,1)} %collective-permute-done.5, bf16[1024,256]{1,0:T(8,128)(2,1)S(1)} %get-tuple-element.65), kind=kLoop, calls=%fused_computation.10 | loop fusion | flops 1048576 | bytes 1572864 | tf_op jit(solution)/shard_map/convert_element_type | solution.py:246
  113.5 1.0 pad_maximum_fusion
  (53 shorter events, 5.6 us)
Async XLA Ops:
  0.6 54.9 %copy-start = (bf16[1024,1024]{1,0:T(8,128)(2,1)S(1)}, bf16[1024,1024]{1,0:T(8,128)(2,1)}, u32[]{:S(2)}) copy-start(bf16[1024,1024]{1,0:T(8,128)(2,1)} %param.20) | copy-start | bytes 6291460
  0.6 15.8 %copy-start.7 = (bf16[256,1024]{1,0:T(8,128)(2,1)S(1)}, bf16[256,1024]{1,0:T(8,128)(2,1)}, u32[]{:S(2)}) copy-start(bf16[256,1024]{1,0:T(8,128)(2,1)} %param.25) | copy-start | bytes 1572868
  6.9 1.6 %copy-start.1 = (bf16[2048,768]{1,0:T(8,128)(2,1)}, bf16[2048,768]{1,0:T(8,128)(2,1)S(1)}, u32[]{:S(2)}) copy-start(bf16[2048,768]{1,0:T(8,128)(2,1)S(1)} %fusion.q_ref.k_ref.v_ref) | copy-start | bytes 9437188
  9.2 10.8 %collective-permute-start = (bf16[256,512]{1,0:T(8,128)(2,1)}, bf16[256,512]{1,0:T(8,128)(2,1)S(1)}, u32[]{:S(2)}, u32[]{:S(2)}) collective-permute-start(bf16[256,512]{1,0:T(8,128)(2,1)} %get-tuple-element.76), channel_id=1, source_target_pairs={{0,4},{4,8},{8,12},{1,5},{5,9},{9,13},{2,6},{6,10},{10,14},{3,7},{... | collective-permute-start | bytes 786440 | tf_op jit(solution)/shard_map/ppermute | solution.py:21
  14.2 9.7 %collective-permute-start.1 = (bf16[256,512]{1,0:T(8,128)(2,1)S(1)}, bf16[256,512]{1,0:T(8,128)(2,1)S(1)}, u32[]{:S(2)}, u32[]{:S(2)}) collective-permute-start(bf16[256,512]{1,0:T(8,128)(2,1)S(1)} %get-tuple-element.75), channel_id=1, source_target_pairs={{4,0},{8,4},{12,8},{5,1},{9,5},{13,9},{6,2},{10,6},{14,10},{7,3},{... | collective-permute-start | bytes 786440 | tf_op jit(solution)/shard_map/ppermute | solution.py:21
  16.4 7.4 %copy-start.12 = (s32[3]{0:T(128)}, s32[3]{0:T(128)S(1)}, u32[]{:S(2)}) copy-start(s32[3]{0:T(128)S(1)} %constant_dynamic-update-slice_fusion.2.scal_ref) | copy-start | bytes 40
  20.0 3.8 %copy-start.5 = (bf16[256,512]{1,0:T(8,128)(2,1)}, bf16[256,512]{1,0:T(8,128)(2,1)S(1)}, u32[]{:S(2)}) copy-start(bf16[256,512]{1,0:T(8,128)(2,1)S(1)} %collective-permute-done.low_ref) | copy-start | bytes 786436
  23.8 0.7 copy-start.6
  36.9 1.4 %copy-start.15 = (s32[3]{0:T(128)S(1)}, s32[3]{0:T(128)}, u32[]{:S(2)}) copy-start(s32[3]{0:T(128)} %constant.165.clone) | copy-start | bytes 40
  38.2 13.0 %collective-permute-start.2 = (bf16[2,1024,256]{2,1,0:T(8,128)(2,1)S(1)}, bf16[2,1024,256]{2,1,0:T(8,128)(2,1)}, u32[]{:S(2)}, u32[]{:S(2)}) collective-permute-start(bf16[2,1024,256]{2,1,0:T(8,128)(2,1)S(1)} %slice.120), channel_id=1, source_target_pairs={{0,1},{1,0},{2,3},{3,2},{4,5},{5,4},{6,7},{7,6},{8,9},{9,8},{10,11... | collective-permute-start | bytes 3145736 | tf_op jit(solution)/shard_map/ppermute | solution.py:230
  38.4 0.5 copy-start.13
  51.2 2.8 %copy-start.2 = (bf16[4,1024,256]{2,1,0:T(8,128)(2,1)S(1)}, bf16[4,1024,256]{2,1,0:T(8,128)(2,1)}, u32[]{:S(2)}) copy-start(bf16[4,1024,256]{2,1,0:T(8,128)(2,1)} %shard_map.123) | copy-start | bytes 6291460
  51.2 4.3 %copy-start.14 = (bf16[1024,256]{1,0:T(8,128)(2,1)S(1)}, bf16[1024,256]{1,0:T(8,128)(2,1)}, u32[]{:S(2)}) copy-start(bf16[1024,256]{1,0:T(8,128)(2,1)} %param.26) | copy-start | bytes 1572868
  55.0 20.8 %collective-permute-start.4 = (bf16[2,1024,256]{2,1,0:T(8,128)(2,1)}, bf16[2,1024,256]{2,1,0:T(8,128)(2,1)}, u32[]{:S(2)}, u32[]{:S(2)}) collective-permute-start(bf16[2,1024,256]{2,1,0:T(8,128)(2,1)} %slice.109), channel_id=1, source_target_pairs={{0,1},{1,0},{2,3},{3,2},{4,5},{5,4},{6,7},{7,6},{8,9},{9,8},{10,11... | collective-permute-start | bytes 3145736 | tf_op jit(solution)/shard_map/ppermute | solution.py:230
  74.0 1.4 %copy-start.4 = (f32[1024,128]{1,0:T(8,128)S(1)}, f32[1024,128]{1,0:T(8,128)}, u32[]{:S(2)}) copy-start(f32[1024,128]{1,0:T(8,128)} %get-tuple-element.64) | copy-start | bytes 1572868
  75.4 1.6 %copy-start.3 = (bf16[4,1024,256]{2,1,0:T(8,128)(2,1)S(1)}, bf16[4,1024,256]{2,1,0:T(8,128)(2,1)}, u32[]{:S(2)}) copy-start(bf16[4,1024,256]{2,1,0:T(8,128)(2,1)} %shard_map.123) | copy-start | bytes 6291460
  75.8 9.8 %copy-start.8 = (bf16[256,1024]{1,0:T(8,128)(2,1)S(1)}, bf16[256,1024]{1,0:T(8,128)(2,1)}, u32[]{:S(2)}) copy-start(bf16[256,1024]{1,0:T(8,128)(2,1)} %param.27) | copy-start | bytes 1572868
  80.0 9.7 %collective-permute-start.6 = (bf16[256,280]{1,0:T(8,128)(2,1)S(1)}, bf16[256,280]{1,0:T(8,128)(2,1)S(1)}, u32[]{:S(2)}, u32[]{:S(2)}) collective-permute-start(bf16[256,280]{1,0:T(8,128)(2,1)S(1)} %get-tuple-element.79), channel_id=1, source_target_pairs={{0,4},{4,8},{8,12},{12,0},{1,5},{5,9},{9,13},{13,1},{2,6},{6,10},{... | collective-permute-start | bytes 430088 | tf_op jit(solution)/shard_map/ppermute | solution.py:273
  81.6 15.6 %collective-permute-start.7 = (bf16[256,280]{1,0:T(8,128)(2,1)S(1)}, bf16[256,280]{1,0:T(8,128)(2,1)S(1)}, u32[]{:S(2)}, u32[]{:S(2)}) collective-permute-start(bf16[256,280]{1,0:T(8,128)(2,1)S(1)} %get-tuple-element.78), channel_id=1, source_target_pairs={{0,8},{4,12},{8,0},{12,4},{1,9},{5,13},{9,1},{13,5},{2,10},{6,14},... | collective-permute-start | bytes 430088 | tf_op jit(solution)/shard_map/ppermute | solution.py:273
  82.6 14.6 %collective-permute-start.8 = (bf16[256,280]{1,0:T(8,128)(2,1)S(1)}, bf16[256,280]{1,0:T(8,128)(2,1)S(1)}, u32[]{:S(2)}, u32[]{:S(2)}) collective-permute-start(bf16[256,280]{1,0:T(8,128)(2,1)S(1)} %get-tuple-element.77), channel_id=1, source_target_pairs={{0,12},{4,0},{8,4},{12,8},{1,13},{5,1},{9,5},{13,9},{2,14},{6,2},{... | collective-permute-start | bytes 430088 | tf_op jit(solution)/shard_map/ppermute | solution.py:273
  86.4 16.3 %collective-permute-start.3 = (bf16[1024,256]{1,0:T(8,128)(2,1)}, bf16[1024,256]{1,0:T(8,128)(2,1)}, u32[]{:S(2)}, u32[]{:S(2)}) collective-permute-start(bf16[1024,256]{1,0:T(8,128)(2,1)} %get-tuple-element.60), channel_id=1, source_target_pairs={{0,2},{1,3},{2,0},{3,1},{4,6},{5,7},{6,4},{7,5},{8,10},{9,11},{10,... | collective-permute-start | bytes 1572872 | tf_op jit(solution)/shard_map/ppermute | solution.py:245
  87.8 24.5 %collective-permute-start.5 = (bf16[1024,256]{1,0:T(8,128)(2,1)}, bf16[1024,256]{1,0:T(8,128)(2,1)}, u32[]{:S(2)}, u32[]{:S(2)}) collective-permute-start(bf16[1024,256]{1,0:T(8,128)(2,1)} %get-tuple-element.66), channel_id=1, source_target_pairs={{0,2},{1,3},{2,0},{3,1},{4,6},{5,7},{6,4},{7,5},{8,10},{9,11},{10,... | collective-permute-start | bytes 1572872 | tf_op jit(solution)/shard_map/ppermute | solution.py:245
  89.7 8.2 %copy-start.9 = (bf16[256,280]{1,0:T(8,128)(2,1)}, bf16[256,280]{1,0:T(8,128)(2,1)S(1)}, u32[]{:S(2)}) copy-start(bf16[256,280]{1,0:T(8,128)(2,1)S(1)} %collective-permute-done.6.refs_1_) | copy-start | bytes 430084
  97.2 0.8 copy-start.10
  97.2 0.7 copy-start.11
  102.5 1.6 %collective-permute-start.9 = (bf16[2,256,256]{2,1,0:T(8,128)(2,1)S(1)}, bf16[2,256,256]{2,1,0:T(8,128)(2,1)S(1)}, u32[]{:S(2)}, u32[]{:S(2)}) collective-permute-start(bf16[2,256,256]{2,1,0:T(8,128)(2,1)S(1)} %pad_maximum_fusion.3), channel_id=1, source_target_pairs={{0,1},{1,0},{2,3},{3,2},{4,5},{5,4},{6,7},{7,6},{8,9},{9,8},{10,11... | collective-permute-start | bytes 786440 | tf_op jit(solution)/shard_map/ppermute | solution.py:230
  104.2 10.4 %collective-permute-start.10 = (bf16[256,256]{1,0:T(8,128)(2,1)S(1)}, bf16[256,256]{1,0:T(8,128)(2,1)S(1)}, u32[]{:S(2)}, u32[]{:S(2)}) collective-permute-start(bf16[256,256]{1,0:T(8,128)(2,1)S(1)} %fusion.18), channel_id=1, source_target_pairs={{0,2},{1,3},{2,0},{3,1},{4,6},{5,7},{6,4},{7,5},{8,10},{9,11},{10,... | collective-permute-start | bytes 393224 | tf_op jit(solution)/shard_map/ppermute | solution.py:245

commit v18 on v15

--- a/solution.py
+++ b/solution.py
@@ -328,7 +328,7 @@
     keyed = project(frames, w_key)
     valued = project(frames, w_value)
     low, high = halos(keyed, valued, "seq")
-    chunks = 2 if frame_count % 512 == 0 else 1
+    chunks = 1
     chunk_rows = frame_count // chunks
     head_devices = lax.axis_size("head")
     paired = head_devices % 2 == 0

time: 111 us -> 108 us (0.973)
  waiting for transfers between devices: 16.6 us -> 22.7 us
  Pallas kernels: 44.5 us -> 40.8 us
  other arithmetic: 11.9 us -> 8.99 us
    ppermute x3 -> x2, waiting for transfers between devices: 0.34 us -> 4.48 us  [chip_pair_sums(): received = lax.ppermute(blocks[:chips], axis, swap)]
    pallas_call x2 -> x1, Pallas kernels: 24.5 us -> 20.8 us  [window_attention(): pl.pallas_call(kernel, cost_estimate=cost, out_shape=jax.ShapeDtypeStruct...]
    convert_element_type x3 -> x2, other arithmetic: 5.1 us -> 3.17 us  [chip_pair_sums(): (blocks[chips + d].astype(jnp.float32) + received[d].astype(jnp.float32))...]
    unnamed x39 -> x32, local copies, waits for them, and re-layouts: 2.74 us -> 1.1 us
    ppermute x3 -> x2, waiting for transfers between devices: 6.53 us -> 7.86 us  [cross_chip_sum(): total = total + lax.ppermute(chip_sums[d], axis, pairs).astype(jnp.float32)]
    convert_element_type x1, other arithmetic: 0.11 us -> 1.4 us  [split_three(): lo = (rest - mid.astype(jnp.float32)).astype(jnp.bfloat16)]
    convert_element_type x1, other arithmetic: 1.34 us -> 0.05 us  [per_device(): local_accum.astype(jnp.bfloat16)]
    slice x2 -> x1, local copies, waits for them, and re-layouts: 2.34 us -> 3.17 us  [chip_pair_sums(): received = lax.ppermute(blocks[:chips], axis, swap)]
  transfers between devices with their start and end apart: 11 -> 9, of which waited for: 5 -> 6; matrix products, arithmetic and copies ran while one was open for 11% -> 7% of each run, Pallas kernels for 29% -> 3%
where the time goes in v18:
time: 108 us
  Pallas kernels  40.8 us (38%)
  waiting for transfers between devices  22.7 us (21%)
  starting transfers between devices  17.6 us (16%)
  matrix products  10.2 us (9%)
  other arithmetic  8.99 us (8%)
  local copies, waits for them, and re-layouts  6.06 us (6%)
  between operations  1.52 us (1%)
    pallas_call x1, Pallas kernels, window_attention(): pl.pallas_call(kernel, cost_estimate=cost, out_shape=jax.ShapeDtypeStruct...  20.8 us
    pallas_call x1, Pallas kernels, latent_attention(): pl.pallas_call(kernel, cost_estimate=cost, out_shape=(jax.ShapeDtypeStruc...  17 us
    ppermute x3, waiting for transfers between devices, exchange_rows(): parts.append(lax.ppermute(block, axis, pairs))  9.51 us
    dot_general x4, matrix products, project(): jnp.dot(source, weight, preferred_element_type=jnp.float32)  8.76 us
    ppermute x2, waiting for transfers between devices, cross_chip_sum(): total = total + lax.ppermute(chip_sums[d], axis, pairs).astype(jnp.float32)  7.86 us
    ppermute x3, starting transfers between devices, exchange_rows(): parts.append(lax.ppermute(block, axis, pairs))  6.69 us
    ppermute x1, starting transfers between devices, halos(): lax.ppermute(tail, axis, forward)  6.42 us
    ppermute x2, waiting for transfers between devices, chip_pair_sums(): received = lax.ppermute(blocks[:chips], axis, swap)  4.48 us
  transfers between devices with their start and end apart: 9, of which 6 were waited for; matrix products, arithmetic and copies ran while one was open for 7% of the time, Pallas kernels for 3%

profile of v18, /device:TPU:0, one launch (start us, length us, event | category | flops | bytes accessed | tf_op | source)
XLA Modules:
  0.0 108.0 jit_solution(8680259958044348211)
XLA Ops:
  0.7 3.7 %convolution_convert_fusion.v_ref = bf16[2048,256]{1,0:T(8,128)(2,1)S(1)} fusion(bf16[2048,1024]{1,0:T(8,128)(2,1)} %param.14, bf16[1024,256]{1,0:T(8,128)(2,1)} %param.19), kind=kOutput, calls=%fused_computation | convolution fusion | flops 1074266112 | bytes 5767168 | tf_op jit(solution)/shard_map/dot_general | solution.py:25
  4.5 1.3 %convolution_convert_fusion.1.k_ref = bf16[2048,256]{1,0:T(8,128)(2,1)S(1)} fusion(bf16[2048,1024]{1,0:T(8,128)(2,1)S(1)} %copy-done.10, bf16[1024,256]{1,0:T(8,128)(2,1)S(1)} %copy-done.11), kind=kOutput, calls=%fused_computation.1 | convolution fusion | flops 1074266112 | bytes 5767168 | tf_op jit(solution)/shard_map/dot_general | solution.py:25
  5.9 1.4 %collective-permute-start.1 = (bf16[256,512]{1,0:T(8,128)(2,1)S(1)}, bf16[256,512]{1,0:T(8,128)(2,1)S(1)}, u32[]{:S(2)}, u32[]{:S(2)}) collective-permute-start(bf16[256,512]{1,0:T(8,128)(2,1)S(1)} %pad_maximum_fusion.3), channel_id=1, source_target_pairs={{4,0},{8,4},{12,8},{5,1},{9,5},{13,9},{6,2},{10,6},{14,10},{7,3},{... | collective-permute-start | bytes 786440 | tf_op jit(solution)/shard_map/ppermute | solution.py:21
  7.4 6.4 %collective-permute-start = (bf16[256,512]{1,0:T(8,128)(2,1)S(1)}, bf16[256,512]{1,0:T(8,128)(2,1)}, u32[]{:S(2)}, u32[]{:S(2)}) collective-permute-start(bf16[256,512]{1,0:T(8,128)(2,1)S(1)} %pad_maximum_fusion.2), channel_id=1, source_target_pairs={{0,4},{4,8},{8,12},{1,5},{5,9},{9,13},{2,6},{6,10},{10,14},{3,7},{... | collective-permute-start | bytes 786440 | tf_op jit(solution)/shard_map/ppermute | solution.py:21
  13.8 2.3 %convolution_convert_fusion.2.q_ref = bf16[2048,256]{1,0:T(8,128)(2,1)} fusion(bf16[2048,1024]{1,0:T(8,128)(2,1)S(1)} %copy-done.10, bf16[1024,256]{1,0:T(8,128)(2,1)S(1)} %copy-done.12), kind=kOutput, calls=%fused_computation.2 | convolution fusion | flops 1074266112 | bytes 5767168 | tf_op jit(solution)/shard_map/dot_general | solution.py:25
  16.9 0.9 pad_maximum_fusion.1.w_ref
  17.7 0.9 collective-permute-done.low_ref
  18.6 20.8 %shard_map.113 = bf16[4,2048,256]{2,1,0:T(8,128)(2,1)} custom-call(s32[3]{0:T(128)} %copy-done.15, bf16[2048,256]{1,0:T(8,128)(2,1)} %convolution_convert_fusion.2.q_ref, bf16[2048,256]{1,0:T(8,128)(2,1)} %copy-done.9, bf16[2048,256]{1,0:T(8,128)(2,1)} %copy-done.8, bf16[256,512]{1,0:T(8,128)(2,1)} %collective-permute-done.low_ref, ...), custom_call_target="tpu_custom_call" | custom-call | flops 3221225472 | bytes 8388608 | tf_op jit(solution)/shard_map/pallas_call | solution.py:93
  39.4 3.2 %slice.88 = bf16[2,2048,256]{2,1,0:T(8,128)(2,1)} slice(bf16[4,2048,256]{2,1,0:T(8,128)(2,1)} %shard_map.113), slice={[0:2], [0:2048], [0:256]} | slice | bytes 4194304 | tf_op jit(solution)/shard_map/slice | solution.py:229
  42.6 1.5 %convolution_convert_fusion.4.q_ref = bf16[1024,256]{1,0:T(8,128)(2,1)} fusion(bf16[1024,1024]{1,0:T(8,128)(2,1)S(1)} %copy-done, bf16[1024,256]{1,0:T(8,128)(2,1)S(1)} %copy-done.13), kind=kOutput, calls=%fused_computation.7 | convolution fusion | flops 537133056 | bytes 3145728 | tf_op jit(solution)/shard_map/dot_general | solution.py:25
  44.1 3.0 %collective-permute-done.2 = bf16[2,2048,256]{2,1,0:T(8,128)(2,1)} collective-permute-done((bf16[2,2048,256]{2,1,0:T(8,128)(2,1)}, bf16[2,2048,256]{2,1,0:T(8,128)(2,1)}, u32[]{:S(2)}, u32[]{:S(2)}) %collective-permute-start.2) | collective-permute-done | bytes 2097184 | tf_op jit(solution)/shard_map/ppermute | solution.py:229
  47.1 3.1 %fusion.1 = (bf16[2048,256]{1,0:T(8,128)(2,1)}, bf16[2048,256]{1,0:T(8,128)(2,1)S(1)}) fusion(bf16[2,2048,256]{2,1,0:T(8,128)(2,1)} %collective-permute-done.2, bf16[4,2048,256]{2,1,0:T(8,128)(2,1)S(1)} %copy-done.1), kind=kLoop, calls=%fused_computation.9 | loop fusion | flops 4194304 | bytes 6291456 | tf_op jit(solution)/shard_map/convert_element_type | solution.py:231
  50.2 17.0 %shard_map.114 = (f32[1024,256]{1,0:T(8,128)}, f32[1024,128]{1,0:T(8,128)}) custom-call(s32[1]{0:T(128)} %bitcast.4.scal_ref, bf16[1024,256]{1,0:T(8,128)(2,1)} %convolution_convert_fusion.4.q_ref, bf16[2048,256]{1,0:T(8,128)(2,1)} %copy-done.9, bf16[2048,256]{1,0:T(8,128)(2,1)} %copy-done.8), custom_call_target="tpu_custom_call" | custom-call | flops 2147483648 | bytes 4194304 | tf_op jit(solution)/shard_map/pallas_call | solution.py:153
  67.2 1.4 %subtract_convert_fusion = (bf16[1024,8]{1,0:T(8,128)(2,1)S(1)}, bf16[1024,8]{1,0:T(8,128)(2,1)S(1)}, bf16[1024,8]{1,0:T(8,128)(2,1)S(1)}) fusion(f32[1024,128]{1,0:T(8,128)} %get-tuple-element.37), kind=kLoop, calls=%fused_computation.19 | loop fusion | flops 49152 | bytes 98304 | tf_op jit(solution)/shard_map/convert_element_type | solution.py:261
  68.6 0.1 copy-done.2
  68.8 0.3 pad_maximum_fusion
  69.1 0.8 constant_dynamic-slice_fusion.3
  69.9 2.6 %collective-permute-start.4 = (bf16[256,280]{1,0:T(8,128)(2,1)S(1)}, bf16[256,280]{1,0:T(8,128)(2,1)S(1)}, u32[]{:S(2)}, u32[]{:S(2)}) collective-permute-start(bf16[256,280]{1,0:T(8,128)(2,1)S(1)} %get-tuple-element.49), channel_id=1, source_target_pairs={{0,4},{4,8},{8,12},{12,0},{1,5},{5,9},{9,13},{13,1},{2,6},{6,10},{... | collective-permute-start | bytes 430088 | tf_op jit(solution)/shard_map/ppermute | solution.py:272
  72.5 2.8 %collective-permute-start.5 = (bf16[256,280]{1,0:T(8,128)(2,1)S(1)}, bf16[256,280]{1,0:T(8,128)(2,1)S(1)}, u32[]{:S(2)}, u32[]{:S(2)}) collective-permute-start(bf16[256,280]{1,0:T(8,128)(2,1)S(1)} %get-tuple-element.48), channel_id=1, source_target_pairs={{0,8},{4,12},{8,0},{12,4},{1,9},{5,13},{9,1},{13,5},{2,10},{6,14},... | collective-permute-start | bytes 430088 | tf_op jit(solution)/shard_map/ppermute | solution.py:272
  75.2 1.3 %collective-permute-start.6 = (bf16[256,280]{1,0:T(8,128)(2,1)S(1)}, bf16[256,280]{1,0:T(8,128)(2,1)S(1)}, u32[]{:S(2)}, u32[]{:S(2)}) collective-permute-start(bf16[256,280]{1,0:T(8,128)(2,1)S(1)} %get-tuple-element.47), channel_id=1, source_target_pairs={{0,12},{4,0},{8,4},{12,8},{1,13},{5,1},{9,5},{13,9},{2,14},{6,2},{... | collective-permute-start | bytes 430088 | tf_op jit(solution)/shard_map/ppermute | solution.py:272
  76.6 0.9 constant_dynamic-slice_fusion.2
  77.4 1.5 %collective-permute-start.3 = (bf16[2048,256]{1,0:T(8,128)(2,1)}, bf16[2048,256]{1,0:T(8,128)(2,1)}, u32[]{:S(2)}, u32[]{:S(2)}) collective-permute-start(bf16[2048,256]{1,0:T(8,128)(2,1)} %get-tuple-element.33), channel_id=1, source_target_pairs={{0,2},{1,3},{2,0},{3,1},{4,6},{5,7},{6,4},{7,5},{8,10},{9,11},{10,... | collective-permute-start | bytes 3145736 | tf_op jit(solution)/shard_map/ppermute | solution.py:244
  78.9 1.6 %collective-permute-done.4.refs_1_ = bf16[256,280]{1,0:T(8,128)(2,1)S(1)} collective-permute-done((bf16[256,280]{1,0:T(8,128)(2,1)S(1)}, bf16[256,280]{1,0:T(8,128)(2,1)S(1)}, u32[]{:S(2)}, u32[]{:S(2)}) %collective-permute-start.4) | collective-permute-done | bytes 143392 | tf_op jit(solution)/shard_map/ppermute | solution.py:272
  80.5 7.9 %collective-permute-done.5.refs_2_ = bf16[256,280]{1,0:T(8,128)(2,1)S(1)} collective-permute-done((bf16[256,280]{1,0:T(8,128)(2,1)S(1)}, bf16[256,280]{1,0:T(8,128)(2,1)S(1)}, u32[]{:S(2)}, u32[]{:S(2)}) %collective-permute-start.5) | collective-permute-done | bytes 143392 | tf_op jit(solution)/shard_map/ppermute | solution.py:272
  88.4 0.7 copy-done.7
  89.2 3.0 %shard_map.115 = bf16[256,256]{1,0:T(8,128)(2,1)} custom-call(bf16[256,280]{1,0:T(8,128)(2,1)} %get-tuple-element.50.refs_0_, bf16[256,280]{1,0:T(8,128)(2,1)} %copy-done.5, bf16[256,280]{1,0:T(8,128)(2,1)} %copy-done.6, bf16[256,280]{1,0:T(8,128)(2,1)} %copy-done.7), custom_call_target="tpu_custom_call" | custom-call | tf_op jit(solution)/shard_map/pallas_call | solution.py:309
  92.2 1.5 %convolution_convert_fusion.3 = bf16[256,1024]{1,0:T(8,128)(2,1)S(1)} fusion(bf16[256,256]{1,0:T(8,128)(2,1)} %shard_map.115, bf16[256,256]{1,0:T(8,128)(2,1)} %get-tuple-element.55, bf16[256,256]{1,0:T(8,128)(2,1)} %get-tuple-element.56, bf16[256,256]{1,0:T(8,128)(2,1)} %get-tuple-element.54, bf16[256,256]{1,0:T(8,128)(2,1)} %get-tuple-element.53), kind=kOutput, calls=%fused_computation.6 | convolution fusion | flops 136577024 | bytes 1179648 | tf_op jit(solution)/shard_map/dot_general | solution.py:369
  93.8 1.5 %collective-permute-done.7 = bf16[2,256,256]{2,1,0:T(8,128)(2,1)S(1)} collective-permute-done((bf16[2,256,256]{2,1,0:T(8,128)(2,1)S(1)}, bf16[2,256,256]{2,1,0:T(8,128)(2,1)S(1)}, u32[]{:S(2)}, u32[]{:S(2)}) %collective-permute-start.7) | collective-permute-done | bytes 262176 | tf_op jit(solution)/shard_map/ppermute | solution.py:229
  95.4 1.5 %collective-permute-start.8 = (bf16[256,256]{1,0:T(8,128)(2,1)S(1)}, bf16[256,256]{1,0:T(8,128)(2,1)S(1)}, u32[]{:S(2)}, u32[]{:S(2)}) collective-permute-start(bf16[256,256]{1,0:T(8,128)(2,1)S(1)} %fusion.10), channel_id=1, source_target_pairs={{0,2},{1,3},{2,0},{3,1},{4,6},{5,7},{6,4},{7,5},{8,10},{9,11},{10,... | collective-permute-start | bytes 393224 | tf_op jit(solution)/shard_map/ppermute | solution.py:244
  96.9 7.9 %collective-permute-done.8 = bf16[256,256]{1,0:T(8,128)(2,1)S(1)} collective-permute-done((bf16[256,256]{1,0:T(8,128)(2,1)S(1)}, bf16[256,256]{1,0:T(8,128)(2,1)S(1)}, u32[]{:S(2)}, u32[]{:S(2)}) %collective-permute-start.8) | collective-permute-done | bytes 131104 | tf_op jit(solution)/shard_map/ppermute | solution.py:244
  104.8 0.7 add_convert_fusion.3
  105.5 2.5 %add_convert_fusion = bf16[2048,256]{1,0:T(8,128)(2,1)} fusion(bf16[2048,256]{1,0:T(8,128)(2,1)} %collective-permute-done.3, bf16[2048,256]{1,0:T(8,128)(2,1)S(1)} %get-tuple-element.32), kind=kLoop, calls=%fused_computation.3 | loop fusion | flops 2097152 | bytes 3145728 | tf_op jit(solution)/shard_map/convert_element_type | solution.py:245
  (45 shorter events, 0.6 us)
Async XLA Ops:
  0.6 42.0 %copy-start = (bf16[1024,1024]{1,0:T(8,128)(2,1)S(1)}, bf16[1024,1024]{1,0:T(8,128)(2,1)}, u32[]{:S(2)}) copy-start(bf16[1024,1024]{1,0:T(8,128)(2,1)} %param.15) | copy-start | bytes 6291460
  0.6 3.8 %copy-start.10 = (bf16[2048,1024]{1,0:T(8,128)(2,1)S(1)}, bf16[2048,1024]{1,0:T(8,128)(2,1)}, u32[]{:S(2)}) copy-start(bf16[2048,1024]{1,0:T(8,128)(2,1)} %param.14) | copy-start | bytes 12582916
  0.7 3.9 %copy-start.11 = (bf16[1024,256]{1,0:T(8,128)(2,1)S(1)}, bf16[1024,256]{1,0:T(8,128)(2,1)}, u32[]{:S(2)}) copy-start(bf16[1024,256]{1,0:T(8,128)(2,1)} %param.18) | copy-start | bytes 1572868
  4.5 1.3 %copy-start.8 = (bf16[2048,256]{1,0:T(8,128)(2,1)}, bf16[2048,256]{1,0:T(8,128)(2,1)S(1)}, u32[]{:S(2)}) copy-start(bf16[2048,256]{1,0:T(8,128)(2,1)S(1)} %convolution_convert_fusion.v_ref) | copy-start | bytes 3145732
  5.8 10.2 %copy-start.9 = (bf16[2048,256]{1,0:T(8,128)(2,1)}, bf16[2048,256]{1,0:T(8,128)(2,1)S(1)}, u32[]{:S(2)}) copy-start(bf16[2048,256]{1,0:T(8,128)(2,1)S(1)} %convolution_convert_fusion.1.k_ref) | copy-start | bytes 3145732
  5.8 8.0 %copy-start.12 = (bf16[1024,256]{1,0:T(8,128)(2,1)S(1)}, bf16[1024,256]{1,0:T(8,128)(2,1)}, u32[]{:S(2)}) copy-start(bf16[1024,256]{1,0:T(8,128)(2,1)} %param.17) | copy-start | bytes 1572868
  5.9 11.8 %collective-permute-start.1 = (bf16[256,512]{1,0:T(8,128)(2,1)S(1)}, bf16[256,512]{1,0:T(8,128)(2,1)S(1)}, u32[]{:S(2)}, u32[]{:S(2)}) collective-permute-start(bf16[256,512]{1,0:T(8,128)(2,1)S(1)} %pad_maximum_fusion.3), channel_id=1, source_target_pairs={{4,0},{8,4},{12,8},{5,1},{9,5},{13,9},{6,2},{10,6},{14,10},{7,3},{... | collective-permute-start | bytes 786440 | tf_op jit(solution)/shard_map/ppermute | solution.py:21
  7.4 9.4 %copy-start.3 = (bf16[256,1024]{1,0:T(8,128)(2,1)S(1)}, bf16[256,1024]{1,0:T(8,128)(2,1)}, u32[]{:S(2)}) copy-start(bf16[256,1024]{1,0:T(8,128)(2,1)} %param.20) | copy-start | bytes 1572868
  7.4 11.2 %collective-permute-start = (bf16[256,512]{1,0:T(8,128)(2,1)S(1)}, bf16[256,512]{1,0:T(8,128)(2,1)}, u32[]{:S(2)}, u32[]{:S(2)}) collective-permute-start(bf16[256,512]{1,0:T(8,128)(2,1)S(1)} %pad_maximum_fusion.2), channel_id=1, source_target_pairs={{0,4},{4,8},{8,12},{1,5},{5,9},{9,13},{2,6},{6,10},{10,14},{3,7},{... | collective-permute-start | bytes 786440 | tf_op jit(solution)/shard_map/ppermute | solution.py:21
  16.8 1.9 %copy-start.15 = (s32[3]{0:T(128)}, s32[3]{0:T(128)S(1)}, u32[]{:S(2)}) copy-start(s32[3]{0:T(128)S(1)} %constant_dynamic-update-slice_fusion.scal_ref) | copy-start | bytes 40
  17.7 0.9 copy-start.14
  39.4 3.2 %copy-start.13 = (bf16[1024,256]{1,0:T(8,128)(2,1)S(1)}, bf16[1024,256]{1,0:T(8,128)(2,1)}, u32[]{:S(2)}) copy-start(bf16[1024,256]{1,0:T(8,128)(2,1)} %param.21) | copy-start | bytes 1572868
  42.6 4.5 %collective-permute-start.2 = (bf16[2,2048,256]{2,1,0:T(8,128)(2,1)}, bf16[2,2048,256]{2,1,0:T(8,128)(2,1)}, u32[]{:S(2)}, u32[]{:S(2)}) collective-permute-start(bf16[2,2048,256]{2,1,0:T(8,128)(2,1)} %slice.88), channel_id=1, source_target_pairs={{0,1},{1,0},{2,3},{3,2},{4,5},{5,4},{6,7},{7,6},{8,9},{9,8},{10,11... | collective-permute-start | bytes 6291464 | tf_op jit(solution)/shard_map/ppermute | solution.py:229
  42.6 4.5 %copy-start.1 = (bf16[4,2048,256]{2,1,0:T(8,128)(2,1)S(1)}, bf16[4,2048,256]{2,1,0:T(8,128)(2,1)}, u32[]{:S(2)}) copy-start(bf16[4,2048,256]{2,1,0:T(8,128)(2,1)} %shard_map.113) | copy-start | bytes 12582916
  67.2 1.5 %copy-start.2 = (f32[1024,256]{1,0:T(8,128)S(1)}, f32[1024,256]{1,0:T(8,128)}, u32[]{:S(2)}) copy-start(f32[1024,256]{1,0:T(8,128)} %get-tuple-element.36) | copy-start | bytes 3145732
  68.8 7.7 %copy-start.4 = (bf16[256,1024]{1,0:T(8,128)(2,1)S(1)}, bf16[256,1024]{1,0:T(8,128)(2,1)}, u32[]{:S(2)}) copy-start(bf16[256,1024]{1,0:T(8,128)(2,1)} %param.22) | copy-start | bytes 1572868
  69.9 10.6 %collective-permute-start.4 = (bf16[256,280]{1,0:T(8,128)(2,1)S(1)}, bf16[256,280]{1,0:T(8,128)(2,1)S(1)}, u32[]{:S(2)}, u32[]{:S(2)}) collective-permute-start(bf16[256,280]{1,0:T(8,128)(2,1)S(1)} %get-tuple-element.49), channel_id=1, source_target_pairs={{0,4},{4,8},{8,12},{12,0},{1,5},{5,9},{9,13},{13,1},{2,6},{6,10},{... | collective-permute-start | bytes 430088 | tf_op jit(solution)/shard_map/ppermute | solution.py:272
  72.5 16.0 %collective-permute-start.5 = (bf16[256,280]{1,0:T(8,128)(2,1)S(1)}, bf16[256,280]{1,0:T(8,128)(2,1)S(1)}, u32[]{:S(2)}, u32[]{:S(2)}) collective-permute-start(bf16[256,280]{1,0:T(8,128)(2,1)S(1)} %get-tuple-element.48), channel_id=1, source_target_pairs={{0,8},{4,12},{8,0},{12,4},{1,9},{5,13},{9,1},{13,5},{2,10},{6,14},... | collective-permute-start | bytes 430088 | tf_op jit(solution)/shard_map/ppermute | solution.py:272
  75.2 13.2 %collective-permute-start.6 = (bf16[256,280]{1,0:T(8,128)(2,1)S(1)}, bf16[256,280]{1,0:T(8,128)(2,1)S(1)}, u32[]{:S(2)}, u32[]{:S(2)}) collective-permute-start(bf16[256,280]{1,0:T(8,128)(2,1)S(1)} %get-tuple-element.47), channel_id=1, source_target_pairs={{0,12},{4,0},{8,4},{12,8},{1,13},{5,1},{9,5},{13,9},{2,14},{6,2},{... | collective-permute-start | bytes 430088 | tf_op jit(solution)/shard_map/ppermute | solution.py:272
  77.4 28.1 %collective-permute-start.3 = (bf16[2048,256]{1,0:T(8,128)(2,1)}, bf16[2048,256]{1,0:T(8,128)(2,1)}, u32[]{:S(2)}, u32[]{:S(2)}) collective-permute-start(bf16[2048,256]{1,0:T(8,128)(2,1)} %get-tuple-element.33), channel_id=1, source_target_pairs={{0,2},{1,3},{2,0},{3,1},{4,6},{5,7},{6,4},{7,5},{8,10},{9,11},{10,... | collective-permute-start | bytes 3145736 | tf_op jit(solution)/shard_map/ppermute | solution.py:244
  80.5 8.7 %copy-start.5 = (bf16[256,280]{1,0:T(8,128)(2,1)}, bf16[256,280]{1,0:T(8,128)(2,1)S(1)}, u32[]{:S(2)}) copy-start(bf16[256,280]{1,0:T(8,128)(2,1)S(1)} %collective-permute-done.4.refs_1_) | copy-start | bytes 430084
  88.4 0.8 copy-start.6
  88.4 0.7 copy-start.7
  93.7 1.6 %collective-permute-start.7 = (bf16[2,256,256]{2,1,0:T(8,128)(2,1)S(1)}, bf16[2,256,256]{2,1,0:T(8,128)(2,1)S(1)}, u32[]{:S(2)}, u32[]{:S(2)}) collective-permute-start(bf16[2,256,256]{2,1,0:T(8,128)(2,1)S(1)} %pad_maximum_fusion.4), channel_id=1, source_target_pairs={{0,1},{1,0},{2,3},{3,2},{4,5},{5,4},{6,7},{7,6},{8,9},{9,8},{10,11... | collective-permute-start | bytes 786440 | tf_op jit(solution)/shard_map/ppermute | solution.py:229
  95.4 9.4 %collective-permute-start.8 = (bf16[256,256]{1,0:T(8,128)(2,1)S(1)}, bf16[256,256]{1,0:T(8,128)(2,1)S(1)}, u32[]{:S(2)}, u32[]{:S(2)}) collective-permute-start(bf16[256,256]{1,0:T(8,128)(2,1)S(1)} %fusion.10), channel_id=1, source_target_pairs={{0,2},{1,3},{2,0},{3,1},{4,6},{5,7},{6,4},{7,5},{8,10},{9,11},{10,... | collective-permute-start | bytes 393224 | tf_op jit(solution)/shard_map/ppermute | solution.py:244

commit v19 on v18

--- a/solution.py
+++ b/solution.py
@@ -333,37 +333,31 @@
     head_devices = lax.axis_size("head")
     paired = head_devices % 2 == 0
     w_ordered = ordered_columns(w_out, "head")
-    parts = [
-        window_attention(
-            query, keyed, valued, low, high, w_ordered, first_frame, length,
-            c * chunk_rows, chunk_rows, head_devices,
-        )
-        for c in range(chunks)
-    ]
     latent_count = latents.shape[0]
     latent_query = project(latents, w_latent_query)
     valid_count = jnp.clip(length - first_frame, 0, frame_count)
-    frame_parts = []
-    if paired:
-        first_sums = chip_pair_sums(parts[0], "head")
-        first_sums, rest, keyed, valued = lax.optimization_barrier(
-            (first_sums, parts[1:], keyed, valued)
-        )
-        frame_parts.append(cross_chip_sum(first_sums, "head"))
-        rest_sums = [chip_pair_sums(blocks, "head") for blocks in rest]
-    else:
-        frame_parts = [plain_block_sum(blocks, "head") for blocks in parts]
     peaks, totals, local_accum = latent_attention(latent_query, keyed, valued, valid_count)
     payload = jnp.concatenate(
         [local_accum.astype(jnp.bfloat16)] + split_three(jnp.concatenate([peaks, totals], axis=1)),
         axis=1,
     )
-    if paired:
-        rest_sums, payload = lax.optimization_barrier((rest_sums, payload))
-        frame_parts.extend(cross_chip_sum(sums, "head") for sums in rest_sums)
-    frames_out = jnp.concatenate(frame_parts, axis=0)
+    payload, query, keyed, valued, low, high = lax.optimization_barrier(
+        (payload, query, keyed, valued, low, high)
+    )
     rows_here = latent_count // seq_devices
     parts = exchange_rows(payload, "seq", rows_here)
+    windows = [
+        window_attention(
+            query, keyed, valued, low, high, w_ordered, first_frame, length,
+            c * chunk_rows, chunk_rows, head_devices,
+        )
+        for c in range(chunks)
+    ]
+    if paired:
+        frame_parts = [cross_chip_sum(chip_pair_sums(blocks, "head"), "head") for blocks in windows]
+    else:
+        frame_parts = [plain_block_sum(blocks, "head") for blocks in windows]
+    frames_out = jnp.concatenate(frame_parts, axis=0)
     summary = merge_parts(parts, head_width, heads_here)
     if paired:
         latent_terms = jnp.dot(

time: 108 us -> 128 us (1.19); the launches traced: 108 us -> 126 us
  waiting for transfers between devices: 22.7 us -> 37.4 us
  matrix products: 10.2 us -> 13.5 us
  starting transfers between devices: 17.6 us -> 15.2 us
  other arithmetic: 8.99 us -> 10.4 us
    ppermute x2, waiting for transfers between devices: 7.86 us -> 24.1 us  [cross_chip_sum(): total = total + lax.ppermute(chip_sums[d], axis, pairs).astype(jnp.float32)]
    dot_general x4, matrix products: 8.76 us -> 12.1 us  [project(): jnp.dot(source, weight, preferred_element_type=jnp.float32)]
    ppermute x2, waiting for transfers between devices: 4.48 us -> 1.52 us  [chip_pair_sums(): received = lax.ppermute(blocks[:chips], axis, swap)]
    ppermute x3, waiting for transfers between devices: 9.51 us -> 11.8 us  [exchange_rows(): parts.append(lax.ppermute(block, axis, pairs))]
    convert_element_type x2, other arithmetic: 3.17 us -> 1.85 us  [chip_pair_sums(): (blocks[chips + d].astype(jnp.float32) + received[d].astype(jnp.float32))...]
  transfers between devices with their start and end apart: 9 -> 9, of which waited for: 6 -> 4; matrix products, arithmetic and copies ran while one was open for 7% -> 13% of each run, Pallas kernels for 3% -> 16%
where the time goes in v19:
time: 128 us; the launch traced here: 126 us
  Pallas kernels  40.8 us (32%)
  waiting for transfers between devices  37.4 us (29%)
  starting transfers between devices  15.2 us (12%)
  matrix products  13.5 us (11%)
  other arithmetic  10.4 us (8%)
  local copies, waits for them, and re-layouts  6.98 us (5%)
  between operations  1.55 us (1%)
    ppermute x2, waiting for transfers between devices, cross_chip_sum(): total = total + lax.ppermute(chip_sums[d], axis, pairs).astype(jnp.float32)  24.1 us
    pallas_call x1, Pallas kernels, window_attention(): pl.pallas_call(kernel, cost_estimate=cost, out_shape=jax.ShapeDtypeStruct...  20.8 us
    pallas_call x1, Pallas kernels, latent_attention(): pl.pallas_call(kernel, cost_estimate=cost, out_shape=(jax.ShapeDtypeStruc...  17 us
    dot_general x4, matrix products, project(): jnp.dot(source, weight, preferred_element_type=jnp.float32)  12.1 us
    ppermute x3, waiting for transfers between devices, exchange_rows(): parts.append(lax.ppermute(block, axis, pairs))  11.8 us
    ppermute x3, starting transfers between devices, exchange_rows(): parts.append(lax.ppermute(block, axis, pairs))  5.87 us
    ppermute x1, starting transfers between devices, halos(): lax.ppermute(tail, axis, forward)  5.64 us
    convert_element_type x2, other arithmetic, cross_chip_sum(): return total.astype(jnp.bfloat16)  3.69 us
  transfers between devices with their start and end apart: 9, of which 4 were waited for; matrix products, arithmetic and copies ran while one was open for 13% of the time, Pallas kernels for 16%

profile of v19, /device:TPU:0, one launch (start us, length us, event | category | flops | bytes accessed | tf_op | source)
XLA Modules:
  0.0 125.8 jit_solution(2014872845647030946)
XLA Ops:
  0.7 3.7 %convolution_convert_fusion.1.v_ref = bf16[2048,256]{1,0:T(8,128)(2,1)S(1)} fusion(bf16[2048,1024]{1,0:T(8,128)(2,1)} %param.14, bf16[1024,256]{1,0:T(8,128)(2,1)} %param.19), kind=kOutput, calls=%fused_computation.1 | convolution fusion | flops 1074266112 | bytes 5767168 | tf_op jit(solution)/shard_map/dot_general | solution.py:25
  4.5 1.3 %convolution_convert_fusion.2.k_ref = bf16[2048,256]{1,0:T(8,128)(2,1)S(1)} fusion(bf16[2048,1024]{1,0:T(8,128)(2,1)S(1)} %copy-done.10, bf16[1024,256]{1,0:T(8,128)(2,1)S(1)} %copy-done.11), kind=kOutput, calls=%fused_computation.2 | convolution fusion | flops 1074266112 | bytes 5767168 | tf_op jit(solution)/shard_map/dot_general | solution.py:25
  5.9 0.8 pad_maximum_fusion.2
  6.7 5.6 %collective-permute-start = (bf16[256,512]{1,0:T(8,128)(2,1)}, bf16[256,512]{1,0:T(8,128)(2,1)}, u32[]{:S(2)}, u32[]{:S(2)}) collective-permute-start(bf16[256,512]{1,0:T(8,128)(2,1)} %pad_maximum_fusion.2), channel_id=1, source_target_pairs={{0,4},{4,8},{8,12},{1,5},{5,9},{9,13},{2,6},{6,10},{10,14},{3,7},{... | collective-permute-start | bytes 786440 | tf_op jit(solution)/shard_map/ppermute | solution.py:21
  12.3 0.7 pad_maximum_fusion.3
  13.1 1.5 %collective-permute-start.1 = (bf16[256,512]{1,0:T(8,128)(2,1)}, bf16[256,512]{1,0:T(8,128)(2,1)}, u32[]{:S(2)}, u32[]{:S(2)}) collective-permute-start(bf16[256,512]{1,0:T(8,128)(2,1)} %pad_maximum_fusion.3), channel_id=1, source_target_pairs={{4,0},{8,4},{12,8},{5,1},{9,5},{13,9},{6,2},{10,6},{14,10},{7,3},{... | collective-permute-start | bytes 786440 | tf_op jit(solution)/shard_map/ppermute | solution.py:21
  15.3 2.5 %convolution_convert_fusion.4.q_ref = bf16[1024,256]{1,0:T(8,128)(2,1)} fusion(bf16[1024,1024]{1,0:T(8,128)(2,1)S(1)} %copy-done, bf16[1024,256]{1,0:T(8,128)(2,1)} %param.21), kind=kOutput, calls=%fused_computation.8 | convolution fusion | flops 537133056 | bytes 3145728 | tf_op jit(solution)/shard_map/dot_general | solution.py:25
  17.8 17.0 %shard_map.113 = (f32[1024,256]{1,0:T(8,128)}, f32[1024,128]{1,0:T(8,128)}) custom-call(s32[1]{0:T(128)} %bitcast.2.scal_ref, bf16[1024,256]{1,0:T(8,128)(2,1)} %convolution_convert_fusion.4.q_ref, bf16[2048,256]{1,0:T(8,128)(2,1)} %copy-done.9, bf16[2048,256]{1,0:T(8,128)(2,1)} %copy-done.8), custom_call_target="tpu_custom_call" | custom-call | flops 2147483648 | bytes 4194304 | tf_op jit(solution)/shard_map/pallas_call | solution.py:153
  34.8 2.1 %subtract_convert_fusion = (bf16[1024,8]{1,0:T(8,128)(2,1)S(1)}, bf16[1024,8]{1,0:T(8,128)(2,1)}, bf16[1024,8]{1,0:T(8,128)(2,1)}) fusion(f32[1024,128]{1,0:T(8,128)} %get-tuple-element.35), kind=kLoop, calls=%fused_computation.20 | loop fusion | flops 49152 | bytes 98304 | tf_op jit(solution)/shard_map/convert_element_type | solution.py:261
  36.9 4.6 %convolution_convert_fusion.q_ref = bf16[2048,256]{1,0:T(8,128)(2,1)} fusion(bf16[2048,1024]{1,0:T(8,128)(2,1)} %param.14, bf16[1024,256]{1,0:T(8,128)(2,1)} %param.17), kind=kOutput, calls=%fused_computation | convolution fusion | flops 1074266112 | bytes 5767168 | tf_op jit(solution)/shard_map/dot_general | solution.py:25
  41.5 1.2 constant_dynamic-slice_fusion.10
  42.8 0.9 pad_maximum_fusion.1.w_ref
  43.7 0.3 pad_maximum_fusion
  44.0 20.8 %shard_map.114 = bf16[4,2048,256]{2,1,0:T(8,128)(2,1)} custom-call(s32[3]{0:T(128)} %copy-done.12, bf16[2048,256]{1,0:T(8,128)(2,1)} %convolution_convert_fusion.q_ref, bf16[2048,256]{1,0:T(8,128)(2,1)} %copy-done.9, bf16[2048,256]{1,0:T(8,128)(2,1)} %copy-done.8, bf16[256,512]{1,0:T(8,128)(2,1)} %collective-permute-done.low_ref, ...), custom_call_target="tpu_custom_call" | custom-call | flops 3221225472 | bytes 8388608 | tf_op jit(solution)/shard_map/pallas_call | solution.py:93
  64.8 3.2 %slice.88 = bf16[2,2048,256]{2,1,0:T(8,128)(2,1)} slice(bf16[4,2048,256]{2,1,0:T(8,128)(2,1)} %shard_map.114), slice={[0:2], [0:2048], [0:256]} | slice | bytes 4194304 | tf_op jit(solution)/shard_map/slice | solution.py:229
  68.0 0.8 constant_dynamic-slice_fusion.3
  68.7 2.6 %collective-permute-start.4 = (bf16[256,280]{1,0:T(8,128)(2,1)S(1)}, bf16[256,280]{1,0:T(8,128)(2,1)S(1)}, u32[]{:S(2)}, u32[]{:S(2)}) collective-permute-start(bf16[256,280]{1,0:T(8,128)(2,1)S(1)} %get-tuple-element.51), channel_id=1, source_target_pairs={{0,4},{4,8},{8,12},{12,0},{1,5},{5,9},{9,13},{13,1},{2,6},{6,10},{... | collective-permute-start | bytes 430088 | tf_op jit(solution)/shard_map/ppermute | solution.py:272
  71.4 2.3 %collective-permute-start.5 = (bf16[256,280]{1,0:T(8,128)(2,1)S(1)}, bf16[256,280]{1,0:T(8,128)(2,1)S(1)}, u32[]{:S(2)}, u32[]{:S(2)}) collective-permute-start(bf16[256,280]{1,0:T(8,128)(2,1)S(1)} %get-tuple-element.50), channel_id=1, source_target_pairs={{0,8},{4,12},{8,0},{12,4},{1,9},{5,13},{9,1},{13,5},{2,10},{6,14},... | collective-permute-start | bytes 430088 | tf_op jit(solution)/shard_map/ppermute | solution.py:272
  73.7 0.9 collective-permute-start.6
  74.6 0.8 constant_dynamic-slice_fusion.2
  75.4 3.6 %collective-permute-done.4.refs_1_ = bf16[256,280]{1,0:T(8,128)(2,1)S(1)} collective-permute-done((bf16[256,280]{1,0:T(8,128)(2,1)S(1)}, bf16[256,280]{1,0:T(8,128)(2,1)S(1)}, u32[]{:S(2)}, u32[]{:S(2)}) %collective-permute-start.4) | collective-permute-done | bytes 143392 | tf_op jit(solution)/shard_map/ppermute | solution.py:272
  79.0 8.2 %collective-permute-done.5.refs_2_ = bf16[256,280]{1,0:T(8,128)(2,1)S(1)} collective-permute-done((bf16[256,280]{1,0:T(8,128)(2,1)S(1)}, bf16[256,280]{1,0:T(8,128)(2,1)S(1)}, u32[]{:S(2)}, u32[]{:S(2)}) %collective-permute-start.5) | collective-permute-done | bytes 143392 | tf_op jit(solution)/shard_map/ppermute | solution.py:272
  87.2 0.7 copy-done.6
  88.0 3.0 %shard_map.115 = bf16[256,256]{1,0:T(8,128)(2,1)} custom-call(bf16[256,280]{1,0:T(8,128)(2,1)} %get-tuple-element.52.refs_0_, bf16[256,280]{1,0:T(8,128)(2,1)} %copy-done.5, bf16[256,280]{1,0:T(8,128)(2,1)} %copy-done.6, bf16[256,280]{1,0:T(8,128)(2,1)} %copy-done.7), custom_call_target="tpu_custom_call" | custom-call | tf_op jit(solution)/shard_map/pallas_call | solution.py:309
  91.0 1.3 %convolution_convert_fusion.3 = bf16[256,1024]{1,0:T(8,128)(2,1)S(1)} fusion(bf16[256,256]{1,0:T(8,128)(2,1)} %shard_map.115, bf16[256,256]{1,0:T(8,128)(2,1)} %get-tuple-element.57, bf16[256,256]{1,0:T(8,128)(2,1)} %get-tuple-element.58, bf16[256,256]{1,0:T(8,128)(2,1)S(1)} %get-tuple-element.56, bf16[256,256]{1,0:T(8,128)(2,1)S(1)} %get-tuple-element.55), kind=kOutput, calls=%fused_computation.7 | convolution fusion | flops 136577024 | bytes 1179648 | tf_op jit(solution)/shard_map/dot_general | solution.py:363
  92.4 1.8 %fusion.2 = bf16[2048,256]{1,0:T(8,128)(2,1)S(1)} fusion(bf16[2,2048,256]{2,1,0:T(8,128)(2,1)} %collective-permute-done.2, bf16[4,2048,256]{2,1,0:T(8,128)(2,1)} %shard_map.114), kind=kLoop, calls=%fused_computation.10 | loop fusion | flops 2097152 | bytes 3145728 | tf_op jit(solution)/shard_map/convert_element_type | solution.py:231
  94.2 1.6 %collective-permute-start.3 = (bf16[2048,256]{1,0:T(8,128)(2,1)S(1)}, bf16[2048,256]{1,0:T(8,128)(2,1)S(1)}, u32[]{:S(2)}, u32[]{:S(2)}) collective-permute-start(bf16[2048,256]{1,0:T(8,128)(2,1)S(1)} %fusion.2), channel_id=1, source_target_pairs={{0,2},{1,3},{2,0},{3,1},{4,6},{5,7},{6,4},{7,5},{8,10},{9,11},{10,... | collective-permute-start | bytes 3145736 | tf_op jit(solution)/shard_map/ppermute | solution.py:244
  95.9 1.5 %collective-permute-done.7 = bf16[2,256,256]{2,1,0:T(8,128)(2,1)S(1)} collective-permute-done((bf16[2,256,256]{2,1,0:T(8,128)(2,1)S(1)}, bf16[2,256,256]{2,1,0:T(8,128)(2,1)S(1)}, u32[]{:S(2)}, u32[]{:S(2)}) %collective-permute-start.7) | collective-permute-done | bytes 262176 | tf_op jit(solution)/shard_map/ppermute | solution.py:229
  97.4 0.6 collective-permute-start.8
  98.0 24.1 %collective-permute-done.8 = bf16[256,256]{1,0:T(8,128)(2,1)S(1)} collective-permute-done((bf16[256,256]{1,0:T(8,128)(2,1)S(1)}, bf16[256,256]{1,0:T(8,128)(2,1)S(1)}, u32[]{:S(2)}, u32[]{:S(2)}) %collective-permute-start.8) | collective-permute-done | bytes 131104 | tf_op jit(solution)/shard_map/ppermute | solution.py:244
  122.1 0.7 add_convert_fusion.2
  122.8 3.0 %fusion = bf16[2048,256]{1,0:T(8,128)(2,1)} fusion(bf16[2048,256]{1,0:T(8,128)(2,1)S(1)} %collective-permute-done.3, bf16[2,2048,256]{2,1,0:T(8,128)(2,1)} %collective-permute-done.2, bf16[4,2048,256]{2,1,0:T(8,128)(2,1)} %shard_map.114), kind=kLoop, calls=%fused_computation.4 | loop fusion | flops 4194304 | bytes 4194304 | tf_op jit(solution)/shard_map/convert_element_type | solution.py:245
  (39 shorter events, 0.6 us)
Async XLA Ops:
  0.6 14.6 %copy-start = (bf16[1024,1024]{1,0:T(8,128)(2,1)S(1)}, bf16[1024,1024]{1,0:T(8,128)(2,1)}, u32[]{:S(2)}) copy-start(bf16[1024,1024]{1,0:T(8,128)(2,1)} %param.15) | copy-start | bytes 6291460
  0.6 3.8 %copy-start.10 = (bf16[2048,1024]{1,0:T(8,128)(2,1)S(1)}, bf16[2048,1024]{1,0:T(8,128)(2,1)}, u32[]{:S(2)}) copy-start(bf16[2048,1024]{1,0:T(8,128)(2,1)} %param.14) | copy-start | bytes 12582916
  0.7 3.9 %copy-start.11 = (bf16[1024,256]{1,0:T(8,128)(2,1)S(1)}, bf16[1024,256]{1,0:T(8,128)(2,1)}, u32[]{:S(2)}) copy-start(bf16[1024,256]{1,0:T(8,128)(2,1)} %param.18) | copy-start | bytes 1572868
  4.5 1.3 %copy-start.8 = (bf16[2048,256]{1,0:T(8,128)(2,1)}, bf16[2048,256]{1,0:T(8,128)(2,1)S(1)}, u32[]{:S(2)}) copy-start(bf16[2048,256]{1,0:T(8,128)(2,1)S(1)} %convolution_convert_fusion.1.v_ref) | copy-start | bytes 3145732
  5.8 7.2 %copy-start.9 = (bf16[2048,256]{1,0:T(8,128)(2,1)}, bf16[2048,256]{1,0:T(8,128)(2,1)S(1)}, u32[]{:S(2)}) copy-start(bf16[2048,256]{1,0:T(8,128)(2,1)S(1)} %convolution_convert_fusion.2.k_ref) | copy-start | bytes 3145732
  6.7 37.3 %collective-permute-start = (bf16[256,512]{1,0:T(8,128)(2,1)}, bf16[256,512]{1,0:T(8,128)(2,1)}, u32[]{:S(2)}, u32[]{:S(2)}) collective-permute-start(bf16[256,512]{1,0:T(8,128)(2,1)} %pad_maximum_fusion.2), channel_id=1, source_target_pairs={{0,4},{4,8},{8,12},{1,5},{5,9},{9,13},{2,6},{6,10},{10,14},{3,7},{... | collective-permute-start | bytes 786440 | tf_op jit(solution)/shard_map/ppermute | solution.py:21
  13.1 30.9 %collective-permute-start.1 = (bf16[256,512]{1,0:T(8,128)(2,1)}, bf16[256,512]{1,0:T(8,128)(2,1)}, u32[]{:S(2)}, u32[]{:S(2)}) collective-permute-start(bf16[256,512]{1,0:T(8,128)(2,1)} %pad_maximum_fusion.3), channel_id=1, source_target_pairs={{4,0},{8,4},{12,8},{5,1},{9,5},{13,9},{6,2},{10,6},{14,10},{7,3},{... | collective-permute-start | bytes 786440 | tf_op jit(solution)/shard_map/ppermute | solution.py:21
  36.9 5.8 %copy-start.1 = (f32[1024,256]{1,0:T(8,128)S(1)}, f32[1024,256]{1,0:T(8,128)}, u32[]{:S(2)}) copy-start(f32[1024,256]{1,0:T(8,128)} %get-tuple-element.34) | copy-start | bytes 3145732
  41.5 2.2 %copy-start.2 = (bf16[1024,8]{1,0:T(8,128)(2,1)S(1)}, bf16[1024,8]{1,0:T(8,128)(2,1)}, u32[]{:S(2)}) copy-start(bf16[1024,8]{1,0:T(8,128)(2,1)} %get-tuple-element.43) | copy-start | bytes 49156
  41.5 2.2 %copy-start.3 = (bf16[1024,8]{1,0:T(8,128)(2,1)S(1)}, bf16[1024,8]{1,0:T(8,128)(2,1)}, u32[]{:S(2)}) copy-start(bf16[1024,8]{1,0:T(8,128)(2,1)} %get-tuple-element.44) | copy-start | bytes 49156
  42.8 1.2 copy-start.12
  64.8 9.8 %copy-start.4 = (bf16[256,1024]{1,0:T(8,128)(2,1)S(1)}, bf16[256,1024]{1,0:T(8,128)(2,1)}, u32[]{:S(2)}) copy-start(bf16[256,1024]{1,0:T(8,128)(2,1)} %param.22) | copy-start | bytes 1572868
  68.0 24.4 %collective-permute-start.2 = (bf16[2,2048,256]{2,1,0:T(8,128)(2,1)}, bf16[2,2048,256]{2,1,0:T(8,128)(2,1)}, u32[]{:S(2)}, u32[]{:S(2)}) collective-permute-start(bf16[2,2048,256]{2,1,0:T(8,128)(2,1)} %slice.88), channel_id=1, source_target_pairs={{0,1},{1,0},{2,3},{3,2},{4,5},{5,4},{6,7},{7,6},{8,9},{9,8},{10,11... | collective-permute-start | bytes 6291464 | tf_op jit(solution)/shard_map/ppermute | solution.py:229
  68.7 10.3 %collective-permute-start.4 = (bf16[256,280]{1,0:T(8,128)(2,1)S(1)}, bf16[256,280]{1,0:T(8,128)(2,1)S(1)}, u32[]{:S(2)}, u32[]{:S(2)}) collective-permute-start(bf16[256,280]{1,0:T(8,128)(2,1)S(1)} %get-tuple-element.51), channel_id=1, source_target_pairs={{0,4},{4,8},{8,12},{12,0},{1,5},{5,9},{9,13},{13,1},{2,6},{6,10},{... | collective-permute-start | bytes 430088 | tf_op jit(solution)/shard_map/ppermute | solution.py:272
  71.4 15.9 %collective-permute-start.5 = (bf16[256,280]{1,0:T(8,128)(2,1)S(1)}, bf16[256,280]{1,0:T(8,128)(2,1)S(1)}, u32[]{:S(2)}, u32[]{:S(2)}) collective-permute-start(bf16[256,280]{1,0:T(8,128)(2,1)S(1)} %get-tuple-element.50), channel_id=1, source_target_pairs={{0,8},{4,12},{8,0},{12,4},{1,9},{5,13},{9,1},{13,5},{2,10},{6,14},... | collective-permute-start | bytes 430088 | tf_op jit(solution)/shard_map/ppermute | solution.py:272
  73.7 13.5 %collective-permute-start.6 = (bf16[256,280]{1,0:T(8,128)(2,1)S(1)}, bf16[256,280]{1,0:T(8,128)(2,1)S(1)}, u32[]{:S(2)}, u32[]{:S(2)}) collective-permute-start(bf16[256,280]{1,0:T(8,128)(2,1)S(1)} %get-tuple-element.49), channel_id=1, source_target_pairs={{0,12},{4,0},{8,4},{12,8},{1,13},{5,1},{9,5},{13,9},{2,14},{6,2},{... | collective-permute-start | bytes 430088 | tf_op jit(solution)/shard_map/ppermute | solution.py:272
  79.0 8.2 %copy-start.5 = (bf16[256,280]{1,0:T(8,128)(2,1)}, bf16[256,280]{1,0:T(8,128)(2,1)S(1)}, u32[]{:S(2)}) copy-start(bf16[256,280]{1,0:T(8,128)(2,1)S(1)} %collective-permute-done.4.refs_1_) | copy-start | bytes 430084
  87.2 0.7 copy-start.6
  87.2 0.8 copy-start.7
  94.2 28.6 %collective-permute-start.3 = (bf16[2048,256]{1,0:T(8,128)(2,1)S(1)}, bf16[2048,256]{1,0:T(8,128)(2,1)S(1)}, u32[]{:S(2)}, u32[]{:S(2)}) collective-permute-start(bf16[2048,256]{1,0:T(8,128)(2,1)S(1)} %fusion.2), channel_id=1, source_target_pairs={{0,2},{1,3},{2,0},{3,1},{4,6},{5,7},{6,4},{7,5},{8,10},{9,11},{10,... | collective-permute-start | bytes 3145736 | tf_op jit(solution)/shard_map/ppermute | solution.py:244
  95.8 1.6 %collective-permute-start.7 = (bf16[2,256,256]{2,1,0:T(8,128)(2,1)S(1)}, bf16[2,256,256]{2,1,0:T(8,128)(2,1)S(1)}, u32[]{:S(2)}, u32[]{:S(2)}) collective-permute-start(bf16[2,256,256]{2,1,0:T(8,128)(2,1)S(1)} %pad_maximum_fusion.4), channel_id=1, source_target_pairs={{0,1},{1,0},{2,3},{3,2},{4,5},{5,4},{6,7},{7,6},{8,9},{9,8},{10,11... | collective-permute-start | bytes 786440 | tf_op jit(solution)/shard_map/ppermute | solution.py:229
  97.4 24.7 %collective-permute-start.8 = (bf16[256,256]{1,0:T(8,128)(2,1)S(1)}, bf16[256,256]{1,0:T(8,128)(2,1)S(1)}, u32[]{:S(2)}, u32[]{:S(2)}) collective-permute-start(bf16[256,256]{1,0:T(8,128)(2,1)S(1)} %fusion.11), channel_id=1, source_target_pairs={{0,2},{1,3},{2,0},{3,1},{4,6},{5,7},{6,4},{7,5},{8,10},{9,11},{10,... | collective-permute-start | bytes 393224 | tf_op jit(solution)/shard_map/ppermute | solution.py:244

commit v20 on v18

--- a/solution.py
+++ b/solution.py
@@ -346,9 +346,11 @@
     frame_parts = []
     if paired:
         first_sums = chip_pair_sums(parts[0], "head")
-        first_sums, rest, keyed, valued = lax.optimization_barrier(
-            (first_sums, parts[1:], keyed, valued)
-        )
+        rest = parts[1:]
+        if rest:
+            first_sums, rest, keyed, valued = lax.optimization_barrier(
+                (first_sums, rest, keyed, valued)
+            )
         frame_parts.append(cross_chip_sum(first_sums, "head"))
         rest_sums = [chip_pair_sums(blocks, "head") for blocks in rest]
     else:

time: 108 us -> 126 us (1.17)
  waiting for transfers between devices: 22.7 us -> 45.2 us
  starting transfers between devices: 17.6 us -> 13.5 us
    ppermute x2, waiting for transfers between devices: 7.86 us -> 23.8 us  [cross_chip_sum(): total = total + lax.ppermute(chip_sums[d], axis, pairs).astype(jnp.float32)]
    ppermute x3, waiting for transfers between devices: 9.51 us -> 15.6 us  [exchange_rows(): parts.append(lax.ppermute(block, axis, pairs))]
    ppermute x1, waiting for transfers between devices: 0.01 us -> 4.31 us  [halos(): lax.ppermute(head, axis, backward)]
    ppermute x2, waiting for transfers between devices: 4.48 us -> 1.52 us  [chip_pair_sums(): received = lax.ppermute(blocks[:chips], axis, swap)]
    ppermute x3, starting transfers between devices: 6.69 us -> 4.6 us  [exchange_rows(): parts.append(lax.ppermute(block, axis, pairs))]
    ppermute x1, starting transfers between devices: 6.42 us -> 5.07 us  [halos(): lax.ppermute(tail, axis, forward)]
    convert_element_type x2, other arithmetic: 3.17 us -> 1.85 us  [chip_pair_sums(): (blocks[chips + d].astype(jnp.float32) + received[d].astype(jnp.float32))...]
    convert_element_type x1, other arithmetic: 1.4 us -> 0.11 us  [split_three(): lo = (rest - mid.astype(jnp.float32)).astype(jnp.bfloat16)]
  transfers between devices with their start and end apart: 9 -> 9, of which waited for: 6 -> 5; matrix products, arithmetic and copies ran while one was open for 7% -> 8% of each run, Pallas kernels for 3% -> 16%
where the time goes in v20:
time: 126 us; the launch traced here: 125 us
  waiting for transfers between devices  45.2 us (36%)
  Pallas kernels  40.8 us (32%)
  starting transfers between devices  13.5 us (11%)
  matrix products  10.1 us (8%)
  other arithmetic  8.19 us (6%)
  local copies, waits for them, and re-layouts  5.88 us (5%)
  between operations  1.56 us (1%)
    ppermute x2, waiting for transfers between devices, cross_chip_sum(): total = total + lax.ppermute(chip_sums[d], axis, pairs).astype(jnp.float32)  23.8 us
    pallas_call x1, Pallas kernels, window_attention(): pl.pallas_call(kernel, cost_estimate=cost, out_shape=jax.ShapeDtypeStruct...  20.8 us
    pallas_call x1, Pallas kernels, latent_attention(): pl.pallas_call(kernel, cost_estimate=cost, out_shape=(jax.ShapeDtypeStruc...  17 us
    ppermute x3, waiting for transfers between devices, exchange_rows(): parts.append(lax.ppermute(block, axis, pairs))  15.6 us
    dot_general x4, matrix products, project(): jnp.dot(source, weight, preferred_element_type=jnp.float32)  8.77 us
    ppermute x1, starting transfers between devices, halos(): lax.ppermute(tail, axis, forward)  5.07 us
    ppermute x3, starting transfers between devices, exchange_rows(): parts.append(lax.ppermute(block, axis, pairs))  4.6 us
    ppermute x1, waiting for transfers between devices, halos(): lax.ppermute(head, axis, backward)  4.31 us
  transfers between devices with their start and end apart: 9, of which 5 were waited for; matrix products, arithmetic and copies ran while one was open for 8% of the time, Pallas kernels for 16%

profile of v20, /device:TPU:0, one launch (start us, length us, event | category | flops | bytes accessed | tf_op | source)
XLA Modules:
  0.0 125.2 jit_solution(9712624536632892946)
XLA Ops:
  0.7 3.7 %convolution_convert_fusion.1.k_ref = bf16[2048,256]{1,0:T(8,128)(2,1)S(1)} fusion(bf16[2048,1024]{1,0:T(8,128)(2,1)} %param.14, bf16[1024,256]{1,0:T(8,128)(2,1)} %param.18), kind=kOutput, calls=%fused_computation.1 | convolution fusion | flops 1074266112 | bytes 5767168 | tf_op jit(solution)/shard_map/dot_general | solution.py:25
  4.4 0.1 copy-done.10
  4.5 1.3 %convolution_convert_fusion.v_ref = bf16[2048,256]{1,0:T(8,128)(2,1)S(1)} fusion(bf16[2048,1024]{1,0:T(8,128)(2,1)S(1)} %copy-done.9, bf16[1024,256]{1,0:T(8,128)(2,1)S(1)} %copy-done.10), kind=kOutput, calls=%fused_computation | convolution fusion | flops 1074266112 | bytes 5767168 | tf_op jit(solution)/shard_map/dot_general | solution.py:25
  5.9 5.1 %collective-permute-start = (bf16[256,512]{1,0:T(8,128)(2,1)S(1)}, bf16[256,512]{1,0:T(8,128)(2,1)S(1)}, u32[]{:S(2)}, u32[]{:S(2)}) collective-permute-start(bf16[256,512]{1,0:T(8,128)(2,1)S(1)} %pad_maximum_fusion.2), channel_id=1, source_target_pairs={{0,4},{4,8},{8,12},{1,5},{5,9},{9,13},{2,6},{6,10},{10,14},{3,7},{... | collective-permute-start | bytes 786440 | tf_op jit(solution)/shard_map/ppermute | solution.py:21
  11.0 1.6 %collective-permute-start.1 = (bf16[256,512]{1,0:T(8,128)(2,1)S(1)}, bf16[256,512]{1,0:T(8,128)(2,1)}, u32[]{:S(2)}, u32[]{:S(2)}) collective-permute-start(bf16[256,512]{1,0:T(8,128)(2,1)S(1)} %pad_maximum_fusion.3), channel_id=1, source_target_pairs={{4,0},{8,4},{12,8},{5,1},{9,5},{13,9},{6,2},{10,6},{14,10},{7,3},{... | collective-permute-start | bytes 786440 | tf_op jit(solution)/shard_map/ppermute | solution.py:21
  12.7 2.3 %convolution_convert_fusion.2.q_ref = bf16[2048,256]{1,0:T(8,128)(2,1)} fusion(bf16[2048,1024]{1,0:T(8,128)(2,1)S(1)} %copy-done.9, bf16[1024,256]{1,0:T(8,128)(2,1)S(1)} %copy-done.11), kind=kOutput, calls=%fused_computation.2 | convolution fusion | flops 1074266112 | bytes 5767168 | tf_op jit(solution)/shard_map/dot_general | solution.py:25
  15.7 0.9 pad_maximum_fusion.1.w_ref
  16.6 4.3 %collective-permute-done.1.high_ref = bf16[256,512]{1,0:T(8,128)(2,1)} collective-permute-done((bf16[256,512]{1,0:T(8,128)(2,1)S(1)}, bf16[256,512]{1,0:T(8,128)(2,1)}, u32[]{:S(2)}, u32[]{:S(2)}) %collective-permute-start.1) | collective-permute-done | bytes 262176 | tf_op jit(solution)/shard_map/ppermute | solution.py:21
  20.9 20.8 %shard_map.113 = bf16[4,2048,256]{2,1,0:T(8,128)(2,1)} custom-call(s32[3]{0:T(128)} %copy-done.14, bf16[2048,256]{1,0:T(8,128)(2,1)} %convolution_convert_fusion.2.q_ref, bf16[2048,256]{1,0:T(8,128)(2,1)} %copy-done.7, bf16[2048,256]{1,0:T(8,128)(2,1)} %copy-done.8, bf16[256,512]{1,0:T(8,128)(2,1)} %copy-done.13, ...), custom_call_target="tpu_custom_call" | custom-call | flops 3221225472 | bytes 8388608 | tf_op jit(solution)/shard_map/pallas_call | solution.py:93
  41.7 3.2 %slice.88 = bf16[2,2048,256]{2,1,0:T(8,128)(2,1)} slice(bf16[4,2048,256]{2,1,0:T(8,128)(2,1)} %shard_map.113), slice={[0:2], [0:2048], [0:256]} | slice | bytes 4194304 | tf_op jit(solution)/shard_map/slice | solution.py:229
  44.9 1.5 %convolution_convert_fusion.4.q_ref = bf16[1024,256]{1,0:T(8,128)(2,1)} fusion(bf16[1024,1024]{1,0:T(8,128)(2,1)S(1)} %copy-done, bf16[1024,256]{1,0:T(8,128)(2,1)S(1)} %copy-done.12), kind=kOutput, calls=%fused_computation.8 | convolution fusion | flops 537133056 | bytes 3145728 | tf_op jit(solution)/shard_map/dot_general | solution.py:25
  46.5 17.0 %shard_map.114 = (f32[1024,256]{1,0:T(8,128)}, f32[1024,128]{1,0:T(8,128)}) custom-call(s32[1]{0:T(128)} %bitcast.4.scal_ref, bf16[1024,256]{1,0:T(8,128)(2,1)} %convolution_convert_fusion.4.q_ref, bf16[2048,256]{1,0:T(8,128)(2,1)} %copy-done.7, bf16[2048,256]{1,0:T(8,128)(2,1)} %copy-done.8), custom_call_target="tpu_custom_call" | custom-call | flops 2147483648 | bytes 4194304 | tf_op jit(solution)/shard_map/pallas_call | solution.py:153
  63.4 1.3 %convert_element_type.119 = bf16[1024,256]{1,0:T(8,128)(2,1)S(1)} convert(f32[1024,256]{1,0:T(8,128)} %get-tuple-element.28) | non-fusion elementwise | flops 262144 | bytes 1572864 | tf_op jit(solution)/shard_map/convert_element_type | solution.py:360
  64.8 0.1 subtract_convert_fusion
  64.9 0.3 pad_maximum_fusion
  65.2 0.8 constant_dynamic-slice_fusion.3
  66.0 1.6 %collective-permute-start.6 = (bf16[256,280]{1,0:T(8,128)(2,1)S(1)}, bf16[256,280]{1,0:T(8,128)(2,1)S(1)}, u32[]{:S(2)}, u32[]{:S(2)}) collective-permute-start(bf16[256,280]{1,0:T(8,128)(2,1)S(1)} %get-tuple-element.37), channel_id=1, source_target_pairs={{0,12},{4,0},{8,4},{12,8},{1,13},{5,1},{9,5},{13,9},{2,14},{6,2},{... | collective-permute-start | bytes 430088 | tf_op jit(solution)/shard_map/ppermute | solution.py:272
  67.5 1.4 %collective-permute-start.5 = (bf16[256,280]{1,0:T(8,128)(2,1)S(1)}, bf16[256,280]{1,0:T(8,128)(2,1)S(1)}, u32[]{:S(2)}, u32[]{:S(2)}) collective-permute-start(bf16[256,280]{1,0:T(8,128)(2,1)S(1)} %get-tuple-element.38), channel_id=1, source_target_pairs={{0,8},{4,12},{8,0},{12,4},{1,9},{5,13},{9,1},{13,5},{2,10},{6,14},... | collective-permute-start | bytes 430088 | tf_op jit(solution)/shard_map/ppermute | solution.py:272
  69.0 1.6 %collective-permute-start.4 = (bf16[256,280]{1,0:T(8,128)(2,1)S(1)}, bf16[256,280]{1,0:T(8,128)(2,1)S(1)}, u32[]{:S(2)}, u32[]{:S(2)}) collective-permute-start(bf16[256,280]{1,0:T(8,128)(2,1)S(1)} %get-tuple-element.39), channel_id=1, source_target_pairs={{0,4},{4,8},{8,12},{12,0},{1,5},{5,9},{9,13},{13,1},{2,6},{6,10},{... | collective-permute-start | bytes 430088 | tf_op jit(solution)/shard_map/ppermute | solution.py:272
  70.6 0.8 constant_dynamic-slice_fusion.2
  71.3 1.9 %collective-permute-done.6.refs_3_ = bf16[256,280]{1,0:T(8,128)(2,1)S(1)} collective-permute-done((bf16[256,280]{1,0:T(8,128)(2,1)S(1)}, bf16[256,280]{1,0:T(8,128)(2,1)S(1)}, u32[]{:S(2)}, u32[]{:S(2)}) %collective-permute-start.6) | collective-permute-done | bytes 143392 | tf_op jit(solution)/shard_map/ppermute | solution.py:272
  73.3 13.6 %collective-permute-done.5.refs_2_ = bf16[256,280]{1,0:T(8,128)(2,1)S(1)} collective-permute-done((bf16[256,280]{1,0:T(8,128)(2,1)S(1)}, bf16[256,280]{1,0:T(8,128)(2,1)S(1)}, u32[]{:S(2)}, u32[]{:S(2)}) %collective-permute-start.5) | collective-permute-done | bytes 143392 | tf_op jit(solution)/shard_map/ppermute | solution.py:272
  86.9 0.7 copy-done.5
  87.7 3.0 %shard_map.115 = bf16[256,256]{1,0:T(8,128)(2,1)} custom-call(bf16[256,280]{1,0:T(8,128)(2,1)} %get-tuple-element.40.refs_0_, bf16[256,280]{1,0:T(8,128)(2,1)} %copy-done.6, bf16[256,280]{1,0:T(8,128)(2,1)} %copy-done.5, bf16[256,280]{1,0:T(8,128)(2,1)} %copy-done.4), custom_call_target="tpu_custom_call" | custom-call | tf_op jit(solution)/shard_map/pallas_call | solution.py:309
  90.7 1.3 %convolution_convert_fusion.3 = bf16[256,1024]{1,0:T(8,128)(2,1)S(1)} fusion(bf16[256,256]{1,0:T(8,128)(2,1)} %shard_map.115, bf16[256,256]{1,0:T(8,128)(2,1)} %get-tuple-element.45, bf16[256,256]{1,0:T(8,128)(2,1)} %get-tuple-element.46, bf16[256,256]{1,0:T(8,128)(2,1)S(1)} %get-tuple-element.44, bf16[256,256]{1,0:T(8,128)(2,1)S(1)} %get-tuple-element.43), kind=kOutput, calls=%fused_computation.7 | convolution fusion | flops 136577024 | bytes 1179648 | tf_op jit(solution)/shard_map/dot_general | solution.py:371
  92.1 1.8 %fusion.2 = bf16[2048,256]{1,0:T(8,128)(2,1)S(1)} fusion(bf16[2,2048,256]{2,1,0:T(8,128)(2,1)} %collective-permute-done.2, bf16[4,2048,256]{2,1,0:T(8,128)(2,1)} %shard_map.113), kind=kLoop, calls=%fused_computation.10 | loop fusion | flops 2097152 | bytes 3145728 | tf_op jit(solution)/shard_map/convert_element_type | solution.py:231
  93.9 1.6 %collective-permute-start.3 = (bf16[2048,256]{1,0:T(8,128)(2,1)S(1)}, bf16[2048,256]{1,0:T(8,128)(2,1)S(1)}, u32[]{:S(2)}, u32[]{:S(2)}) collective-permute-start(bf16[2048,256]{1,0:T(8,128)(2,1)S(1)} %fusion.2), channel_id=1, source_target_pairs={{0,2},{1,3},{2,0},{3,1},{4,6},{5,7},{6,4},{7,5},{8,10},{9,11},{10,... | collective-permute-start | bytes 3145736 | tf_op jit(solution)/shard_map/ppermute | solution.py:244
  95.6 1.5 %collective-permute-done.7 = bf16[2,256,256]{2,1,0:T(8,128)(2,1)S(1)} collective-permute-done((bf16[2,256,256]{2,1,0:T(8,128)(2,1)S(1)}, bf16[2,256,256]{2,1,0:T(8,128)(2,1)S(1)}, u32[]{:S(2)}, u32[]{:S(2)}) %collective-permute-start.7) | collective-permute-done | bytes 262176 | tf_op jit(solution)/shard_map/ppermute | solution.py:229
  97.2 0.6 collective-permute-start.8
  97.8 23.8 %collective-permute-done.8 = bf16[256,256]{1,0:T(8,128)(2,1)S(1)} collective-permute-done((bf16[256,256]{1,0:T(8,128)(2,1)S(1)}, bf16[256,256]{1,0:T(8,128)(2,1)S(1)}, u32[]{:S(2)}, u32[]{:S(2)}) %collective-permute-start.8) | collective-permute-done | bytes 131104 | tf_op jit(solution)/shard_map/ppermute | solution.py:244
  121.6 0.7 add_convert_fusion.2
  122.3 3.0 %fusion = bf16[2048,256]{1,0:T(8,128)(2,1)} fusion(bf16[2048,256]{1,0:T(8,128)(2,1)S(1)} %collective-permute-done.3, bf16[2,2048,256]{2,1,0:T(8,128)(2,1)} %collective-permute-done.2, bf16[4,2048,256]{2,1,0:T(8,128)(2,1)} %shard_map.113), kind=kLoop, calls=%fused_computation.4 | loop fusion | flops 4194304 | bytes 4194304 | tf_op jit(solution)/shard_map/convert_element_type | solution.py:245
  (43 shorter events, 0.6 us)
Async XLA Ops:
  0.6 44.3 %copy-start = (bf16[1024,1024]{1,0:T(8,128)(2,1)S(1)}, bf16[1024,1024]{1,0:T(8,128)(2,1)}, u32[]{:S(2)}) copy-start(bf16[1024,1024]{1,0:T(8,128)(2,1)} %param.15) | copy-start | bytes 6291460
  0.6 3.8 %copy-start.9 = (bf16[2048,1024]{1,0:T(8,128)(2,1)S(1)}, bf16[2048,1024]{1,0:T(8,128)(2,1)}, u32[]{:S(2)}) copy-start(bf16[2048,1024]{1,0:T(8,128)(2,1)} %param.14) | copy-start | bytes 12582916
  0.7 3.9 %copy-start.10 = (bf16[1024,256]{1,0:T(8,128)(2,1)S(1)}, bf16[1024,256]{1,0:T(8,128)(2,1)}, u32[]{:S(2)}) copy-start(bf16[1024,256]{1,0:T(8,128)(2,1)} %param.19) | copy-start | bytes 1572868
  4.5 1.3 %copy-start.7 = (bf16[2048,256]{1,0:T(8,128)(2,1)}, bf16[2048,256]{1,0:T(8,128)(2,1)S(1)}, u32[]{:S(2)}) copy-start(bf16[2048,256]{1,0:T(8,128)(2,1)S(1)} %convolution_convert_fusion.1.k_ref) | copy-start | bytes 3145732
  5.8 9.1 %copy-start.8 = (bf16[2048,256]{1,0:T(8,128)(2,1)}, bf16[2048,256]{1,0:T(8,128)(2,1)S(1)}, u32[]{:S(2)}) copy-start(bf16[2048,256]{1,0:T(8,128)(2,1)S(1)} %convolution_convert_fusion.v_ref) | copy-start | bytes 3145732
  5.8 6.8 %copy-start.11 = (bf16[1024,256]{1,0:T(8,128)(2,1)S(1)}, bf16[1024,256]{1,0:T(8,128)(2,1)}, u32[]{:S(2)}) copy-start(bf16[1024,256]{1,0:T(8,128)(2,1)} %param.17) | copy-start | bytes 1572868
  5.9 10.7 %collective-permute-start = (bf16[256,512]{1,0:T(8,128)(2,1)S(1)}, bf16[256,512]{1,0:T(8,128)(2,1)S(1)}, u32[]{:S(2)}, u32[]{:S(2)}) collective-permute-start(bf16[256,512]{1,0:T(8,128)(2,1)S(1)} %pad_maximum_fusion.2), channel_id=1, source_target_pairs={{0,4},{4,8},{8,12},{1,5},{5,9},{9,13},{2,6},{6,10},{10,14},{3,7},{... | collective-permute-start | bytes 786440 | tf_op jit(solution)/shard_map/ppermute | solution.py:21
  11.0 4.6 %copy-start.2 = (bf16[256,1024]{1,0:T(8,128)(2,1)S(1)}, bf16[256,1024]{1,0:T(8,128)(2,1)}, u32[]{:S(2)}) copy-start(bf16[256,1024]{1,0:T(8,128)(2,1)} %param.20) | copy-start | bytes 1572868
  11.0 9.9 %collective-permute-start.1 = (bf16[256,512]{1,0:T(8,128)(2,1)S(1)}, bf16[256,512]{1,0:T(8,128)(2,1)}, u32[]{:S(2)}, u32[]{:S(2)}) collective-permute-start(bf16[256,512]{1,0:T(8,128)(2,1)S(1)} %pad_maximum_fusion.3), channel_id=1, source_target_pairs={{4,0},{8,4},{12,8},{5,1},{9,5},{13,9},{6,2},{10,6},{14,10},{7,3},{... | collective-permute-start | bytes 786440 | tf_op jit(solution)/shard_map/ppermute | solution.py:21
  15.6 5.3 %copy-start.14 = (s32[3]{0:T(128)}, s32[3]{0:T(128)S(1)}, u32[]{:S(2)}) copy-start(s32[3]{0:T(128)S(1)} %constant_dynamic-update-slice_fusion.scal_ref) | copy-start | bytes 40
  16.6 4.3 %copy-start.13 = (bf16[256,512]{1,0:T(8,128)(2,1)}, bf16[256,512]{1,0:T(8,128)(2,1)S(1)}, u32[]{:S(2)}) copy-start(bf16[256,512]{1,0:T(8,128)(2,1)S(1)} %collective-permute-done.low_ref) | copy-start | bytes 786436
  41.7 3.2 %copy-start.12 = (bf16[1024,256]{1,0:T(8,128)(2,1)S(1)}, bf16[1024,256]{1,0:T(8,128)(2,1)}, u32[]{:S(2)}) copy-start(bf16[1024,256]{1,0:T(8,128)(2,1)} %param.21) | copy-start | bytes 1572868
  44.9 47.2 %collective-permute-start.2 = (bf16[2,2048,256]{2,1,0:T(8,128)(2,1)}, bf16[2,2048,256]{2,1,0:T(8,128)(2,1)}, u32[]{:S(2)}, u32[]{:S(2)}) collective-permute-start(bf16[2,2048,256]{2,1,0:T(8,128)(2,1)} %slice.88), channel_id=1, source_target_pairs={{0,1},{1,0},{2,3},{3,2},{4,5},{5,4},{6,7},{7,6},{8,9},{9,8},{10,11... | collective-permute-start | bytes 6291464 | tf_op jit(solution)/shard_map/ppermute | solution.py:229
  63.4 1.4 %copy-start.1 = (f32[1024,128]{1,0:T(8,128)S(1)}, f32[1024,128]{1,0:T(8,128)}, u32[]{:S(2)}) copy-start(f32[1024,128]{1,0:T(8,128)} %get-tuple-element.29) | copy-start | bytes 1572868
  64.9 5.7 %copy-start.3 = (bf16[256,1024]{1,0:T(8,128)(2,1)S(1)}, bf16[256,1024]{1,0:T(8,128)(2,1)}, u32[]{:S(2)}) copy-start(bf16[256,1024]{1,0:T(8,128)(2,1)} %param.22) | copy-start | bytes 1572868
  66.0 7.3 %collective-permute-start.6 = (bf16[256,280]{1,0:T(8,128)(2,1)S(1)}, bf16[256,280]{1,0:T(8,128)(2,1)S(1)}, u32[]{:S(2)}, u32[]{:S(2)}) collective-permute-start(bf16[256,280]{1,0:T(8,128)(2,1)S(1)} %get-tuple-element.37), channel_id=1, source_target_pairs={{0,12},{4,0},{8,4},{12,8},{1,13},{5,1},{9,5},{13,9},{2,14},{6,2},{... | collective-permute-start | bytes 430088 | tf_op jit(solution)/shard_map/ppermute | solution.py:272
  67.5 19.4 %collective-permute-start.5 = (bf16[256,280]{1,0:T(8,128)(2,1)S(1)}, bf16[256,280]{1,0:T(8,128)(2,1)S(1)}, u32[]{:S(2)}, u32[]{:S(2)}) collective-permute-start(bf16[256,280]{1,0:T(8,128)(2,1)S(1)} %get-tuple-element.38), channel_id=1, source_target_pairs={{0,8},{4,12},{8,0},{12,4},{1,9},{5,13},{9,1},{13,5},{2,10},{6,14},... | collective-permute-start | bytes 430088 | tf_op jit(solution)/shard_map/ppermute | solution.py:272
  69.0 17.9 %collective-permute-start.4 = (bf16[256,280]{1,0:T(8,128)(2,1)S(1)}, bf16[256,280]{1,0:T(8,128)(2,1)S(1)}, u32[]{:S(2)}, u32[]{:S(2)}) collective-permute-start(bf16[256,280]{1,0:T(8,128)(2,1)S(1)} %get-tuple-element.39), channel_id=1, source_target_pairs={{0,4},{4,8},{8,12},{12,0},{1,5},{5,9},{9,13},{13,1},{2,6},{6,10},{... | collective-permute-start | bytes 430088 | tf_op jit(solution)/shard_map/ppermute | solution.py:272
  73.3 13.6 %copy-start.4 = (bf16[256,280]{1,0:T(8,128)(2,1)}, bf16[256,280]{1,0:T(8,128)(2,1)S(1)}, u32[]{:S(2)}) copy-start(bf16[256,280]{1,0:T(8,128)(2,1)S(1)} %collective-permute-done.6.refs_3_) | copy-start | bytes 430084
  86.9 0.7 copy-start.5
  86.9 0.8 copy-start.6
  93.9 28.4 %collective-permute-start.3 = (bf16[2048,256]{1,0:T(8,128)(2,1)S(1)}, bf16[2048,256]{1,0:T(8,128)(2,1)S(1)}, u32[]{:S(2)}, u32[]{:S(2)}) collective-permute-start(bf16[2048,256]{1,0:T(8,128)(2,1)S(1)} %fusion.2), channel_id=1, source_target_pairs={{0,2},{1,3},{2,0},{3,1},{4,6},{5,7},{6,4},{7,5},{8,10},{9,11},{10,... | collective-permute-start | bytes 3145736 | tf_op jit(solution)/shard_map/ppermute | solution.py:244
  95.5 1.6 %collective-permute-start.7 = (bf16[2,256,256]{2,1,0:T(8,128)(2,1)S(1)}, bf16[2,256,256]{2,1,0:T(8,128)(2,1)S(1)}, u32[]{:S(2)}, u32[]{:S(2)}) collective-permute-start(bf16[2,256,256]{2,1,0:T(8,128)(2,1)S(1)} %pad_maximum_fusion.4), channel_id=1, source_target_pairs={{0,1},{1,0},{2,3},{3,2},{4,5},{5,4},{6,7},{7,6},{8,9},{9,8},{10,11... | collective-permute-start | bytes 786440 | tf_op jit(solution)/shard_map/ppermute | solution.py:229
  97.2 24.4 %collective-permute-start.8 = (bf16[256,256]{1,0:T(8,128)(2,1)S(1)}, bf16[256,256]{1,0:T(8,128)(2,1)S(1)}, u32[]{:S(2)}, u32[]{:S(2)}) collective-permute-start(bf16[256,256]{1,0:T(8,128)(2,1)S(1)} %fusion.11), channel_id=1, source_target_pairs={{0,2},{1,3},{2,0},{3,1},{4,6},{5,7},{6,4},{7,5},{8,10},{9,11},{10,... | collective-permute-start | bytes 393224 | tf_op jit(solution)/shard_map/ppermute | solution.py:244

commit v21 on v18

--- a/solution.py
+++ b/solution.py
@@ -26,9 +26,10 @@
 
 
 def window_kernel(
-    scal_ref, q_ref, k_ref, v_ref, low_ref, high_ref, w_ref, o_ref, kbuf, vbuf, att_ref, *,
-    heads, scale
+    scal_ref, q_ref, k_ref, v_ref, low_ref, high_ref, w_ref, *rest, heads, scale, groups
 ):
+    out_refs = rest[:groups]
+    kbuf, vbuf, att_ref = rest[groups:]
     tq = q_ref.shape[0]
     frame_count, width = k_ref.shape
     span = tq + 2 * HALF
@@ -68,9 +69,12 @@
         divisor = jnp.where(query_valid, denom, 1.0)
         att_ref[:, cols] = jnp.where(query_valid, blended / divisor, 0.0).astype(jnp.bfloat16)
     result = jnp.dot(att_ref[...], w_ref[...], preferred_element_type=jnp.float32)
-    block_width = o_ref.shape[2]
-    for b in range(o_ref.shape[0]):
-        o_ref[b] = result[:, b * block_width : (b + 1) * block_width].astype(jnp.bfloat16)
+    per_group = out_refs[0].shape[0]
+    block_width = out_refs[0].shape[2]
+    for b in range(groups * per_group):
+        out_refs[b // per_group][b % per_group] = result[
+            :, b * block_width : (b + 1) * block_width
+        ].astype(jnp.bfloat16)
 
 
 def window_attention(
@@ -83,7 +87,10 @@
     block_base = row_base // tq
     span = tq + 2 * HALF
     scal = jnp.array([0, 0, row_base], jnp.int32).at[0].set(first_frame).at[1].set(length)
-    kernel = functools.partial(window_kernel, heads=width // HD, scale=HD ** (-0.5))
+    groups = 2 if blocks % 2 == 0 else 1
+    kernel = functools.partial(
+        window_kernel, heads=width // HD, scale=HD ** (-0.5), groups=groups
+    )
     cost = pl.CostEstimate(
         flops=4 * rows * span * width + 2 * rows * width * out_width,
         transcendentals=rows * span * (width // HD),
@@ -93,7 +100,9 @@
     return pl.pallas_call(
         kernel,
         cost_estimate=cost,
-        out_shape=jax.ShapeDtypeStruct((blocks, rows, block_width), jnp.bfloat16),
+        out_shape=[
+            jax.ShapeDtypeStruct((blocks // groups, rows, block_width), jnp.bfloat16)
+        ] * groups,
         grid_spec=pltpu.PrefetchScalarGridSpec(
             num_scalar_prefetch=1,
             grid=(rows // tq,),
@@ -105,7 +114,9 @@
                 pl.BlockSpec(high.shape, full),
                 pl.BlockSpec(w_out.shape, full),
             ],
-            out_specs=pl.BlockSpec((blocks, tq, block_width), lambda i, s: (0, i, 0)),
+            out_specs=[
+                pl.BlockSpec((blocks // groups, tq, block_width), lambda i, s: (0, i, 0))
+            ] * groups,
             scratch_shapes=[
                 pltpu.VMEM((frame_count + 2 * HALF, width), jnp.bfloat16),
                 pltpu.VMEM((frame_count + 2 * HALF, width), jnp.bfloat16),
@@ -226,9 +237,10 @@
     count = lax.axis_size(axis)
     chips = count // 2
     swap = [(i, i ^ 1) for i in range(count)]
-    received = lax.ppermute(blocks[:chips], axis, swap)
+    theirs, mine = blocks
+    received = lax.ppermute(theirs, axis, swap)
     return [
-        (blocks[chips + d].astype(jnp.float32) + received[d].astype(jnp.float32)).astype(
+        (mine[d].astype(jnp.float32) + received[d].astype(jnp.float32)).astype(
             jnp.bfloat16
         )
         for d in range(chips)
@@ -352,7 +364,7 @@
         frame_parts.append(cross_chip_sum(first_sums, "head"))
         rest_sums = [chip_pair_sums(blocks, "head") for blocks in rest]
     else:
-        frame_parts = [plain_block_sum(blocks, "head") for blocks in parts]
+        frame_parts = [plain_block_sum(blocks[0], "head") for blocks in parts]
     peaks, totals, local_accum = latent_attention(latent_query, keyed, valued, valid_count)
     payload = jnp.concatenate(
         [local_accum.astype(jnp.bfloat16)] + split_three(jnp.concatenate([peaks, totals], axis=1)),
@@ -373,7 +385,8 @@
         latent_blocks = jnp.stack(
             [latent_terms[:, j * block_width : (j + 1) * block_width] for j in range(head_devices)]
         )
-        latents_out = cross_chip_sum(chip_pair_sums(latent_blocks, "head"), "head")
+        halves = (latent_blocks[: head_devices // 2], latent_blocks[head_devices // 2 :])
+        latents_out = cross_chip_sum(chip_pair_sums(halves, "head"), "head")
     else:
         latent_terms = jnp.dot(summary, w_latent_out, preferred_element_type=jnp.float32)
         latents_out = column_sum(latent_terms.astype(jnp.bfloat16), "head")

time: 108 us -> 105 us (0.972)
  local copies, waits for them, and re-layouts: 6.06 us -> 2.87 us
    slice x1 -> x0, local copies, waits for them, and re-layouts: 3.17 us -> none  [chip_pair_sums(): received = lax.ppermute(blocks[:chips], axis, swap)]
  transfers between devices with their start and end apart: 9 -> 9, of which waited for: 6 -> 6; matrix products, arithmetic and copies ran while one was open for 7% -> 8% of each run, Pallas kernels for 3% -> 3%
where the time goes in v21:
time: 105 us
  Pallas kernels  40.8 us (39%)
  waiting for transfers between devices  22.7 us (22%)
  starting transfers between devices  17.6 us (17%)
  matrix products  10.3 us (10%)
  other arithmetic  8.98 us (9%)
  local copies, waits for them, and re-layouts  2.87 us (3%)
  between operations  1.53 us (1%)
    pallas_call x1, Pallas kernels, window_attention(): pl.pallas_call(kernel, cost_estimate=cost, out_shape=[jax.ShapeDtypeStruc...  20.8 us
    pallas_call x1, Pallas kernels, latent_attention(): pl.pallas_call(kernel, cost_estimate=cost, out_shape=(jax.ShapeDtypeStruc...  17 us
    ppermute x3, waiting for transfers between devices, exchange_rows(): parts.append(lax.ppermute(block, axis, pairs))  9.5 us
    dot_general x4, matrix products, project(): jnp.dot(source, weight, preferred_element_type=jnp.float32)  8.79 us
    ppermute x2, waiting for transfers between devices, cross_chip_sum(): total = total + lax.ppermute(chip_sums[d], axis, pairs).astype(jnp.float32)  7.86 us
    ppermute x3, starting transfers between devices, exchange_rows(): parts.append(lax.ppermute(block, axis, pairs))  6.69 us
    ppermute x1, starting transfers between devices, halos(): lax.ppermute(tail, axis, forward)  6.4 us
    ppermute x2, waiting for transfers between devices, chip_pair_sums(): received = lax.ppermute(theirs, axis, swap)  4.44 us
  transfers between devices with their start and end apart: 9, of which 6 were waited for; matrix products, arithmetic and copies ran while one was open for 8% of the time, Pallas kernels for 3%

profile of v21, /device:TPU:0, one launch (start us, length us, event | category | flops | bytes accessed | tf_op | source)
XLA Modules:
  0.0 104.8 jit_solution(8570659046449123565)
XLA Ops:
  0.7 3.7 %convolution_convert_fusion.v_ref = bf16[2048,256]{1,0:T(8,128)(2,1)S(1)} fusion(bf16[2048,1024]{1,0:T(8,128)(2,1)} %param.14, bf16[1024,256]{1,0:T(8,128)(2,1)} %param.19), kind=kOutput, calls=%fused_computation | convolution fusion | flops 1074266112 | bytes 5767168 | tf_op jit(solution)/shard_map/dot_general | solution.py:25
  4.4 0.1 copy-done.11
  4.5 1.3 %convolution_convert_fusion.1.k_ref = bf16[2048,256]{1,0:T(8,128)(2,1)S(1)} fusion(bf16[2048,1024]{1,0:T(8,128)(2,1)S(1)} %copy-done.10, bf16[1024,256]{1,0:T(8,128)(2,1)S(1)} %copy-done.11), kind=kOutput, calls=%fused_computation.1 | convolution fusion | flops 1074266112 | bytes 5767168 | tf_op jit(solution)/shard_map/dot_general | solution.py:25
  5.9 1.4 %collective-permute-start.1 = (bf16[256,512]{1,0:T(8,128)(2,1)S(1)}, bf16[256,512]{1,0:T(8,128)(2,1)S(1)}, u32[]{:S(2)}, u32[]{:S(2)}) collective-permute-start(bf16[256,512]{1,0:T(8,128)(2,1)S(1)} %pad_maximum_fusion.3), channel_id=1, source_target_pairs={{4,0},{8,4},{12,8},{5,1},{9,5},{13,9},{6,2},{10,6},{14,10},{7,3},{... | collective-permute-start | bytes 786440 | tf_op jit(solution)/shard_map/ppermute | solution.py:21
  7.4 6.4 %collective-permute-start = (bf16[256,512]{1,0:T(8,128)(2,1)S(1)}, bf16[256,512]{1,0:T(8,128)(2,1)}, u32[]{:S(2)}, u32[]{:S(2)}) collective-permute-start(bf16[256,512]{1,0:T(8,128)(2,1)S(1)} %pad_maximum_fusion.2), channel_id=1, source_target_pairs={{0,4},{4,8},{8,12},{1,5},{5,9},{9,13},{2,6},{6,10},{10,14},{3,7},{... | collective-permute-start | bytes 786440 | tf_op jit(solution)/shard_map/ppermute | solution.py:21
  13.8 2.2 %convolution_convert_fusion.2.q_ref = bf16[2048,256]{1,0:T(8,128)(2,1)} fusion(bf16[2048,1024]{1,0:T(8,128)(2,1)S(1)} %copy-done.10, bf16[1024,256]{1,0:T(8,128)(2,1)S(1)} %copy-done.12), kind=kOutput, calls=%fused_computation.2 | convolution fusion | flops 1074266112 | bytes 5767168 | tf_op jit(solution)/shard_map/dot_general | solution.py:25
  16.8 0.9 pad_maximum_fusion.1.w_ref
  17.7 0.9 collective-permute-done.low_ref
  18.6 20.8 %shard_map.113 = (bf16[2,2048,256]{2,1,0:T(8,128)(2,1)}, bf16[2,2048,256]{2,1,0:T(8,128)(2,1)}) custom-call(s32[3]{0:T(128)} %copy-done.15, bf16[2048,256]{1,0:T(8,128)(2,1)} %convolution_convert_fusion.2.q_ref, bf16[2048,256]{1,0:T(8,128)(2,1)} %copy-done.9, bf16[2048,256]{1,0:T(8,128)(2,1)} %copy-done.8, bf16[256,512]{1,0:T(8,128)(2,1)} %collective-permute-done.low_ref, ...), custom_call_target="tpu_custom_call" | custom-call | flops 3221225472 | bytes 8388608 | tf_op jit(solution)/shard_map/pallas_call | solution.py:100
  39.4 1.6 %convolution_convert_fusion.4.q_ref = bf16[1024,256]{1,0:T(8,128)(2,1)} fusion(bf16[1024,1024]{1,0:T(8,128)(2,1)S(1)} %copy-done, bf16[1024,256]{1,0:T(8,128)(2,1)S(1)} %copy-done.13), kind=kOutput, calls=%fused_computation.7 | convolution fusion | flops 537133056 | bytes 3145728 | tf_op jit(solution)/shard_map/dot_general | solution.py:25
  41.0 2.9 %collective-permute-done.2 = bf16[2,2048,256]{2,1,0:T(8,128)(2,1)} collective-permute-done((bf16[2,2048,256]{2,1,0:T(8,128)(2,1)}, bf16[2,2048,256]{2,1,0:T(8,128)(2,1)}, u32[]{:S(2)}, u32[]{:S(2)}) %collective-permute-start.2) | collective-permute-done | bytes 2097184 | tf_op jit(solution)/shard_map/ppermute | solution.py:241
  43.9 3.1 %fusion.1 = (bf16[2048,256]{1,0:T(8,128)(2,1)}, bf16[2048,256]{1,0:T(8,128)(2,1)S(1)}) fusion(bf16[2,2048,256]{2,1,0:T(8,128)(2,1)} %collective-permute-done.2, bf16[2,2048,256]{2,1,0:T(8,128)(2,1)S(1)} %copy-done.1), kind=kLoop, calls=%fused_computation.9 | loop fusion | flops 4194304 | bytes 6291456 | tf_op jit(solution)/shard_map/convert_element_type | solution.py:243
  47.0 17.0 %shard_map.114 = (f32[1024,256]{1,0:T(8,128)}, f32[1024,128]{1,0:T(8,128)}) custom-call(s32[1]{0:T(128)} %bitcast.4.scal_ref, bf16[1024,256]{1,0:T(8,128)(2,1)} %convolution_convert_fusion.4.q_ref, bf16[2048,256]{1,0:T(8,128)(2,1)} %copy-done.9, bf16[2048,256]{1,0:T(8,128)(2,1)} %copy-done.8), custom_call_target="tpu_custom_call" | custom-call | flops 2147483648 | bytes 4194304 | tf_op jit(solution)/shard_map/pallas_call | solution.py:164
  64.0 1.4 %subtract_convert_fusion = (bf16[1024,8]{1,0:T(8,128)(2,1)S(1)}, bf16[1024,8]{1,0:T(8,128)(2,1)S(1)}, bf16[1024,8]{1,0:T(8,128)(2,1)S(1)}) fusion(f32[1024,128]{1,0:T(8,128)} %get-tuple-element.41), kind=kLoop, calls=%fused_computation.19 | loop fusion | flops 49152 | bytes 98304 | tf_op jit(solution)/shard_map/convert_element_type | solution.py:273
  65.4 0.1 copy-done.2
  65.6 0.3 pad_maximum_fusion
  65.9 0.8 constant_dynamic-slice_fusion.3
  66.7 2.6 %collective-permute-start.4 = (bf16[256,280]{1,0:T(8,128)(2,1)S(1)}, bf16[256,280]{1,0:T(8,128)(2,1)S(1)}, u32[]{:S(2)}, u32[]{:S(2)}) collective-permute-start(bf16[256,280]{1,0:T(8,128)(2,1)S(1)} %get-tuple-element.53), channel_id=1, source_target_pairs={{0,4},{4,8},{8,12},{12,0},{1,5},{5,9},{9,13},{13,1},{2,6},{6,10},{... | collective-permute-start | bytes 430088 | tf_op jit(solution)/shard_map/ppermute | solution.py:284
  69.3 2.8 %collective-permute-start.5 = (bf16[256,280]{1,0:T(8,128)(2,1)S(1)}, bf16[256,280]{1,0:T(8,128)(2,1)S(1)}, u32[]{:S(2)}, u32[]{:S(2)}) collective-permute-start(bf16[256,280]{1,0:T(8,128)(2,1)S(1)} %get-tuple-element.52), channel_id=1, source_target_pairs={{0,8},{4,12},{8,0},{12,4},{1,9},{5,13},{9,1},{13,5},{2,10},{6,14},... | collective-permute-start | bytes 430088 | tf_op jit(solution)/shard_map/ppermute | solution.py:284
  72.0 1.3 %collective-permute-start.6 = (bf16[256,280]{1,0:T(8,128)(2,1)S(1)}, bf16[256,280]{1,0:T(8,128)(2,1)S(1)}, u32[]{:S(2)}, u32[]{:S(2)}) collective-permute-start(bf16[256,280]{1,0:T(8,128)(2,1)S(1)} %get-tuple-element.51), channel_id=1, source_target_pairs={{0,12},{4,0},{8,4},{12,8},{1,13},{5,1},{9,5},{13,9},{2,14},{6,2},{... | collective-permute-start | bytes 430088 | tf_op jit(solution)/shard_map/ppermute | solution.py:284
  73.4 0.8 constant_dynamic-slice_fusion.2
  74.2 1.5 %collective-permute-start.3 = (bf16[2048,256]{1,0:T(8,128)(2,1)}, bf16[2048,256]{1,0:T(8,128)(2,1)}, u32[]{:S(2)}, u32[]{:S(2)}) collective-permute-start(bf16[2048,256]{1,0:T(8,128)(2,1)} %get-tuple-element.37), channel_id=1, source_target_pairs={{0,2},{1,3},{2,0},{3,1},{4,6},{5,7},{6,4},{7,5},{8,10},{9,11},{10,... | collective-permute-start | bytes 3145736 | tf_op jit(solution)/shard_map/ppermute | solution.py:256
  75.7 1.6 %collective-permute-done.4.refs_1_ = bf16[256,280]{1,0:T(8,128)(2,1)S(1)} collective-permute-done((bf16[256,280]{1,0:T(8,128)(2,1)S(1)}, bf16[256,280]{1,0:T(8,128)(2,1)S(1)}, u32[]{:S(2)}, u32[]{:S(2)}) %collective-permute-start.4) | collective-permute-done | bytes 143392 | tf_op jit(solution)/shard_map/ppermute | solution.py:284
  77.3 7.9 %collective-permute-done.5.refs_2_ = bf16[256,280]{1,0:T(8,128)(2,1)S(1)} collective-permute-done((bf16[256,280]{1,0:T(8,128)(2,1)S(1)}, bf16[256,280]{1,0:T(8,128)(2,1)S(1)}, u32[]{:S(2)}, u32[]{:S(2)}) %collective-permute-start.5) | collective-permute-done | bytes 143392 | tf_op jit(solution)/shard_map/ppermute | solution.py:284
  85.2 0.7 copy-done.7
  86.0 3.0 %shard_map.115 = bf16[256,256]{1,0:T(8,128)(2,1)} custom-call(bf16[256,280]{1,0:T(8,128)(2,1)} %get-tuple-element.54.refs_0_, bf16[256,280]{1,0:T(8,128)(2,1)} %copy-done.5, bf16[256,280]{1,0:T(8,128)(2,1)} %copy-done.6, bf16[256,280]{1,0:T(8,128)(2,1)} %copy-done.7), custom_call_target="tpu_custom_call" | custom-call | tf_op jit(solution)/shard_map/pallas_call | solution.py:321
  89.0 1.5 %convolution_convert_fusion.3 = bf16[256,1024]{1,0:T(8,128)(2,1)S(1)} fusion(bf16[256,256]{1,0:T(8,128)(2,1)} %shard_map.115, bf16[256,256]{1,0:T(8,128)(2,1)} %get-tuple-element.59, bf16[256,256]{1,0:T(8,128)(2,1)} %get-tuple-element.60, bf16[256,256]{1,0:T(8,128)(2,1)} %get-tuple-element.58, bf16[256,256]{1,0:T(8,128)(2,1)} %get-tuple-element.57), kind=kOutput, calls=%fused_computation.6 | convolution fusion | flops 136577024 | bytes 1179648 | tf_op jit(solution)/shard_map/dot_general | solution.py:381
  90.6 1.5 %collective-permute-done.7 = bf16[2,256,256]{2,1,0:T(8,128)(2,1)S(1)} collective-permute-done((bf16[2,256,256]{2,1,0:T(8,128)(2,1)S(1)}, bf16[2,256,256]{2,1,0:T(8,128)(2,1)S(1)}, u32[]{:S(2)}, u32[]{:S(2)}) %collective-permute-start.7) | collective-permute-done | bytes 262176 | tf_op jit(solution)/shard_map/ppermute | solution.py:241
  92.2 1.6 %collective-permute-start.8 = (bf16[256,256]{1,0:T(8,128)(2,1)S(1)}, bf16[256,256]{1,0:T(8,128)(2,1)S(1)}, u32[]{:S(2)}, u32[]{:S(2)}) collective-permute-start(bf16[256,256]{1,0:T(8,128)(2,1)S(1)} %fusion.10), channel_id=1, source_target_pairs={{0,2},{1,3},{2,0},{3,1},{4,6},{5,7},{6,4},{7,5},{8,10},{9,11},{10,... | collective-permute-start | bytes 393224 | tf_op jit(solution)/shard_map/ppermute | solution.py:256
  93.7 7.9 %collective-permute-done.8 = bf16[256,256]{1,0:T(8,128)(2,1)S(1)} collective-permute-done((bf16[256,256]{1,0:T(8,128)(2,1)S(1)}, bf16[256,256]{1,0:T(8,128)(2,1)S(1)}, u32[]{:S(2)}, u32[]{:S(2)}) %collective-permute-start.8) | collective-permute-done | bytes 131104 | tf_op jit(solution)/shard_map/ppermute | solution.py:256
  101.6 0.7 add_convert_fusion.3
  102.3 2.5 %add_convert_fusion = bf16[2048,256]{1,0:T(8,128)(2,1)} fusion(bf16[2048,256]{1,0:T(8,128)(2,1)} %collective-permute-done.3, bf16[2048,256]{1,0:T(8,128)(2,1)S(1)} %get-tuple-element.36), kind=kLoop, calls=%fused_computation.3 | loop fusion | flops 2097152 | bytes 3145728 | tf_op jit(solution)/shard_map/convert_element_type | solution.py:257
  (44 shorter events, 0.5 us)
Async XLA Ops:
  0.6 38.8 %copy-start = (bf16[1024,1024]{1,0:T(8,128)(2,1)S(1)}, bf16[1024,1024]{1,0:T(8,128)(2,1)}, u32[]{:S(2)}) copy-start(bf16[1024,1024]{1,0:T(8,128)(2,1)} %param.15) | copy-start | bytes 6291460
  0.6 3.8 %copy-start.10 = (bf16[2048,1024]{1,0:T(8,128)(2,1)S(1)}, bf16[2048,1024]{1,0:T(8,128)(2,1)}, u32[]{:S(2)}) copy-start(bf16[2048,1024]{1,0:T(8,128)(2,1)} %param.14) | copy-start | bytes 12582916
  0.7 3.9 %copy-start.11 = (bf16[1024,256]{1,0:T(8,128)(2,1)S(1)}, bf16[1024,256]{1,0:T(8,128)(2,1)}, u32[]{:S(2)}) copy-start(bf16[1024,256]{1,0:T(8,128)(2,1)} %param.18) | copy-start | bytes 1572868
  4.5 1.3 %copy-start.8 = (bf16[2048,256]{1,0:T(8,128)(2,1)}, bf16[2048,256]{1,0:T(8,128)(2,1)S(1)}, u32[]{:S(2)}) copy-start(bf16[2048,256]{1,0:T(8,128)(2,1)S(1)} %convolution_convert_fusion.v_ref) | copy-start | bytes 3145732
  5.8 10.2 %copy-start.9 = (bf16[2048,256]{1,0:T(8,128)(2,1)}, bf16[2048,256]{1,0:T(8,128)(2,1)S(1)}, u32[]{:S(2)}) copy-start(bf16[2048,256]{1,0:T(8,128)(2,1)S(1)} %convolution_convert_fusion.1.k_ref) | copy-start | bytes 3145732
  5.8 8.0 %copy-start.12 = (bf16[1024,256]{1,0:T(8,128)(2,1)S(1)}, bf16[1024,256]{1,0:T(8,128)(2,1)}, u32[]{:S(2)}) copy-start(bf16[1024,256]{1,0:T(8,128)(2,1)} %param.17) | copy-start | bytes 1572868
  5.9 11.8 %collective-permute-start.1 = (bf16[256,512]{1,0:T(8,128)(2,1)S(1)}, bf16[256,512]{1,0:T(8,128)(2,1)S(1)}, u32[]{:S(2)}, u32[]{:S(2)}) collective-permute-start(bf16[256,512]{1,0:T(8,128)(2,1)S(1)} %pad_maximum_fusion.3), channel_id=1, source_target_pairs={{4,0},{8,4},{12,8},{5,1},{9,5},{13,9},{6,2},{10,6},{14,10},{7,3},{... | collective-permute-start | bytes 786440 | tf_op jit(solution)/shard_map/ppermute | solution.py:21
  7.4 9.4 %copy-start.3 = (bf16[256,1024]{1,0:T(8,128)(2,1)S(1)}, bf16[256,1024]{1,0:T(8,128)(2,1)}, u32[]{:S(2)}) copy-start(bf16[256,1024]{1,0:T(8,128)(2,1)} %param.20) | copy-start | bytes 1572868
  7.4 11.2 %collective-permute-start = (bf16[256,512]{1,0:T(8,128)(2,1)S(1)}, bf16[256,512]{1,0:T(8,128)(2,1)}, u32[]{:S(2)}, u32[]{:S(2)}) collective-permute-start(bf16[256,512]{1,0:T(8,128)(2,1)S(1)} %pad_maximum_fusion.2), channel_id=1, source_target_pairs={{0,4},{4,8},{8,12},{1,5},{5,9},{9,13},{2,6},{6,10},{10,14},{3,7},{... | collective-permute-start | bytes 786440 | tf_op jit(solution)/shard_map/ppermute | solution.py:21
  16.7 1.9 %copy-start.15 = (s32[3]{0:T(128)}, s32[3]{0:T(128)S(1)}, u32[]{:S(2)}) copy-start(s32[3]{0:T(128)S(1)} %constant_dynamic-update-slice_fusion.scal_ref) | copy-start | bytes 40
  17.7 21.7 %copy-start.13 = (bf16[1024,256]{1,0:T(8,128)(2,1)S(1)}, bf16[1024,256]{1,0:T(8,128)(2,1)}, u32[]{:S(2)}) copy-start(bf16[1024,256]{1,0:T(8,128)(2,1)} %param.21) | copy-start | bytes 1572868
  17.7 0.9 copy-start.14
  39.4 4.5 %collective-permute-start.2 = (bf16[2,2048,256]{2,1,0:T(8,128)(2,1)}, bf16[2,2048,256]{2,1,0:T(8,128)(2,1)}, u32[]{:S(2)}, u32[]{:S(2)}) collective-permute-start(bf16[2,2048,256]{2,1,0:T(8,128)(2,1)} %get-tuple-element.35), channel_id=1, source_target_pairs={{0,1},{1,0},{2,3},{3,2},{4,5},{5,4},{6,7},{7,6},{8,9},{9,8},{10,11... | collective-permute-start | bytes 6291464 | tf_op jit(solution)/shard_map/ppermute | solution.py:241
  39.4 4.5 %copy-start.1 = (bf16[2,2048,256]{2,1,0:T(8,128)(2,1)S(1)}, bf16[2,2048,256]{2,1,0:T(8,128)(2,1)}, u32[]{:S(2)}) copy-start(bf16[2,2048,256]{2,1,0:T(8,128)(2,1)} %get-tuple-element.34) | copy-start | bytes 6291460
  64.0 1.5 %copy-start.2 = (f32[1024,256]{1,0:T(8,128)S(1)}, f32[1024,256]{1,0:T(8,128)}, u32[]{:S(2)}) copy-start(f32[1024,256]{1,0:T(8,128)} %get-tuple-element.40) | copy-start | bytes 3145732
  65.6 7.7 %copy-start.4 = (bf16[256,1024]{1,0:T(8,128)(2,1)S(1)}, bf16[256,1024]{1,0:T(8,128)(2,1)}, u32[]{:S(2)}) copy-start(bf16[256,1024]{1,0:T(8,128)(2,1)} %param.22) | copy-start | bytes 1572868
  66.7 10.6 %collective-permute-start.4 = (bf16[256,280]{1,0:T(8,128)(2,1)S(1)}, bf16[256,280]{1,0:T(8,128)(2,1)S(1)}, u32[]{:S(2)}, u32[]{:S(2)}) collective-permute-start(bf16[256,280]{1,0:T(8,128)(2,1)S(1)} %get-tuple-element.53), channel_id=1, source_target_pairs={{0,4},{4,8},{8,12},{12,0},{1,5},{5,9},{9,13},{13,1},{2,6},{6,10},{... | collective-permute-start | bytes 430088 | tf_op jit(solution)/shard_map/ppermute | solution.py:284
  69.3 15.9 %collective-permute-start.5 = (bf16[256,280]{1,0:T(8,128)(2,1)S(1)}, bf16[256,280]{1,0:T(8,128)(2,1)S(1)}, u32[]{:S(2)}, u32[]{:S(2)}) collective-permute-start(bf16[256,280]{1,0:T(8,128)(2,1)S(1)} %get-tuple-element.52), channel_id=1, source_target_pairs={{0,8},{4,12},{8,0},{12,4},{1,9},{5,13},{9,1},{13,5},{2,10},{6,14},... | collective-permute-start | bytes 430088 | tf_op jit(solution)/shard_map/ppermute | solution.py:284
  72.0 13.2 %collective-permute-start.6 = (bf16[256,280]{1,0:T(8,128)(2,1)S(1)}, bf16[256,280]{1,0:T(8,128)(2,1)S(1)}, u32[]{:S(2)}, u32[]{:S(2)}) collective-permute-start(bf16[256,280]{1,0:T(8,128)(2,1)S(1)} %get-tuple-element.51), channel_id=1, source_target_pairs={{0,12},{4,0},{8,4},{12,8},{1,13},{5,1},{9,5},{13,9},{2,14},{6,2},{... | collective-permute-start | bytes 430088 | tf_op jit(solution)/shard_map/ppermute | solution.py:284
  74.2 28.1 %collective-permute-start.3 = (bf16[2048,256]{1,0:T(8,128)(2,1)}, bf16[2048,256]{1,0:T(8,128)(2,1)}, u32[]{:S(2)}, u32[]{:S(2)}) collective-permute-start(bf16[2048,256]{1,0:T(8,128)(2,1)} %get-tuple-element.37), channel_id=1, source_target_pairs={{0,2},{1,3},{2,0},{3,1},{4,6},{5,7},{6,4},{7,5},{8,10},{9,11},{10,... | collective-permute-start | bytes 3145736 | tf_op jit(solution)/shard_map/ppermute | solution.py:256
  77.3 8.7 %copy-start.5 = (bf16[256,280]{1,0:T(8,128)(2,1)}, bf16[256,280]{1,0:T(8,128)(2,1)S(1)}, u32[]{:S(2)}) copy-start(bf16[256,280]{1,0:T(8,128)(2,1)S(1)} %collective-permute-done.4.refs_1_) | copy-start | bytes 430084
  85.2 0.8 copy-start.6
  85.2 0.7 copy-start.7
  90.5 1.6 %collective-permute-start.7 = (bf16[2,256,256]{2,1,0:T(8,128)(2,1)S(1)}, bf16[2,256,256]{2,1,0:T(8,128)(2,1)S(1)}, u32[]{:S(2)}, u32[]{:S(2)}) collective-permute-start(bf16[2,256,256]{2,1,0:T(8,128)(2,1)S(1)} %pad_maximum_fusion.4), channel_id=1, source_target_pairs={{0,1},{1,0},{2,3},{3,2},{4,5},{5,4},{6,7},{7,6},{8,9},{9,8},{10,11... | collective-permute-start | bytes 786440 | tf_op jit(solution)/shard_map/ppermute | solution.py:241
  92.2 9.4 %collective-permute-start.8 = (bf16[256,256]{1,0:T(8,128)(2,1)S(1)}, bf16[256,256]{1,0:T(8,128)(2,1)S(1)}, u32[]{:S(2)}, u32[]{:S(2)}) collective-permute-start(bf16[256,256]{1,0:T(8,128)(2,1)S(1)} %fusion.10), channel_id=1, source_target_pairs={{0,2},{1,3},{2,0},{3,1},{4,6},{5,7},{6,4},{7,5},{8,10},{9,11},{10,... | collective-permute-start | bytes 393224 | tf_op jit(solution)/shard_map/ppermute | solution.py:256
